TPU v7x, 32 devices: a whole 2x2x4 slice. The times are simulated.
32 devices in a mesh: corr: 2 (over x), tx: 8 (over z, core), ty: 2 (over y).
Axes of the slice: x: 2, y: 2, z: 4, core: 2. Of those that a mesh axis runs over, the one named last changes fastest.
Arguments:
- fields: float32 [2, 256, 64, 128], P(None, 'tx', 'ty'), may hold values from 0.5 to 3.5
- wind: float32 [2, 256, 64, 128], P(None, 'tx', 'ty'), may hold values from -4 to 4
- diffusion: float32 [2, 128], replicated, may hold values from 0.5 to 20
Outputs:
- levels: float32 [2, 2, 256, 64, 128], P('corr', None, 'tx', 'ty')
All inputs are finite; a program needn't handle non-finite values.
Results may differ from a plain program's by a relative error of at most 0.0003.
Values sent between devices are 32-bit elements; how exact they have to be, the bound alone decides.
No kernel may reach another device: no remote copies, remote signals or barrier semaphores. Data moves between devices by JAX's collectives and lax.ppermute only.
A program may use at most 64 MiB of HBM per device.

v0:
```python
import jax
import jax.numpy as jnp
import numpy as np
from jax import lax
from jax.experimental import pallas as pl
from jax.experimental.pallas import tpu as pltpu
from jax.sharding import PartitionSpec as P

STEPS = 8


DT = 0.1
A_RATE = 1.0
B_RATE = 3.0


def quad_cycle(count):
    table = np.zeros((count, 5))
    for m in range(count):
        first = max(0, m - 3)
        nodes = [float(j - m) for j in range(first, m + 2)]
        for i, xi in enumerate(nodes):
            coeffs = [1.0]
            for xo in nodes:
                if xo != xi:
                    widened = [0.0] * (len(coeffs) + 1)
                    for k, c in enumerate(coeffs):
                        widened[k] = widened[k] - xo * c / (xi - xo)
                        widened[k + 1] = widened[k + 1] + c / (xi - xo)
                    coeffs = widened
            integral = 0.0
            for k, c in enumerate(coeffs):
                integral = integral + c / (k + 1)
            table[m, first + i - (m - 3)] = integral
    return table


def thomas_kernel(diag_ref, up_ref, low_ref, out_ref, c_ref, d_ref):
    n = diag_ref.shape[0]
    lanes = lax.broadcasted_iota(jnp.int32, diag_ref.shape[1:], 1)
    zero = jnp.zeros(diag_ref.shape[1:], jnp.float32)

    def forward(j, carry):
        cprev, dprev = carry
        low = low_ref[j]
        inv = 1.0 / (diag_ref[j] + low * cprev)
        c = -up_ref[j] * inv
        d = (jnp.where(lanes == j, 1.0, 0.0) + low * dprev) * inv
        c_ref[j] = c
        d_ref[j] = d
        return c, d

    lax.fori_loop(0, n, forward, (zero, zero))

    def backward(i, x):
        j = n - 1 - i
        x = d_ref[j] - c_ref[j] * x
        out_ref[j] = x
        return x

    lax.fori_loop(0, n, backward, zero)


def vertical(diffusion):
    species, depth = diffusion.shape
    keep = (jnp.arange(depth) < depth - 1).astype(jnp.float32)
    upper = diffusion * keep[None, :]
    lower = jnp.concatenate([jnp.zeros((species, 1), jnp.float32), upper[:, :-1]], 1)

    def table(v):
        return jnp.broadcast_to(v.T[:, :, None], (depth, species, depth))

    rows = pl.pallas_call(
        thomas_kernel,
        out_shape=jax.ShapeDtypeStruct((depth, species, depth), jnp.float32),
        scratch_shapes=[pltpu.VMEM((depth, species, depth), jnp.float32)] * 2,
        cost_estimate=pl.CostEstimate(
            flops=12 * depth * species * depth,
            transcendentals=0,
            bytes_accessed=4 * 4 * depth * species * depth,
        ),
    )(table(1.0 + lower + upper), table(upper), table(lower))
    inverse = jnp.transpose(rows, (1, 0, 2))
    return (inverse, upper, lower)


def vertical_apply(w, upper, lower):
    zero_col = jnp.zeros(w.shape[:-1] + (1,), jnp.float32)
    beneath = jnp.concatenate([zero_col, w[..., :-1]], -1)
    overhead = jnp.concatenate([w[..., 1:], zero_col], -1)
    lo = lower[:, None, None, :]
    up = upper[:, None, None, :]
    return (lo + up) * w - lo * beneath - up * overhead


def ring_halo(block, axes, dim, width):
    sizes = [lax.axis_size(axis) for axis in axes]
    size = int(np.prod(sizes))

    def mesh_index(ring_pos):
        idx = []
        for n in sizes:
            idx.append(ring_pos % n)
            ring_pos //= n
        lin = 0
        for d, n in zip(idx, sizes):
            lin = lin * n + d
        return lin

    length = block.shape[dim]
    up = [(mesh_index(g), mesh_index((g + 1) % size)) for g in range(size)]
    down = [(j, i) for i, j in up]
    last = lax.slice_in_dim(block, length - width, length, axis=dim)
    first = lax.slice_in_dim(block, 0, width, axis=dim)
    before = lax.ppermute(last, axes, up)
    after = lax.ppermute(first, axes, down)
    return before, after


def tendency(state, wind):
    west, east = ring_halo(state, ("corr", "tx"), 2, 2)
    south, north = ring_halo(state, ("ty",), 3, 2)
    px = jnp.concatenate([west, state, east], 2)
    py = jnp.concatenate([south, state, north], 3)
    center = state
    dx1 = (
        -px[:, :, 4:] + 8.0 * px[:, :, 3:-1] - 8.0 * px[:, :, 1:-3] + px[:, :, :-4]
    ) / 12.0
    dx2 = (
        -px[:, :, 4:]
        + 16.0 * px[:, :, 3:-1]
        - 30.0 * center
        + 16.0 * px[:, :, 1:-3]
        - px[:, :, :-4]
    ) / 12.0
    dy1 = (
        -py[:, :, :, 4:]
        + 8.0 * py[:, :, :, 3:-1]
        - 8.0 * py[:, :, :, 1:-3]
        + py[:, :, :, :-4]
    ) / 12.0
    dy2 = (
        -py[:, :, :, 4:]
        + 16.0 * py[:, :, :, 3:-1]
        - 30.0 * center
        + 16.0 * py[:, :, :, 1:-3]
        - py[:, :, :, :-4]
    ) / 12.0
    kappa = jnp.array([0.5, 1.0], jnp.float32)[None, :, None, None, None]
    first = center[:, 0]
    second = center[:, 1]
    square_term = first * first * second
    react = jnp.stack(
        [A_RATE - (B_RATE + 1.0) * first + square_term, B_RATE * first - square_term], 1
    )
    flow = -(wind[0][None, None] * dx1 + wind[1][None, None] * dy1)
    return DT * (flow + kappa * (dx2 + dy2) + react)


def column_solve(rhs, inverse):
    return jnp.einsum(
        "lsxyk,sjk->lsxyj", rhs, inverse, precision=lax.Precision.HIGHEST
    )


def on_device(fields, wind, diffusion):
    inverse, upper, lower = vertical(diffusion)
    table = quad_cycle(STEPS)
    depth = lax.axis_size("corr")
    slab = fields.shape[1] // depth
    start = lax.axis_index("corr") * slab
    own_fields = lax.dynamic_slice_in_dim(fields, start, slab, 1)
    own_wind = lax.dynamic_slice_in_dim(wind, start, slab, 1)

    states = [own_fields] * depth
    e_hist = [dict() for _ in range(depth)]
    d_hist = [dict() for _ in range(depth)]
    g_now = [None] * depth
    for k in range(STEPS + depth - 1):
        active = [
            l for l in range(depth)
            if 0 <= k - l < STEPS or (k - l == STEPS and l < depth - 1)
        ]
        stacked = jnp.stack([states[l] for l in active], 0)
        own_e = tendency(stacked, own_wind)
        feeds = [l for l in active if l < depth - 1]
        if feeds:
            lows = [active.index(l) for l in feeds]
            lo, hi = lows[0], lows[-1] + 1
            own_g = vertical_apply(stacked[lo:hi], upper, lower)
            for i, l in enumerate(feeds):
                m = k - l
                g_now[l] = own_g[i]
                d_hist[l][m] = own_e[lo + i] - own_g[i]
        moving = [l for l in active if k - l < STEPS]
        rhs = []
        for l in moving:
            m = k - l
            i = active.index(l)
            e_hist[l][m] = own_e[i]
            total = states[l] + own_e[i]
            if l > 0:
                quad = None
                for slot in range(5):
                    node = m - 3 + slot
                    if node >= 0:
                        term = float(table[m, slot]) * d_hist[l - 1][node]
                        quad = term if quad is None else quad + term
                total = total + (quad + g_now[l - 1] - e_hist[l - 1][m])
            rhs.append(total)
        solved = column_solve(jnp.stack(rhs, 0), inverse)
        for i, l in enumerate(moving):
            states[l] = solved[i]
    me = lax.axis_index("corr")
    result = jnp.stack(states, 0)
    out = jnp.zeros((1,) + own_fields.shape[:1] + fields.shape[1:], jnp.float32)
    out = lax.dynamic_update_slice_in_dim(
        out, lax.dynamic_index_in_dim(result, me, 0), start, 2
    )
    for shift in range(1, depth):
        pairs = [(c, (c + shift) % depth) for c in range(depth)]
        sent = lax.dynamic_index_in_dim(result, (me + shift) % depth, 0)
        got = lax.ppermute(sent, "corr", pairs)
        origin = (me - shift) % depth
        out = lax.dynamic_update_slice_in_dim(out, got, origin * slab, 2)
    return out


def solution(mesh):
    placed = (P(None, "tx", "ty", None), P(None, "tx", "ty", None), P())
    return jax.shard_map(
        on_device,
        mesh=mesh,
        in_specs=placed,
        out_specs=P("corr", None, "tx", "ty", None),
        check_vma=False,
    )
```

profile of v0, /device:TPU:0, one launch (start us, length us, event | category | flops | bytes accessed | tf_op | source)
XLA Modules:
  0.0 143.5 jit_solution(16437013289413901730)
XLA Ops:
  1.8 5.4 %collective-permute-start = (f32[1,2,2,32,128]{4,3,2,1,0:T(8,128)}, f32[1,2,2,32,128]{4,3,2,1,0:T(8,128)}, u32[]{:S(2)}, u32[]{:S(2)}) collective-permute-start(f32[1,2,2,32,128]{4,3,2,1,0:T(8,128)} %get-tuple-element.100), channel_id=1, source_target_pairs={{16,0},{2,16},{18,2},{4,18},{20,4},{6,20},{22,6},{8,22},{24,8},{10... | collective-permute-start | bytes 196616 | tf_op jit(solution)/shard_map/ppermute | solution.py:116
  7.8 1.5 %collective-permute-start.2 = (f32[1,2,16,2,128]{4,3,2,1,0:T(2,128)}, f32[1,2,16,2,128]{4,3,2,1,0:T(2,128)}, u32[]{:S(2)}, u32[]{:S(2)}) collective-permute-start(f32[1,2,16,2,128]{4,3,2,1,0:T(2,128)} %get-tuple-element.102), channel_id=1, source_target_pairs={{1,0},{0,1},{3,2},{2,3},{5,4},{4,5},{7,6},{6,7},{9,8},{8,9},{11,10... | collective-permute-start | bytes 98312 | tf_op jit(solution)/shard_map/ppermute | solution.py:116
  14.1 1.4 copy.14
  17.2 1.7 %broadcast_in_dim.10.up_ref = f32[128,2,128]{2,1,0:T(2,128)} broadcast(f32[128,2]{1,0:T(8,128)} %copy.14), dimensions={0,1} | broadcast | bytes 132096 | tf_op jit(solution)/shard_map/broadcast_in_dim | solution.py:71
  18.9 3.9 %shard_map.118 = f32[128,2,128]{2,1,0:T(2,128)} custom-call(f32[128,2,128]{2,1,0:T(2,128)} %broadcast_in_dim.9.diag_ref, f32[128,2,128]{2,1,0:T(2,128)} %broadcast_in_dim.10.up_ref, f32[128,2,128]{2,1,0:T(2,128)} %broadcast_in_dim.11.low_ref), custom_call_target="tpu_custom_call" | custom-call | flops 393216 | bytes 524288 | tf_op jit(solution)/shard_map/pallas_call | solution.py:73
  22.8 1.8 %fusion.109 = f32[1,2,16,32,128]{4,3,2,1,0:T(8,128)S(1)} fusion(f32[1,1,16,32,128]{4,3,2,1,0:T(8,128)} %get-tuple-element.105, f32[1,1,16,32,128]{4,3,2,1,0:T(8,128)S(1)} %get-tuple-element.104, f32[1,2,16,32,128]{4,3,2,1,0:T(8,128)S(1)} %dynamic-slice_bitcast_fusion, f32[1,2,16,2,128]{4,3,2,1,0:T(2,128)} %collective-permute-done.3, ...), kind=kLoop, calls=%fused_computation.269 | loop fusion | flops 5767168 | bytes 2818060 | tf_op jit(solution)/shard_map/mul | solution.py:157
  25.7 1.6 %collective-permute-start.6 = (f32[2,2,16,2,128]{4,3,2,1,0:T(2,128)S(1)}, f32[2,2,16,2,128]{4,3,2,1,0:T(2,128)S(1)}, u32[]{:S(2)}, u32[]{:S(2)}) collective-permute-start(f32[2,2,16,2,128]{4,3,2,1,0:T(2,128)S(1)} %get-tuple-element.90), channel_id=1, source_target_pairs={{1,0},{0,1},{3,2},{2,3},{5,4},{4,5},{7,6},{6,7},{9,8},{8,9},{11,10... | collective-permute-start | bytes 196616 | tf_op jit(solution)/shard_map/ppermute | solution.py:116
  27.8 3.4 %collective-permute-start.4 = (f32[2,2,2,32,128]{4,3,2,1,0:T(8,128)S(1)}, f32[2,2,2,32,128]{4,3,2,1,0:T(8,128)S(1)}, u32[]{:S(2)}, u32[]{:S(2)}) collective-permute-start(f32[2,2,2,32,128]{4,3,2,1,0:T(8,128)S(1)} %get-tuple-element.86), channel_id=1, source_target_pairs={{16,0},{2,16},{18,2},{4,18},{20,4},{6,20},{22,6},{8,22},{24,8},{10... | collective-permute-start | bytes 393224 | tf_op jit(solution)/shard_map/ppermute | solution.py:116
  31.8 1.9 %collective-permute-done.4 = f32[2,2,2,32,128]{4,3,2,1,0:T(8,128)S(1)} collective-permute-done((f32[2,2,2,32,128]{4,3,2,1,0:T(8,128)S(1)}, f32[2,2,2,32,128]{4,3,2,1,0:T(8,128)S(1)}, u32[]{:S(2)}, u32[]{:S(2)}) %collective-permute-start.4) | collective-permute-done | bytes 131104 | tf_op jit(solution)/shard_map/ppermute | solution.py:116
  33.7 4.6 %collective-permute-done.5 = f32[2,2,2,32,128]{4,3,2,1,0:T(8,128)S(1)} collective-permute-done((f32[2,2,2,32,128]{4,3,2,1,0:T(8,128)S(1)}, f32[2,2,2,32,128]{4,3,2,1,0:T(8,128)S(1)}, u32[]{:S(2)}, u32[]{:S(2)}) %collective-permute-start.5) | collective-permute-done | bytes 131104 | tf_op jit(solution)/shard_map/ppermute | solution.py:115
  38.6 1.5 %fusion.43 = f32[2,2,16,32,128]{4,3,2,1,0:T(8,128)S(1)} fusion(f32[2,1,16,32,128]{4,3,2,1,0:T(8,128)S(1)} %get-tuple-element.93, f32[2,1,16,32,128]{4,3,2,1,0:T(8,128)S(1)} %get-tuple-element.92, f32[1,2,16,32,128]{4,3,2,1,0:T(8,128)S(1)} %dynamic-slice_bitcast_fusion, f32[1,2,16,32,128]{4,3,2,1,0:T(8,128)S(1)} %convolution_bitcast_fusion.8, ...), kind=kLoop, calls=%fused_computation.160 | loop fusion | flops 9699328 | bytes 12058632 | tf_op jit(solution)/shard_map/mul | solution.py:157
  42.1 2.0 %collective-permute-start.9 = (f32[2,2,2,32,128]{4,3,2,1,0:T(8,128)S(1)}, f32[2,2,2,32,128]{4,3,2,1,0:T(8,128)S(1)}, u32[]{:S(2)}, u32[]{:S(2)}) collective-permute-start(f32[2,2,2,32,128]{4,3,2,1,0:T(8,128)S(1)} %get-tuple-element.79), channel_id=1, source_target_pairs={{0,16},{16,2},{2,18},{18,4},{4,20},{20,6},{6,22},{22,8},{8,24},{24... | collective-permute-start | bytes 393224 | tf_op jit(solution)/shard_map/ppermute | solution.py:115
  44.1 1.5 %collective-permute-start.10 = (f32[2,2,16,2,128]{4,3,2,1,0:T(2,128)S(1)}, f32[2,2,16,2,128]{4,3,2,1,0:T(2,128)S(1)}, u32[]{:S(2)}, u32[]{:S(2)}) collective-permute-start(f32[2,2,16,2,128]{4,3,2,1,0:T(2,128)S(1)} %get-tuple-element.80), channel_id=1, source_target_pairs={{1,0},{0,1},{3,2},{2,3},{5,4},{4,5},{7,6},{6,7},{9,8},{8,9},{11,10... | collective-permute-start | bytes 196616 | tf_op jit(solution)/shard_map/ppermute | solution.py:116
  46.3 2.0 %collective-permute-done.10 = f32[2,2,16,2,128]{4,3,2,1,0:T(2,128)S(1)} collective-permute-done((f32[2,2,16,2,128]{4,3,2,1,0:T(2,128)S(1)}, f32[2,2,16,2,128]{4,3,2,1,0:T(2,128)S(1)}, u32[]{:S(2)}, u32[]{:S(2)}) %collective-permute-start.10) | collective-permute-done | bytes 65568 | tf_op jit(solution)/shard_map/ppermute | solution.py:116
  48.4 1.5 %collective-permute-done.11 = f32[2,2,16,2,128]{4,3,2,1,0:T(2,128)S(1)} collective-permute-done((f32[2,2,16,2,128]{4,3,2,1,0:T(2,128)S(1)}, f32[2,2,16,2,128]{4,3,2,1,0:T(2,128)S(1)}, u32[]{:S(2)}, u32[]{:S(2)}) %collective-permute-start.11) | collective-permute-done | bytes 65568 | tf_op jit(solution)/shard_map/ppermute | solution.py:115
  49.9 2.1 %fusion.47 = f32[2,2,16,32,128]{4,3,2,1,0:T(8,128)S(1)} fusion(f32[2,1,16,32,128]{4,3,2,1,0:T(8,128)S(1)} %get-tuple-element.83, f32[2,1,16,32,128]{4,3,2,1,0:T(8,128)S(1)} %get-tuple-element.82, f32[2,2,16,32,128]{4,3,2,1,0:T(8,128)S(1)} %convolution_bitcast_fusion.6, f32[2,2,16,2,128]{4,3,2,1,0:T(2,128)S(1)} %collective-permute-done.11, ...), kind=kLoop, calls=%fused_computation.165 | loop fusion | flops 11534336 | bytes 4063240 | tf_op jit(solution)/shard_map/mul | solution.py:157
  58.4 2.2 %collective-permute-done.14 = f32[2,2,16,2,128]{4,3,2,1,0:T(2,128)S(1)} collective-permute-done((f32[2,2,16,2,128]{4,3,2,1,0:T(2,128)S(1)}, f32[2,2,16,2,128]{4,3,2,1,0:T(2,128)S(1)}, u32[]{:S(2)}, u32[]{:S(2)}) %collective-permute-start.14) | collective-permute-done | bytes 65568 | tf_op jit(solution)/shard_map/ppermute | solution.py:116
  62.4 2.1 %fusion.51 = f32[2,2,16,32,128]{4,3,2,1,0:T(8,128)S(1)} fusion(f32[2,1,16,32,128]{4,3,2,1,0:T(8,128)S(1)} %get-tuple-element.75, f32[2,1,16,32,128]{4,3,2,1,0:T(8,128)S(1)} %get-tuple-element.74, f32[2,2,16,32,128]{4,3,2,1,0:T(8,128)S(1)} %convolution_bitcast_fusion.5, f32[2,2,16,2,128]{4,3,2,1,0:T(2,128)S(1)} %collective-permute-done.15, ...), kind=kLoop, calls=%fused_computation.170 | loop fusion | flops 11534336 | bytes 4063240 | tf_op jit(solution)/shard_map/mul | solution.py:157
  70.8 2.0 %collective-permute-done.18 = f32[2,2,16,2,128]{4,3,2,1,0:T(2,128)S(1)} collective-permute-done((f32[2,2,16,2,128]{4,3,2,1,0:T(2,128)S(1)}, f32[2,2,16,2,128]{4,3,2,1,0:T(2,128)S(1)}, u32[]{:S(2)}, u32[]{:S(2)}) %collective-permute-start.18) | collective-permute-done | bytes 65568 | tf_op jit(solution)/shard_map/ppermute | solution.py:116
  74.7 2.1 %fusion.55 = f32[2,2,16,32,128]{4,3,2,1,0:T(8,128)S(1)} fusion(f32[2,1,16,32,128]{4,3,2,1,0:T(8,128)S(1)} %get-tuple-element.67, f32[2,1,16,32,128]{4,3,2,1,0:T(8,128)S(1)} %get-tuple-element.66, f32[2,2,16,32,128]{4,3,2,1,0:T(8,128)S(1)} %convolution_bitcast_fusion.4, f32[2,2,16,2,128]{4,3,2,1,0:T(2,128)S(1)} %collective-permute-done.19, ...), kind=kLoop, calls=%fused_computation.175 | loop fusion | flops 11534336 | bytes 4063240 | tf_op jit(solution)/shard_map/mul | solution.py:157
  78.9 1.3 collective-permute-start.20
  83.3 2.0 %collective-permute-done.22 = f32[2,2,16,2,128]{4,3,2,1,0:T(2,128)S(1)} collective-permute-done((f32[2,2,16,2,128]{4,3,2,1,0:T(2,128)S(1)}, f32[2,2,16,2,128]{4,3,2,1,0:T(2,128)S(1)}, u32[]{:S(2)}, u32[]{:S(2)}) %collective-permute-start.22) | collective-permute-done | bytes 65568 | tf_op jit(solution)/shard_map/ppermute | solution.py:116
  87.3 2.1 %fusion.59 = f32[2,2,16,32,128]{4,3,2,1,0:T(8,128)S(1)} fusion(f32[2,1,16,32,128]{4,3,2,1,0:T(8,128)S(1)} %get-tuple-element.59, f32[2,1,16,32,128]{4,3,2,1,0:T(8,128)S(1)} %get-tuple-element.58, f32[2,2,16,32,128]{4,3,2,1,0:T(8,128)S(1)} %convolution_bitcast_fusion.3, f32[2,2,16,2,128]{4,3,2,1,0:T(2,128)S(1)} %collective-permute-done.23, ...), kind=kLoop, calls=%fused_computation.180 | loop fusion | flops 11534336 | bytes 4063240 | tf_op jit(solution)/shard_map/mul | solution.py:157
  95.7 2.0 %collective-permute-done.26 = f32[2,2,16,2,128]{4,3,2,1,0:T(2,128)S(1)} collective-permute-done((f32[2,2,16,2,128]{4,3,2,1,0:T(2,128)S(1)}, f32[2,2,16,2,128]{4,3,2,1,0:T(2,128)S(1)}, u32[]{:S(2)}, u32[]{:S(2)}) %collective-permute-start.26) | collective-permute-done | bytes 65568 | tf_op jit(solution)/shard_map/ppermute | solution.py:116
  99.7 2.1 %fusion.63 = f32[2,2,16,32,128]{4,3,2,1,0:T(8,128)S(1)} fusion(f32[2,1,16,32,128]{4,3,2,1,0:T(8,128)S(1)} %get-tuple-element.51, f32[2,1,16,32,128]{4,3,2,1,0:T(8,128)S(1)} %get-tuple-element.50, f32[2,2,16,32,128]{4,3,2,1,0:T(8,128)S(1)} %convolution_bitcast_fusion.2, f32[2,2,16,2,128]{4,3,2,1,0:T(2,128)S(1)} %collective-permute-done.27, ...), kind=kLoop, calls=%fused_computation.185 | loop fusion | flops 11534336 | bytes 4063240 | tf_op jit(solution)/shard_map/mul | solution.py:157
  103.9 1.3 collective-permute-start.28
  108.2 2.0 %collective-permute-done.30 = f32[2,2,16,2,128]{4,3,2,1,0:T(2,128)S(1)} collective-permute-done((f32[2,2,16,2,128]{4,3,2,1,0:T(2,128)S(1)}, f32[2,2,16,2,128]{4,3,2,1,0:T(2,128)S(1)}, u32[]{:S(2)}, u32[]{:S(2)}) %collective-permute-start.30) | collective-permute-done | bytes 65568 | tf_op jit(solution)/shard_map/ppermute | solution.py:116
  112.3 2.1 %fusion.67 = f32[2,2,16,32,128]{4,3,2,1,0:T(8,128)S(1)} fusion(f32[2,1,16,32,128]{4,3,2,1,0:T(8,128)S(1)} %get-tuple-element.43, f32[2,1,16,32,128]{4,3,2,1,0:T(8,128)S(1)} %get-tuple-element.42, f32[2,2,16,32,128]{4,3,2,1,0:T(8,128)S(1)} %convolution_bitcast_fusion.1, f32[2,2,16,2,128]{4,3,2,1,0:T(2,128)S(1)} %collective-permute-done.31, ...), kind=kLoop, calls=%fused_computation.190 | loop fusion | flops 11534336 | bytes 4063240 | tf_op jit(solution)/shard_map/mul | solution.py:157
  116.5 1.2 collective-permute-start.32
  120.8 2.0 %collective-permute-done.34 = f32[2,2,16,2,128]{4,3,2,1,0:T(2,128)S(1)} collective-permute-done((f32[2,2,16,2,128]{4,3,2,1,0:T(2,128)S(1)}, f32[2,2,16,2,128]{4,3,2,1,0:T(2,128)S(1)}, u32[]{:S(2)}, u32[]{:S(2)}) %collective-permute-start.34) | collective-permute-done | bytes 65568 | tf_op jit(solution)/shard_map/ppermute | solution.py:116
  124.8 2.1 %fusion.71 = f32[2,2,16,32,128]{4,3,2,1,0:T(8,128)S(1)} fusion(f32[2,1,16,32,128]{4,3,2,1,0:T(8,128)S(1)} %get-tuple-element.35, f32[2,1,16,32,128]{4,3,2,1,0:T(8,128)S(1)} %get-tuple-element.34, f32[2,2,16,32,128]{4,3,2,1,0:T(8,128)S(1)} %convolution_bitcast_fusion, f32[2,2,16,2,128]{4,3,2,1,0:T(2,128)S(1)} %collective-permute-done.35, ...), kind=kLoop, calls=%fused_computation.195 | loop fusion | flops 11534336 | bytes 4063240 | tf_op jit(solution)/shard_map/mul | solution.py:157
  130.5 12.2 %collective-permute-done.36 = f32[1,2,16,32,128]{4,3,2,1,0:T(8,128)S(1)} collective-permute-done((f32[1,2,16,32,128]{4,3,2,1,0:T(8,128)S(1)}, f32[1,2,16,32,128]{4,3,2,1,0:T(8,128)S(1)}, u32[]{:S(2)}, u32[]{:S(2)}) %collective-permute-start.36) | collective-permute-done | bytes 524320 | tf_op jit(solution)/shard_map/ppermute | solution.py:223
  (136 shorter events, 64.0 us)
Async XLA Ops:
  1.8 21.0 %collective-permute-start = (f32[1,2,2,32,128]{4,3,2,1,0:T(8,128)}, f32[1,2,2,32,128]{4,3,2,1,0:T(8,128)}, u32[]{:S(2)}, u32[]{:S(2)}) collective-permute-start(f32[1,2,2,32,128]{4,3,2,1,0:T(8,128)} %get-tuple-element.100), channel_id=1, source_target_pairs={{16,0},{2,16},{18,2},{4,18},{20,4},{6,20},{22,6},{8,22},{24,8},{10... | collective-permute-start | bytes 196616 | tf_op jit(solution)/shard_map/ppermute | solution.py:116
  7.2 15.6 %collective-permute-start.1 = (f32[1,2,2,32,128]{4,3,2,1,0:T(8,128)}, f32[1,2,2,32,128]{4,3,2,1,0:T(8,128)}, u32[]{:S(2)}, u32[]{:S(2)}) collective-permute-start(f32[1,2,2,32,128]{4,3,2,1,0:T(8,128)} %get-tuple-element.101), channel_id=1, source_target_pairs={{0,16},{16,2},{2,18},{18,4},{4,20},{20,6},{6,22},{22,8},{8,24},{24... | collective-permute-start | bytes 196616 | tf_op jit(solution)/shard_map/ppermute | solution.py:115
  7.8 14.9 %collective-permute-start.2 = (f32[1,2,16,2,128]{4,3,2,1,0:T(2,128)}, f32[1,2,16,2,128]{4,3,2,1,0:T(2,128)}, u32[]{:S(2)}, u32[]{:S(2)}) collective-permute-start(f32[1,2,16,2,128]{4,3,2,1,0:T(2,128)} %get-tuple-element.102), channel_id=1, source_target_pairs={{1,0},{0,1},{3,2},{2,3},{5,4},{4,5},{7,6},{6,7},{9,8},{8,9},{11,10... | collective-permute-start | bytes 98312 | tf_op jit(solution)/shard_map/ppermute | solution.py:116
  9.3 13.4 %collective-permute-start.3 = (f32[1,2,16,2,128]{4,3,2,1,0:T(2,128)}, f32[1,2,16,2,128]{4,3,2,1,0:T(2,128)}, u32[]{:S(2)}, u32[]{:S(2)}) collective-permute-start(f32[1,2,16,2,128]{4,3,2,1,0:T(2,128)} %get-tuple-element.103), channel_id=1, source_target_pairs={{0,1},{1,0},{2,3},{3,2},{4,5},{5,4},{6,7},{7,6},{8,9},{9,8},{10,11... | collective-permute-start | bytes 98312 | tf_op jit(solution)/shard_map/ppermute | solution.py:115
  25.7 5.5 %collective-permute-start.6 = (f32[2,2,16,2,128]{4,3,2,1,0:T(2,128)S(1)}, f32[2,2,16,2,128]{4,3,2,1,0:T(2,128)S(1)}, u32[]{:S(2)}, u32[]{:S(2)}) collective-permute-start(f32[2,2,16,2,128]{4,3,2,1,0:T(2,128)S(1)} %get-tuple-element.90), channel_id=1, source_target_pairs={{1,0},{0,1},{3,2},{2,3},{5,4},{4,5},{7,6},{6,7},{9,8},{8,9},{11,10... | collective-permute-start | bytes 196616 | tf_op jit(solution)/shard_map/ppermute | solution.py:116
  27.3 4.3 %collective-permute-start.7 = (f32[2,2,16,2,128]{4,3,2,1,0:T(2,128)S(1)}, f32[2,2,16,2,128]{4,3,2,1,0:T(2,128)S(1)}, u32[]{:S(2)}, u32[]{:S(2)}) collective-permute-start(f32[2,2,16,2,128]{4,3,2,1,0:T(2,128)S(1)} %get-tuple-element.91), channel_id=1, source_target_pairs={{0,1},{1,0},{2,3},{3,2},{4,5},{5,4},{6,7},{7,6},{8,9},{9,8},{10,11... | collective-permute-start | bytes 196616 | tf_op jit(solution)/shard_map/ppermute | solution.py:115
  27.8 5.9 %collective-permute-start.4 = (f32[2,2,2,32,128]{4,3,2,1,0:T(8,128)S(1)}, f32[2,2,2,32,128]{4,3,2,1,0:T(8,128)S(1)}, u32[]{:S(2)}, u32[]{:S(2)}) collective-permute-start(f32[2,2,2,32,128]{4,3,2,1,0:T(8,128)S(1)} %get-tuple-element.86), channel_id=1, source_target_pairs={{16,0},{2,16},{18,2},{4,18},{20,4},{6,20},{22,6},{8,22},{24,8},{10... | collective-permute-start | bytes 393224 | tf_op jit(solution)/shard_map/ppermute | solution.py:116
  31.2 7.1 %collective-permute-start.5 = (f32[2,2,2,32,128]{4,3,2,1,0:T(8,128)S(1)}, f32[2,2,2,32,128]{4,3,2,1,0:T(8,128)S(1)}, u32[]{:S(2)}, u32[]{:S(2)}) collective-permute-start(f32[2,2,2,32,128]{4,3,2,1,0:T(8,128)S(1)} %get-tuple-element.87), channel_id=1, source_target_pairs={{0,16},{16,2},{2,18},{18,4},{4,20},{20,6},{6,22},{22,8},{8,24},{24... | collective-permute-start | bytes 393224 | tf_op jit(solution)/shard_map/ppermute | solution.py:115
  42.0 7.9 %collective-permute-start.8 = (f32[2,2,2,32,128]{4,3,2,1,0:T(8,128)S(1)}, f32[2,2,2,32,128]{4,3,2,1,0:T(8,128)S(1)}, u32[]{:S(2)}, u32[]{:S(2)}) collective-permute-start(f32[2,2,2,32,128]{4,3,2,1,0:T(8,128)S(1)} %get-tuple-element.78), channel_id=1, source_target_pairs={{16,0},{2,16},{18,2},{4,18},{20,4},{6,20},{22,6},{8,22},{24,8},{10... | collective-permute-start | bytes 393224 | tf_op jit(solution)/shard_map/ppermute | solution.py:116
  42.1 7.8 %collective-permute-start.9 = (f32[2,2,2,32,128]{4,3,2,1,0:T(8,128)S(1)}, f32[2,2,2,32,128]{4,3,2,1,0:T(8,128)S(1)}, u32[]{:S(2)}, u32[]{:S(2)}) collective-permute-start(f32[2,2,2,32,128]{4,3,2,1,0:T(8,128)S(1)} %get-tuple-element.79), channel_id=1, source_target_pairs={{0,16},{16,2},{2,18},{18,4},{4,20},{20,6},{6,22},{22,8},{8,24},{24... | collective-permute-start | bytes 393224 | tf_op jit(solution)/shard_map/ppermute | solution.py:115
  44.1 4.3 %collective-permute-start.10 = (f32[2,2,16,2,128]{4,3,2,1,0:T(2,128)S(1)}, f32[2,2,16,2,128]{4,3,2,1,0:T(2,128)S(1)}, u32[]{:S(2)}, u32[]{:S(2)}) collective-permute-start(f32[2,2,16,2,128]{4,3,2,1,0:T(2,128)S(1)} %get-tuple-element.80), channel_id=1, source_target_pairs={{1,0},{0,1},{3,2},{2,3},{5,4},{4,5},{7,6},{6,7},{9,8},{8,9},{11,10... | collective-permute-start | bytes 196616 | tf_op jit(solution)/shard_map/ppermute | solution.py:116
  45.6 4.3 %collective-permute-start.11 = (f32[2,2,16,2,128]{4,3,2,1,0:T(2,128)S(1)}, f32[2,2,16,2,128]{4,3,2,1,0:T(2,128)S(1)}, u32[]{:S(2)}, u32[]{:S(2)}) collective-permute-start(f32[2,2,16,2,128]{4,3,2,1,0:T(2,128)S(1)} %get-tuple-element.81), channel_id=1, source_target_pairs={{0,1},{1,0},{2,3},{3,2},{4,5},{5,4},{6,7},{7,6},{8,9},{9,8},{10,11... | collective-permute-start | bytes 196616 | tf_op jit(solution)/shard_map/ppermute | solution.py:115
  54.0 7.3 %collective-permute-start.12 = (f32[2,2,2,32,128]{4,3,2,1,0:T(8,128)S(1)}, f32[2,2,2,32,128]{4,3,2,1,0:T(8,128)S(1)}, u32[]{:S(2)}, u32[]{:S(2)}) collective-permute-start(f32[2,2,2,32,128]{4,3,2,1,0:T(8,128)S(1)} %get-tuple-element.70), channel_id=1, source_target_pairs={{16,0},{2,16},{18,2},{4,18},{20,4},{6,20},{22,6},{8,22},{24,8},{10... | collective-permute-start | bytes 393224 | tf_op jit(solution)/shard_map/ppermute | solution.py:116
  55.2 7.2 %collective-permute-start.13 = (f32[2,2,2,32,128]{4,3,2,1,0:T(8,128)S(1)}, f32[2,2,2,32,128]{4,3,2,1,0:T(8,128)S(1)}, u32[]{:S(2)}, u32[]{:S(2)}) collective-permute-start(f32[2,2,2,32,128]{4,3,2,1,0:T(8,128)S(1)} %get-tuple-element.71), channel_id=1, source_target_pairs={{0,16},{16,2},{2,18},{18,4},{4,20},{20,6},{6,22},{22,8},{8,24},{24... | collective-permute-start | bytes 393224 | tf_op jit(solution)/shard_map/ppermute | solution.py:115
  56.1 4.5 %collective-permute-start.14 = (f32[2,2,16,2,128]{4,3,2,1,0:T(2,128)S(1)}, f32[2,2,16,2,128]{4,3,2,1,0:T(2,128)S(1)}, u32[]{:S(2)}, u32[]{:S(2)}) collective-permute-start(f32[2,2,16,2,128]{4,3,2,1,0:T(2,128)S(1)} %get-tuple-element.72), channel_id=1, source_target_pairs={{1,0},{0,1},{3,2},{2,3},{5,4},{4,5},{7,6},{6,7},{9,8},{8,9},{11,10... | collective-permute-start | bytes 196616 | tf_op jit(solution)/shard_map/ppermute | solution.py:116
  57.1 4.3 %collective-permute-start.15 = (f32[2,2,16,2,128]{4,3,2,1,0:T(2,128)S(1)}, f32[2,2,16,2,128]{4,3,2,1,0:T(2,128)S(1)}, u32[]{:S(2)}, u32[]{:S(2)}) collective-permute-start(f32[2,2,16,2,128]{4,3,2,1,0:T(2,128)S(1)} %get-tuple-element.73), channel_id=1, source_target_pairs={{0,1},{1,0},{2,3},{3,2},{4,5},{5,4},{6,7},{7,6},{8,9},{9,8},{10,11... | collective-permute-start | bytes 196616 | tf_op jit(solution)/shard_map/ppermute | solution.py:115
  66.5 7.3 %collective-permute-start.16 = (f32[2,2,2,32,128]{4,3,2,1,0:T(8,128)S(1)}, f32[2,2,2,32,128]{4,3,2,1,0:T(8,128)S(1)}, u32[]{:S(2)}, u32[]{:S(2)}) collective-permute-start(f32[2,2,2,32,128]{4,3,2,1,0:T(8,128)S(1)} %get-tuple-element.62), channel_id=1, source_target_pairs={{16,0},{2,16},{18,2},{4,18},{20,4},{6,20},{22,6},{8,22},{24,8},{10... | collective-permute-start | bytes 393224 | tf_op jit(solution)/shard_map/ppermute | solution.py:116
  67.6 7.1 %collective-permute-start.17 = (f32[2,2,2,32,128]{4,3,2,1,0:T(8,128)S(1)}, f32[2,2,2,32,128]{4,3,2,1,0:T(8,128)S(1)}, u32[]{:S(2)}, u32[]{:S(2)}) collective-permute-start(f32[2,2,2,32,128]{4,3,2,1,0:T(8,128)S(1)} %get-tuple-element.63), channel_id=1, source_target_pairs={{0,16},{16,2},{2,18},{18,4},{4,20},{20,6},{6,22},{22,8},{8,24},{24... | collective-permute-start | bytes 393224 | tf_op jit(solution)/shard_map/ppermute | solution.py:115
  78.9 7.4 %collective-permute-start.20 = (f32[2,2,2,32,128]{4,3,2,1,0:T(8,128)S(1)}, f32[2,2,2,32,128]{4,3,2,1,0:T(8,128)S(1)}, u32[]{:S(2)}, u32[]{:S(2)}) collective-permute-start(f32[2,2,2,32,128]{4,3,2,1,0:T(8,128)S(1)} %get-tuple-element.54), channel_id=1, source_target_pairs={{16,0},{2,16},{18,2},{4,18},{20,4},{6,20},{22,6},{8,22},{24,8},{10... | collective-permute-start | bytes 393224 | tf_op jit(solution)/shard_map/ppermute | solution.py:116
  80.2 7.1 %collective-permute-start.21 = (f32[2,2,2,32,128]{4,3,2,1,0:T(8,128)S(1)}, f32[2,2,2,32,128]{4,3,2,1,0:T(8,128)S(1)}, u32[]{:S(2)}, u32[]{:S(2)}) collective-permute-start(f32[2,2,2,32,128]{4,3,2,1,0:T(8,128)S(1)} %get-tuple-element.55), channel_id=1, source_target_pairs={{0,16},{16,2},{2,18},{18,4},{4,20},{20,6},{6,22},{22,8},{8,24},{24... | collective-permute-start | bytes 393224 | tf_op jit(solution)/shard_map/ppermute | solution.py:115
  82.1 4.3 %collective-permute-start.23 = (f32[2,2,16,2,128]{4,3,2,1,0:T(2,128)S(1)}, f32[2,2,16,2,128]{4,3,2,1,0:T(2,128)S(1)}, u32[]{:S(2)}, u32[]{:S(2)}) collective-permute-start(f32[2,2,16,2,128]{4,3,2,1,0:T(2,128)S(1)} %get-tuple-element.57), channel_id=1, source_target_pairs={{0,1},{1,0},{2,3},{3,2},{4,5},{5,4},{6,7},{7,6},{8,9},{9,8},{10,11... | collective-permute-start | bytes 196616 | tf_op jit(solution)/shard_map/ppermute | solution.py:115
  91.4 7.3 %collective-permute-start.24 = (f32[2,2,2,32,128]{4,3,2,1,0:T(8,128)S(1)}, f32[2,2,2,32,128]{4,3,2,1,0:T(8,128)S(1)}, u32[]{:S(2)}, u32[]{:S(2)}) collective-permute-start(f32[2,2,2,32,128]{4,3,2,1,0:T(8,128)S(1)} %get-tuple-element.46), channel_id=1, source_target_pairs={{16,0},{2,16},{18,2},{4,18},{20,4},{6,20},{22,6},{8,22},{24,8},{10... | collective-permute-start | bytes 393224 | tf_op jit(solution)/shard_map/ppermute | solution.py:116
  92.6 7.1 %collective-permute-start.25 = (f32[2,2,2,32,128]{4,3,2,1,0:T(8,128)S(1)}, f32[2,2,2,32,128]{4,3,2,1,0:T(8,128)S(1)}, u32[]{:S(2)}, u32[]{:S(2)}) collective-permute-start(f32[2,2,2,32,128]{4,3,2,1,0:T(8,128)S(1)} %get-tuple-element.47), channel_id=1, source_target_pairs={{0,16},{16,2},{2,18},{18,4},{4,20},{20,6},{6,22},{22,8},{8,24},{24... | collective-permute-start | bytes 393224 | tf_op jit(solution)/shard_map/ppermute | solution.py:115
  93.5 4.3 %collective-permute-start.26 = (f32[2,2,16,2,128]{4,3,2,1,0:T(2,128)S(1)}, f32[2,2,16,2,128]{4,3,2,1,0:T(2,128)S(1)}, u32[]{:S(2)}, u32[]{:S(2)}) collective-permute-start(f32[2,2,16,2,128]{4,3,2,1,0:T(2,128)S(1)} %get-tuple-element.48), channel_id=1, source_target_pairs={{1,0},{0,1},{3,2},{2,3},{5,4},{4,5},{7,6},{6,7},{9,8},{8,9},{11,10... | collective-permute-start | bytes 196616 | tf_op jit(solution)/shard_map/ppermute | solution.py:116
  94.4 4.3 %collective-permute-start.27 = (f32[2,2,16,2,128]{4,3,2,1,0:T(2,128)S(1)}, f32[2,2,16,2,128]{4,3,2,1,0:T(2,128)S(1)}, u32[]{:S(2)}, u32[]{:S(2)}) collective-permute-start(f32[2,2,16,2,128]{4,3,2,1,0:T(2,128)S(1)} %get-tuple-element.49), channel_id=1, source_target_pairs={{0,1},{1,0},{2,3},{3,2},{4,5},{5,4},{6,7},{7,6},{8,9},{9,8},{10,11... | collective-permute-start | bytes 196616 | tf_op jit(solution)/shard_map/ppermute | solution.py:115
  103.9 7.4 %collective-permute-start.28 = (f32[2,2,2,32,128]{4,3,2,1,0:T(8,128)S(1)}, f32[2,2,2,32,128]{4,3,2,1,0:T(8,128)S(1)}, u32[]{:S(2)}, u32[]{:S(2)}) collective-permute-start(f32[2,2,2,32,128]{4,3,2,1,0:T(8,128)S(1)} %get-tuple-element.38), channel_id=1, source_target_pairs={{16,0},{2,16},{18,2},{4,18},{20,4},{6,20},{22,6},{8,22},{24,8},{10... | collective-permute-start | bytes 393224 | tf_op jit(solution)/shard_map/ppermute | solution.py:116
  105.2 7.1 %collective-permute-start.29 = (f32[2,2,2,32,128]{4,3,2,1,0:T(8,128)S(1)}, f32[2,2,2,32,128]{4,3,2,1,0:T(8,128)S(1)}, u32[]{:S(2)}, u32[]{:S(2)}) collective-permute-start(f32[2,2,2,32,128]{4,3,2,1,0:T(8,128)S(1)} %get-tuple-element.39), channel_id=1, source_target_pairs={{0,16},{16,2},{2,18},{18,4},{4,20},{20,6},{6,22},{22,8},{8,24},{24... | collective-permute-start | bytes 393224 | tf_op jit(solution)/shard_map/ppermute | solution.py:115
  107.0 4.3 %collective-permute-start.31 = (f32[2,2,16,2,128]{4,3,2,1,0:T(2,128)S(1)}, f32[2,2,16,2,128]{4,3,2,1,0:T(2,128)S(1)}, u32[]{:S(2)}, u32[]{:S(2)}) collective-permute-start(f32[2,2,16,2,128]{4,3,2,1,0:T(2,128)S(1)} %get-tuple-element.41), channel_id=1, source_target_pairs={{0,1},{1,0},{2,3},{3,2},{4,5},{5,4},{6,7},{7,6},{8,9},{9,8},{10,11... | collective-permute-start | bytes 196616 | tf_op jit(solution)/shard_map/ppermute | solution.py:115
  116.5 7.3 %collective-permute-start.32 = (f32[2,2,2,32,128]{4,3,2,1,0:T(8,128)S(1)}, f32[2,2,2,32,128]{4,3,2,1,0:T(8,128)S(1)}, u32[]{:S(2)}, u32[]{:S(2)}) collective-permute-start(f32[2,2,2,32,128]{4,3,2,1,0:T(8,128)S(1)} %get-tuple-element.30), channel_id=1, source_target_pairs={{16,0},{2,16},{18,2},{4,18},{20,4},{6,20},{22,6},{8,22},{24,8},{10... | collective-permute-start | bytes 393224 | tf_op jit(solution)/shard_map/ppermute | solution.py:116
  117.7 7.1 %collective-permute-start.33 = (f32[2,2,2,32,128]{4,3,2,1,0:T(8,128)S(1)}, f32[2,2,2,32,128]{4,3,2,1,0:T(8,128)S(1)}, u32[]{:S(2)}, u32[]{:S(2)}) collective-permute-start(f32[2,2,2,32,128]{4,3,2,1,0:T(8,128)S(1)} %get-tuple-element.31), channel_id=1, source_target_pairs={{0,16},{16,2},{2,18},{18,4},{4,20},{20,6},{6,22},{22,8},{8,24},{24... | collective-permute-start | bytes 393224 | tf_op jit(solution)/shard_map/ppermute | solution.py:115
  119.6 4.3 %collective-permute-start.35 = (f32[2,2,16,2,128]{4,3,2,1,0:T(2,128)S(1)}, f32[2,2,16,2,128]{4,3,2,1,0:T(2,128)S(1)}, u32[]{:S(2)}, u32[]{:S(2)}) collective-permute-start(f32[2,2,16,2,128]{4,3,2,1,0:T(2,128)S(1)} %get-tuple-element.33), channel_id=1, source_target_pairs={{0,1},{1,0},{2,3},{3,2},{4,5},{5,4},{6,7},{7,6},{8,9},{9,8},{10,11... | collective-permute-start | bytes 196616 | tf_op jit(solution)/shard_map/ppermute | solution.py:115
  129.4 13.2 %collective-permute-start.36 = (f32[1,2,16,32,128]{4,3,2,1,0:T(8,128)S(1)}, f32[1,2,16,32,128]{4,3,2,1,0:T(8,128)S(1)}, u32[]{:S(2)}, u32[]{:S(2)}) collective-permute-start(f32[1,2,16,32,128]{4,3,2,1,0:T(8,128)S(1)} %get-tuple-element.26), channel_id=1, source_target_pairs={{0,16},{16,0},{1,17},{17,1},{2,18},{18,2},{3,19},{19,3},{4,20},{20... | collective-permute-start | bytes 1572872 | tf_op jit(solution)/shard_map/ppermute | solution.py:223
  (12 other events, 81.5 us)
where the time goes:
time: 144 us; the launch traced here: 143 us
  waiting for transfers between devices  46.7 us (32%)
  starting transfers between devices  42.7 us (30%)
  other arithmetic  28.6 us (20%)
  local copies, waits for them, and re-layouts  12.3 us (9%)
  matrix products  8.79 us (6%)
  Pallas kernels  3.89 us (3%)
    ppermute x18, starting transfers between devices, ring_halo(): after = lax.ppermute(first, axes, down)  26.8 us
    ppermute x18, waiting for transfers between devices, ring_halo(): before = lax.ppermute(last, axes, up)  18.1 us
    mul x9, other arithmetic, tendency(): return DT * (flow + kappa * (dx2 + dy2) + react)  18.1 us
    ppermute x18, waiting for transfers between devices, ring_halo(): after = lax.ppermute(first, axes, down)  16.3 us
    ppermute x18, starting transfers between devices, ring_halo(): before = lax.ppermute(last, axes, up)  14.9 us
    ppermute x1, waiting for transfers between devices, on_device(): got = lax.ppermute(sent, 'corr', pairs)  12.2 us
    dot_general x9, matrix products, column_solve(): jnp.einsum('lsxyk,sjk->lsxyj', rhs, inverse, precision=lax.Precision.HIGH...  8.79 us
    pallas_call x1, Pallas kernels, vertical(): pl.pallas_call(thomas_kernel, out_shape=jax.ShapeDtypeStruct((depth, spec...  3.89 us
  transfers between devices with their start and end apart: 37, of which 24 were waited for; matrix products, arithmetic and copies ran while one was open for 8% of the time, Pallas kernels for 3%

commit v1 on v0

--- a/solution.py
+++ b/solution.py
@@ -35,16 +35,25 @@
     return table
 
 
-def thomas_kernel(diag_ref, up_ref, low_ref, out_ref, c_ref, d_ref):
-    n = diag_ref.shape[0]
-    lanes = lax.broadcasted_iota(jnp.int32, diag_ref.shape[1:], 1)
-    zero = jnp.zeros(diag_ref.shape[1:], jnp.float32)
+def thomas_kernel(up_ref, low_ref, out_ref, c_ref, d_ref):
+    n = out_ref.shape[0]
+    shape = out_ref.shape[1:]
+    lanes = lax.broadcasted_iota(jnp.int32, shape, 1)
+    species = lax.broadcasted_iota(jnp.int32, shape, 0)
+    zero = jnp.zeros(shape, jnp.float32)
+
+    def column(ref, j):
+        value = jnp.full(shape, ref[0, j], jnp.float32)
+        for s in range(1, shape[0]):
+            value = jnp.where(species == s, ref[s, j], value)
+        return value
 
     def forward(j, carry):
         cprev, dprev = carry
-        low = low_ref[j]
-        inv = 1.0 / (diag_ref[j] + low * cprev)
-        c = -up_ref[j] * inv
+        up = column(up_ref, j)
+        low = column(low_ref, j)
+        inv = 1.0 / ((1.0 + low + up) + low * cprev)
+        c = -up * inv
         d = (jnp.where(lanes == j, 1.0, 0.0) + low * dprev) * inv
         c_ref[j] = c
         d_ref[j] = d
@@ -66,20 +75,17 @@
     keep = (jnp.arange(depth) < depth - 1).astype(jnp.float32)
     upper = diffusion * keep[None, :]
     lower = jnp.concatenate([jnp.zeros((species, 1), jnp.float32), upper[:, :-1]], 1)
-
-    def table(v):
-        return jnp.broadcast_to(v.T[:, :, None], (depth, species, depth))
-
     rows = pl.pallas_call(
         thomas_kernel,
         out_shape=jax.ShapeDtypeStruct((depth, species, depth), jnp.float32),
+        in_specs=[pl.BlockSpec(memory_space=pltpu.SMEM)] * 2,
         scratch_shapes=[pltpu.VMEM((depth, species, depth), jnp.float32)] * 2,
         cost_estimate=pl.CostEstimate(
             flops=12 * depth * species * depth,
             transcendentals=0,
-            bytes_accessed=4 * 4 * depth * species * depth,
+            bytes_accessed=4 * 2 * depth * species * depth,
         ),
-    )(table(1.0 + lower + upper), table(upper), table(lower))
+    )(upper, lower)
     inverse = jnp.transpose(rows, (1, 0, 2))
     return (inverse, upper, lower)
 
@@ -112,6 +118,11 @@
     down = [(j, i) for i, j in up]
     last = lax.slice_in_dim(block, length - width, length, axis=dim)
     first = lax.slice_in_dim(block, 0, width, axis=dim)
+    if size == 2:
+        got = lax.ppermute(jnp.concatenate([first, last], dim), axes, up)
+        after = lax.slice_in_dim(got, 0, width, axis=dim)
+        before = lax.slice_in_dim(got, width, 2 * width, axis=dim)
+        return before, after
     before = lax.ppermute(last, axes, up)
     after = lax.ppermute(first, axes, down)
     return before, after

time: 144 us -> 144 us (level)
  waiting for transfers between devices: 46.7 us -> 56.6 us
  local copies, waits for them, and re-layouts: 12.3 us -> 6.89 us
  starting transfers between devices: 42.7 us -> 39.3 us
    ppermute x0 -> x9, waiting for transfers between devices: none -> 17.4 us  [ring_halo(): got = lax.ppermute(jnp.concatenate([first, last], dim), axes, up)]
    ppermute x0 -> x9, starting transfers between devices: none -> 10.6 us  [ring_halo(): got = lax.ppermute(jnp.concatenate([first, last], dim), axes, up)]
    ppermute x18 -> x9, waiting for transfers between devices: 16.3 us -> 7.67 us  [ring_halo(): after = lax.ppermute(first, axes, down)]
    ppermute x18 -> x9, starting transfers between devices: 26.8 us -> 18.6 us  [ring_halo(): after = lax.ppermute(first, axes, down)]
    ppermute x18 -> x9, starting transfers between devices: 14.9 us -> 8.8 us  [ring_halo(): before = lax.ppermute(last, axes, up)]
    broadcast_in_dim x3 -> x0, local copies, waits for them, and re-layouts: 3.41 us -> none  [table(): return jnp.broadcast_to(v.T[:, :, None], (depth, species, depth))]
    transpose x3 -> x0, local copies, waits for them, and re-layouts: 2.28 us -> none  [table(): return jnp.broadcast_to(v.T[:, :, None], (depth, species, depth))]
    ppermute x18 -> x9, waiting for transfers between devices: 18.1 us -> 18.2 us  [ring_halo(): before = lax.ppermute(last, axes, up)]
  transfers between devices with their start and end apart: 37 -> 28, of which waited for: 24 -> 21; matrix products, arithmetic and copies ran while one was open for 8% -> 3% of each run, Pallas kernels for 3% -> 3%
where the time goes in v1:
time: 144 us
  waiting for transfers between devices  56.6 us (39%)
  starting transfers between devices  39.3 us (27%)
  other arithmetic  27.4 us (19%)
  matrix products  8.78 us (6%)
  local copies, waits for them, and re-layouts  6.89 us (5%)
  Pallas kernels  4.11 us (3%)
    ppermute x9, starting transfers between devices, ring_halo(): after = lax.ppermute(first, axes, down)  18.6 us
    ppermute x9, waiting for transfers between devices, ring_halo(): before = lax.ppermute(last, axes, up)  18.2 us
    ppermute x9, waiting for transfers between devices, ring_halo(): got = lax.ppermute(jnp.concatenate([first, last], dim), axes, up)  17.4 us
    mul x9, other arithmetic, tendency(): return DT * (flow + kappa * (dx2 + dy2) + react)  17 us
    ppermute x1, waiting for transfers between devices, on_device(): got = lax.ppermute(sent, 'corr', pairs)  13.3 us
    ppermute x9, starting transfers between devices, ring_halo(): got = lax.ppermute(jnp.concatenate([first, last], dim), axes, up)  10.6 us
    ppermute x9, starting transfers between devices, ring_halo(): before = lax.ppermute(last, axes, up)  8.8 us
    dot_general x9, matrix products, column_solve(): jnp.einsum('lsxyk,sjk->lsxyj', rhs, inverse, precision=lax.Precision.HIGH...  8.78 us
  transfers between devices with their start and end apart: 28, of which 21 were waited for; matrix products, arithmetic and copies ran while one was open for 3% of the time, Pallas kernels for 3%

profile of v1, /device:TPU:0, one launch (start us, length us, event | category | flops | bytes accessed | tf_op | source)
XLA Modules:
  0.0 143.8 jit_solution(12245305412691450778)
XLA Ops:
  1.2 3.0 %collective-permute-start.2 = (f32[1,2,16,4,128]{4,3,2,1,0:T(4,128)S(1)}, f32[1,2,16,4,128]{4,3,2,1,0:T(4,128)S(1)}, u32[]{:S(2)}, u32[]{:S(2)}) collective-permute-start(f32[1,2,16,4,128]{4,3,2,1,0:T(4,128)S(1)} %pad_maximum_fusion.43), channel_id=1, source_target_pairs={{0,1},{1,0},{2,3},{3,2},{4,5},{5,4},{6,7},{7,6},{8,9},{9,8},{10,11... | collective-permute-start | bytes 196616 | tf_op jit(solution)/shard_map/ppermute | solution.py:122
  4.2 3.8 %collective-permute-start = (f32[1,2,2,32,128]{4,3,2,1,0:T(8,128)S(1)}, f32[1,2,2,32,128]{4,3,2,1,0:T(8,128)S(1)}, u32[]{:S(2)}, u32[]{:S(2)}) collective-permute-start(f32[1,2,2,32,128]{4,3,2,1,0:T(8,128)S(1)} %get-tuple-element.100), channel_id=1, source_target_pairs={{16,0},{2,16},{18,2},{4,18},{20,4},{6,20},{22,6},{8,22},{24,8},{10... | collective-permute-start | bytes 196616 | tf_op jit(solution)/shard_map/ppermute | solution.py:127
  10.0 4.1 %shard_map.118 = f32[128,2,128]{2,1,0:T(2,128)} custom-call(f32[2,128]{1,0:T(2,128)} %copy-done.4, f32[2,128]{1,0:T(2,128)} %get-tuple-element.125.low_ref), custom_call_target="tpu_custom_call" | custom-call | flops 393216 | bytes 262144 | tf_op jit(solution)/shard_map/pallas_call | solution.py:78
  17.1 4.5 %collective-permute-start.3 = (f32[2,2,2,32,128]{4,3,2,1,0:T(8,128)S(1)}, f32[2,2,2,32,128]{4,3,2,1,0:T(8,128)S(1)}, u32[]{:S(2)}, u32[]{:S(2)}) collective-permute-start(f32[2,2,2,32,128]{4,3,2,1,0:T(8,128)S(1)} %get-tuple-element.86), channel_id=1, source_target_pairs={{16,0},{2,16},{18,2},{4,18},{20,4},{6,20},{22,6},{8,22},{24,8},{10... | collective-permute-start | bytes 393224 | tf_op jit(solution)/shard_map/ppermute | solution.py:127
  22.4 4.3 %collective-permute-done.5 = f32[2,2,16,4,128]{4,3,2,1,0:T(4,128)S(1)} collective-permute-done((f32[2,2,16,4,128]{4,3,2,1,0:T(4,128)S(1)}, f32[2,2,16,4,128]{4,3,2,1,0:T(4,128)S(1)}, u32[]{:S(2)}, u32[]{:S(2)}) %collective-permute-start.5) | collective-permute-done | bytes 131104 | tf_op jit(solution)/shard_map/ppermute | solution.py:122
  27.0 1.7 %collective-permute-done.4 = f32[2,2,2,32,128]{4,3,2,1,0:T(8,128)S(1)} collective-permute-done((f32[2,2,2,32,128]{4,3,2,1,0:T(8,128)S(1)}, f32[2,2,2,32,128]{4,3,2,1,0:T(8,128)S(1)}, u32[]{:S(2)}, u32[]{:S(2)}) %collective-permute-start.4) | collective-permute-done | bytes 131104 | tf_op jit(solution)/shard_map/ppermute | solution.py:126
  35.9 2.4 %collective-permute-done.8 = f32[2,2,16,4,128]{4,3,2,1,0:T(4,128)S(1)} collective-permute-done((f32[2,2,16,4,128]{4,3,2,1,0:T(4,128)S(1)}, f32[2,2,16,4,128]{4,3,2,1,0:T(4,128)S(1)}, u32[]{:S(2)}, u32[]{:S(2)}) %collective-permute-start.8) | collective-permute-done | bytes 131104 | tf_op jit(solution)/shard_map/ppermute | solution.py:122
  38.9 3.5 %collective-permute-done.7 = f32[2,2,2,32,128]{4,3,2,1,0:T(8,128)S(1)} collective-permute-done((f32[2,2,2,32,128]{4,3,2,1,0:T(8,128)S(1)}, f32[2,2,2,32,128]{4,3,2,1,0:T(8,128)S(1)}, u32[]{:S(2)}, u32[]{:S(2)}) %collective-permute-start.7) | collective-permute-done | bytes 131104 | tf_op jit(solution)/shard_map/ppermute | solution.py:126
  42.4 2.1 %fusion.47 = f32[2,2,16,32,128]{4,3,2,1,0:T(8,128)S(1)} fusion(f32[2,1,16,32,128]{4,3,2,1,0:T(8,128)S(1)} %get-tuple-element.83, f32[2,1,16,32,128]{4,3,2,1,0:T(8,128)S(1)} %get-tuple-element.82, f32[2,2,16,32,128]{4,3,2,1,0:T(8,128)S(1)} %convolution_bitcast_fusion.6, f32[2,2,16,2,128]{4,3,2,1,0:T(2,128)S(1)} %get-tuple-element.119, ...), kind=kLoop, calls=%fused_computation.165 | loop fusion | flops 11534336 | bytes 4063240 | tf_op jit(solution)/shard_map/mul | solution.py:168
  48.4 4.4 %collective-permute-start.9 = (f32[2,2,2,32,128]{4,3,2,1,0:T(8,128)S(1)}, f32[2,2,2,32,128]{4,3,2,1,0:T(8,128)S(1)}, u32[]{:S(2)}, u32[]{:S(2)}) collective-permute-start(f32[2,2,2,32,128]{4,3,2,1,0:T(8,128)S(1)} %get-tuple-element.70), channel_id=1, source_target_pairs={{16,0},{2,16},{18,2},{4,18},{20,4},{6,20},{22,6},{8,22},{24,8},{10... | collective-permute-start | bytes 393224 | tf_op jit(solution)/shard_map/ppermute | solution.py:127
  52.9 2.6 %collective-permute-done.10 = f32[2,2,2,32,128]{4,3,2,1,0:T(8,128)S(1)} collective-permute-done((f32[2,2,2,32,128]{4,3,2,1,0:T(8,128)S(1)}, f32[2,2,2,32,128]{4,3,2,1,0:T(8,128)S(1)}, u32[]{:S(2)}, u32[]{:S(2)}) %collective-permute-start.10) | collective-permute-done | bytes 131104 | tf_op jit(solution)/shard_map/ppermute | solution.py:126
  55.5 2.1 %fusion.51 = f32[2,2,16,32,128]{4,3,2,1,0:T(8,128)S(1)} fusion(f32[2,1,16,32,128]{4,3,2,1,0:T(8,128)S(1)} %get-tuple-element.75, f32[2,1,16,32,128]{4,3,2,1,0:T(8,128)S(1)} %get-tuple-element.74, f32[2,2,16,32,128]{4,3,2,1,0:T(8,128)S(1)} %convolution_bitcast_fusion.5, f32[2,2,16,2,128]{4,3,2,1,0:T(2,128)S(1)} %get-tuple-element.117, ...), kind=kLoop, calls=%fused_computation.170 | loop fusion | flops 11534336 | bytes 4063240 | tf_op jit(solution)/shard_map/mul | solution.py:168
  60.5 4.2 %collective-permute-start.12 = (f32[2,2,2,32,128]{4,3,2,1,0:T(8,128)S(1)}, f32[2,2,2,32,128]{4,3,2,1,0:T(8,128)S(1)}, u32[]{:S(2)}, u32[]{:S(2)}) collective-permute-start(f32[2,2,2,32,128]{4,3,2,1,0:T(8,128)S(1)} %get-tuple-element.62), channel_id=1, source_target_pairs={{16,0},{2,16},{18,2},{4,18},{20,4},{6,20},{22,6},{8,22},{24,8},{10... | collective-permute-start | bytes 393224 | tf_op jit(solution)/shard_map/ppermute | solution.py:127
  65.0 2.2 %collective-permute-done.12 = f32[2,2,2,32,128]{4,3,2,1,0:T(8,128)S(1)} collective-permute-done((f32[2,2,2,32,128]{4,3,2,1,0:T(8,128)S(1)}, f32[2,2,2,32,128]{4,3,2,1,0:T(8,128)S(1)}, u32[]{:S(2)}, u32[]{:S(2)}) %collective-permute-start.12) | collective-permute-done | bytes 131104 | tf_op jit(solution)/shard_map/ppermute | solution.py:127
  67.2 4.6 %collective-permute-done.13 = f32[2,2,2,32,128]{4,3,2,1,0:T(8,128)S(1)} collective-permute-done((f32[2,2,2,32,128]{4,3,2,1,0:T(8,128)S(1)}, f32[2,2,2,32,128]{4,3,2,1,0:T(8,128)S(1)}, u32[]{:S(2)}, u32[]{:S(2)}) %collective-permute-start.13) | collective-permute-done | bytes 131104 | tf_op jit(solution)/shard_map/ppermute | solution.py:126
  71.8 2.1 %fusion.55 = f32[2,2,16,32,128]{4,3,2,1,0:T(8,128)S(1)} fusion(f32[2,1,16,32,128]{4,3,2,1,0:T(8,128)S(1)} %get-tuple-element.67, f32[2,1,16,32,128]{4,3,2,1,0:T(8,128)S(1)} %get-tuple-element.66, f32[2,2,16,32,128]{4,3,2,1,0:T(8,128)S(1)} %convolution_bitcast_fusion.4, f32[2,2,16,2,128]{4,3,2,1,0:T(2,128)S(1)} %get-tuple-element.115, ...), kind=kLoop, calls=%fused_computation.175 | loop fusion | flops 11534336 | bytes 4063240 | tf_op jit(solution)/shard_map/mul | solution.py:168
  77.9 2.0 %collective-permute-start.16 = (f32[2,2,2,32,128]{4,3,2,1,0:T(8,128)S(1)}, f32[2,2,2,32,128]{4,3,2,1,0:T(8,128)S(1)}, u32[]{:S(2)}, u32[]{:S(2)}) collective-permute-start(f32[2,2,2,32,128]{4,3,2,1,0:T(8,128)S(1)} %get-tuple-element.55), channel_id=1, source_target_pairs={{0,16},{16,2},{2,18},{18,4},{4,20},{20,6},{6,22},{22,8},{8,24},{24... | collective-permute-start | bytes 393224 | tf_op jit(solution)/shard_map/ppermute | solution.py:126
  82.8 2.3 %collective-permute-done.16 = f32[2,2,2,32,128]{4,3,2,1,0:T(8,128)S(1)} collective-permute-done((f32[2,2,2,32,128]{4,3,2,1,0:T(8,128)S(1)}, f32[2,2,2,32,128]{4,3,2,1,0:T(8,128)S(1)}, u32[]{:S(2)}, u32[]{:S(2)}) %collective-permute-start.16) | collective-permute-done | bytes 131104 | tf_op jit(solution)/shard_map/ppermute | solution.py:126
  85.2 2.1 %fusion.59 = f32[2,2,16,32,128]{4,3,2,1,0:T(8,128)S(1)} fusion(f32[2,1,16,32,128]{4,3,2,1,0:T(8,128)S(1)} %get-tuple-element.59, f32[2,1,16,32,128]{4,3,2,1,0:T(8,128)S(1)} %get-tuple-element.58, f32[2,2,16,32,128]{4,3,2,1,0:T(8,128)S(1)} %convolution_bitcast_fusion.3, f32[2,2,16,2,128]{4,3,2,1,0:T(2,128)S(1)} %get-tuple-element.113, ...), kind=kLoop, calls=%fused_computation.180 | loop fusion | flops 11534336 | bytes 4063240 | tf_op jit(solution)/shard_map/mul | solution.py:168
  90.2 2.0 %collective-permute-start.19 = (f32[2,2,2,32,128]{4,3,2,1,0:T(8,128)S(1)}, f32[2,2,2,32,128]{4,3,2,1,0:T(8,128)S(1)}, u32[]{:S(2)}, u32[]{:S(2)}) collective-permute-start(f32[2,2,2,32,128]{4,3,2,1,0:T(8,128)S(1)} %get-tuple-element.47), channel_id=1, source_target_pairs={{0,16},{16,2},{2,18},{18,4},{4,20},{20,6},{6,22},{22,8},{8,24},{24... | collective-permute-start | bytes 393224 | tf_op jit(solution)/shard_map/ppermute | solution.py:126
  92.2 3.1 %collective-permute-done.20 = f32[2,2,16,4,128]{4,3,2,1,0:T(4,128)S(1)} collective-permute-done((f32[2,2,16,4,128]{4,3,2,1,0:T(4,128)S(1)}, f32[2,2,16,4,128]{4,3,2,1,0:T(4,128)S(1)}, u32[]{:S(2)}, u32[]{:S(2)}) %collective-permute-start.20) | collective-permute-done | bytes 131104 | tf_op jit(solution)/shard_map/ppermute | solution.py:122
  95.6 2.0 %collective-permute-done.19 = f32[2,2,2,32,128]{4,3,2,1,0:T(8,128)S(1)} collective-permute-done((f32[2,2,2,32,128]{4,3,2,1,0:T(8,128)S(1)}, f32[2,2,2,32,128]{4,3,2,1,0:T(8,128)S(1)}, u32[]{:S(2)}, u32[]{:S(2)}) %collective-permute-start.19) | collective-permute-done | bytes 131104 | tf_op jit(solution)/shard_map/ppermute | solution.py:126
  97.6 2.1 %fusion.63 = f32[2,2,16,32,128]{4,3,2,1,0:T(8,128)S(1)} fusion(f32[2,1,16,32,128]{4,3,2,1,0:T(8,128)S(1)} %get-tuple-element.51, f32[2,1,16,32,128]{4,3,2,1,0:T(8,128)S(1)} %get-tuple-element.50, f32[2,2,16,32,128]{4,3,2,1,0:T(8,128)S(1)} %convolution_bitcast_fusion.2, f32[2,2,16,2,128]{4,3,2,1,0:T(2,128)S(1)} %get-tuple-element.111, ...), kind=kLoop, calls=%fused_computation.185 | loop fusion | flops 11534336 | bytes 4063240 | tf_op jit(solution)/shard_map/mul | solution.py:168
  102.1 1.6 %collective-permute-start.23 = (f32[2,2,16,4,128]{4,3,2,1,0:T(4,128)S(1)}, f32[2,2,16,4,128]{4,3,2,1,0:T(4,128)S(1)}, u32[]{:S(2)}, u32[]{:S(2)}) collective-permute-start(f32[2,2,16,4,128]{4,3,2,1,0:T(4,128)S(1)} %pad_maximum_fusion.41), channel_id=1, source_target_pairs={{0,1},{1,0},{2,3},{3,2},{4,5},{5,4},{6,7},{7,6},{8,9},{9,8},{10,11... | collective-permute-start | bytes 393224 | tf_op jit(solution)/shard_map/ppermute | solution.py:122
  103.8 2.0 %collective-permute-start.22 = (f32[2,2,2,32,128]{4,3,2,1,0:T(8,128)S(1)}, f32[2,2,2,32,128]{4,3,2,1,0:T(8,128)S(1)}, u32[]{:S(2)}, u32[]{:S(2)}) collective-permute-start(f32[2,2,2,32,128]{4,3,2,1,0:T(8,128)S(1)} %get-tuple-element.39), channel_id=1, source_target_pairs={{0,16},{16,2},{2,18},{18,4},{4,20},{20,6},{6,22},{22,8},{8,24},{24... | collective-permute-start | bytes 393224 | tf_op jit(solution)/shard_map/ppermute | solution.py:126
  105.8 2.3 %collective-permute-done.23 = f32[2,2,16,4,128]{4,3,2,1,0:T(4,128)S(1)} collective-permute-done((f32[2,2,16,4,128]{4,3,2,1,0:T(4,128)S(1)}, f32[2,2,16,4,128]{4,3,2,1,0:T(4,128)S(1)}, u32[]{:S(2)}, u32[]{:S(2)}) %collective-permute-start.23) | collective-permute-done | bytes 131104 | tf_op jit(solution)/shard_map/ppermute | solution.py:122
  111.0 2.1 %fusion.67 = f32[2,2,16,32,128]{4,3,2,1,0:T(8,128)S(1)} fusion(f32[2,1,16,32,128]{4,3,2,1,0:T(8,128)S(1)} %get-tuple-element.43, f32[2,1,16,32,128]{4,3,2,1,0:T(8,128)S(1)} %get-tuple-element.42, f32[2,2,16,32,128]{4,3,2,1,0:T(8,128)S(1)} %convolution_bitcast_fusion.1, f32[2,2,16,2,128]{4,3,2,1,0:T(2,128)S(1)} %get-tuple-element.109, ...), kind=kLoop, calls=%fused_computation.190 | loop fusion | flops 11534336 | bytes 4063240 | tf_op jit(solution)/shard_map/mul | solution.py:168
  116.1 2.0 %collective-permute-start.25 = (f32[2,2,2,32,128]{4,3,2,1,0:T(8,128)S(1)}, f32[2,2,2,32,128]{4,3,2,1,0:T(8,128)S(1)}, u32[]{:S(2)}, u32[]{:S(2)}) collective-permute-start(f32[2,2,2,32,128]{4,3,2,1,0:T(8,128)S(1)} %get-tuple-element.31), channel_id=1, source_target_pairs={{0,16},{16,2},{2,18},{18,4},{4,20},{20,6},{6,22},{22,8},{8,24},{24... | collective-permute-start | bytes 393224 | tf_op jit(solution)/shard_map/ppermute | solution.py:126
  118.2 3.7 %collective-permute-done.26 = f32[2,2,16,4,128]{4,3,2,1,0:T(4,128)S(1)} collective-permute-done((f32[2,2,16,4,128]{4,3,2,1,0:T(4,128)S(1)}, f32[2,2,16,4,128]{4,3,2,1,0:T(4,128)S(1)}, u32[]{:S(2)}, u32[]{:S(2)}) %collective-permute-start.26) | collective-permute-done | bytes 131104 | tf_op jit(solution)/shard_map/ppermute | solution.py:122
  121.9 1.8 %collective-permute-done.24 = f32[2,2,2,32,128]{4,3,2,1,0:T(8,128)S(1)} collective-permute-done((f32[2,2,2,32,128]{4,3,2,1,0:T(8,128)S(1)}, f32[2,2,2,32,128]{4,3,2,1,0:T(8,128)S(1)}, u32[]{:S(2)}, u32[]{:S(2)}) %collective-permute-start.24) | collective-permute-done | bytes 131104 | tf_op jit(solution)/shard_map/ppermute | solution.py:127
  123.7 2.1 %fusion.71 = f32[2,2,16,32,128]{4,3,2,1,0:T(8,128)S(1)} fusion(f32[2,1,16,32,128]{4,3,2,1,0:T(8,128)S(1)} %get-tuple-element.35, f32[2,1,16,32,128]{4,3,2,1,0:T(8,128)S(1)} %get-tuple-element.34, f32[2,2,16,32,128]{4,3,2,1,0:T(8,128)S(1)} %convolution_bitcast_fusion, f32[2,2,16,2,128]{4,3,2,1,0:T(2,128)S(1)} %get-tuple-element.107, ...), kind=kLoop, calls=%fused_computation.195 | loop fusion | flops 11534336 | bytes 4063240 | tf_op jit(solution)/shard_map/mul | solution.py:168
  129.6 13.3 %collective-permute-done.27 = f32[1,2,16,32,128]{4,3,2,1,0:T(8,128)S(1)} collective-permute-done((f32[1,2,16,32,128]{4,3,2,1,0:T(8,128)S(1)}, f32[1,2,16,32,128]{4,3,2,1,0:T(8,128)S(1)}, u32[]{:S(2)}, u32[]{:S(2)}) %collective-permute-start.27) | collective-permute-done | bytes 524320 | tf_op jit(solution)/shard_map/ppermute | solution.py:234
  (137 shorter events, 44.8 us)
Async XLA Ops:
  1.2 14.1 %collective-permute-start.2 = (f32[1,2,16,4,128]{4,3,2,1,0:T(4,128)S(1)}, f32[1,2,16,4,128]{4,3,2,1,0:T(4,128)S(1)}, u32[]{:S(2)}, u32[]{:S(2)}) collective-permute-start(f32[1,2,16,4,128]{4,3,2,1,0:T(4,128)S(1)} %pad_maximum_fusion.43), channel_id=1, source_target_pairs={{0,1},{1,0},{2,3},{3,2},{4,5},{5,4},{6,7},{7,6},{8,9},{9,8},{10,11... | collective-permute-start | bytes 196616 | tf_op jit(solution)/shard_map/ppermute | solution.py:122
  4.2 11.1 %collective-permute-start = (f32[1,2,2,32,128]{4,3,2,1,0:T(8,128)S(1)}, f32[1,2,2,32,128]{4,3,2,1,0:T(8,128)S(1)}, u32[]{:S(2)}, u32[]{:S(2)}) collective-permute-start(f32[1,2,2,32,128]{4,3,2,1,0:T(8,128)S(1)} %get-tuple-element.100), channel_id=1, source_target_pairs={{16,0},{2,16},{18,2},{4,18},{20,4},{6,20},{22,6},{8,22},{24,8},{10... | collective-permute-start | bytes 196616 | tf_op jit(solution)/shard_map/ppermute | solution.py:127
  8.0 7.3 %collective-permute-start.1 = (f32[1,2,2,32,128]{4,3,2,1,0:T(8,128)S(1)}, f32[1,2,2,32,128]{4,3,2,1,0:T(8,128)S(1)}, u32[]{:S(2)}, u32[]{:S(2)}) collective-permute-start(f32[1,2,2,32,128]{4,3,2,1,0:T(8,128)S(1)} %get-tuple-element.101), channel_id=1, source_target_pairs={{0,16},{16,2},{2,18},{18,4},{4,20},{20,6},{6,22},{22,8},{8,24},{24... | collective-permute-start | bytes 196616 | tf_op jit(solution)/shard_map/ppermute | solution.py:126
  8.1 7.2 %copy-start.2 = (f32[2,32,32,128]{3,2,1,0:T(8,128)S(1)}, f32[2,32,32,128]{3,2,1,0:T(8,128)}, u32[]{:S(2)}) copy-start(f32[2,32,32,128]{3,2,1,0:T(8,128)} %param.12) | copy-start | bytes 3145732
  8.1 7.2 %copy-start.7 = (f32[2]{0:T(128)S(1)}, f32[2]{0:T(128)}, u32[]{:S(2)}) copy-start(f32[2]{0:T(128)} %constant.131.clone) | copy-start | bytes 28
  17.1 9.9 %collective-permute-start.3 = (f32[2,2,2,32,128]{4,3,2,1,0:T(8,128)S(1)}, f32[2,2,2,32,128]{4,3,2,1,0:T(8,128)S(1)}, u32[]{:S(2)}, u32[]{:S(2)}) collective-permute-start(f32[2,2,2,32,128]{4,3,2,1,0:T(8,128)S(1)} %get-tuple-element.86), channel_id=1, source_target_pairs={{16,0},{2,16},{18,2},{4,18},{20,4},{6,20},{22,6},{8,22},{24,8},{10... | collective-permute-start | bytes 393224 | tf_op jit(solution)/shard_map/ppermute | solution.py:127
  21.6 7.1 %collective-permute-start.4 = (f32[2,2,2,32,128]{4,3,2,1,0:T(8,128)S(1)}, f32[2,2,2,32,128]{4,3,2,1,0:T(8,128)S(1)}, u32[]{:S(2)}, u32[]{:S(2)}) collective-permute-start(f32[2,2,2,32,128]{4,3,2,1,0:T(8,128)S(1)} %get-tuple-element.87), channel_id=1, source_target_pairs={{0,16},{16,2},{2,18},{18,4},{4,20},{20,6},{6,22},{22,8},{8,24},{24... | collective-permute-start | bytes 393224 | tf_op jit(solution)/shard_map/ppermute | solution.py:126
  21.7 5.0 %collective-permute-start.5 = (f32[2,2,16,4,128]{4,3,2,1,0:T(4,128)S(1)}, f32[2,2,16,4,128]{4,3,2,1,0:T(4,128)S(1)}, u32[]{:S(2)}, u32[]{:S(2)}) collective-permute-start(f32[2,2,16,4,128]{4,3,2,1,0:T(4,128)S(1)} %pad_maximum_fusion.35), channel_id=1, source_target_pairs={{0,1},{1,0},{2,3},{3,2},{4,5},{5,4},{6,7},{7,6},{8,9},{9,8},{10,11... | collective-permute-start | bytes 393224 | tf_op jit(solution)/shard_map/ppermute | solution.py:122
  33.3 5.0 %collective-permute-start.8 = (f32[2,2,16,4,128]{4,3,2,1,0:T(4,128)S(1)}, f32[2,2,16,4,128]{4,3,2,1,0:T(4,128)S(1)}, u32[]{:S(2)}, u32[]{:S(2)}) collective-permute-start(f32[2,2,16,4,128]{4,3,2,1,0:T(4,128)S(1)} %pad_maximum_fusion.36), channel_id=1, source_target_pairs={{0,1},{1,0},{2,3},{3,2},{4,5},{5,4},{6,7},{7,6},{8,9},{9,8},{10,11... | collective-permute-start | bytes 393224 | tf_op jit(solution)/shard_map/ppermute | solution.py:122
  33.9 5.0 %collective-permute-start.6 = (f32[2,2,2,32,128]{4,3,2,1,0:T(8,128)S(1)}, f32[2,2,2,32,128]{4,3,2,1,0:T(8,128)S(1)}, u32[]{:S(2)}, u32[]{:S(2)}) collective-permute-start(f32[2,2,2,32,128]{4,3,2,1,0:T(8,128)S(1)} %get-tuple-element.78), channel_id=1, source_target_pairs={{16,0},{2,16},{18,2},{4,18},{20,4},{6,20},{22,6},{8,22},{24,8},{10... | collective-permute-start | bytes 393224 | tf_op jit(solution)/shard_map/ppermute | solution.py:127
  35.3 7.1 %collective-permute-start.7 = (f32[2,2,2,32,128]{4,3,2,1,0:T(8,128)S(1)}, f32[2,2,2,32,128]{4,3,2,1,0:T(8,128)S(1)}, u32[]{:S(2)}, u32[]{:S(2)}) collective-permute-start(f32[2,2,2,32,128]{4,3,2,1,0:T(8,128)S(1)} %get-tuple-element.79), channel_id=1, source_target_pairs={{0,16},{16,2},{2,18},{18,4},{4,20},{20,6},{6,22},{22,8},{8,24},{24... | collective-permute-start | bytes 393224 | tf_op jit(solution)/shard_map/ppermute | solution.py:126
  46.7 6.1 %collective-permute-start.11 = (f32[2,2,16,4,128]{4,3,2,1,0:T(4,128)S(1)}, f32[2,2,16,4,128]{4,3,2,1,0:T(4,128)S(1)}, u32[]{:S(2)}, u32[]{:S(2)}) collective-permute-start(f32[2,2,16,4,128]{4,3,2,1,0:T(4,128)S(1)} %pad_maximum_fusion.37), channel_id=1, source_target_pairs={{0,1},{1,0},{2,3},{3,2},{4,5},{5,4},{6,7},{7,6},{8,9},{9,8},{10,11... | collective-permute-start | bytes 393224 | tf_op jit(solution)/shard_map/ppermute | solution.py:122
  48.4 7.2 %collective-permute-start.10 = (f32[2,2,2,32,128]{4,3,2,1,0:T(8,128)S(1)}, f32[2,2,2,32,128]{4,3,2,1,0:T(8,128)S(1)}, u32[]{:S(2)}, u32[]{:S(2)}) collective-permute-start(f32[2,2,2,32,128]{4,3,2,1,0:T(8,128)S(1)} %get-tuple-element.71), channel_id=1, source_target_pairs={{0,16},{16,2},{2,18},{18,4},{4,20},{20,6},{6,22},{22,8},{8,24},{24... | collective-permute-start | bytes 393224 | tf_op jit(solution)/shard_map/ppermute | solution.py:126
  48.4 7.1 %collective-permute-start.9 = (f32[2,2,2,32,128]{4,3,2,1,0:T(8,128)S(1)}, f32[2,2,2,32,128]{4,3,2,1,0:T(8,128)S(1)}, u32[]{:S(2)}, u32[]{:S(2)}) collective-permute-start(f32[2,2,2,32,128]{4,3,2,1,0:T(8,128)S(1)} %get-tuple-element.70), channel_id=1, source_target_pairs={{16,0},{2,16},{18,2},{4,18},{20,4},{6,20},{22,6},{8,22},{24,8},{10... | collective-permute-start | bytes 393224 | tf_op jit(solution)/shard_map/ppermute | solution.py:127
  59.9 5.0 %collective-permute-start.14 = (f32[2,2,16,4,128]{4,3,2,1,0:T(4,128)S(1)}, f32[2,2,16,4,128]{4,3,2,1,0:T(4,128)S(1)}, u32[]{:S(2)}, u32[]{:S(2)}) collective-permute-start(f32[2,2,16,4,128]{4,3,2,1,0:T(4,128)S(1)} %pad_maximum_fusion.38), channel_id=1, source_target_pairs={{0,1},{1,0},{2,3},{3,2},{4,5},{5,4},{6,7},{7,6},{8,9},{9,8},{10,11... | collective-permute-start | bytes 393224 | tf_op jit(solution)/shard_map/ppermute | solution.py:122
  60.5 6.7 %collective-permute-start.12 = (f32[2,2,2,32,128]{4,3,2,1,0:T(8,128)S(1)}, f32[2,2,2,32,128]{4,3,2,1,0:T(8,128)S(1)}, u32[]{:S(2)}, u32[]{:S(2)}) collective-permute-start(f32[2,2,2,32,128]{4,3,2,1,0:T(8,128)S(1)} %get-tuple-element.62), channel_id=1, source_target_pairs={{16,0},{2,16},{18,2},{4,18},{20,4},{6,20},{22,6},{8,22},{24,8},{10... | collective-permute-start | bytes 393224 | tf_op jit(solution)/shard_map/ppermute | solution.py:127
  64.7 7.1 %collective-permute-start.13 = (f32[2,2,2,32,128]{4,3,2,1,0:T(8,128)S(1)}, f32[2,2,2,32,128]{4,3,2,1,0:T(8,128)S(1)}, u32[]{:S(2)}, u32[]{:S(2)}) collective-permute-start(f32[2,2,2,32,128]{4,3,2,1,0:T(8,128)S(1)} %get-tuple-element.63), channel_id=1, source_target_pairs={{0,16},{16,2},{2,18},{18,4},{4,20},{20,6},{6,22},{22,8},{8,24},{24... | collective-permute-start | bytes 393224 | tf_op jit(solution)/shard_map/ppermute | solution.py:126
  76.2 5.0 %collective-permute-start.17 = (f32[2,2,16,4,128]{4,3,2,1,0:T(4,128)S(1)}, f32[2,2,16,4,128]{4,3,2,1,0:T(4,128)S(1)}, u32[]{:S(2)}, u32[]{:S(2)}) collective-permute-start(f32[2,2,16,4,128]{4,3,2,1,0:T(4,128)S(1)} %pad_maximum_fusion.39), channel_id=1, source_target_pairs={{0,1},{1,0},{2,3},{3,2},{4,5},{5,4},{6,7},{7,6},{8,9},{9,8},{10,11... | collective-permute-start | bytes 393224 | tf_op jit(solution)/shard_map/ppermute | solution.py:122
  77.8 5.0 %collective-permute-start.15 = (f32[2,2,2,32,128]{4,3,2,1,0:T(8,128)S(1)}, f32[2,2,2,32,128]{4,3,2,1,0:T(8,128)S(1)}, u32[]{:S(2)}, u32[]{:S(2)}) collective-permute-start(f32[2,2,2,32,128]{4,3,2,1,0:T(8,128)S(1)} %get-tuple-element.54), channel_id=1, source_target_pairs={{16,0},{2,16},{18,2},{4,18},{20,4},{6,20},{22,6},{8,22},{24,8},{10... | collective-permute-start | bytes 393224 | tf_op jit(solution)/shard_map/ppermute | solution.py:127
  77.9 7.3 %collective-permute-start.16 = (f32[2,2,2,32,128]{4,3,2,1,0:T(8,128)S(1)}, f32[2,2,2,32,128]{4,3,2,1,0:T(8,128)S(1)}, u32[]{:S(2)}, u32[]{:S(2)}) collective-permute-start(f32[2,2,2,32,128]{4,3,2,1,0:T(8,128)S(1)} %get-tuple-element.55), channel_id=1, source_target_pairs={{0,16},{16,2},{2,18},{18,4},{4,20},{20,6},{6,22},{22,8},{8,24},{24... | collective-permute-start | bytes 393224 | tf_op jit(solution)/shard_map/ppermute | solution.py:126
  89.5 5.8 %collective-permute-start.20 = (f32[2,2,16,4,128]{4,3,2,1,0:T(4,128)S(1)}, f32[2,2,16,4,128]{4,3,2,1,0:T(4,128)S(1)}, u32[]{:S(2)}, u32[]{:S(2)}) collective-permute-start(f32[2,2,16,4,128]{4,3,2,1,0:T(4,128)S(1)} %pad_maximum_fusion.40), channel_id=1, source_target_pairs={{0,1},{1,0},{2,3},{3,2},{4,5},{5,4},{6,7},{7,6},{8,9},{9,8},{10,11... | collective-permute-start | bytes 393224 | tf_op jit(solution)/shard_map/ppermute | solution.py:122
  90.1 5.5 %collective-permute-start.18 = (f32[2,2,2,32,128]{4,3,2,1,0:T(8,128)S(1)}, f32[2,2,2,32,128]{4,3,2,1,0:T(8,128)S(1)}, u32[]{:S(2)}, u32[]{:S(2)}) collective-permute-start(f32[2,2,2,32,128]{4,3,2,1,0:T(8,128)S(1)} %get-tuple-element.46), channel_id=1, source_target_pairs={{16,0},{2,16},{18,2},{4,18},{20,4},{6,20},{22,6},{8,22},{24,8},{10... | collective-permute-start | bytes 393224 | tf_op jit(solution)/shard_map/ppermute | solution.py:127
  90.2 7.5 %collective-permute-start.19 = (f32[2,2,2,32,128]{4,3,2,1,0:T(8,128)S(1)}, f32[2,2,2,32,128]{4,3,2,1,0:T(8,128)S(1)}, u32[]{:S(2)}, u32[]{:S(2)}) collective-permute-start(f32[2,2,2,32,128]{4,3,2,1,0:T(8,128)S(1)} %get-tuple-element.47), channel_id=1, source_target_pairs={{0,16},{16,2},{2,18},{18,4},{4,20},{20,6},{6,22},{22,8},{8,24},{24... | collective-permute-start | bytes 393224 | tf_op jit(solution)/shard_map/ppermute | solution.py:126
  102.1 6.1 %collective-permute-start.23 = (f32[2,2,16,4,128]{4,3,2,1,0:T(4,128)S(1)}, f32[2,2,16,4,128]{4,3,2,1,0:T(4,128)S(1)}, u32[]{:S(2)}, u32[]{:S(2)}) collective-permute-start(f32[2,2,16,4,128]{4,3,2,1,0:T(4,128)S(1)} %pad_maximum_fusion.41), channel_id=1, source_target_pairs={{0,1},{1,0},{2,3},{3,2},{4,5},{5,4},{6,7},{7,6},{8,9},{9,8},{10,11... | collective-permute-start | bytes 393224 | tf_op jit(solution)/shard_map/ppermute | solution.py:122
  103.7 5.8 %collective-permute-start.21 = (f32[2,2,2,32,128]{4,3,2,1,0:T(8,128)S(1)}, f32[2,2,2,32,128]{4,3,2,1,0:T(8,128)S(1)}, u32[]{:S(2)}, u32[]{:S(2)}) collective-permute-start(f32[2,2,2,32,128]{4,3,2,1,0:T(8,128)S(1)} %get-tuple-element.38), channel_id=1, source_target_pairs={{16,0},{2,16},{18,2},{4,18},{20,4},{6,20},{22,6},{8,22},{24,8},{10... | collective-permute-start | bytes 393224 | tf_op jit(solution)/shard_map/ppermute | solution.py:127
  103.8 7.3 %collective-permute-start.22 = (f32[2,2,2,32,128]{4,3,2,1,0:T(8,128)S(1)}, f32[2,2,2,32,128]{4,3,2,1,0:T(8,128)S(1)}, u32[]{:S(2)}, u32[]{:S(2)}) collective-permute-start(f32[2,2,2,32,128]{4,3,2,1,0:T(8,128)S(1)} %get-tuple-element.39), channel_id=1, source_target_pairs={{0,16},{16,2},{2,18},{18,4},{4,20},{20,6},{6,22},{22,8},{8,24},{24... | collective-permute-start | bytes 393224 | tf_op jit(solution)/shard_map/ppermute | solution.py:126
  115.0 10.9 %copy-start = (f32[2,2,16,32,128]{4,3,2,1,0:T(8,128)}, f32[2,2,16,32,128]{4,3,2,1,0:T(8,128)S(1)}, u32[]{:S(2)}) copy-start(f32[2,2,16,32,128]{4,3,2,1,0:T(8,128)S(1)} %convolution_bitcast_fusion) | copy-start | bytes 3145732
  115.5 6.3 %collective-permute-start.26 = (f32[2,2,16,4,128]{4,3,2,1,0:T(4,128)S(1)}, f32[2,2,16,4,128]{4,3,2,1,0:T(4,128)S(1)}, u32[]{:S(2)}, u32[]{:S(2)}) collective-permute-start(f32[2,2,16,4,128]{4,3,2,1,0:T(4,128)S(1)} %pad_maximum_fusion.42), channel_id=1, source_target_pairs={{0,1},{1,0},{2,3},{3,2},{4,5},{5,4},{6,7},{7,6},{8,9},{9,8},{10,11... | collective-permute-start | bytes 393224 | tf_op jit(solution)/shard_map/ppermute | solution.py:122
  116.1 7.7 %collective-permute-start.24 = (f32[2,2,2,32,128]{4,3,2,1,0:T(8,128)S(1)}, f32[2,2,2,32,128]{4,3,2,1,0:T(8,128)S(1)}, u32[]{:S(2)}, u32[]{:S(2)}) collective-permute-start(f32[2,2,2,32,128]{4,3,2,1,0:T(8,128)S(1)} %get-tuple-element.30), channel_id=1, source_target_pairs={{16,0},{2,16},{18,2},{4,18},{20,4},{6,20},{22,6},{8,22},{24,8},{10... | collective-permute-start | bytes 393224 | tf_op jit(solution)/shard_map/ppermute | solution.py:127
  116.1 7.6 %collective-permute-start.25 = (f32[2,2,2,32,128]{4,3,2,1,0:T(8,128)S(1)}, f32[2,2,2,32,128]{4,3,2,1,0:T(8,128)S(1)}, u32[]{:S(2)}, u32[]{:S(2)}) collective-permute-start(f32[2,2,2,32,128]{4,3,2,1,0:T(8,128)S(1)} %get-tuple-element.31), channel_id=1, source_target_pairs={{0,16},{16,2},{2,18},{18,4},{4,20},{20,6},{6,22},{22,8},{8,24},{24... | collective-permute-start | bytes 393224 | tf_op jit(solution)/shard_map/ppermute | solution.py:126
  128.3 14.6 %copy-start.3 = (f32[1,2,32,32,128]{4,3,2,1,0:T(8,128)}, f32[1,2,32,32,128]{4,3,2,1,0:T(8,128)S(1)}, u32[]{:S(2)}) copy-start(f32[1,2,32,32,128]{4,3,2,1,0:T(8,128)S(1)} %get-tuple-element.27) | copy-start | bytes 3145732
  128.3 14.6 %collective-permute-start.27 = (f32[1,2,16,32,128]{4,3,2,1,0:T(8,128)S(1)}, f32[1,2,16,32,128]{4,3,2,1,0:T(8,128)S(1)}, u32[]{:S(2)}, u32[]{:S(2)}) collective-permute-start(f32[1,2,16,32,128]{4,3,2,1,0:T(8,128)S(1)} %get-tuple-element.26), channel_id=1, source_target_pairs={{0,16},{16,0},{1,17},{17,1},{2,18},{18,2},{3,19},{19,3},{4,20},{20... | collective-permute-start | bytes 1572872 | tf_op jit(solution)/shard_map/ppermute | solution.py:234
  (7 other events, 5.9 us)

commit v2 on v1

--- a/solution.py
+++ b/solution.py
@@ -99,22 +99,24 @@
     return (lo + up) * w - lo * beneath - up * overhead
 
 
-def ring_halo(block, axes, dim, width):
-    sizes = [lax.axis_size(axis) for axis in axes]
-    size = int(np.prod(sizes))
-
-    def mesh_index(ring_pos):
-        idx = []
-        for n in sizes:
-            idx.append(ring_pos % n)
-            ring_pos //= n
-        lin = 0
-        for d, n in zip(idx, sizes):
-            lin = lin * n + d
-        return lin
-
+def slab_of(corr, tile, depth):
+    return jnp.where(tile % 2 == 0, corr, depth - 1 - corr)
+
+
+def x_ring():
+    depth, tiles = lax.axis_size("corr"), lax.axis_size("tx")
+    order = []
+    for tile in range(tiles):
+        for q in range(depth):
+            corr = q if tile % 2 == 0 else depth - 1 - q
+            order.append(corr * tiles + tile)
+    return order
+
+
+def ring_halo(block, axes, order, dim, width):
+    size = len(order)
     length = block.shape[dim]
-    up = [(mesh_index(g), mesh_index((g + 1) % size)) for g in range(size)]
+    up = [(order[g], order[(g + 1) % size]) for g in range(size)]
     down = [(j, i) for i, j in up]
     last = lax.slice_in_dim(block, length - width, length, axis=dim)
     first = lax.slice_in_dim(block, 0, width, axis=dim)
@@ -129,8 +131,8 @@
 
 
 def tendency(state, wind):
-    west, east = ring_halo(state, ("corr", "tx"), 2, 2)
-    south, north = ring_halo(state, ("ty",), 3, 2)
+    west, east = ring_halo(state, ("corr", "tx"), x_ring(), 2, 2)
+    south, north = ring_halo(state, ("ty",), list(range(lax.axis_size("ty"))), 3, 2)
     px = jnp.concatenate([west, state, east], 2)
     py = jnp.concatenate([south, state, north], 3)
     center = state
@@ -179,7 +181,9 @@
     table = quad_cycle(STEPS)
     depth = lax.axis_size("corr")
     slab = fields.shape[1] // depth
-    start = lax.axis_index("corr") * slab
+    me = lax.axis_index("corr")
+    tile = lax.axis_index("tx")
+    start = slab_of(me, tile, depth) * slab
     own_fields = lax.dynamic_slice_in_dim(fields, start, slab, 1)
     own_wind = lax.dynamic_slice_in_dim(wind, start, slab, 1)
 
@@ -222,7 +226,6 @@
         solved = column_solve(jnp.stack(rhs, 0), inverse)
         for i, l in enumerate(moving):
             states[l] = solved[i]
-    me = lax.axis_index("corr")
     result = jnp.stack(states, 0)
     out = jnp.zeros((1,) + own_fields.shape[:1] + fields.shape[1:], jnp.float32)
     out = lax.dynamic_update_slice_in_dim(
@@ -233,7 +236,9 @@
         sent = lax.dynamic_index_in_dim(result, (me + shift) % depth, 0)
         got = lax.ppermute(sent, "corr", pairs)
         origin = (me - shift) % depth
-        out = lax.dynamic_update_slice_in_dim(out, got, origin * slab, 2)
+        out = lax.dynamic_update_slice_in_dim(
+            out, got, slab_of(origin, tile, depth) * slab, 2
+        )
     return out
 
 

time: 144 us -> 130 us (0.903)
  waiting for transfers between devices: 56.6 us -> 46.8 us
  starting transfers between devices: 39.3 us -> 34.7 us
    ppermute x1, waiting for transfers between devices: 13.3 us -> 9.23 us  [on_device(): got = lax.ppermute(sent, 'corr', pairs)]
    ppermute x9, starting transfers between devices: 18.6 us -> 15 us  [ring_halo(): after = lax.ppermute(first, axes, down)]
    ppermute x9, waiting for transfers between devices: 7.67 us -> 5.59 us  [ring_halo(): after = lax.ppermute(first, axes, down)]
    ppermute x9, waiting for transfers between devices: 18.2 us -> 16.4 us  [ring_halo(): before = lax.ppermute(last, axes, up)]
    ppermute x9, waiting for transfers between devices: 17.4 us -> 15.6 us  [ring_halo(): got = lax.ppermute(jnp.concatenate([first, last], dim), axes, up)]
where the time goes in v2:
time: 130 us; the launch traced here: 129 us
  waiting for transfers between devices  46.8 us (36%)
  starting transfers between devices  34.7 us (27%)
  other arithmetic  27.4 us (21%)
  matrix products  8.79 us (7%)
  local copies, waits for them, and re-layouts  6.89 us (5%)
  Pallas kernels  4.11 us (3%)
    mul x9, other arithmetic, tendency(): return DT * (flow + kappa * (dx2 + dy2) + react)  17 us
    ppermute x9, waiting for transfers between devices, ring_halo(): before = lax.ppermute(last, axes, up)  16.4 us
    ppermute x9, waiting for transfers between devices, ring_halo(): got = lax.ppermute(jnp.concatenate([first, last], dim), axes, up)  15.6 us
    ppermute x9, starting transfers between devices, ring_halo(): after = lax.ppermute(first, axes, down)  15 us
    ppermute x9, starting transfers between devices, ring_halo(): got = lax.ppermute(jnp.concatenate([first, last], dim), axes, up)  10.2 us
    ppermute x1, waiting for transfers between devices, on_device(): got = lax.ppermute(sent, 'corr', pairs)  9.23 us
    ppermute x9, starting transfers between devices, ring_halo(): before = lax.ppermute(last, axes, up)  8.8 us
    dot_general x9, matrix products, column_solve(): jnp.einsum('lsxyk,sjk->lsxyj', rhs, inverse, precision=lax.Precision.HIGH...  8.79 us
  transfers between devices with their start and end apart: 28, of which 21 were waited for; matrix products, arithmetic and copies ran while one was open for 3% of the time, Pallas kernels for 3%

profile of v2, /device:TPU:0, one launch (start us, length us, event | category | flops | bytes accessed | tf_op | source)
XLA Modules:
  0.0 129.4 jit_solution(17577059670823942113)
XLA Ops:
  1.2 3.0 %collective-permute-start.2 = (f32[1,2,16,4,128]{4,3,2,1,0:T(4,128)S(1)}, f32[1,2,16,4,128]{4,3,2,1,0:T(4,128)S(1)}, u32[]{:S(2)}, u32[]{:S(2)}) collective-permute-start(f32[1,2,16,4,128]{4,3,2,1,0:T(4,128)S(1)} %pad_maximum_fusion.43), channel_id=1, source_target_pairs={{0,1},{1,0},{2,3},{3,2},{4,5},{5,4},{6,7},{7,6},{8,9},{9,8},{10,11... | collective-permute-start | bytes 196616 | tf_op jit(solution)/shard_map/ppermute | solution.py:124
  4.2 2.8 %collective-permute-start = (f32[1,2,2,32,128]{4,3,2,1,0:T(8,128)S(1)}, f32[1,2,2,32,128]{4,3,2,1,0:T(8,128)S(1)}, u32[]{:S(2)}, u32[]{:S(2)}) collective-permute-start(f32[1,2,2,32,128]{4,3,2,1,0:T(8,128)S(1)} %get-tuple-element.100), channel_id=1, source_target_pairs={{16,0},{18,16},{2,18},{4,2},{20,4},{22,20},{6,22},{8,6},{24,8},{26... | collective-permute-start | bytes 196616 | tf_op jit(solution)/shard_map/ppermute | solution.py:129
  9.1 4.1 %shard_map.118 = f32[128,2,128]{2,1,0:T(2,128)} custom-call(f32[2,128]{1,0:T(2,128)} %copy-done.4, f32[2,128]{1,0:T(2,128)} %get-tuple-element.125.low_ref), custom_call_target="tpu_custom_call" | custom-call | flops 393216 | bytes 262144 | tf_op jit(solution)/shard_map/pallas_call | solution.py:78
  16.2 3.6 %collective-permute-start.3 = (f32[2,2,2,32,128]{4,3,2,1,0:T(8,128)S(1)}, f32[2,2,2,32,128]{4,3,2,1,0:T(8,128)S(1)}, u32[]{:S(2)}, u32[]{:S(2)}) collective-permute-start(f32[2,2,2,32,128]{4,3,2,1,0:T(8,128)S(1)} %get-tuple-element.86), channel_id=1, source_target_pairs={{16,0},{18,16},{2,18},{4,2},{20,4},{22,20},{6,22},{8,6},{24,8},{26... | collective-permute-start | bytes 393224 | tf_op jit(solution)/shard_map/ppermute | solution.py:129
  20.6 4.3 %collective-permute-done.5 = f32[2,2,16,4,128]{4,3,2,1,0:T(4,128)S(1)} collective-permute-done((f32[2,2,16,4,128]{4,3,2,1,0:T(4,128)S(1)}, f32[2,2,16,4,128]{4,3,2,1,0:T(4,128)S(1)}, u32[]{:S(2)}, u32[]{:S(2)}) %collective-permute-start.5) | collective-permute-done | bytes 131104 | tf_op jit(solution)/shard_map/ppermute | solution.py:124
  33.2 2.4 %collective-permute-done.8 = f32[2,2,16,4,128]{4,3,2,1,0:T(4,128)S(1)} collective-permute-done((f32[2,2,16,4,128]{4,3,2,1,0:T(4,128)S(1)}, f32[2,2,16,4,128]{4,3,2,1,0:T(4,128)S(1)}, u32[]{:S(2)}, u32[]{:S(2)}) %collective-permute-start.8) | collective-permute-done | bytes 131104 | tf_op jit(solution)/shard_map/ppermute | solution.py:124
  36.2 2.6 %collective-permute-done.7 = f32[2,2,2,32,128]{4,3,2,1,0:T(8,128)S(1)} collective-permute-done((f32[2,2,2,32,128]{4,3,2,1,0:T(8,128)S(1)}, f32[2,2,2,32,128]{4,3,2,1,0:T(8,128)S(1)}, u32[]{:S(2)}, u32[]{:S(2)}) %collective-permute-start.7) | collective-permute-done | bytes 131104 | tf_op jit(solution)/shard_map/ppermute | solution.py:128
  38.7 2.1 %fusion.47 = f32[2,2,16,32,128]{4,3,2,1,0:T(8,128)S(1)} fusion(f32[2,1,16,32,128]{4,3,2,1,0:T(8,128)S(1)} %get-tuple-element.83, f32[2,1,16,32,128]{4,3,2,1,0:T(8,128)S(1)} %get-tuple-element.82, f32[2,2,16,32,128]{4,3,2,1,0:T(8,128)S(1)} %convolution_bitcast_fusion.6, f32[2,2,16,2,128]{4,3,2,1,0:T(2,128)S(1)} %get-tuple-element.119, ...), kind=kLoop, calls=%fused_computation.165 | loop fusion | flops 11534336 | bytes 4063240 | tf_op jit(solution)/shard_map/mul | solution.py:170
  43.1 1.6 %collective-permute-start.11 = (f32[2,2,16,4,128]{4,3,2,1,0:T(4,128)S(1)}, f32[2,2,16,4,128]{4,3,2,1,0:T(4,128)S(1)}, u32[]{:S(2)}, u32[]{:S(2)}) collective-permute-start(f32[2,2,16,4,128]{4,3,2,1,0:T(4,128)S(1)} %pad_maximum_fusion.37), channel_id=1, source_target_pairs={{0,1},{1,0},{2,3},{3,2},{4,5},{5,4},{6,7},{7,6},{8,9},{9,8},{10,11... | collective-permute-start | bytes 393224 | tf_op jit(solution)/shard_map/ppermute | solution.py:124
  44.8 3.5 %collective-permute-start.9 = (f32[2,2,2,32,128]{4,3,2,1,0:T(8,128)S(1)}, f32[2,2,2,32,128]{4,3,2,1,0:T(8,128)S(1)}, u32[]{:S(2)}, u32[]{:S(2)}) collective-permute-start(f32[2,2,2,32,128]{4,3,2,1,0:T(8,128)S(1)} %get-tuple-element.70), channel_id=1, source_target_pairs={{16,0},{18,16},{2,18},{4,2},{20,4},{22,20},{6,22},{8,6},{24,8},{26... | collective-permute-start | bytes 393224 | tf_op jit(solution)/shard_map/ppermute | solution.py:129
  48.4 2.6 %collective-permute-done.10 = f32[2,2,2,32,128]{4,3,2,1,0:T(8,128)S(1)} collective-permute-done((f32[2,2,2,32,128]{4,3,2,1,0:T(8,128)S(1)}, f32[2,2,2,32,128]{4,3,2,1,0:T(8,128)S(1)}, u32[]{:S(2)}, u32[]{:S(2)}) %collective-permute-start.10) | collective-permute-done | bytes 131104 | tf_op jit(solution)/shard_map/ppermute | solution.py:128
  51.0 2.1 %fusion.51 = f32[2,2,16,32,128]{4,3,2,1,0:T(8,128)S(1)} fusion(f32[2,1,16,32,128]{4,3,2,1,0:T(8,128)S(1)} %get-tuple-element.75, f32[2,1,16,32,128]{4,3,2,1,0:T(8,128)S(1)} %get-tuple-element.74, f32[2,2,16,32,128]{4,3,2,1,0:T(8,128)S(1)} %convolution_bitcast_fusion.5, f32[2,2,16,2,128]{4,3,2,1,0:T(2,128)S(1)} %get-tuple-element.117, ...), kind=kLoop, calls=%fused_computation.170 | loop fusion | flops 11534336 | bytes 4063240 | tf_op jit(solution)/shard_map/mul | solution.py:170
  56.0 3.3 %collective-permute-start.12 = (f32[2,2,2,32,128]{4,3,2,1,0:T(8,128)S(1)}, f32[2,2,2,32,128]{4,3,2,1,0:T(8,128)S(1)}, u32[]{:S(2)}, u32[]{:S(2)}) collective-permute-start(f32[2,2,2,32,128]{4,3,2,1,0:T(8,128)S(1)} %get-tuple-element.62), channel_id=1, source_target_pairs={{16,0},{18,16},{2,18},{4,2},{20,4},{22,20},{6,22},{8,6},{24,8},{26... | collective-permute-start | bytes 393224 | tf_op jit(solution)/shard_map/ppermute | solution.py:129
  61.8 3.7 %collective-permute-done.13 = f32[2,2,2,32,128]{4,3,2,1,0:T(8,128)S(1)} collective-permute-done((f32[2,2,2,32,128]{4,3,2,1,0:T(8,128)S(1)}, f32[2,2,2,32,128]{4,3,2,1,0:T(8,128)S(1)}, u32[]{:S(2)}, u32[]{:S(2)}) %collective-permute-start.13) | collective-permute-done | bytes 131104 | tf_op jit(solution)/shard_map/ppermute | solution.py:128
  65.5 2.1 %fusion.55 = f32[2,2,16,32,128]{4,3,2,1,0:T(8,128)S(1)} fusion(f32[2,1,16,32,128]{4,3,2,1,0:T(8,128)S(1)} %get-tuple-element.67, f32[2,1,16,32,128]{4,3,2,1,0:T(8,128)S(1)} %get-tuple-element.66, f32[2,2,16,32,128]{4,3,2,1,0:T(8,128)S(1)} %convolution_bitcast_fusion.4, f32[2,2,16,2,128]{4,3,2,1,0:T(2,128)S(1)} %get-tuple-element.115, ...), kind=kLoop, calls=%fused_computation.175 | loop fusion | flops 11534336 | bytes 4063240 | tf_op jit(solution)/shard_map/mul | solution.py:170
  69.9 1.6 %collective-permute-start.17 = (f32[2,2,16,4,128]{4,3,2,1,0:T(4,128)S(1)}, f32[2,2,16,4,128]{4,3,2,1,0:T(4,128)S(1)}, u32[]{:S(2)}, u32[]{:S(2)}) collective-permute-start(f32[2,2,16,4,128]{4,3,2,1,0:T(4,128)S(1)} %pad_maximum_fusion.39), channel_id=1, source_target_pairs={{0,1},{1,0},{2,3},{3,2},{4,5},{5,4},{6,7},{7,6},{8,9},{9,8},{10,11... | collective-permute-start | bytes 393224 | tf_op jit(solution)/shard_map/ppermute | solution.py:124
  71.6 2.0 %collective-permute-start.16 = (f32[2,2,2,32,128]{4,3,2,1,0:T(8,128)S(1)}, f32[2,2,2,32,128]{4,3,2,1,0:T(8,128)S(1)}, u32[]{:S(2)}, u32[]{:S(2)}) collective-permute-start(f32[2,2,2,32,128]{4,3,2,1,0:T(8,128)S(1)} %get-tuple-element.55), channel_id=1, source_target_pairs={{0,16},{16,18},{18,2},{2,4},{4,20},{20,22},{22,6},{6,8},{8,24},{24... | collective-permute-start | bytes 393224 | tf_op jit(solution)/shard_map/ppermute | solution.py:128
  75.0 1.5 %collective-permute-done.15 = f32[2,2,2,32,128]{4,3,2,1,0:T(8,128)S(1)} collective-permute-done((f32[2,2,2,32,128]{4,3,2,1,0:T(8,128)S(1)}, f32[2,2,2,32,128]{4,3,2,1,0:T(8,128)S(1)}, u32[]{:S(2)}, u32[]{:S(2)}) %collective-permute-start.15) | collective-permute-done | bytes 131104 | tf_op jit(solution)/shard_map/ppermute | solution.py:129
  77.8 2.1 %fusion.59 = f32[2,2,16,32,128]{4,3,2,1,0:T(8,128)S(1)} fusion(f32[2,1,16,32,128]{4,3,2,1,0:T(8,128)S(1)} %get-tuple-element.59, f32[2,1,16,32,128]{4,3,2,1,0:T(8,128)S(1)} %get-tuple-element.58, f32[2,2,16,32,128]{4,3,2,1,0:T(8,128)S(1)} %convolution_bitcast_fusion.3, f32[2,2,16,2,128]{4,3,2,1,0:T(2,128)S(1)} %get-tuple-element.113, ...), kind=kLoop, calls=%fused_computation.180 | loop fusion | flops 11534336 | bytes 4063240 | tf_op jit(solution)/shard_map/mul | solution.py:170
  82.9 2.0 %collective-permute-start.19 = (f32[2,2,2,32,128]{4,3,2,1,0:T(8,128)S(1)}, f32[2,2,2,32,128]{4,3,2,1,0:T(8,128)S(1)}, u32[]{:S(2)}, u32[]{:S(2)}) collective-permute-start(f32[2,2,2,32,128]{4,3,2,1,0:T(8,128)S(1)} %get-tuple-element.47), channel_id=1, source_target_pairs={{0,16},{16,18},{18,2},{2,4},{4,20},{20,22},{22,6},{6,8},{8,24},{24... | collective-permute-start | bytes 393224 | tf_op jit(solution)/shard_map/ppermute | solution.py:128
  84.9 2.3 %collective-permute-done.20 = f32[2,2,16,4,128]{4,3,2,1,0:T(4,128)S(1)} collective-permute-done((f32[2,2,16,4,128]{4,3,2,1,0:T(4,128)S(1)}, f32[2,2,16,4,128]{4,3,2,1,0:T(4,128)S(1)}, u32[]{:S(2)}, u32[]{:S(2)}) %collective-permute-start.20) | collective-permute-done | bytes 131104 | tf_op jit(solution)/shard_map/ppermute | solution.py:124
  87.8 1.5 %collective-permute-done.19 = f32[2,2,2,32,128]{4,3,2,1,0:T(8,128)S(1)} collective-permute-done((f32[2,2,2,32,128]{4,3,2,1,0:T(8,128)S(1)}, f32[2,2,2,32,128]{4,3,2,1,0:T(8,128)S(1)}, u32[]{:S(2)}, u32[]{:S(2)}) %collective-permute-start.19) | collective-permute-done | bytes 131104 | tf_op jit(solution)/shard_map/ppermute | solution.py:128
  89.3 2.1 %fusion.63 = f32[2,2,16,32,128]{4,3,2,1,0:T(8,128)S(1)} fusion(f32[2,1,16,32,128]{4,3,2,1,0:T(8,128)S(1)} %get-tuple-element.51, f32[2,1,16,32,128]{4,3,2,1,0:T(8,128)S(1)} %get-tuple-element.50, f32[2,2,16,32,128]{4,3,2,1,0:T(8,128)S(1)} %convolution_bitcast_fusion.2, f32[2,2,16,2,128]{4,3,2,1,0:T(2,128)S(1)} %get-tuple-element.111, ...), kind=kLoop, calls=%fused_computation.185 | loop fusion | flops 11534336 | bytes 4063240 | tf_op jit(solution)/shard_map/mul | solution.py:170
  93.8 1.6 %collective-permute-start.23 = (f32[2,2,16,4,128]{4,3,2,1,0:T(4,128)S(1)}, f32[2,2,16,4,128]{4,3,2,1,0:T(4,128)S(1)}, u32[]{:S(2)}, u32[]{:S(2)}) collective-permute-start(f32[2,2,16,4,128]{4,3,2,1,0:T(4,128)S(1)} %pad_maximum_fusion.41), channel_id=1, source_target_pairs={{0,1},{1,0},{2,3},{3,2},{4,5},{5,4},{6,7},{7,6},{8,9},{9,8},{10,11... | collective-permute-start | bytes 393224 | tf_op jit(solution)/shard_map/ppermute | solution.py:124
  95.5 2.0 %collective-permute-start.22 = (f32[2,2,2,32,128]{4,3,2,1,0:T(8,128)S(1)}, f32[2,2,2,32,128]{4,3,2,1,0:T(8,128)S(1)}, u32[]{:S(2)}, u32[]{:S(2)}) collective-permute-start(f32[2,2,2,32,128]{4,3,2,1,0:T(8,128)S(1)} %get-tuple-element.39), channel_id=1, source_target_pairs={{0,16},{16,18},{18,2},{2,4},{4,20},{20,22},{22,6},{6,8},{8,24},{24... | collective-permute-start | bytes 393224 | tf_op jit(solution)/shard_map/ppermute | solution.py:128
  98.8 1.6 %collective-permute-done.21 = f32[2,2,2,32,128]{4,3,2,1,0:T(8,128)S(1)} collective-permute-done((f32[2,2,2,32,128]{4,3,2,1,0:T(8,128)S(1)}, f32[2,2,2,32,128]{4,3,2,1,0:T(8,128)S(1)}, u32[]{:S(2)}, u32[]{:S(2)}) %collective-permute-start.21) | collective-permute-done | bytes 131104 | tf_op jit(solution)/shard_map/ppermute | solution.py:129
  100.4 2.7 %collective-permute-done.22 = f32[2,2,2,32,128]{4,3,2,1,0:T(8,128)S(1)} collective-permute-done((f32[2,2,2,32,128]{4,3,2,1,0:T(8,128)S(1)}, f32[2,2,2,32,128]{4,3,2,1,0:T(8,128)S(1)}, u32[]{:S(2)}, u32[]{:S(2)}) %collective-permute-start.22) | collective-permute-done | bytes 131104 | tf_op jit(solution)/shard_map/ppermute | solution.py:128
  103.1 2.1 %fusion.67 = f32[2,2,16,32,128]{4,3,2,1,0:T(8,128)S(1)} fusion(f32[2,1,16,32,128]{4,3,2,1,0:T(8,128)S(1)} %get-tuple-element.43, f32[2,1,16,32,128]{4,3,2,1,0:T(8,128)S(1)} %get-tuple-element.42, f32[2,2,16,32,128]{4,3,2,1,0:T(8,128)S(1)} %convolution_bitcast_fusion.1, f32[2,2,16,2,128]{4,3,2,1,0:T(2,128)S(1)} %get-tuple-element.109, ...), kind=kLoop, calls=%fused_computation.190 | loop fusion | flops 11534336 | bytes 4063240 | tf_op jit(solution)/shard_map/mul | solution.py:170
  107.7 2.0 %collective-permute-start.25 = (f32[2,2,2,32,128]{4,3,2,1,0:T(8,128)S(1)}, f32[2,2,2,32,128]{4,3,2,1,0:T(8,128)S(1)}, u32[]{:S(2)}, u32[]{:S(2)}) collective-permute-start(f32[2,2,2,32,128]{4,3,2,1,0:T(8,128)S(1)} %get-tuple-element.31), channel_id=1, source_target_pairs={{0,16},{16,18},{18,2},{2,4},{4,20},{20,22},{22,6},{6,8},{8,24},{24... | collective-permute-start | bytes 393224 | tf_op jit(solution)/shard_map/ppermute | solution.py:128
  109.8 2.8 %collective-permute-done.26 = f32[2,2,16,4,128]{4,3,2,1,0:T(4,128)S(1)} collective-permute-done((f32[2,2,16,4,128]{4,3,2,1,0:T(4,128)S(1)}, f32[2,2,16,4,128]{4,3,2,1,0:T(4,128)S(1)}, u32[]{:S(2)}, u32[]{:S(2)}) %collective-permute-start.26) | collective-permute-done | bytes 131104 | tf_op jit(solution)/shard_map/ppermute | solution.py:124
  114.0 2.1 %fusion.71 = f32[2,2,16,32,128]{4,3,2,1,0:T(8,128)S(1)} fusion(f32[2,1,16,32,128]{4,3,2,1,0:T(8,128)S(1)} %get-tuple-element.35, f32[2,1,16,32,128]{4,3,2,1,0:T(8,128)S(1)} %get-tuple-element.34, f32[2,2,16,32,128]{4,3,2,1,0:T(8,128)S(1)} %convolution_bitcast_fusion, f32[2,2,16,2,128]{4,3,2,1,0:T(2,128)S(1)} %get-tuple-element.107, ...), kind=kLoop, calls=%fused_computation.195 | loop fusion | flops 11534336 | bytes 4063240 | tf_op jit(solution)/shard_map/mul | solution.py:170
  119.4 9.2 %collective-permute-done.27 = f32[1,2,16,32,128]{4,3,2,1,0:T(8,128)S(1)} collective-permute-done((f32[1,2,16,32,128]{4,3,2,1,0:T(8,128)S(1)}, f32[1,2,16,32,128]{4,3,2,1,0:T(8,128)S(1)}, u32[]{:S(2)}, u32[]{:S(2)}) %collective-permute-start.27) | collective-permute-done | bytes 524320 | tf_op jit(solution)/shard_map/ppermute | solution.py:237
  (137 shorter events, 43.6 us)
Async XLA Ops:
  1.2 13.1 %collective-permute-start.2 = (f32[1,2,16,4,128]{4,3,2,1,0:T(4,128)S(1)}, f32[1,2,16,4,128]{4,3,2,1,0:T(4,128)S(1)}, u32[]{:S(2)}, u32[]{:S(2)}) collective-permute-start(f32[1,2,16,4,128]{4,3,2,1,0:T(4,128)S(1)} %pad_maximum_fusion.43), channel_id=1, source_target_pairs={{0,1},{1,0},{2,3},{3,2},{4,5},{5,4},{6,7},{7,6},{8,9},{9,8},{10,11... | collective-permute-start | bytes 196616 | tf_op jit(solution)/shard_map/ppermute | solution.py:124
  4.2 10.1 %collective-permute-start = (f32[1,2,2,32,128]{4,3,2,1,0:T(8,128)S(1)}, f32[1,2,2,32,128]{4,3,2,1,0:T(8,128)S(1)}, u32[]{:S(2)}, u32[]{:S(2)}) collective-permute-start(f32[1,2,2,32,128]{4,3,2,1,0:T(8,128)S(1)} %get-tuple-element.100), channel_id=1, source_target_pairs={{16,0},{18,16},{2,18},{4,2},{20,4},{22,20},{6,22},{8,6},{24,8},{26... | collective-permute-start | bytes 196616 | tf_op jit(solution)/shard_map/ppermute | solution.py:129
  7.0 7.3 %collective-permute-start.1 = (f32[1,2,2,32,128]{4,3,2,1,0:T(8,128)S(1)}, f32[1,2,2,32,128]{4,3,2,1,0:T(8,128)S(1)}, u32[]{:S(2)}, u32[]{:S(2)}) collective-permute-start(f32[1,2,2,32,128]{4,3,2,1,0:T(8,128)S(1)} %get-tuple-element.101), channel_id=1, source_target_pairs={{0,16},{16,18},{18,2},{2,4},{4,20},{20,22},{22,6},{6,8},{8,24},{24... | collective-permute-start | bytes 196616 | tf_op jit(solution)/shard_map/ppermute | solution.py:128
  7.1 7.2 %copy-start.2 = (f32[2,32,32,128]{3,2,1,0:T(8,128)S(1)}, f32[2,32,32,128]{3,2,1,0:T(8,128)}, u32[]{:S(2)}) copy-start(f32[2,32,32,128]{3,2,1,0:T(8,128)} %param.12) | copy-start | bytes 3145732
  7.2 7.2 %copy-start.7 = (f32[2]{0:T(128)S(1)}, f32[2]{0:T(128)}, u32[]{:S(2)}) copy-start(f32[2]{0:T(128)} %constant.141.clone) | copy-start | bytes 28
  16.2 9.0 %collective-permute-start.3 = (f32[2,2,2,32,128]{4,3,2,1,0:T(8,128)S(1)}, f32[2,2,2,32,128]{4,3,2,1,0:T(8,128)S(1)}, u32[]{:S(2)}, u32[]{:S(2)}) collective-permute-start(f32[2,2,2,32,128]{4,3,2,1,0:T(8,128)S(1)} %get-tuple-element.86), channel_id=1, source_target_pairs={{16,0},{18,16},{2,18},{4,2},{20,4},{22,20},{6,22},{8,6},{24,8},{26... | collective-permute-start | bytes 393224 | tf_op jit(solution)/shard_map/ppermute | solution.py:129
  19.8 6.2 %collective-permute-start.4 = (f32[2,2,2,32,128]{4,3,2,1,0:T(8,128)S(1)}, f32[2,2,2,32,128]{4,3,2,1,0:T(8,128)S(1)}, u32[]{:S(2)}, u32[]{:S(2)}) collective-permute-start(f32[2,2,2,32,128]{4,3,2,1,0:T(8,128)S(1)} %get-tuple-element.87), channel_id=1, source_target_pairs={{0,16},{16,18},{18,2},{2,4},{4,20},{20,22},{22,6},{6,8},{8,24},{24... | collective-permute-start | bytes 393224 | tf_op jit(solution)/shard_map/ppermute | solution.py:128
  19.8 5.0 %collective-permute-start.5 = (f32[2,2,16,4,128]{4,3,2,1,0:T(4,128)S(1)}, f32[2,2,16,4,128]{4,3,2,1,0:T(4,128)S(1)}, u32[]{:S(2)}, u32[]{:S(2)}) collective-permute-start(f32[2,2,16,4,128]{4,3,2,1,0:T(4,128)S(1)} %pad_maximum_fusion.35), channel_id=1, source_target_pairs={{0,1},{1,0},{2,3},{3,2},{4,5},{5,4},{6,7},{7,6},{8,9},{9,8},{10,11... | collective-permute-start | bytes 393224 | tf_op jit(solution)/shard_map/ppermute | solution.py:124
  30.5 5.0 %collective-permute-start.8 = (f32[2,2,16,4,128]{4,3,2,1,0:T(4,128)S(1)}, f32[2,2,16,4,128]{4,3,2,1,0:T(4,128)S(1)}, u32[]{:S(2)}, u32[]{:S(2)}) collective-permute-start(f32[2,2,16,4,128]{4,3,2,1,0:T(4,128)S(1)} %pad_maximum_fusion.36), channel_id=1, source_target_pairs={{0,1},{1,0},{2,3},{3,2},{4,5},{5,4},{6,7},{7,6},{8,9},{9,8},{10,11... | collective-permute-start | bytes 393224 | tf_op jit(solution)/shard_map/ppermute | solution.py:124
  31.1 5.0 %collective-permute-start.6 = (f32[2,2,2,32,128]{4,3,2,1,0:T(8,128)S(1)}, f32[2,2,2,32,128]{4,3,2,1,0:T(8,128)S(1)}, u32[]{:S(2)}, u32[]{:S(2)}) collective-permute-start(f32[2,2,2,32,128]{4,3,2,1,0:T(8,128)S(1)} %get-tuple-element.78), channel_id=1, source_target_pairs={{16,0},{18,16},{2,18},{4,2},{20,4},{22,20},{6,22},{8,6},{24,8},{26... | collective-permute-start | bytes 393224 | tf_op jit(solution)/shard_map/ppermute | solution.py:129
  32.6 6.2 %collective-permute-start.7 = (f32[2,2,2,32,128]{4,3,2,1,0:T(8,128)S(1)}, f32[2,2,2,32,128]{4,3,2,1,0:T(8,128)S(1)}, u32[]{:S(2)}, u32[]{:S(2)}) collective-permute-start(f32[2,2,2,32,128]{4,3,2,1,0:T(8,128)S(1)} %get-tuple-element.79), channel_id=1, source_target_pairs={{0,16},{16,18},{18,2},{2,4},{4,20},{20,22},{22,6},{6,8},{8,24},{24... | collective-permute-start | bytes 393224 | tf_op jit(solution)/shard_map/ppermute | solution.py:128
  43.1 5.2 %collective-permute-start.11 = (f32[2,2,16,4,128]{4,3,2,1,0:T(4,128)S(1)}, f32[2,2,16,4,128]{4,3,2,1,0:T(4,128)S(1)}, u32[]{:S(2)}, u32[]{:S(2)}) collective-permute-start(f32[2,2,16,4,128]{4,3,2,1,0:T(4,128)S(1)} %pad_maximum_fusion.37), channel_id=1, source_target_pairs={{0,1},{1,0},{2,3},{3,2},{4,5},{5,4},{6,7},{7,6},{8,9},{9,8},{10,11... | collective-permute-start | bytes 393224 | tf_op jit(solution)/shard_map/ppermute | solution.py:124
  44.7 6.3 %collective-permute-start.10 = (f32[2,2,2,32,128]{4,3,2,1,0:T(8,128)S(1)}, f32[2,2,2,32,128]{4,3,2,1,0:T(8,128)S(1)}, u32[]{:S(2)}, u32[]{:S(2)}) collective-permute-start(f32[2,2,2,32,128]{4,3,2,1,0:T(8,128)S(1)} %get-tuple-element.71), channel_id=1, source_target_pairs={{0,16},{16,18},{18,2},{2,4},{4,20},{20,22},{22,6},{6,8},{8,24},{24... | collective-permute-start | bytes 393224 | tf_op jit(solution)/shard_map/ppermute | solution.py:128
  44.8 6.2 %collective-permute-start.9 = (f32[2,2,2,32,128]{4,3,2,1,0:T(8,128)S(1)}, f32[2,2,2,32,128]{4,3,2,1,0:T(8,128)S(1)}, u32[]{:S(2)}, u32[]{:S(2)}) collective-permute-start(f32[2,2,2,32,128]{4,3,2,1,0:T(8,128)S(1)} %get-tuple-element.70), channel_id=1, source_target_pairs={{16,0},{18,16},{2,18},{4,2},{20,4},{22,20},{6,22},{8,6},{24,8},{26... | collective-permute-start | bytes 393224 | tf_op jit(solution)/shard_map/ppermute | solution.py:129
  55.3 5.0 %collective-permute-start.14 = (f32[2,2,16,4,128]{4,3,2,1,0:T(4,128)S(1)}, f32[2,2,16,4,128]{4,3,2,1,0:T(4,128)S(1)}, u32[]{:S(2)}, u32[]{:S(2)}) collective-permute-start(f32[2,2,16,4,128]{4,3,2,1,0:T(4,128)S(1)} %pad_maximum_fusion.38), channel_id=1, source_target_pairs={{0,1},{1,0},{2,3},{3,2},{4,5},{5,4},{6,7},{7,6},{8,9},{9,8},{10,11... | collective-permute-start | bytes 393224 | tf_op jit(solution)/shard_map/ppermute | solution.py:124
  56.0 5.8 %collective-permute-start.12 = (f32[2,2,2,32,128]{4,3,2,1,0:T(8,128)S(1)}, f32[2,2,2,32,128]{4,3,2,1,0:T(8,128)S(1)}, u32[]{:S(2)}, u32[]{:S(2)}) collective-permute-start(f32[2,2,2,32,128]{4,3,2,1,0:T(8,128)S(1)} %get-tuple-element.62), channel_id=1, source_target_pairs={{16,0},{18,16},{2,18},{4,2},{20,4},{22,20},{6,22},{8,6},{24,8},{26... | collective-permute-start | bytes 393224 | tf_op jit(solution)/shard_map/ppermute | solution.py:129
  59.3 6.2 %collective-permute-start.13 = (f32[2,2,2,32,128]{4,3,2,1,0:T(8,128)S(1)}, f32[2,2,2,32,128]{4,3,2,1,0:T(8,128)S(1)}, u32[]{:S(2)}, u32[]{:S(2)}) collective-permute-start(f32[2,2,2,32,128]{4,3,2,1,0:T(8,128)S(1)} %get-tuple-element.63), channel_id=1, source_target_pairs={{0,16},{16,18},{18,2},{2,4},{4,20},{20,22},{22,6},{6,8},{8,24},{24... | collective-permute-start | bytes 393224 | tf_op jit(solution)/shard_map/ppermute | solution.py:128
  69.9 5.0 %collective-permute-start.17 = (f32[2,2,16,4,128]{4,3,2,1,0:T(4,128)S(1)}, f32[2,2,16,4,128]{4,3,2,1,0:T(4,128)S(1)}, u32[]{:S(2)}, u32[]{:S(2)}) collective-permute-start(f32[2,2,16,4,128]{4,3,2,1,0:T(4,128)S(1)} %pad_maximum_fusion.39), channel_id=1, source_target_pairs={{0,1},{1,0},{2,3},{3,2},{4,5},{5,4},{6,7},{7,6},{8,9},{9,8},{10,11... | collective-permute-start | bytes 393224 | tf_op jit(solution)/shard_map/ppermute | solution.py:124
  71.5 5.0 %collective-permute-start.15 = (f32[2,2,2,32,128]{4,3,2,1,0:T(8,128)S(1)}, f32[2,2,2,32,128]{4,3,2,1,0:T(8,128)S(1)}, u32[]{:S(2)}, u32[]{:S(2)}) collective-permute-start(f32[2,2,2,32,128]{4,3,2,1,0:T(8,128)S(1)} %get-tuple-element.54), channel_id=1, source_target_pairs={{16,0},{18,16},{2,18},{4,2},{20,4},{22,20},{6,22},{8,6},{24,8},{26... | collective-permute-start | bytes 393224 | tf_op jit(solution)/shard_map/ppermute | solution.py:129
  71.6 6.3 %collective-permute-start.16 = (f32[2,2,2,32,128]{4,3,2,1,0:T(8,128)S(1)}, f32[2,2,2,32,128]{4,3,2,1,0:T(8,128)S(1)}, u32[]{:S(2)}, u32[]{:S(2)}) collective-permute-start(f32[2,2,2,32,128]{4,3,2,1,0:T(8,128)S(1)} %get-tuple-element.55), channel_id=1, source_target_pairs={{0,16},{16,18},{18,2},{2,4},{4,20},{20,22},{22,6},{6,8},{8,24},{24... | collective-permute-start | bytes 393224 | tf_op jit(solution)/shard_map/ppermute | solution.py:128
  82.2 5.0 %collective-permute-start.20 = (f32[2,2,16,4,128]{4,3,2,1,0:T(4,128)S(1)}, f32[2,2,16,4,128]{4,3,2,1,0:T(4,128)S(1)}, u32[]{:S(2)}, u32[]{:S(2)}) collective-permute-start(f32[2,2,16,4,128]{4,3,2,1,0:T(4,128)S(1)} %pad_maximum_fusion.40), channel_id=1, source_target_pairs={{0,1},{1,0},{2,3},{3,2},{4,5},{5,4},{6,7},{7,6},{8,9},{9,8},{10,11... | collective-permute-start | bytes 393224 | tf_op jit(solution)/shard_map/ppermute | solution.py:124
  82.8 5.0 %collective-permute-start.18 = (f32[2,2,2,32,128]{4,3,2,1,0:T(8,128)S(1)}, f32[2,2,2,32,128]{4,3,2,1,0:T(8,128)S(1)}, u32[]{:S(2)}, u32[]{:S(2)}) collective-permute-start(f32[2,2,2,32,128]{4,3,2,1,0:T(8,128)S(1)} %get-tuple-element.46), channel_id=1, source_target_pairs={{16,0},{18,16},{2,18},{4,2},{20,4},{22,20},{6,22},{8,6},{24,8},{26... | collective-permute-start | bytes 393224 | tf_op jit(solution)/shard_map/ppermute | solution.py:129
  82.9 6.5 %collective-permute-start.19 = (f32[2,2,2,32,128]{4,3,2,1,0:T(8,128)S(1)}, f32[2,2,2,32,128]{4,3,2,1,0:T(8,128)S(1)}, u32[]{:S(2)}, u32[]{:S(2)}) collective-permute-start(f32[2,2,2,32,128]{4,3,2,1,0:T(8,128)S(1)} %get-tuple-element.47), channel_id=1, source_target_pairs={{0,16},{16,18},{18,2},{2,4},{4,20},{20,22},{22,6},{6,8},{8,24},{24... | collective-permute-start | bytes 393224 | tf_op jit(solution)/shard_map/ppermute | solution.py:128
  93.8 5.0 %collective-permute-start.23 = (f32[2,2,16,4,128]{4,3,2,1,0:T(4,128)S(1)}, f32[2,2,16,4,128]{4,3,2,1,0:T(4,128)S(1)}, u32[]{:S(2)}, u32[]{:S(2)}) collective-permute-start(f32[2,2,16,4,128]{4,3,2,1,0:T(4,128)S(1)} %pad_maximum_fusion.41), channel_id=1, source_target_pairs={{0,1},{1,0},{2,3},{3,2},{4,5},{5,4},{6,7},{7,6},{8,9},{9,8},{10,11... | collective-permute-start | bytes 393224 | tf_op jit(solution)/shard_map/ppermute | solution.py:124
  95.4 5.0 %collective-permute-start.21 = (f32[2,2,2,32,128]{4,3,2,1,0:T(8,128)S(1)}, f32[2,2,2,32,128]{4,3,2,1,0:T(8,128)S(1)}, u32[]{:S(2)}, u32[]{:S(2)}) collective-permute-start(f32[2,2,2,32,128]{4,3,2,1,0:T(8,128)S(1)} %get-tuple-element.38), channel_id=1, source_target_pairs={{16,0},{18,16},{2,18},{4,2},{20,4},{22,20},{6,22},{8,6},{24,8},{26... | collective-permute-start | bytes 393224 | tf_op jit(solution)/shard_map/ppermute | solution.py:129
  95.5 7.6 %collective-permute-start.22 = (f32[2,2,2,32,128]{4,3,2,1,0:T(8,128)S(1)}, f32[2,2,2,32,128]{4,3,2,1,0:T(8,128)S(1)}, u32[]{:S(2)}, u32[]{:S(2)}) collective-permute-start(f32[2,2,2,32,128]{4,3,2,1,0:T(8,128)S(1)} %get-tuple-element.39), channel_id=1, source_target_pairs={{0,16},{16,18},{18,2},{2,4},{4,20},{20,22},{22,6},{6,8},{8,24},{24... | collective-permute-start | bytes 393224 | tf_op jit(solution)/shard_map/ppermute | solution.py:128
  107.0 9.1 %copy-start = (f32[2,2,16,32,128]{4,3,2,1,0:T(8,128)}, f32[2,2,16,32,128]{4,3,2,1,0:T(8,128)S(1)}, u32[]{:S(2)}) copy-start(f32[2,2,16,32,128]{4,3,2,1,0:T(8,128)S(1)} %convolution_bitcast_fusion) | copy-start | bytes 3145732
  107.6 5.0 %collective-permute-start.26 = (f32[2,2,16,4,128]{4,3,2,1,0:T(4,128)S(1)}, f32[2,2,16,4,128]{4,3,2,1,0:T(4,128)S(1)}, u32[]{:S(2)}, u32[]{:S(2)}) collective-permute-start(f32[2,2,16,4,128]{4,3,2,1,0:T(4,128)S(1)} %pad_maximum_fusion.42), channel_id=1, source_target_pairs={{0,1},{1,0},{2,3},{3,2},{4,5},{5,4},{6,7},{7,6},{8,9},{9,8},{10,11... | collective-permute-start | bytes 393224 | tf_op jit(solution)/shard_map/ppermute | solution.py:124
  107.7 5.0 %collective-permute-start.24 = (f32[2,2,2,32,128]{4,3,2,1,0:T(8,128)S(1)}, f32[2,2,2,32,128]{4,3,2,1,0:T(8,128)S(1)}, u32[]{:S(2)}, u32[]{:S(2)}) collective-permute-start(f32[2,2,2,32,128]{4,3,2,1,0:T(8,128)S(1)} %get-tuple-element.30), channel_id=1, source_target_pairs={{16,0},{18,16},{2,18},{4,2},{20,4},{22,20},{6,22},{8,6},{24,8},{26... | collective-permute-start | bytes 393224 | tf_op jit(solution)/shard_map/ppermute | solution.py:129
  107.7 6.3 %collective-permute-start.25 = (f32[2,2,2,32,128]{4,3,2,1,0:T(8,128)S(1)}, f32[2,2,2,32,128]{4,3,2,1,0:T(8,128)S(1)}, u32[]{:S(2)}, u32[]{:S(2)}) collective-permute-start(f32[2,2,2,32,128]{4,3,2,1,0:T(8,128)S(1)} %get-tuple-element.31), channel_id=1, source_target_pairs={{0,16},{16,18},{18,2},{2,4},{4,20},{20,22},{22,6},{6,8},{8,24},{24... | collective-permute-start | bytes 393224 | tf_op jit(solution)/shard_map/ppermute | solution.py:128
  118.6 10.0 %copy-start.3 = (f32[1,2,32,32,128]{4,3,2,1,0:T(8,128)}, f32[1,2,32,32,128]{4,3,2,1,0:T(8,128)S(1)}, u32[]{:S(2)}) copy-start(f32[1,2,32,32,128]{4,3,2,1,0:T(8,128)S(1)} %get-tuple-element.27) | copy-start | bytes 3145732
  118.6 10.0 %collective-permute-start.27 = (f32[1,2,16,32,128]{4,3,2,1,0:T(8,128)S(1)}, f32[1,2,16,32,128]{4,3,2,1,0:T(8,128)S(1)}, u32[]{:S(2)}, u32[]{:S(2)}) collective-permute-start(f32[1,2,16,32,128]{4,3,2,1,0:T(8,128)S(1)} %get-tuple-element.26), channel_id=1, source_target_pairs={{0,16},{16,0},{1,17},{17,1},{2,18},{18,2},{3,19},{19,3},{4,20},{20... | collective-permute-start | bytes 1572872 | tf_op jit(solution)/shard_map/ppermute | solution.py:237
  (7 other events, 5.9 us)

commit v3 on v2

--- a/solution.py
+++ b/solution.py
@@ -234,7 +234,14 @@
     for shift in range(1, depth):
         pairs = [(c, (c + shift) % depth) for c in range(depth)]
         sent = lax.dynamic_index_in_dim(result, (me + shift) % depth, 0)
-        got = lax.ppermute(sent, "corr", pairs)
+        half = sent.shape[3] // 2
+        got = jnp.concatenate(
+            [
+                lax.ppermute(sent[:, :, :, :half], "corr", pairs),
+                lax.ppermute(sent[:, :, :, half:], "corr", pairs),
+            ],
+            3,
+        )
         origin = (me - shift) % depth
         out = lax.dynamic_update_slice_in_dim(
             out, got, slab_of(origin, tile, depth) * slab, 2

time: 130 us -> 130 us (level)
    ppermute x1 -> x2, waiting for transfers between devices: 9.23 us -> 7.91 us  [the longest x1 5.1 us: on_device(): lax.ppermute(sent[:, :, :, :half], 'corr', pairs)]
  transfers between devices with their start and end apart: 28 -> 29, of which waited for: 21 -> 22; matrix products, arithmetic and copies ran while one was open for 3% -> 3% of each run, Pallas kernels for 3% -> 3%
where the time goes in v3:
time: 130 us
  waiting for transfers between devices  45.5 us (35%)
  starting transfers between devices  36 us (28%)
  other arithmetic  28.3 us (22%)
  matrix products  8.77 us (7%)
  local copies, waits for them, and re-layouts  6.11 us (5%)
  Pallas kernels  4.11 us (3%)
    mul x9, other arithmetic, tendency(): return DT * (flow + kappa * (dx2 + dy2) + react)  17 us
    ppermute x9, waiting for transfers between devices, ring_halo(): before = lax.ppermute(last, axes, up)  16.4 us
    ppermute x9, waiting for transfers between devices, ring_halo(): got = lax.ppermute(jnp.concatenate([first, last], dim), axes, up)  15.6 us
    ppermute x9, starting transfers between devices, ring_halo(): after = lax.ppermute(first, axes, down)  15 us
    ppermute x9, starting transfers between devices, ring_halo(): got = lax.ppermute(jnp.concatenate([first, last], dim), axes, up)  10.2 us
    ppermute x9, starting transfers between devices, ring_halo(): before = lax.ppermute(last, axes, up)  8.8 us
    dot_general x9, matrix products, column_solve(): jnp.einsum('lsxyk,sjk->lsxyj', rhs, inverse, precision=lax.Precision.HIGH...  8.77 us
    ppermute x9, waiting for transfers between devices, ring_halo(): after = lax.ppermute(first, axes, down)  5.59 us
  transfers between devices with their start and end apart: 29, of which 22 were waited for; matrix products, arithmetic and copies ran while one was open for 3% of the time, Pallas kernels for 3%

profile of v3, /device:TPU:0, one launch (start us, length us, event | category | flops | bytes accessed | tf_op | source)
XLA Modules:
  0.0 129.5 jit_solution(6711904470351535088)
XLA Ops:
  1.2 3.0 %collective-permute-start.2 = (f32[1,2,16,4,128]{4,3,2,1,0:T(4,128)S(1)}, f32[1,2,16,4,128]{4,3,2,1,0:T(4,128)S(1)}, u32[]{:S(2)}, u32[]{:S(2)}) collective-permute-start(f32[1,2,16,4,128]{4,3,2,1,0:T(4,128)S(1)} %pad_maximum_fusion.43), channel_id=1, source_target_pairs={{0,1},{1,0},{2,3},{3,2},{4,5},{5,4},{6,7},{7,6},{8,9},{9,8},{10,11... | collective-permute-start | bytes 196616 | tf_op jit(solution)/shard_map/ppermute | solution.py:124
  4.2 2.8 %collective-permute-start = (f32[1,2,2,32,128]{4,3,2,1,0:T(8,128)S(1)}, f32[1,2,2,32,128]{4,3,2,1,0:T(8,128)S(1)}, u32[]{:S(2)}, u32[]{:S(2)}) collective-permute-start(f32[1,2,2,32,128]{4,3,2,1,0:T(8,128)S(1)} %get-tuple-element.102), channel_id=1, source_target_pairs={{16,0},{18,16},{2,18},{4,2},{20,4},{22,20},{6,22},{8,6},{24,8},{26... | collective-permute-start | bytes 196616 | tf_op jit(solution)/shard_map/ppermute | solution.py:129
  9.1 4.1 %shard_map.118 = f32[128,2,128]{2,1,0:T(2,128)} custom-call(f32[2,128]{1,0:T(2,128)} %copy-done.4, f32[2,128]{1,0:T(2,128)} %get-tuple-element.127.low_ref), custom_call_target="tpu_custom_call" | custom-call | flops 393216 | bytes 262144 | tf_op jit(solution)/shard_map/pallas_call | solution.py:78
  16.2 3.6 %collective-permute-start.3 = (f32[2,2,2,32,128]{4,3,2,1,0:T(8,128)S(1)}, f32[2,2,2,32,128]{4,3,2,1,0:T(8,128)S(1)}, u32[]{:S(2)}, u32[]{:S(2)}) collective-permute-start(f32[2,2,2,32,128]{4,3,2,1,0:T(8,128)S(1)} %get-tuple-element.86), channel_id=1, source_target_pairs={{16,0},{18,16},{2,18},{4,2},{20,4},{22,20},{6,22},{8,6},{24,8},{26... | collective-permute-start | bytes 393224 | tf_op jit(solution)/shard_map/ppermute | solution.py:129
  20.6 4.3 %collective-permute-done.5 = f32[2,2,16,4,128]{4,3,2,1,0:T(4,128)S(1)} collective-permute-done((f32[2,2,16,4,128]{4,3,2,1,0:T(4,128)S(1)}, f32[2,2,16,4,128]{4,3,2,1,0:T(4,128)S(1)}, u32[]{:S(2)}, u32[]{:S(2)}) %collective-permute-start.5) | collective-permute-done | bytes 131104 | tf_op jit(solution)/shard_map/ppermute | solution.py:124
  33.3 2.4 %collective-permute-done.8 = f32[2,2,16,4,128]{4,3,2,1,0:T(4,128)S(1)} collective-permute-done((f32[2,2,16,4,128]{4,3,2,1,0:T(4,128)S(1)}, f32[2,2,16,4,128]{4,3,2,1,0:T(4,128)S(1)}, u32[]{:S(2)}, u32[]{:S(2)}) %collective-permute-start.8) | collective-permute-done | bytes 131104 | tf_op jit(solution)/shard_map/ppermute | solution.py:124
  36.2 2.6 %collective-permute-done.7 = f32[2,2,2,32,128]{4,3,2,1,0:T(8,128)S(1)} collective-permute-done((f32[2,2,2,32,128]{4,3,2,1,0:T(8,128)S(1)}, f32[2,2,2,32,128]{4,3,2,1,0:T(8,128)S(1)}, u32[]{:S(2)}, u32[]{:S(2)}) %collective-permute-start.7) | collective-permute-done | bytes 131104 | tf_op jit(solution)/shard_map/ppermute | solution.py:128
  38.8 2.1 %fusion.47 = f32[2,2,16,32,128]{4,3,2,1,0:T(8,128)S(1)} fusion(f32[2,1,16,32,128]{4,3,2,1,0:T(8,128)S(1)} %get-tuple-element.83, f32[2,1,16,32,128]{4,3,2,1,0:T(8,128)S(1)} %get-tuple-element.82, f32[2,2,16,32,128]{4,3,2,1,0:T(8,128)S(1)} %convolution_bitcast_fusion.6, f32[2,2,16,2,128]{4,3,2,1,0:T(2,128)S(1)} %get-tuple-element.121, ...), kind=kLoop, calls=%fused_computation.165 | loop fusion | flops 11534336 | bytes 4063240 | tf_op jit(solution)/shard_map/mul | solution.py:170
  43.1 1.6 %collective-permute-start.11 = (f32[2,2,16,4,128]{4,3,2,1,0:T(4,128)S(1)}, f32[2,2,16,4,128]{4,3,2,1,0:T(4,128)S(1)}, u32[]{:S(2)}, u32[]{:S(2)}) collective-permute-start(f32[2,2,16,4,128]{4,3,2,1,0:T(4,128)S(1)} %pad_maximum_fusion.37), channel_id=1, source_target_pairs={{0,1},{1,0},{2,3},{3,2},{4,5},{5,4},{6,7},{7,6},{8,9},{9,8},{10,11... | collective-permute-start | bytes 393224 | tf_op jit(solution)/shard_map/ppermute | solution.py:124
  44.8 3.5 %collective-permute-start.9 = (f32[2,2,2,32,128]{4,3,2,1,0:T(8,128)S(1)}, f32[2,2,2,32,128]{4,3,2,1,0:T(8,128)S(1)}, u32[]{:S(2)}, u32[]{:S(2)}) collective-permute-start(f32[2,2,2,32,128]{4,3,2,1,0:T(8,128)S(1)} %get-tuple-element.70), channel_id=1, source_target_pairs={{16,0},{18,16},{2,18},{4,2},{20,4},{22,20},{6,22},{8,6},{24,8},{26... | collective-permute-start | bytes 393224 | tf_op jit(solution)/shard_map/ppermute | solution.py:129
  48.4 2.6 %collective-permute-done.10 = f32[2,2,2,32,128]{4,3,2,1,0:T(8,128)S(1)} collective-permute-done((f32[2,2,2,32,128]{4,3,2,1,0:T(8,128)S(1)}, f32[2,2,2,32,128]{4,3,2,1,0:T(8,128)S(1)}, u32[]{:S(2)}, u32[]{:S(2)}) %collective-permute-start.10) | collective-permute-done | bytes 131104 | tf_op jit(solution)/shard_map/ppermute | solution.py:128
  51.0 2.1 %fusion.51 = f32[2,2,16,32,128]{4,3,2,1,0:T(8,128)S(1)} fusion(f32[2,1,16,32,128]{4,3,2,1,0:T(8,128)S(1)} %get-tuple-element.75, f32[2,1,16,32,128]{4,3,2,1,0:T(8,128)S(1)} %get-tuple-element.74, f32[2,2,16,32,128]{4,3,2,1,0:T(8,128)S(1)} %convolution_bitcast_fusion.5, f32[2,2,16,2,128]{4,3,2,1,0:T(2,128)S(1)} %get-tuple-element.119, ...), kind=kLoop, calls=%fused_computation.170 | loop fusion | flops 11534336 | bytes 4063240 | tf_op jit(solution)/shard_map/mul | solution.py:170
  56.0 3.3 %collective-permute-start.12 = (f32[2,2,2,32,128]{4,3,2,1,0:T(8,128)S(1)}, f32[2,2,2,32,128]{4,3,2,1,0:T(8,128)S(1)}, u32[]{:S(2)}, u32[]{:S(2)}) collective-permute-start(f32[2,2,2,32,128]{4,3,2,1,0:T(8,128)S(1)} %get-tuple-element.62), channel_id=1, source_target_pairs={{16,0},{18,16},{2,18},{4,2},{20,4},{22,20},{6,22},{8,6},{24,8},{26... | collective-permute-start | bytes 393224 | tf_op jit(solution)/shard_map/ppermute | solution.py:129
  61.8 3.7 %collective-permute-done.13 = f32[2,2,2,32,128]{4,3,2,1,0:T(8,128)S(1)} collective-permute-done((f32[2,2,2,32,128]{4,3,2,1,0:T(8,128)S(1)}, f32[2,2,2,32,128]{4,3,2,1,0:T(8,128)S(1)}, u32[]{:S(2)}, u32[]{:S(2)}) %collective-permute-start.13) | collective-permute-done | bytes 131104 | tf_op jit(solution)/shard_map/ppermute | solution.py:128
  65.5 2.1 %fusion.55 = f32[2,2,16,32,128]{4,3,2,1,0:T(8,128)S(1)} fusion(f32[2,1,16,32,128]{4,3,2,1,0:T(8,128)S(1)} %get-tuple-element.67, f32[2,1,16,32,128]{4,3,2,1,0:T(8,128)S(1)} %get-tuple-element.66, f32[2,2,16,32,128]{4,3,2,1,0:T(8,128)S(1)} %convolution_bitcast_fusion.4, f32[2,2,16,2,128]{4,3,2,1,0:T(2,128)S(1)} %get-tuple-element.117, ...), kind=kLoop, calls=%fused_computation.175 | loop fusion | flops 11534336 | bytes 4063240 | tf_op jit(solution)/shard_map/mul | solution.py:170
  69.9 1.6 %collective-permute-start.17 = (f32[2,2,16,4,128]{4,3,2,1,0:T(4,128)S(1)}, f32[2,2,16,4,128]{4,3,2,1,0:T(4,128)S(1)}, u32[]{:S(2)}, u32[]{:S(2)}) collective-permute-start(f32[2,2,16,4,128]{4,3,2,1,0:T(4,128)S(1)} %pad_maximum_fusion.39), channel_id=1, source_target_pairs={{0,1},{1,0},{2,3},{3,2},{4,5},{5,4},{6,7},{7,6},{8,9},{9,8},{10,11... | collective-permute-start | bytes 393224 | tf_op jit(solution)/shard_map/ppermute | solution.py:124
  71.6 2.0 %collective-permute-start.16 = (f32[2,2,2,32,128]{4,3,2,1,0:T(8,128)S(1)}, f32[2,2,2,32,128]{4,3,2,1,0:T(8,128)S(1)}, u32[]{:S(2)}, u32[]{:S(2)}) collective-permute-start(f32[2,2,2,32,128]{4,3,2,1,0:T(8,128)S(1)} %get-tuple-element.55), channel_id=1, source_target_pairs={{0,16},{16,18},{18,2},{2,4},{4,20},{20,22},{22,6},{6,8},{8,24},{24... | collective-permute-start | bytes 393224 | tf_op jit(solution)/shard_map/ppermute | solution.py:128
  75.0 1.6 %collective-permute-done.15 = f32[2,2,2,32,128]{4,3,2,1,0:T(8,128)S(1)} collective-permute-done((f32[2,2,2,32,128]{4,3,2,1,0:T(8,128)S(1)}, f32[2,2,2,32,128]{4,3,2,1,0:T(8,128)S(1)}, u32[]{:S(2)}, u32[]{:S(2)}) %collective-permute-start.15) | collective-permute-done | bytes 131104 | tf_op jit(solution)/shard_map/ppermute | solution.py:129
  77.9 2.1 %fusion.59 = f32[2,2,16,32,128]{4,3,2,1,0:T(8,128)S(1)} fusion(f32[2,1,16,32,128]{4,3,2,1,0:T(8,128)S(1)} %get-tuple-element.59, f32[2,1,16,32,128]{4,3,2,1,0:T(8,128)S(1)} %get-tuple-element.58, f32[2,2,16,32,128]{4,3,2,1,0:T(8,128)S(1)} %convolution_bitcast_fusion.3, f32[2,2,16,2,128]{4,3,2,1,0:T(2,128)S(1)} %get-tuple-element.115, ...), kind=kLoop, calls=%fused_computation.180 | loop fusion | flops 11534336 | bytes 4063240 | tf_op jit(solution)/shard_map/mul | solution.py:170
  82.9 2.0 %collective-permute-start.19 = (f32[2,2,2,32,128]{4,3,2,1,0:T(8,128)S(1)}, f32[2,2,2,32,128]{4,3,2,1,0:T(8,128)S(1)}, u32[]{:S(2)}, u32[]{:S(2)}) collective-permute-start(f32[2,2,2,32,128]{4,3,2,1,0:T(8,128)S(1)} %get-tuple-element.47), channel_id=1, source_target_pairs={{0,16},{16,18},{18,2},{2,4},{4,20},{20,22},{22,6},{6,8},{8,24},{24... | collective-permute-start | bytes 393224 | tf_op jit(solution)/shard_map/ppermute | solution.py:128
  84.9 2.4 %collective-permute-done.20 = f32[2,2,16,4,128]{4,3,2,1,0:T(4,128)S(1)} collective-permute-done((f32[2,2,16,4,128]{4,3,2,1,0:T(4,128)S(1)}, f32[2,2,16,4,128]{4,3,2,1,0:T(4,128)S(1)}, u32[]{:S(2)}, u32[]{:S(2)}) %collective-permute-start.20) | collective-permute-done | bytes 131104 | tf_op jit(solution)/shard_map/ppermute | solution.py:124
  89.3 2.1 %fusion.63 = f32[2,2,16,32,128]{4,3,2,1,0:T(8,128)S(1)} fusion(f32[2,1,16,32,128]{4,3,2,1,0:T(8,128)S(1)} %get-tuple-element.51, f32[2,1,16,32,128]{4,3,2,1,0:T(8,128)S(1)} %get-tuple-element.50, f32[2,2,16,32,128]{4,3,2,1,0:T(8,128)S(1)} %convolution_bitcast_fusion.2, f32[2,2,16,2,128]{4,3,2,1,0:T(2,128)S(1)} %get-tuple-element.113, ...), kind=kLoop, calls=%fused_computation.185 | loop fusion | flops 11534336 | bytes 4063240 | tf_op jit(solution)/shard_map/mul | solution.py:170
  93.8 1.6 %collective-permute-start.23 = (f32[2,2,16,4,128]{4,3,2,1,0:T(4,128)S(1)}, f32[2,2,16,4,128]{4,3,2,1,0:T(4,128)S(1)}, u32[]{:S(2)}, u32[]{:S(2)}) collective-permute-start(f32[2,2,16,4,128]{4,3,2,1,0:T(4,128)S(1)} %pad_maximum_fusion.41), channel_id=1, source_target_pairs={{0,1},{1,0},{2,3},{3,2},{4,5},{5,4},{6,7},{7,6},{8,9},{9,8},{10,11... | collective-permute-start | bytes 393224 | tf_op jit(solution)/shard_map/ppermute | solution.py:124
  95.5 2.0 %collective-permute-start.22 = (f32[2,2,2,32,128]{4,3,2,1,0:T(8,128)S(1)}, f32[2,2,2,32,128]{4,3,2,1,0:T(8,128)S(1)}, u32[]{:S(2)}, u32[]{:S(2)}) collective-permute-start(f32[2,2,2,32,128]{4,3,2,1,0:T(8,128)S(1)} %get-tuple-element.39), channel_id=1, source_target_pairs={{0,16},{16,18},{18,2},{2,4},{4,20},{20,22},{22,6},{6,8},{8,24},{24... | collective-permute-start | bytes 393224 | tf_op jit(solution)/shard_map/ppermute | solution.py:128
  98.9 1.6 %collective-permute-done.21 = f32[2,2,2,32,128]{4,3,2,1,0:T(8,128)S(1)} collective-permute-done((f32[2,2,2,32,128]{4,3,2,1,0:T(8,128)S(1)}, f32[2,2,2,32,128]{4,3,2,1,0:T(8,128)S(1)}, u32[]{:S(2)}, u32[]{:S(2)}) %collective-permute-start.21) | collective-permute-done | bytes 131104 | tf_op jit(solution)/shard_map/ppermute | solution.py:129
  100.4 2.7 %collective-permute-done.22 = f32[2,2,2,32,128]{4,3,2,1,0:T(8,128)S(1)} collective-permute-done((f32[2,2,2,32,128]{4,3,2,1,0:T(8,128)S(1)}, f32[2,2,2,32,128]{4,3,2,1,0:T(8,128)S(1)}, u32[]{:S(2)}, u32[]{:S(2)}) %collective-permute-start.22) | collective-permute-done | bytes 131104 | tf_op jit(solution)/shard_map/ppermute | solution.py:128
  103.1 2.1 %fusion.67 = f32[2,2,16,32,128]{4,3,2,1,0:T(8,128)S(1)} fusion(f32[2,1,16,32,128]{4,3,2,1,0:T(8,128)S(1)} %get-tuple-element.43, f32[2,1,16,32,128]{4,3,2,1,0:T(8,128)S(1)} %get-tuple-element.42, f32[2,2,16,32,128]{4,3,2,1,0:T(8,128)S(1)} %convolution_bitcast_fusion.1, f32[2,2,16,2,128]{4,3,2,1,0:T(2,128)S(1)} %get-tuple-element.111, ...), kind=kLoop, calls=%fused_computation.190 | loop fusion | flops 11534336 | bytes 4063240 | tf_op jit(solution)/shard_map/mul | solution.py:170
  107.8 2.0 %collective-permute-start.25 = (f32[2,2,2,32,128]{4,3,2,1,0:T(8,128)S(1)}, f32[2,2,2,32,128]{4,3,2,1,0:T(8,128)S(1)}, u32[]{:S(2)}, u32[]{:S(2)}) collective-permute-start(f32[2,2,2,32,128]{4,3,2,1,0:T(8,128)S(1)} %get-tuple-element.31), channel_id=1, source_target_pairs={{0,16},{16,18},{18,2},{2,4},{4,20},{20,22},{22,6},{6,8},{8,24},{24... | collective-permute-start | bytes 393224 | tf_op jit(solution)/shard_map/ppermute | solution.py:128
  109.8 2.8 %collective-permute-done.26 = f32[2,2,16,4,128]{4,3,2,1,0:T(4,128)S(1)} collective-permute-done((f32[2,2,16,4,128]{4,3,2,1,0:T(4,128)S(1)}, f32[2,2,16,4,128]{4,3,2,1,0:T(4,128)S(1)}, u32[]{:S(2)}, u32[]{:S(2)}) %collective-permute-start.26) | collective-permute-done | bytes 131104 | tf_op jit(solution)/shard_map/ppermute | solution.py:124
  114.0 2.1 %fusion.71 = f32[2,2,16,32,128]{4,3,2,1,0:T(8,128)S(1)} fusion(f32[2,1,16,32,128]{4,3,2,1,0:T(8,128)S(1)} %get-tuple-element.35, f32[2,1,16,32,128]{4,3,2,1,0:T(8,128)S(1)} %get-tuple-element.34, f32[2,2,16,32,128]{4,3,2,1,0:T(8,128)S(1)} %convolution_bitcast_fusion, f32[2,2,16,2,128]{4,3,2,1,0:T(2,128)S(1)} %get-tuple-element.109, ...), kind=kLoop, calls=%fused_computation.195 | loop fusion | flops 11534336 | bytes 4063240 | tf_op jit(solution)/shard_map/mul | solution.py:170
  120.8 5.1 %collective-permute-done.27 = f32[1,2,16,16,128]{4,3,2,1,0:T(8,128)S(1)} collective-permute-done((f32[1,2,16,16,128]{4,3,2,1,0:T(8,128)S(1)}, f32[1,2,16,16,128]{4,3,2,1,0:T(8,128)S(1)}, u32[]{:S(2)}, u32[]{:S(2)}) %collective-permute-start.27) | collective-permute-done | bytes 262176 | tf_op jit(solution)/shard_map/ppermute | solution.py:240
  125.9 2.8 %collective-permute-done.28 = f32[1,2,16,16,128]{4,3,2,1,0:T(8,128)S(1)} collective-permute-done((f32[1,2,16,16,128]{4,3,2,1,0:T(8,128)S(1)}, f32[1,2,16,16,128]{4,3,2,1,0:T(8,128)S(1)}, u32[]{:S(2)}, u32[]{:S(2)}) %collective-permute-start.28) | collective-permute-done | bytes 262176 | tf_op jit(solution)/shard_map/ppermute | solution.py:241
  (140 shorter events, 46.4 us)
Async XLA Ops:
  1.2 13.2 %collective-permute-start.2 = (f32[1,2,16,4,128]{4,3,2,1,0:T(4,128)S(1)}, f32[1,2,16,4,128]{4,3,2,1,0:T(4,128)S(1)}, u32[]{:S(2)}, u32[]{:S(2)}) collective-permute-start(f32[1,2,16,4,128]{4,3,2,1,0:T(4,128)S(1)} %pad_maximum_fusion.43), channel_id=1, source_target_pairs={{0,1},{1,0},{2,3},{3,2},{4,5},{5,4},{6,7},{7,6},{8,9},{9,8},{10,11... | collective-permute-start | bytes 196616 | tf_op jit(solution)/shard_map/ppermute | solution.py:124
  4.2 10.2 %collective-permute-start = (f32[1,2,2,32,128]{4,3,2,1,0:T(8,128)S(1)}, f32[1,2,2,32,128]{4,3,2,1,0:T(8,128)S(1)}, u32[]{:S(2)}, u32[]{:S(2)}) collective-permute-start(f32[1,2,2,32,128]{4,3,2,1,0:T(8,128)S(1)} %get-tuple-element.102), channel_id=1, source_target_pairs={{16,0},{18,16},{2,18},{4,2},{20,4},{22,20},{6,22},{8,6},{24,8},{26... | collective-permute-start | bytes 196616 | tf_op jit(solution)/shard_map/ppermute | solution.py:129
  7.0 7.3 %collective-permute-start.1 = (f32[1,2,2,32,128]{4,3,2,1,0:T(8,128)S(1)}, f32[1,2,2,32,128]{4,3,2,1,0:T(8,128)S(1)}, u32[]{:S(2)}, u32[]{:S(2)}) collective-permute-start(f32[1,2,2,32,128]{4,3,2,1,0:T(8,128)S(1)} %get-tuple-element.103), channel_id=1, source_target_pairs={{0,16},{16,18},{18,2},{2,4},{4,20},{20,22},{22,6},{6,8},{8,24},{24... | collective-permute-start | bytes 196616 | tf_op jit(solution)/shard_map/ppermute | solution.py:128
  7.1 7.2 %copy-start.2 = (f32[2,32,32,128]{3,2,1,0:T(8,128)S(1)}, f32[2,32,32,128]{3,2,1,0:T(8,128)}, u32[]{:S(2)}) copy-start(f32[2,32,32,128]{3,2,1,0:T(8,128)} %param.12) | copy-start | bytes 3145732
  16.2 9.0 %collective-permute-start.3 = (f32[2,2,2,32,128]{4,3,2,1,0:T(8,128)S(1)}, f32[2,2,2,32,128]{4,3,2,1,0:T(8,128)S(1)}, u32[]{:S(2)}, u32[]{:S(2)}) collective-permute-start(f32[2,2,2,32,128]{4,3,2,1,0:T(8,128)S(1)} %get-tuple-element.86), channel_id=1, source_target_pairs={{16,0},{18,16},{2,18},{4,2},{20,4},{22,20},{6,22},{8,6},{24,8},{26... | collective-permute-start | bytes 393224 | tf_op jit(solution)/shard_map/ppermute | solution.py:129
  19.8 6.2 %collective-permute-start.4 = (f32[2,2,2,32,128]{4,3,2,1,0:T(8,128)S(1)}, f32[2,2,2,32,128]{4,3,2,1,0:T(8,128)S(1)}, u32[]{:S(2)}, u32[]{:S(2)}) collective-permute-start(f32[2,2,2,32,128]{4,3,2,1,0:T(8,128)S(1)} %get-tuple-element.87), channel_id=1, source_target_pairs={{0,16},{16,18},{18,2},{2,4},{4,20},{20,22},{22,6},{6,8},{8,24},{24... | collective-permute-start | bytes 393224 | tf_op jit(solution)/shard_map/ppermute | solution.py:128
  19.9 5.0 %collective-permute-start.5 = (f32[2,2,16,4,128]{4,3,2,1,0:T(4,128)S(1)}, f32[2,2,16,4,128]{4,3,2,1,0:T(4,128)S(1)}, u32[]{:S(2)}, u32[]{:S(2)}) collective-permute-start(f32[2,2,16,4,128]{4,3,2,1,0:T(4,128)S(1)} %pad_maximum_fusion.35), channel_id=1, source_target_pairs={{0,1},{1,0},{2,3},{3,2},{4,5},{5,4},{6,7},{7,6},{8,9},{9,8},{10,11... | collective-permute-start | bytes 393224 | tf_op jit(solution)/shard_map/ppermute | solution.py:124
  30.6 5.0 %collective-permute-start.8 = (f32[2,2,16,4,128]{4,3,2,1,0:T(4,128)S(1)}, f32[2,2,16,4,128]{4,3,2,1,0:T(4,128)S(1)}, u32[]{:S(2)}, u32[]{:S(2)}) collective-permute-start(f32[2,2,16,4,128]{4,3,2,1,0:T(4,128)S(1)} %pad_maximum_fusion.36), channel_id=1, source_target_pairs={{0,1},{1,0},{2,3},{3,2},{4,5},{5,4},{6,7},{7,6},{8,9},{9,8},{10,11... | collective-permute-start | bytes 393224 | tf_op jit(solution)/shard_map/ppermute | solution.py:124
  31.2 5.0 %collective-permute-start.6 = (f32[2,2,2,32,128]{4,3,2,1,0:T(8,128)S(1)}, f32[2,2,2,32,128]{4,3,2,1,0:T(8,128)S(1)}, u32[]{:S(2)}, u32[]{:S(2)}) collective-permute-start(f32[2,2,2,32,128]{4,3,2,1,0:T(8,128)S(1)} %get-tuple-element.78), channel_id=1, source_target_pairs={{16,0},{18,16},{2,18},{4,2},{20,4},{22,20},{6,22},{8,6},{24,8},{26... | collective-permute-start | bytes 393224 | tf_op jit(solution)/shard_map/ppermute | solution.py:129
  32.6 6.2 %collective-permute-start.7 = (f32[2,2,2,32,128]{4,3,2,1,0:T(8,128)S(1)}, f32[2,2,2,32,128]{4,3,2,1,0:T(8,128)S(1)}, u32[]{:S(2)}, u32[]{:S(2)}) collective-permute-start(f32[2,2,2,32,128]{4,3,2,1,0:T(8,128)S(1)} %get-tuple-element.79), channel_id=1, source_target_pairs={{0,16},{16,18},{18,2},{2,4},{4,20},{20,22},{22,6},{6,8},{8,24},{24... | collective-permute-start | bytes 393224 | tf_op jit(solution)/shard_map/ppermute | solution.py:128
  43.1 5.2 %collective-permute-start.11 = (f32[2,2,16,4,128]{4,3,2,1,0:T(4,128)S(1)}, f32[2,2,16,4,128]{4,3,2,1,0:T(4,128)S(1)}, u32[]{:S(2)}, u32[]{:S(2)}) collective-permute-start(f32[2,2,16,4,128]{4,3,2,1,0:T(4,128)S(1)} %pad_maximum_fusion.37), channel_id=1, source_target_pairs={{0,1},{1,0},{2,3},{3,2},{4,5},{5,4},{6,7},{7,6},{8,9},{9,8},{10,11... | collective-permute-start | bytes 393224 | tf_op jit(solution)/shard_map/ppermute | solution.py:124
  44.8 6.3 %collective-permute-start.10 = (f32[2,2,2,32,128]{4,3,2,1,0:T(8,128)S(1)}, f32[2,2,2,32,128]{4,3,2,1,0:T(8,128)S(1)}, u32[]{:S(2)}, u32[]{:S(2)}) collective-permute-start(f32[2,2,2,32,128]{4,3,2,1,0:T(8,128)S(1)} %get-tuple-element.71), channel_id=1, source_target_pairs={{0,16},{16,18},{18,2},{2,4},{4,20},{20,22},{22,6},{6,8},{8,24},{24... | collective-permute-start | bytes 393224 | tf_op jit(solution)/shard_map/ppermute | solution.py:128
  44.8 6.2 %collective-permute-start.9 = (f32[2,2,2,32,128]{4,3,2,1,0:T(8,128)S(1)}, f32[2,2,2,32,128]{4,3,2,1,0:T(8,128)S(1)}, u32[]{:S(2)}, u32[]{:S(2)}) collective-permute-start(f32[2,2,2,32,128]{4,3,2,1,0:T(8,128)S(1)} %get-tuple-element.70), channel_id=1, source_target_pairs={{16,0},{18,16},{2,18},{4,2},{20,4},{22,20},{6,22},{8,6},{24,8},{26... | collective-permute-start | bytes 393224 | tf_op jit(solution)/shard_map/ppermute | solution.py:129
  55.4 5.0 %collective-permute-start.14 = (f32[2,2,16,4,128]{4,3,2,1,0:T(4,128)S(1)}, f32[2,2,16,4,128]{4,3,2,1,0:T(4,128)S(1)}, u32[]{:S(2)}, u32[]{:S(2)}) collective-permute-start(f32[2,2,16,4,128]{4,3,2,1,0:T(4,128)S(1)} %pad_maximum_fusion.38), channel_id=1, source_target_pairs={{0,1},{1,0},{2,3},{3,2},{4,5},{5,4},{6,7},{7,6},{8,9},{9,8},{10,11... | collective-permute-start | bytes 393224 | tf_op jit(solution)/shard_map/ppermute | solution.py:124
  56.0 5.8 %collective-permute-start.12 = (f32[2,2,2,32,128]{4,3,2,1,0:T(8,128)S(1)}, f32[2,2,2,32,128]{4,3,2,1,0:T(8,128)S(1)}, u32[]{:S(2)}, u32[]{:S(2)}) collective-permute-start(f32[2,2,2,32,128]{4,3,2,1,0:T(8,128)S(1)} %get-tuple-element.62), channel_id=1, source_target_pairs={{16,0},{18,16},{2,18},{4,2},{20,4},{22,20},{6,22},{8,6},{24,8},{26... | collective-permute-start | bytes 393224 | tf_op jit(solution)/shard_map/ppermute | solution.py:129
  59.3 6.2 %collective-permute-start.13 = (f32[2,2,2,32,128]{4,3,2,1,0:T(8,128)S(1)}, f32[2,2,2,32,128]{4,3,2,1,0:T(8,128)S(1)}, u32[]{:S(2)}, u32[]{:S(2)}) collective-permute-start(f32[2,2,2,32,128]{4,3,2,1,0:T(8,128)S(1)} %get-tuple-element.63), channel_id=1, source_target_pairs={{0,16},{16,18},{18,2},{2,4},{4,20},{20,22},{22,6},{6,8},{8,24},{24... | collective-permute-start | bytes 393224 | tf_op jit(solution)/shard_map/ppermute | solution.py:128
  69.9 5.0 %collective-permute-start.17 = (f32[2,2,16,4,128]{4,3,2,1,0:T(4,128)S(1)}, f32[2,2,16,4,128]{4,3,2,1,0:T(4,128)S(1)}, u32[]{:S(2)}, u32[]{:S(2)}) collective-permute-start(f32[2,2,16,4,128]{4,3,2,1,0:T(4,128)S(1)} %pad_maximum_fusion.39), channel_id=1, source_target_pairs={{0,1},{1,0},{2,3},{3,2},{4,5},{5,4},{6,7},{7,6},{8,9},{9,8},{10,11... | collective-permute-start | bytes 393224 | tf_op jit(solution)/shard_map/ppermute | solution.py:124
  71.5 5.0 %collective-permute-start.15 = (f32[2,2,2,32,128]{4,3,2,1,0:T(8,128)S(1)}, f32[2,2,2,32,128]{4,3,2,1,0:T(8,128)S(1)}, u32[]{:S(2)}, u32[]{:S(2)}) collective-permute-start(f32[2,2,2,32,128]{4,3,2,1,0:T(8,128)S(1)} %get-tuple-element.54), channel_id=1, source_target_pairs={{16,0},{18,16},{2,18},{4,2},{20,4},{22,20},{6,22},{8,6},{24,8},{26... | collective-permute-start | bytes 393224 | tf_op jit(solution)/shard_map/ppermute | solution.py:129
  71.6 6.3 %collective-permute-start.16 = (f32[2,2,2,32,128]{4,3,2,1,0:T(8,128)S(1)}, f32[2,2,2,32,128]{4,3,2,1,0:T(8,128)S(1)}, u32[]{:S(2)}, u32[]{:S(2)}) collective-permute-start(f32[2,2,2,32,128]{4,3,2,1,0:T(8,128)S(1)} %get-tuple-element.55), channel_id=1, source_target_pairs={{0,16},{16,18},{18,2},{2,4},{4,20},{20,22},{22,6},{6,8},{8,24},{24... | collective-permute-start | bytes 393224 | tf_op jit(solution)/shard_map/ppermute | solution.py:128
  82.2 5.0 %collective-permute-start.20 = (f32[2,2,16,4,128]{4,3,2,1,0:T(4,128)S(1)}, f32[2,2,16,4,128]{4,3,2,1,0:T(4,128)S(1)}, u32[]{:S(2)}, u32[]{:S(2)}) collective-permute-start(f32[2,2,16,4,128]{4,3,2,1,0:T(4,128)S(1)} %pad_maximum_fusion.40), channel_id=1, source_target_pairs={{0,1},{1,0},{2,3},{3,2},{4,5},{5,4},{6,7},{7,6},{8,9},{9,8},{10,11... | collective-permute-start | bytes 393224 | tf_op jit(solution)/shard_map/ppermute | solution.py:124
  82.8 5.0 %collective-permute-start.18 = (f32[2,2,2,32,128]{4,3,2,1,0:T(8,128)S(1)}, f32[2,2,2,32,128]{4,3,2,1,0:T(8,128)S(1)}, u32[]{:S(2)}, u32[]{:S(2)}) collective-permute-start(f32[2,2,2,32,128]{4,3,2,1,0:T(8,128)S(1)} %get-tuple-element.46), channel_id=1, source_target_pairs={{16,0},{18,16},{2,18},{4,2},{20,4},{22,20},{6,22},{8,6},{24,8},{26... | collective-permute-start | bytes 393224 | tf_op jit(solution)/shard_map/ppermute | solution.py:129
  82.9 6.5 %collective-permute-start.19 = (f32[2,2,2,32,128]{4,3,2,1,0:T(8,128)S(1)}, f32[2,2,2,32,128]{4,3,2,1,0:T(8,128)S(1)}, u32[]{:S(2)}, u32[]{:S(2)}) collective-permute-start(f32[2,2,2,32,128]{4,3,2,1,0:T(8,128)S(1)} %get-tuple-element.47), channel_id=1, source_target_pairs={{0,16},{16,18},{18,2},{2,4},{4,20},{20,22},{22,6},{6,8},{8,24},{24... | collective-permute-start | bytes 393224 | tf_op jit(solution)/shard_map/ppermute | solution.py:128
  93.8 5.0 %collective-permute-start.23 = (f32[2,2,16,4,128]{4,3,2,1,0:T(4,128)S(1)}, f32[2,2,16,4,128]{4,3,2,1,0:T(4,128)S(1)}, u32[]{:S(2)}, u32[]{:S(2)}) collective-permute-start(f32[2,2,16,4,128]{4,3,2,1,0:T(4,128)S(1)} %pad_maximum_fusion.41), channel_id=1, source_target_pairs={{0,1},{1,0},{2,3},{3,2},{4,5},{5,4},{6,7},{7,6},{8,9},{9,8},{10,11... | collective-permute-start | bytes 393224 | tf_op jit(solution)/shard_map/ppermute | solution.py:124
  95.4 5.0 %collective-permute-start.21 = (f32[2,2,2,32,128]{4,3,2,1,0:T(8,128)S(1)}, f32[2,2,2,32,128]{4,3,2,1,0:T(8,128)S(1)}, u32[]{:S(2)}, u32[]{:S(2)}) collective-permute-start(f32[2,2,2,32,128]{4,3,2,1,0:T(8,128)S(1)} %get-tuple-element.38), channel_id=1, source_target_pairs={{16,0},{18,16},{2,18},{4,2},{20,4},{22,20},{6,22},{8,6},{24,8},{26... | collective-permute-start | bytes 393224 | tf_op jit(solution)/shard_map/ppermute | solution.py:129
  95.5 7.6 %collective-permute-start.22 = (f32[2,2,2,32,128]{4,3,2,1,0:T(8,128)S(1)}, f32[2,2,2,32,128]{4,3,2,1,0:T(8,128)S(1)}, u32[]{:S(2)}, u32[]{:S(2)}) collective-permute-start(f32[2,2,2,32,128]{4,3,2,1,0:T(8,128)S(1)} %get-tuple-element.39), channel_id=1, source_target_pairs={{0,16},{16,18},{18,2},{2,4},{4,20},{20,22},{22,6},{6,8},{8,24},{24... | collective-permute-start | bytes 393224 | tf_op jit(solution)/shard_map/ppermute | solution.py:128
  107.1 9.1 %copy-start = (f32[2,2,16,32,128]{4,3,2,1,0:T(8,128)}, f32[2,2,16,32,128]{4,3,2,1,0:T(8,128)S(1)}, u32[]{:S(2)}) copy-start(f32[2,2,16,32,128]{4,3,2,1,0:T(8,128)S(1)} %convolution_bitcast_fusion) | copy-start | bytes 3145732
  107.6 5.0 %collective-permute-start.26 = (f32[2,2,16,4,128]{4,3,2,1,0:T(4,128)S(1)}, f32[2,2,16,4,128]{4,3,2,1,0:T(4,128)S(1)}, u32[]{:S(2)}, u32[]{:S(2)}) collective-permute-start(f32[2,2,16,4,128]{4,3,2,1,0:T(4,128)S(1)} %pad_maximum_fusion.42), channel_id=1, source_target_pairs={{0,1},{1,0},{2,3},{3,2},{4,5},{5,4},{6,7},{7,6},{8,9},{9,8},{10,11... | collective-permute-start | bytes 393224 | tf_op jit(solution)/shard_map/ppermute | solution.py:124
  107.7 5.0 %collective-permute-start.24 = (f32[2,2,2,32,128]{4,3,2,1,0:T(8,128)S(1)}, f32[2,2,2,32,128]{4,3,2,1,0:T(8,128)S(1)}, u32[]{:S(2)}, u32[]{:S(2)}) collective-permute-start(f32[2,2,2,32,128]{4,3,2,1,0:T(8,128)S(1)} %get-tuple-element.30), channel_id=1, source_target_pairs={{16,0},{18,16},{2,18},{4,2},{20,4},{22,20},{6,22},{8,6},{24,8},{26... | collective-permute-start | bytes 393224 | tf_op jit(solution)/shard_map/ppermute | solution.py:129
  107.8 6.3 %collective-permute-start.25 = (f32[2,2,2,32,128]{4,3,2,1,0:T(8,128)S(1)}, f32[2,2,2,32,128]{4,3,2,1,0:T(8,128)S(1)}, u32[]{:S(2)}, u32[]{:S(2)}) collective-permute-start(f32[2,2,2,32,128]{4,3,2,1,0:T(8,128)S(1)} %get-tuple-element.31), channel_id=1, source_target_pairs={{0,16},{16,18},{18,2},{2,4},{4,20},{20,22},{22,6},{6,8},{8,24},{24... | collective-permute-start | bytes 393224 | tf_op jit(solution)/shard_map/ppermute | solution.py:128
  118.6 10.1 %copy-start.3 = (f32[1,2,32,32,128]{4,3,2,1,0:T(8,128)}, f32[1,2,32,32,128]{4,3,2,1,0:T(8,128)S(1)}, u32[]{:S(2)}) copy-start(f32[1,2,32,32,128]{4,3,2,1,0:T(8,128)S(1)} %get-tuple-element.27) | copy-start | bytes 3145732
  118.7 7.2 %collective-permute-start.27 = (f32[1,2,16,16,128]{4,3,2,1,0:T(8,128)S(1)}, f32[1,2,16,16,128]{4,3,2,1,0:T(8,128)S(1)}, u32[]{:S(2)}, u32[]{:S(2)}) collective-permute-start(f32[1,2,16,16,128]{4,3,2,1,0:T(8,128)S(1)} %get-tuple-element.96), channel_id=1, source_target_pairs={{0,16},{16,0},{1,17},{17,1},{2,18},{18,2},{3,19},{19,3},{4,20},{20... | collective-permute-start | bytes 786440 | tf_op jit(solution)/shard_map/ppermute | solution.py:240
  119.5 9.2 %collective-permute-start.28 = (f32[1,2,16,16,128]{4,3,2,1,0:T(8,128)S(1)}, f32[1,2,16,16,128]{4,3,2,1,0:T(8,128)S(1)}, u32[]{:S(2)}, u32[]{:S(2)}) collective-permute-start(f32[1,2,16,16,128]{4,3,2,1,0:T(8,128)S(1)} %get-tuple-element.97), channel_id=1, source_target_pairs={{0,16},{16,0},{1,17},{17,1},{2,18},{18,2},{3,19},{19,3},{4,20},{20... | collective-permute-start | bytes 786440 | tf_op jit(solution)/shard_map/ppermute | solution.py:241
  (8 other events, 13.2 us)

commit v4 on v3

--- a/solution.py
+++ b/solution.py
@@ -136,29 +136,20 @@
     px = jnp.concatenate([west, state, east], 2)
     py = jnp.concatenate([south, state, north], 3)
     center = state
-    dx1 = (
-        -px[:, :, 4:] + 8.0 * px[:, :, 3:-1] - 8.0 * px[:, :, 1:-3] + px[:, :, :-4]
-    ) / 12.0
-    dx2 = (
-        -px[:, :, 4:]
-        + 16.0 * px[:, :, 3:-1]
-        - 30.0 * center
-        + 16.0 * px[:, :, 1:-3]
-        - px[:, :, :-4]
-    ) / 12.0
-    dy1 = (
-        -py[:, :, :, 4:]
-        + 8.0 * py[:, :, :, 3:-1]
-        - 8.0 * py[:, :, :, 1:-3]
-        + py[:, :, :, :-4]
-    ) / 12.0
-    dy2 = (
-        -py[:, :, :, 4:]
-        + 16.0 * py[:, :, :, 3:-1]
-        - 30.0 * center
-        + 16.0 * py[:, :, :, 1:-3]
-        - py[:, :, :, :-4]
-    ) / 12.0
+    twelfth = 1.0 / 12.0
+    far_x = px[:, :, :-4] - px[:, :, 4:]
+    near_x = px[:, :, 3:-1] - px[:, :, 1:-3]
+    far_sum_x = px[:, :, :-4] + px[:, :, 4:]
+    near_sum_x = px[:, :, 3:-1] + px[:, :, 1:-3]
+    far_y = py[:, :, :, :-4] - py[:, :, :, 4:]
+    near_y = py[:, :, :, 3:-1] - py[:, :, :, 1:-3]
+    far_sum_y = py[:, :, :, :-4] + py[:, :, :, 4:]
+    near_sum_y = py[:, :, :, 3:-1] + py[:, :, :, 1:-3]
+    dx1 = (far_x + 8.0 * near_x) * twelfth
+    dy1 = (far_y + 8.0 * near_y) * twelfth
+    laplace = (
+        16.0 * (near_sum_x + near_sum_y) - (far_sum_x + far_sum_y) - 60.0 * center
+    ) * twelfth
     kappa = jnp.array([0.5, 1.0], jnp.float32)[None, :, None, None, None]
     first = center[:, 0]
     second = center[:, 1]
@@ -167,7 +158,7 @@
         [A_RATE - (B_RATE + 1.0) * first + square_term, B_RATE * first - square_term], 1
     )
     flow = -(wind[0][None, None] * dx1 + wind[1][None, None] * dy1)
-    return DT * (flow + kappa * (dx2 + dy2) + react)
+    return DT * (flow + kappa * laplace + react)
 
 
 def column_solve(rhs, inverse):

time: 130 us -> 124 us (0.954)
  waiting for transfers between devices: 45.5 us -> 34.6 us
  starting transfers between devices: 36 us -> 43.2 us
  other arithmetic: 28.3 us -> 25.6 us
    ppermute x9, starting transfers between devices: 15 us -> 29.4 us  [ring_halo(): after = lax.ppermute(first, axes, down)]
    ppermute x9, starting transfers between devices: 8.8 us -> 2.03 us  [ring_halo(): before = lax.ppermute(last, axes, up)]
    ppermute x9, waiting for transfers between devices: 15.6 us -> 9.84 us  [ring_halo(): got = lax.ppermute(jnp.concatenate([first, last], dim), axes, up)]
    ppermute x9, waiting for transfers between devices: 5.59 us -> 1.87 us  [ring_halo(): after = lax.ppermute(first, axes, down)]
    mul x9, other arithmetic: 17 us -> 14.5 us  [tendency(): return DT * (flow + kappa * laplace + react)]
  transfers between devices with their start and end apart: 29 -> 29, of which waited for: 22 -> 16; matrix products, arithmetic and copies ran while one was open for 3% -> 3% of each run, Pallas kernels for 3% -> 3%
where the time goes in v4:
time: 124 us; the launch traced here: 123 us
  starting transfers between devices  43.2 us (35%)
  waiting for transfers between devices  34.6 us (28%)
  other arithmetic  25.6 us (21%)
  matrix products  8.81 us (7%)
  local copies, waits for them, and re-layouts  6.22 us (5%)
  Pallas kernels  4.11 us (3%)
    ppermute x9, starting transfers between devices, ring_halo(): after = lax.ppermute(first, axes, down)  29.4 us
    ppermute x9, waiting for transfers between devices, ring_halo(): before = lax.ppermute(last, axes, up)  15.8 us
    mul x9, other arithmetic, tendency(): return DT * (flow + kappa * laplace + react)  14.5 us
    ppermute x9, waiting for transfers between devices, ring_halo(): got = lax.ppermute(jnp.concatenate([first, last], dim), axes, up)  9.84 us
    ppermute x9, starting transfers between devices, ring_halo(): got = lax.ppermute(jnp.concatenate([first, last], dim), axes, up)  9.68 us
    dot_general x9, matrix products, column_solve(): jnp.einsum('lsxyk,sjk->lsxyj', rhs, inverse, precision=lax.Precision.HIGH...  8.81 us
    ppermute x1, waiting for transfers between devices, on_device(): lax.ppermute(sent[:, :, :, :half], 'corr', pairs)  4.35 us
    pallas_call x1, Pallas kernels, vertical(): pl.pallas_call(thomas_kernel, out_shape=jax.ShapeDtypeStruct((depth, spec...  4.11 us
  transfers between devices with their start and end apart: 29, of which 16 were waited for; matrix products, arithmetic and copies ran while one was open for 3% of the time, Pallas kernels for 3%

profile of v4, /device:TPU:0, one launch (start us, length us, event | category | flops | bytes accessed | tf_op | source)
XLA Modules:
  0.0 123.3 jit_solution(8061697207291752357)
XLA Ops:
  1.2 3.0 %collective-permute-start.2 = (f32[1,2,16,4,128]{4,3,2,1,0:T(4,128)S(1)}, f32[1,2,16,4,128]{4,3,2,1,0:T(4,128)S(1)}, u32[]{:S(2)}, u32[]{:S(2)}) collective-permute-start(f32[1,2,16,4,128]{4,3,2,1,0:T(4,128)S(1)} %pad_maximum_fusion.43), channel_id=1, source_target_pairs={{0,1},{1,0},{2,3},{3,2},{4,5},{5,4},{6,7},{7,6},{8,9},{9,8},{10,11... | collective-permute-start | bytes 196616 | tf_op jit(solution)/shard_map/ppermute | solution.py:124
  4.2 1.6 %collective-permute-start = (f32[1,2,2,32,128]{4,3,2,1,0:T(8,128)S(1)}, f32[1,2,2,32,128]{4,3,2,1,0:T(8,128)S(1)}, u32[]{:S(2)}, u32[]{:S(2)}) collective-permute-start(f32[1,2,2,32,128]{4,3,2,1,0:T(8,128)S(1)} %get-tuple-element.102), channel_id=1, source_target_pairs={{0,16},{16,18},{18,2},{2,4},{4,20},{20,22},{22,6},{6,8},{8,24},{24... | collective-permute-start | bytes 196616 | tf_op jit(solution)/shard_map/ppermute | solution.py:128
  5.8 2.1 %collective-permute-start.1 = (f32[1,2,2,32,128]{4,3,2,1,0:T(8,128)S(1)}, f32[1,2,2,32,128]{4,3,2,1,0:T(8,128)S(1)}, u32[]{:S(2)}, u32[]{:S(2)}) collective-permute-start(f32[1,2,2,32,128]{4,3,2,1,0:T(8,128)S(1)} %get-tuple-element.103), channel_id=1, source_target_pairs={{16,0},{18,16},{2,18},{4,2},{20,4},{22,20},{6,22},{8,6},{24,8},{26... | collective-permute-start | bytes 196616 | tf_op jit(solution)/shard_map/ppermute | solution.py:129
  9.9 4.1 %shard_map.118 = f32[128,2,128]{2,1,0:T(2,128)} custom-call(f32[2,128]{1,0:T(2,128)} %copy-done.4, f32[2,128]{1,0:T(2,128)} %get-tuple-element.127.low_ref), custom_call_target="tpu_custom_call" | custom-call | flops 393216 | bytes 262144 | tf_op jit(solution)/shard_map/pallas_call | solution.py:78
  17.0 3.5 %collective-permute-start.4 = (f32[2,2,2,32,128]{4,3,2,1,0:T(8,128)S(1)}, f32[2,2,2,32,128]{4,3,2,1,0:T(8,128)S(1)}, u32[]{:S(2)}, u32[]{:S(2)}) collective-permute-start(f32[2,2,2,32,128]{4,3,2,1,0:T(8,128)S(1)} %get-tuple-element.86), channel_id=1, source_target_pairs={{16,0},{18,16},{2,18},{4,2},{20,4},{22,20},{6,22},{8,6},{24,8},{26... | collective-permute-start | bytes 393224 | tf_op jit(solution)/shard_map/ppermute | solution.py:129
  20.9 4.8 %collective-permute-done.5 = f32[2,2,16,4,128]{4,3,2,1,0:T(4,128)S(1)} collective-permute-done((f32[2,2,16,4,128]{4,3,2,1,0:T(4,128)S(1)}, f32[2,2,16,4,128]{4,3,2,1,0:T(4,128)S(1)}, u32[]{:S(2)}, u32[]{:S(2)}) %collective-permute-start.5) | collective-permute-done | bytes 131104 | tf_op jit(solution)/shard_map/ppermute | solution.py:124
  30.4 3.5 %collective-permute-start.7 = (f32[2,2,2,32,128]{4,3,2,1,0:T(8,128)S(1)}, f32[2,2,2,32,128]{4,3,2,1,0:T(8,128)S(1)}, u32[]{:S(2)}, u32[]{:S(2)}) collective-permute-start(f32[2,2,2,32,128]{4,3,2,1,0:T(8,128)S(1)} %get-tuple-element.79), channel_id=1, source_target_pairs={{16,0},{18,16},{2,18},{4,2},{20,4},{22,20},{6,22},{8,6},{24,8},{26... | collective-permute-start | bytes 393224 | tf_op jit(solution)/shard_map/ppermute | solution.py:129
  35.3 2.3 %collective-permute-done.6 = f32[2,2,2,32,128]{4,3,2,1,0:T(8,128)S(1)} collective-permute-done((f32[2,2,2,32,128]{4,3,2,1,0:T(8,128)S(1)}, f32[2,2,2,32,128]{4,3,2,1,0:T(8,128)S(1)}, u32[]{:S(2)}, u32[]{:S(2)}) %collective-permute-start.6) | collective-permute-done | bytes 131104 | tf_op jit(solution)/shard_map/ppermute | solution.py:128
  37.6 1.8 %fusion.37 = f32[2,2,16,32,128]{4,3,2,1,0:T(8,128)S(1)} fusion(f32[2,1,16,32,128]{4,3,2,1,0:T(8,128)S(1)} %get-tuple-element.83, f32[2,1,16,32,128]{4,3,2,1,0:T(8,128)S(1)} %get-tuple-element.82, f32[2,2,16,32,128]{4,3,2,1,0:T(8,128)S(1)} %convolution_bitcast_fusion.6, f32[2,2,16,2,128]{4,3,2,1,0:T(2,128)S(1)} %get-tuple-element.121, ...), kind=kLoop, calls=%fused_computation.152 | loop fusion | flops 9175040 | bytes 4063240 | tf_op jit(solution)/shard_map/mul | solution.py:161
  41.6 1.8 %collective-permute-start.11 = (f32[2,2,16,4,128]{4,3,2,1,0:T(4,128)S(1)}, f32[2,2,16,4,128]{4,3,2,1,0:T(4,128)S(1)}, u32[]{:S(2)}, u32[]{:S(2)}) collective-permute-start(f32[2,2,16,4,128]{4,3,2,1,0:T(4,128)S(1)} %pad_maximum_fusion.37), channel_id=1, source_target_pairs={{0,1},{1,0},{2,3},{3,2},{4,5},{5,4},{6,7},{7,6},{8,9},{9,8},{10,11... | collective-permute-start | bytes 393224 | tf_op jit(solution)/shard_map/ppermute | solution.py:124
  43.5 2.6 %collective-permute-start.10 = (f32[2,2,2,32,128]{4,3,2,1,0:T(8,128)S(1)}, f32[2,2,2,32,128]{4,3,2,1,0:T(8,128)S(1)}, u32[]{:S(2)}, u32[]{:S(2)}) collective-permute-start(f32[2,2,2,32,128]{4,3,2,1,0:T(8,128)S(1)} %get-tuple-element.71), channel_id=1, source_target_pairs={{16,0},{18,16},{2,18},{4,2},{20,4},{22,20},{6,22},{8,6},{24,8},{26... | collective-permute-start | bytes 393224 | tf_op jit(solution)/shard_map/ppermute | solution.py:129
  46.7 1.9 %collective-permute-done.10 = f32[2,2,2,32,128]{4,3,2,1,0:T(8,128)S(1)} collective-permute-done((f32[2,2,2,32,128]{4,3,2,1,0:T(8,128)S(1)}, f32[2,2,2,32,128]{4,3,2,1,0:T(8,128)S(1)}, u32[]{:S(2)}, u32[]{:S(2)}) %collective-permute-start.10) | collective-permute-done | bytes 131104 | tf_op jit(solution)/shard_map/ppermute | solution.py:129
  48.6 3.7 %collective-permute-done.9 = f32[2,2,2,32,128]{4,3,2,1,0:T(8,128)S(1)} collective-permute-done((f32[2,2,2,32,128]{4,3,2,1,0:T(8,128)S(1)}, f32[2,2,2,32,128]{4,3,2,1,0:T(8,128)S(1)}, u32[]{:S(2)}, u32[]{:S(2)}) %collective-permute-start.9) | collective-permute-done | bytes 131104 | tf_op jit(solution)/shard_map/ppermute | solution.py:128
  52.3 1.8 %fusion.41 = f32[2,2,16,32,128]{4,3,2,1,0:T(8,128)S(1)} fusion(f32[2,1,16,32,128]{4,3,2,1,0:T(8,128)S(1)} %get-tuple-element.75, f32[2,1,16,32,128]{4,3,2,1,0:T(8,128)S(1)} %get-tuple-element.74, f32[2,2,16,32,128]{4,3,2,1,0:T(8,128)S(1)} %convolution_bitcast_fusion.5, f32[2,2,16,2,128]{4,3,2,1,0:T(2,128)S(1)} %get-tuple-element.119, ...), kind=kLoop, calls=%fused_computation.157 | loop fusion | flops 9175040 | bytes 4063240 | tf_op jit(solution)/shard_map/mul | solution.py:161
  56.8 3.5 %collective-permute-start.13 = (f32[2,2,2,32,128]{4,3,2,1,0:T(8,128)S(1)}, f32[2,2,2,32,128]{4,3,2,1,0:T(8,128)S(1)}, u32[]{:S(2)}, u32[]{:S(2)}) collective-permute-start(f32[2,2,2,32,128]{4,3,2,1,0:T(8,128)S(1)} %get-tuple-element.63), channel_id=1, source_target_pairs={{16,0},{18,16},{2,18},{4,2},{20,4},{22,20},{6,22},{8,6},{24,8},{26... | collective-permute-start | bytes 393224 | tf_op jit(solution)/shard_map/ppermute | solution.py:129
  63.0 1.8 %fusion.45 = f32[2,2,16,32,128]{4,3,2,1,0:T(8,128)S(1)} fusion(f32[2,1,16,32,128]{4,3,2,1,0:T(8,128)S(1)} %get-tuple-element.67, f32[2,1,16,32,128]{4,3,2,1,0:T(8,128)S(1)} %get-tuple-element.66, f32[2,2,16,32,128]{4,3,2,1,0:T(8,128)S(1)} %convolution_bitcast_fusion.4, f32[2,2,16,2,128]{4,3,2,1,0:T(2,128)S(1)} %get-tuple-element.117, ...), kind=kLoop, calls=%fused_computation.162 | loop fusion | flops 9175040 | bytes 4063240 | tf_op jit(solution)/shard_map/mul | solution.py:161
  67.1 1.8 %collective-permute-start.17 = (f32[2,2,16,4,128]{4,3,2,1,0:T(4,128)S(1)}, f32[2,2,16,4,128]{4,3,2,1,0:T(4,128)S(1)}, u32[]{:S(2)}, u32[]{:S(2)}) collective-permute-start(f32[2,2,16,4,128]{4,3,2,1,0:T(4,128)S(1)} %pad_maximum_fusion.39), channel_id=1, source_target_pairs={{0,1},{1,0},{2,3},{3,2},{4,5},{5,4},{6,7},{7,6},{8,9},{9,8},{10,11... | collective-permute-start | bytes 393224 | tf_op jit(solution)/shard_map/ppermute | solution.py:124
  69.0 3.5 %collective-permute-start.16 = (f32[2,2,2,32,128]{4,3,2,1,0:T(8,128)S(1)}, f32[2,2,2,32,128]{4,3,2,1,0:T(8,128)S(1)}, u32[]{:S(2)}, u32[]{:S(2)}) collective-permute-start(f32[2,2,2,32,128]{4,3,2,1,0:T(8,128)S(1)} %get-tuple-element.55), channel_id=1, source_target_pairs={{16,0},{18,16},{2,18},{4,2},{20,4},{22,20},{6,22},{8,6},{24,8},{26... | collective-permute-start | bytes 393224 | tf_op jit(solution)/shard_map/ppermute | solution.py:129
  72.6 2.6 %collective-permute-done.15 = f32[2,2,2,32,128]{4,3,2,1,0:T(8,128)S(1)} collective-permute-done((f32[2,2,2,32,128]{4,3,2,1,0:T(8,128)S(1)}, f32[2,2,2,32,128]{4,3,2,1,0:T(8,128)S(1)}, u32[]{:S(2)}, u32[]{:S(2)}) %collective-permute-start.15) | collective-permute-done | bytes 131104 | tf_op jit(solution)/shard_map/ppermute | solution.py:128
  75.1 1.8 %fusion.49 = f32[2,2,16,32,128]{4,3,2,1,0:T(8,128)S(1)} fusion(f32[2,1,16,32,128]{4,3,2,1,0:T(8,128)S(1)} %get-tuple-element.59, f32[2,1,16,32,128]{4,3,2,1,0:T(8,128)S(1)} %get-tuple-element.58, f32[2,2,16,32,128]{4,3,2,1,0:T(8,128)S(1)} %convolution_bitcast_fusion.3, f32[2,2,16,2,128]{4,3,2,1,0:T(2,128)S(1)} %get-tuple-element.115, ...), kind=kLoop, calls=%fused_computation.167 | loop fusion | flops 9175040 | bytes 4063240 | tf_op jit(solution)/shard_map/mul | solution.py:161
  79.7 3.5 %collective-permute-start.19 = (f32[2,2,2,32,128]{4,3,2,1,0:T(8,128)S(1)}, f32[2,2,2,32,128]{4,3,2,1,0:T(8,128)S(1)}, u32[]{:S(2)}, u32[]{:S(2)}) collective-permute-start(f32[2,2,2,32,128]{4,3,2,1,0:T(8,128)S(1)} %get-tuple-element.47), channel_id=1, source_target_pairs={{16,0},{18,16},{2,18},{4,2},{20,4},{22,20},{6,22},{8,6},{24,8},{26... | collective-permute-start | bytes 393224 | tf_op jit(solution)/shard_map/ppermute | solution.py:129
  84.3 1.5 %collective-permute-done.18 = f32[2,2,2,32,128]{4,3,2,1,0:T(8,128)S(1)} collective-permute-done((f32[2,2,2,32,128]{4,3,2,1,0:T(8,128)S(1)}, f32[2,2,2,32,128]{4,3,2,1,0:T(8,128)S(1)}, u32[]{:S(2)}, u32[]{:S(2)}) %collective-permute-start.18) | collective-permute-done | bytes 131104 | tf_op jit(solution)/shard_map/ppermute | solution.py:128
  85.9 1.8 %fusion.53 = f32[2,2,16,32,128]{4,3,2,1,0:T(8,128)S(1)} fusion(f32[2,1,16,32,128]{4,3,2,1,0:T(8,128)S(1)} %get-tuple-element.51, f32[2,1,16,32,128]{4,3,2,1,0:T(8,128)S(1)} %get-tuple-element.50, f32[2,2,16,32,128]{4,3,2,1,0:T(8,128)S(1)} %convolution_bitcast_fusion.2, f32[2,2,16,2,128]{4,3,2,1,0:T(2,128)S(1)} %get-tuple-element.113, ...), kind=kLoop, calls=%fused_computation.172 | loop fusion | flops 9175040 | bytes 4063240 | tf_op jit(solution)/shard_map/mul | solution.py:161
  90.0 1.8 %collective-permute-start.23 = (f32[2,2,16,4,128]{4,3,2,1,0:T(4,128)S(1)}, f32[2,2,16,4,128]{4,3,2,1,0:T(4,128)S(1)}, u32[]{:S(2)}, u32[]{:S(2)}) collective-permute-start(f32[2,2,16,4,128]{4,3,2,1,0:T(4,128)S(1)} %pad_maximum_fusion.41), channel_id=1, source_target_pairs={{0,1},{1,0},{2,3},{3,2},{4,5},{5,4},{6,7},{7,6},{8,9},{9,8},{10,11... | collective-permute-start | bytes 393224 | tf_op jit(solution)/shard_map/ppermute | solution.py:124
  91.8 3.5 %collective-permute-start.22 = (f32[2,2,2,32,128]{4,3,2,1,0:T(8,128)S(1)}, f32[2,2,2,32,128]{4,3,2,1,0:T(8,128)S(1)}, u32[]{:S(2)}, u32[]{:S(2)}) collective-permute-start(f32[2,2,2,32,128]{4,3,2,1,0:T(8,128)S(1)} %get-tuple-element.39), channel_id=1, source_target_pairs={{16,0},{18,16},{2,18},{4,2},{20,4},{22,20},{6,22},{8,6},{24,8},{26... | collective-permute-start | bytes 393224 | tf_op jit(solution)/shard_map/ppermute | solution.py:129
  95.4 2.6 %collective-permute-done.21 = f32[2,2,2,32,128]{4,3,2,1,0:T(8,128)S(1)} collective-permute-done((f32[2,2,2,32,128]{4,3,2,1,0:T(8,128)S(1)}, f32[2,2,2,32,128]{4,3,2,1,0:T(8,128)S(1)}, u32[]{:S(2)}, u32[]{:S(2)}) %collective-permute-start.21) | collective-permute-done | bytes 131104 | tf_op jit(solution)/shard_map/ppermute | solution.py:128
  98.0 1.8 %fusion.57 = f32[2,2,16,32,128]{4,3,2,1,0:T(8,128)S(1)} fusion(f32[2,1,16,32,128]{4,3,2,1,0:T(8,128)S(1)} %get-tuple-element.43, f32[2,1,16,32,128]{4,3,2,1,0:T(8,128)S(1)} %get-tuple-element.42, f32[2,2,16,32,128]{4,3,2,1,0:T(8,128)S(1)} %convolution_bitcast_fusion.1, f32[2,2,16,2,128]{4,3,2,1,0:T(2,128)S(1)} %get-tuple-element.111, ...), kind=kLoop, calls=%fused_computation.177 | loop fusion | flops 9175040 | bytes 4063240 | tf_op jit(solution)/shard_map/mul | solution.py:161
  102.6 3.5 %collective-permute-start.25 = (f32[2,2,2,32,128]{4,3,2,1,0:T(8,128)S(1)}, f32[2,2,2,32,128]{4,3,2,1,0:T(8,128)S(1)}, u32[]{:S(2)}, u32[]{:S(2)}) collective-permute-start(f32[2,2,2,32,128]{4,3,2,1,0:T(8,128)S(1)} %get-tuple-element.31), channel_id=1, source_target_pairs={{16,0},{18,16},{2,18},{4,2},{20,4},{22,20},{6,22},{8,6},{24,8},{26... | collective-permute-start | bytes 393224 | tf_op jit(solution)/shard_map/ppermute | solution.py:129
  108.8 1.8 %fusion.61 = f32[2,2,16,32,128]{4,3,2,1,0:T(8,128)S(1)} fusion(f32[2,1,16,32,128]{4,3,2,1,0:T(8,128)S(1)} %get-tuple-element.35, f32[2,1,16,32,128]{4,3,2,1,0:T(8,128)S(1)} %get-tuple-element.34, f32[2,2,16,32,128]{4,3,2,1,0:T(8,128)S(1)} %convolution_bitcast_fusion, f32[2,2,16,2,128]{4,3,2,1,0:T(2,128)S(1)} %get-tuple-element.109, ...), kind=kLoop, calls=%fused_computation.182 | loop fusion | flops 9175040 | bytes 4063240 | tf_op jit(solution)/shard_map/mul | solution.py:161
  113.3 2.0 %collective-permute-start.28 = (f32[1,2,16,16,128]{4,3,2,1,0:T(8,128)S(1)}, f32[1,2,16,16,128]{4,3,2,1,0:T(8,128)S(1)}, u32[]{:S(2)}, u32[]{:S(2)}) collective-permute-start(f32[1,2,16,16,128]{4,3,2,1,0:T(8,128)S(1)} %get-tuple-element.97), channel_id=1, source_target_pairs={{0,16},{16,0},{1,17},{17,1},{2,18},{18,2},{3,19},{19,3},{4,20},{20... | collective-permute-start | bytes 786440 | tf_op jit(solution)/shard_map/ppermute | solution.py:232
  115.3 4.3 %collective-permute-done.27 = f32[1,2,16,16,128]{4,3,2,1,0:T(8,128)S(1)} collective-permute-done((f32[1,2,16,16,128]{4,3,2,1,0:T(8,128)S(1)}, f32[1,2,16,16,128]{4,3,2,1,0:T(8,128)S(1)}, u32[]{:S(2)}, u32[]{:S(2)}) %collective-permute-start.27) | collective-permute-done | bytes 262176 | tf_op jit(solution)/shard_map/ppermute | solution.py:231
  119.6 2.8 %collective-permute-done.28 = f32[1,2,16,16,128]{4,3,2,1,0:T(8,128)S(1)} collective-permute-done((f32[1,2,16,16,128]{4,3,2,1,0:T(8,128)S(1)}, f32[1,2,16,16,128]{4,3,2,1,0:T(8,128)S(1)}, u32[]{:S(2)}, u32[]{:S(2)}) %collective-permute-start.28) | collective-permute-done | bytes 262176 | tf_op jit(solution)/shard_map/ppermute | solution.py:232
  (140 shorter events, 37.9 us)
Async XLA Ops:
  1.2 13.9 %collective-permute-start.2 = (f32[1,2,16,4,128]{4,3,2,1,0:T(4,128)S(1)}, f32[1,2,16,4,128]{4,3,2,1,0:T(4,128)S(1)}, u32[]{:S(2)}, u32[]{:S(2)}) collective-permute-start(f32[1,2,16,4,128]{4,3,2,1,0:T(4,128)S(1)} %pad_maximum_fusion.43), channel_id=1, source_target_pairs={{0,1},{1,0},{2,3},{3,2},{4,5},{5,4},{6,7},{7,6},{8,9},{9,8},{10,11... | collective-permute-start | bytes 196616 | tf_op jit(solution)/shard_map/ppermute | solution.py:124
  4.2 10.9 %collective-permute-start = (f32[1,2,2,32,128]{4,3,2,1,0:T(8,128)S(1)}, f32[1,2,2,32,128]{4,3,2,1,0:T(8,128)S(1)}, u32[]{:S(2)}, u32[]{:S(2)}) collective-permute-start(f32[1,2,2,32,128]{4,3,2,1,0:T(8,128)S(1)} %get-tuple-element.102), channel_id=1, source_target_pairs={{0,16},{16,18},{18,2},{2,4},{4,20},{20,22},{22,6},{6,8},{8,24},{24... | collective-permute-start | bytes 196616 | tf_op jit(solution)/shard_map/ppermute | solution.py:128
  5.8 9.4 %collective-permute-start.1 = (f32[1,2,2,32,128]{4,3,2,1,0:T(8,128)S(1)}, f32[1,2,2,32,128]{4,3,2,1,0:T(8,128)S(1)}, u32[]{:S(2)}, u32[]{:S(2)}) collective-permute-start(f32[1,2,2,32,128]{4,3,2,1,0:T(8,128)S(1)} %get-tuple-element.103), channel_id=1, source_target_pairs={{16,0},{18,16},{2,18},{4,2},{20,4},{22,20},{6,22},{8,6},{24,8},{26... | collective-permute-start | bytes 196616 | tf_op jit(solution)/shard_map/ppermute | solution.py:129
  7.9 7.2 %copy-start.2 = (f32[2,32,32,128]{3,2,1,0:T(8,128)S(1)}, f32[2,32,32,128]{3,2,1,0:T(8,128)}, u32[]{:S(2)}) copy-start(f32[2,32,32,128]{3,2,1,0:T(8,128)} %param.12) | copy-start | bytes 3145732
  17.0 9.0 %collective-permute-start.3 = (f32[2,2,2,32,128]{4,3,2,1,0:T(8,128)S(1)}, f32[2,2,2,32,128]{4,3,2,1,0:T(8,128)S(1)}, u32[]{:S(2)}, u32[]{:S(2)}) collective-permute-start(f32[2,2,2,32,128]{4,3,2,1,0:T(8,128)S(1)} %get-tuple-element.87), channel_id=1, source_target_pairs={{0,16},{16,18},{18,2},{2,4},{4,20},{20,22},{22,6},{6,8},{8,24},{24... | collective-permute-start | bytes 393224 | tf_op jit(solution)/shard_map/ppermute | solution.py:128
  17.0 9.0 %collective-permute-start.4 = (f32[2,2,2,32,128]{4,3,2,1,0:T(8,128)S(1)}, f32[2,2,2,32,128]{4,3,2,1,0:T(8,128)S(1)}, u32[]{:S(2)}, u32[]{:S(2)}) collective-permute-start(f32[2,2,2,32,128]{4,3,2,1,0:T(8,128)S(1)} %get-tuple-element.86), channel_id=1, source_target_pairs={{16,0},{18,16},{2,18},{4,2},{20,4},{22,20},{6,22},{8,6},{24,8},{26... | collective-permute-start | bytes 393224 | tf_op jit(solution)/shard_map/ppermute | solution.py:129
  20.6 5.0 %collective-permute-start.5 = (f32[2,2,16,4,128]{4,3,2,1,0:T(4,128)S(1)}, f32[2,2,16,4,128]{4,3,2,1,0:T(4,128)S(1)}, u32[]{:S(2)}, u32[]{:S(2)}) collective-permute-start(f32[2,2,16,4,128]{4,3,2,1,0:T(4,128)S(1)} %pad_maximum_fusion.35), channel_id=1, source_target_pairs={{0,1},{1,0},{2,3},{3,2},{4,5},{5,4},{6,7},{7,6},{8,9},{9,8},{10,11... | collective-permute-start | bytes 393224 | tf_op jit(solution)/shard_map/ppermute | solution.py:124
  30.3 5.0 %collective-permute-start.8 = (f32[2,2,16,4,128]{4,3,2,1,0:T(4,128)S(1)}, f32[2,2,16,4,128]{4,3,2,1,0:T(4,128)S(1)}, u32[]{:S(2)}, u32[]{:S(2)}) collective-permute-start(f32[2,2,16,4,128]{4,3,2,1,0:T(4,128)S(1)} %pad_maximum_fusion.36), channel_id=1, source_target_pairs={{0,1},{1,0},{2,3},{3,2},{4,5},{5,4},{6,7},{7,6},{8,9},{9,8},{10,11... | collective-permute-start | bytes 393224 | tf_op jit(solution)/shard_map/ppermute | solution.py:124
  30.4 7.3 %collective-permute-start.6 = (f32[2,2,2,32,128]{4,3,2,1,0:T(8,128)S(1)}, f32[2,2,2,32,128]{4,3,2,1,0:T(8,128)S(1)}, u32[]{:S(2)}, u32[]{:S(2)}) collective-permute-start(f32[2,2,2,32,128]{4,3,2,1,0:T(8,128)S(1)} %get-tuple-element.78), channel_id=1, source_target_pairs={{0,16},{16,18},{18,2},{2,4},{4,20},{20,22},{22,6},{6,8},{8,24},{24... | collective-permute-start | bytes 393224 | tf_op jit(solution)/shard_map/ppermute | solution.py:128
  30.4 7.2 %collective-permute-start.7 = (f32[2,2,2,32,128]{4,3,2,1,0:T(8,128)S(1)}, f32[2,2,2,32,128]{4,3,2,1,0:T(8,128)S(1)}, u32[]{:S(2)}, u32[]{:S(2)}) collective-permute-start(f32[2,2,2,32,128]{4,3,2,1,0:T(8,128)S(1)} %get-tuple-element.79), channel_id=1, source_target_pairs={{16,0},{18,16},{2,18},{4,2},{20,4},{22,20},{6,22},{8,6},{24,8},{26... | collective-permute-start | bytes 393224 | tf_op jit(solution)/shard_map/ppermute | solution.py:129
  41.6 5.0 %collective-permute-start.11 = (f32[2,2,16,4,128]{4,3,2,1,0:T(4,128)S(1)}, f32[2,2,16,4,128]{4,3,2,1,0:T(4,128)S(1)}, u32[]{:S(2)}, u32[]{:S(2)}) collective-permute-start(f32[2,2,16,4,128]{4,3,2,1,0:T(4,128)S(1)} %pad_maximum_fusion.37), channel_id=1, source_target_pairs={{0,1},{1,0},{2,3},{3,2},{4,5},{5,4},{6,7},{7,6},{8,9},{9,8},{10,11... | collective-permute-start | bytes 393224 | tf_op jit(solution)/shard_map/ppermute | solution.py:124
  43.5 5.1 %collective-permute-start.10 = (f32[2,2,2,32,128]{4,3,2,1,0:T(8,128)S(1)}, f32[2,2,2,32,128]{4,3,2,1,0:T(8,128)S(1)}, u32[]{:S(2)}, u32[]{:S(2)}) collective-permute-start(f32[2,2,2,32,128]{4,3,2,1,0:T(8,128)S(1)} %get-tuple-element.71), channel_id=1, source_target_pairs={{16,0},{18,16},{2,18},{4,2},{20,4},{22,20},{6,22},{8,6},{24,8},{26... | collective-permute-start | bytes 393224 | tf_op jit(solution)/shard_map/ppermute | solution.py:129
  46.1 6.2 %collective-permute-start.9 = (f32[2,2,2,32,128]{4,3,2,1,0:T(8,128)S(1)}, f32[2,2,2,32,128]{4,3,2,1,0:T(8,128)S(1)}, u32[]{:S(2)}, u32[]{:S(2)}) collective-permute-start(f32[2,2,2,32,128]{4,3,2,1,0:T(8,128)S(1)} %get-tuple-element.70), channel_id=1, source_target_pairs={{0,16},{16,18},{18,2},{2,4},{4,20},{20,22},{22,6},{6,8},{8,24},{24... | collective-permute-start | bytes 393224 | tf_op jit(solution)/shard_map/ppermute | solution.py:128
  56.3 5.0 %collective-permute-start.14 = (f32[2,2,16,4,128]{4,3,2,1,0:T(4,128)S(1)}, f32[2,2,16,4,128]{4,3,2,1,0:T(4,128)S(1)}, u32[]{:S(2)}, u32[]{:S(2)}) collective-permute-start(f32[2,2,16,4,128]{4,3,2,1,0:T(4,128)S(1)} %pad_maximum_fusion.38), channel_id=1, source_target_pairs={{0,1},{1,0},{2,3},{3,2},{4,5},{5,4},{6,7},{7,6},{8,9},{9,8},{10,11... | collective-permute-start | bytes 393224 | tf_op jit(solution)/shard_map/ppermute | solution.py:124
  56.7 6.3 %collective-permute-start.12 = (f32[2,2,2,32,128]{4,3,2,1,0:T(8,128)S(1)}, f32[2,2,2,32,128]{4,3,2,1,0:T(8,128)S(1)}, u32[]{:S(2)}, u32[]{:S(2)}) collective-permute-start(f32[2,2,2,32,128]{4,3,2,1,0:T(8,128)S(1)} %get-tuple-element.62), channel_id=1, source_target_pairs={{0,16},{16,18},{18,2},{2,4},{4,20},{20,22},{22,6},{6,8},{8,24},{24... | collective-permute-start | bytes 393224 | tf_op jit(solution)/shard_map/ppermute | solution.py:128
  56.8 6.2 %collective-permute-start.13 = (f32[2,2,2,32,128]{4,3,2,1,0:T(8,128)S(1)}, f32[2,2,2,32,128]{4,3,2,1,0:T(8,128)S(1)}, u32[]{:S(2)}, u32[]{:S(2)}) collective-permute-start(f32[2,2,2,32,128]{4,3,2,1,0:T(8,128)S(1)} %get-tuple-element.63), channel_id=1, source_target_pairs={{16,0},{18,16},{2,18},{4,2},{20,4},{22,20},{6,22},{8,6},{24,8},{26... | collective-permute-start | bytes 393224 | tf_op jit(solution)/shard_map/ppermute | solution.py:129
  67.1 5.4 %collective-permute-start.17 = (f32[2,2,16,4,128]{4,3,2,1,0:T(4,128)S(1)}, f32[2,2,16,4,128]{4,3,2,1,0:T(4,128)S(1)}, u32[]{:S(2)}, u32[]{:S(2)}) collective-permute-start(f32[2,2,16,4,128]{4,3,2,1,0:T(4,128)S(1)} %pad_maximum_fusion.39), channel_id=1, source_target_pairs={{0,1},{1,0},{2,3},{3,2},{4,5},{5,4},{6,7},{7,6},{8,9},{9,8},{10,11... | collective-permute-start | bytes 393224 | tf_op jit(solution)/shard_map/ppermute | solution.py:124
  68.9 6.3 %collective-permute-start.15 = (f32[2,2,2,32,128]{4,3,2,1,0:T(8,128)S(1)}, f32[2,2,2,32,128]{4,3,2,1,0:T(8,128)S(1)}, u32[]{:S(2)}, u32[]{:S(2)}) collective-permute-start(f32[2,2,2,32,128]{4,3,2,1,0:T(8,128)S(1)} %get-tuple-element.54), channel_id=1, source_target_pairs={{0,16},{16,18},{18,2},{2,4},{4,20},{20,22},{22,6},{6,8},{8,24},{24... | collective-permute-start | bytes 393224 | tf_op jit(solution)/shard_map/ppermute | solution.py:128
  69.0 6.2 %collective-permute-start.16 = (f32[2,2,2,32,128]{4,3,2,1,0:T(8,128)S(1)}, f32[2,2,2,32,128]{4,3,2,1,0:T(8,128)S(1)}, u32[]{:S(2)}, u32[]{:S(2)}) collective-permute-start(f32[2,2,2,32,128]{4,3,2,1,0:T(8,128)S(1)} %get-tuple-element.55), channel_id=1, source_target_pairs={{16,0},{18,16},{2,18},{4,2},{20,4},{22,20},{6,22},{8,6},{24,8},{26... | collective-permute-start | bytes 393224 | tf_op jit(solution)/shard_map/ppermute | solution.py:129
  79.2 5.0 %collective-permute-start.20 = (f32[2,2,16,4,128]{4,3,2,1,0:T(4,128)S(1)}, f32[2,2,16,4,128]{4,3,2,1,0:T(4,128)S(1)}, u32[]{:S(2)}, u32[]{:S(2)}) collective-permute-start(f32[2,2,16,4,128]{4,3,2,1,0:T(4,128)S(1)} %pad_maximum_fusion.40), channel_id=1, source_target_pairs={{0,1},{1,0},{2,3},{3,2},{4,5},{5,4},{6,7},{7,6},{8,9},{9,8},{10,11... | collective-permute-start | bytes 393224 | tf_op jit(solution)/shard_map/ppermute | solution.py:124
  79.6 6.3 %collective-permute-start.18 = (f32[2,2,2,32,128]{4,3,2,1,0:T(8,128)S(1)}, f32[2,2,2,32,128]{4,3,2,1,0:T(8,128)S(1)}, u32[]{:S(2)}, u32[]{:S(2)}) collective-permute-start(f32[2,2,2,32,128]{4,3,2,1,0:T(8,128)S(1)} %get-tuple-element.46), channel_id=1, source_target_pairs={{0,16},{16,18},{18,2},{2,4},{4,20},{20,22},{22,6},{6,8},{8,24},{24... | collective-permute-start | bytes 393224 | tf_op jit(solution)/shard_map/ppermute | solution.py:128
  79.7 6.2 %collective-permute-start.19 = (f32[2,2,2,32,128]{4,3,2,1,0:T(8,128)S(1)}, f32[2,2,2,32,128]{4,3,2,1,0:T(8,128)S(1)}, u32[]{:S(2)}, u32[]{:S(2)}) collective-permute-start(f32[2,2,2,32,128]{4,3,2,1,0:T(8,128)S(1)} %get-tuple-element.47), channel_id=1, source_target_pairs={{16,0},{18,16},{2,18},{4,2},{20,4},{22,20},{6,22},{8,6},{24,8},{26... | collective-permute-start | bytes 393224 | tf_op jit(solution)/shard_map/ppermute | solution.py:129
  90.0 5.4 %collective-permute-start.23 = (f32[2,2,16,4,128]{4,3,2,1,0:T(4,128)S(1)}, f32[2,2,16,4,128]{4,3,2,1,0:T(4,128)S(1)}, u32[]{:S(2)}, u32[]{:S(2)}) collective-permute-start(f32[2,2,16,4,128]{4,3,2,1,0:T(4,128)S(1)} %pad_maximum_fusion.41), channel_id=1, source_target_pairs={{0,1},{1,0},{2,3},{3,2},{4,5},{5,4},{6,7},{7,6},{8,9},{9,8},{10,11... | collective-permute-start | bytes 393224 | tf_op jit(solution)/shard_map/ppermute | solution.py:124
  91.8 6.3 %collective-permute-start.21 = (f32[2,2,2,32,128]{4,3,2,1,0:T(8,128)S(1)}, f32[2,2,2,32,128]{4,3,2,1,0:T(8,128)S(1)}, u32[]{:S(2)}, u32[]{:S(2)}) collective-permute-start(f32[2,2,2,32,128]{4,3,2,1,0:T(8,128)S(1)} %get-tuple-element.38), channel_id=1, source_target_pairs={{0,16},{16,18},{18,2},{2,4},{4,20},{20,22},{22,6},{6,8},{8,24},{24... | collective-permute-start | bytes 393224 | tf_op jit(solution)/shard_map/ppermute | solution.py:128
  91.8 6.2 %collective-permute-start.22 = (f32[2,2,2,32,128]{4,3,2,1,0:T(8,128)S(1)}, f32[2,2,2,32,128]{4,3,2,1,0:T(8,128)S(1)}, u32[]{:S(2)}, u32[]{:S(2)}) collective-permute-start(f32[2,2,2,32,128]{4,3,2,1,0:T(8,128)S(1)} %get-tuple-element.39), channel_id=1, source_target_pairs={{16,0},{18,16},{2,18},{4,2},{20,4},{22,20},{6,22},{8,6},{24,8},{26... | collective-permute-start | bytes 393224 | tf_op jit(solution)/shard_map/ppermute | solution.py:129
  101.7 9.0 %copy-start = (f32[2,2,16,32,128]{4,3,2,1,0:T(8,128)}, f32[2,2,16,32,128]{4,3,2,1,0:T(8,128)S(1)}, u32[]{:S(2)}) copy-start(f32[2,2,16,32,128]{4,3,2,1,0:T(8,128)S(1)} %convolution_bitcast_fusion) | copy-start | bytes 3145732
  102.2 5.0 %collective-permute-start.26 = (f32[2,2,16,4,128]{4,3,2,1,0:T(4,128)S(1)}, f32[2,2,16,4,128]{4,3,2,1,0:T(4,128)S(1)}, u32[]{:S(2)}, u32[]{:S(2)}) collective-permute-start(f32[2,2,16,4,128]{4,3,2,1,0:T(4,128)S(1)} %pad_maximum_fusion.42), channel_id=1, source_target_pairs={{0,1},{1,0},{2,3},{3,2},{4,5},{5,4},{6,7},{7,6},{8,9},{9,8},{10,11... | collective-permute-start | bytes 393224 | tf_op jit(solution)/shard_map/ppermute | solution.py:124
  102.5 6.3 %collective-permute-start.24 = (f32[2,2,2,32,128]{4,3,2,1,0:T(8,128)S(1)}, f32[2,2,2,32,128]{4,3,2,1,0:T(8,128)S(1)}, u32[]{:S(2)}, u32[]{:S(2)}) collective-permute-start(f32[2,2,2,32,128]{4,3,2,1,0:T(8,128)S(1)} %get-tuple-element.30), channel_id=1, source_target_pairs={{0,16},{16,18},{18,2},{2,4},{4,20},{20,22},{22,6},{6,8},{8,24},{24... | collective-permute-start | bytes 393224 | tf_op jit(solution)/shard_map/ppermute | solution.py:128
  102.6 6.2 %collective-permute-start.25 = (f32[2,2,2,32,128]{4,3,2,1,0:T(8,128)S(1)}, f32[2,2,2,32,128]{4,3,2,1,0:T(8,128)S(1)}, u32[]{:S(2)}, u32[]{:S(2)}) collective-permute-start(f32[2,2,2,32,128]{4,3,2,1,0:T(8,128)S(1)} %get-tuple-element.31), channel_id=1, source_target_pairs={{16,0},{18,16},{2,18},{4,2},{20,4},{22,20},{6,22},{8,6},{24,8},{26... | collective-permute-start | bytes 393224 | tf_op jit(solution)/shard_map/ppermute | solution.py:129
  113.1 9.3 %copy-start.3 = (f32[1,2,32,32,128]{4,3,2,1,0:T(8,128)}, f32[1,2,32,32,128]{4,3,2,1,0:T(8,128)S(1)}, u32[]{:S(2)}) copy-start(f32[1,2,32,32,128]{4,3,2,1,0:T(8,128)S(1)} %get-tuple-element.27) | copy-start | bytes 3145732
  113.2 6.4 %collective-permute-start.27 = (f32[1,2,16,16,128]{4,3,2,1,0:T(8,128)S(1)}, f32[1,2,16,16,128]{4,3,2,1,0:T(8,128)S(1)}, u32[]{:S(2)}, u32[]{:S(2)}) collective-permute-start(f32[1,2,16,16,128]{4,3,2,1,0:T(8,128)S(1)} %get-tuple-element.96), channel_id=1, source_target_pairs={{0,16},{16,0},{1,17},{17,1},{2,18},{18,2},{3,19},{19,3},{4,20},{20... | collective-permute-start | bytes 786440 | tf_op jit(solution)/shard_map/ppermute | solution.py:231
  113.3 9.2 %collective-permute-start.28 = (f32[1,2,16,16,128]{4,3,2,1,0:T(8,128)S(1)}, f32[1,2,16,16,128]{4,3,2,1,0:T(8,128)S(1)}, u32[]{:S(2)}, u32[]{:S(2)}) collective-permute-start(f32[1,2,16,16,128]{4,3,2,1,0:T(8,128)S(1)} %get-tuple-element.97), channel_id=1, source_target_pairs={{0,16},{16,0},{1,17},{17,1},{2,18},{18,2},{3,19},{19,3},{4,20},{20... | collective-permute-start | bytes 786440 | tf_op jit(solution)/shard_map/ppermute | solution.py:232
  (8 other events, 13.2 us)

commit v5 on v4

--- a/solution.py
+++ b/solution.py
@@ -163,7 +163,7 @@
 
 def column_solve(rhs, inverse):
     return jnp.einsum(
-        "lsxyk,sjk->lsxyj", rhs, inverse, precision=lax.Precision.HIGHEST
+        "lsxyk,sjk->lsxyj", rhs, inverse, precision=lax.Precision.HIGH
     )
 
 

time: 124 us -> 121 us (0.976)
  matrix products: 8.81 us -> 5.51 us
    dot_general x9, matrix products: 8.81 us -> 5.51 us  [column_solve(): jnp.einsum('lsxyk,sjk->lsxyj', rhs, inverse, precision=lax.Precision.HIGH)]
where the time goes in v5:
time: 121 us; the launch traced here: 120 us
  starting transfers between devices  43.2 us (36%)
  waiting for transfers between devices  34.6 us (29%)
  other arithmetic  25.6 us (21%)
  local copies, waits for them, and re-layouts  6.22 us (5%)
  matrix products  5.51 us (5%)
  Pallas kernels  4.11 us (3%)
    ppermute x9, starting transfers between devices, ring_halo(): after = lax.ppermute(first, axes, down)  29.4 us
    ppermute x9, waiting for transfers between devices, ring_halo(): before = lax.ppermute(last, axes, up)  15.8 us
    mul x9, other arithmetic, tendency(): return DT * (flow + kappa * laplace + react)  14.5 us
    ppermute x9, waiting for transfers between devices, ring_halo(): got = lax.ppermute(jnp.concatenate([first, last], dim), axes, up)  9.83 us
    ppermute x9, starting transfers between devices, ring_halo(): got = lax.ppermute(jnp.concatenate([first, last], dim), axes, up)  9.68 us
    dot_general x9, matrix products, column_solve(): jnp.einsum('lsxyk,sjk->lsxyj', rhs, inverse, precision=lax.Precision.HIGH)  5.51 us
    ppermute x1, waiting for transfers between devices, on_device(): lax.ppermute(sent[:, :, :, :half], 'corr', pairs)  4.35 us
    pallas_call x1, Pallas kernels, vertical(): pl.pallas_call(thomas_kernel, out_shape=jax.ShapeDtypeStruct((depth, spec...  4.11 us
  transfers between devices with their start and end apart: 29, of which 16 were waited for; matrix products, arithmetic and copies ran while one was open for 3% of the time, Pallas kernels for 3%

profile of v5, /device:TPU:0, one launch (start us, length us, event | category | flops | bytes accessed | tf_op | source)
XLA Modules:
  0.0 120.0 jit_solution(7498822449282398755)
XLA Ops:
  1.2 3.0 %collective-permute-start.2 = (f32[1,2,16,4,128]{4,3,2,1,0:T(4,128)S(1)}, f32[1,2,16,4,128]{4,3,2,1,0:T(4,128)S(1)}, u32[]{:S(2)}, u32[]{:S(2)}) collective-permute-start(f32[1,2,16,4,128]{4,3,2,1,0:T(4,128)S(1)} %pad_maximum_fusion.43), channel_id=1, source_target_pairs={{0,1},{1,0},{2,3},{3,2},{4,5},{5,4},{6,7},{7,6},{8,9},{9,8},{10,11... | collective-permute-start | bytes 196616 | tf_op jit(solution)/shard_map/ppermute | solution.py:124
  4.2 1.6 %collective-permute-start = (f32[1,2,2,32,128]{4,3,2,1,0:T(8,128)S(1)}, f32[1,2,2,32,128]{4,3,2,1,0:T(8,128)S(1)}, u32[]{:S(2)}, u32[]{:S(2)}) collective-permute-start(f32[1,2,2,32,128]{4,3,2,1,0:T(8,128)S(1)} %get-tuple-element.102), channel_id=1, source_target_pairs={{0,16},{16,18},{18,2},{2,4},{4,20},{20,22},{22,6},{6,8},{8,24},{24... | collective-permute-start | bytes 196616 | tf_op jit(solution)/shard_map/ppermute | solution.py:128
  5.8 2.1 %collective-permute-start.1 = (f32[1,2,2,32,128]{4,3,2,1,0:T(8,128)S(1)}, f32[1,2,2,32,128]{4,3,2,1,0:T(8,128)S(1)}, u32[]{:S(2)}, u32[]{:S(2)}) collective-permute-start(f32[1,2,2,32,128]{4,3,2,1,0:T(8,128)S(1)} %get-tuple-element.103), channel_id=1, source_target_pairs={{16,0},{18,16},{2,18},{4,2},{20,4},{22,20},{6,22},{8,6},{24,8},{26... | collective-permute-start | bytes 196616 | tf_op jit(solution)/shard_map/ppermute | solution.py:129
  9.9 4.1 %shard_map.118 = f32[128,2,128]{2,1,0:T(2,128)} custom-call(f32[2,128]{1,0:T(2,128)} %copy-done.4, f32[2,128]{1,0:T(2,128)} %get-tuple-element.127.low_ref), custom_call_target="tpu_custom_call" | custom-call | flops 393216 | bytes 262144 | tf_op jit(solution)/shard_map/pallas_call | solution.py:78
  16.9 3.5 %collective-permute-start.4 = (f32[2,2,2,32,128]{4,3,2,1,0:T(8,128)S(1)}, f32[2,2,2,32,128]{4,3,2,1,0:T(8,128)S(1)}, u32[]{:S(2)}, u32[]{:S(2)}) collective-permute-start(f32[2,2,2,32,128]{4,3,2,1,0:T(8,128)S(1)} %get-tuple-element.86), channel_id=1, source_target_pairs={{16,0},{18,16},{2,18},{4,2},{20,4},{22,20},{6,22},{8,6},{24,8},{26... | collective-permute-start | bytes 393224 | tf_op jit(solution)/shard_map/ppermute | solution.py:129
  20.7 4.8 %collective-permute-done.5 = f32[2,2,16,4,128]{4,3,2,1,0:T(4,128)S(1)} collective-permute-done((f32[2,2,16,4,128]{4,3,2,1,0:T(4,128)S(1)}, f32[2,2,16,4,128]{4,3,2,1,0:T(4,128)S(1)}, u32[]{:S(2)}, u32[]{:S(2)}) %collective-permute-start.5) | collective-permute-done | bytes 131104 | tf_op jit(solution)/shard_map/ppermute | solution.py:124
  29.8 3.5 %collective-permute-start.7 = (f32[2,2,2,32,128]{4,3,2,1,0:T(8,128)S(1)}, f32[2,2,2,32,128]{4,3,2,1,0:T(8,128)S(1)}, u32[]{:S(2)}, u32[]{:S(2)}) collective-permute-start(f32[2,2,2,32,128]{4,3,2,1,0:T(8,128)S(1)} %get-tuple-element.79), channel_id=1, source_target_pairs={{16,0},{18,16},{2,18},{4,2},{20,4},{22,20},{6,22},{8,6},{24,8},{26... | collective-permute-start | bytes 393224 | tf_op jit(solution)/shard_map/ppermute | solution.py:129
  34.7 2.3 %collective-permute-done.6 = f32[2,2,2,32,128]{4,3,2,1,0:T(8,128)S(1)} collective-permute-done((f32[2,2,2,32,128]{4,3,2,1,0:T(8,128)S(1)}, f32[2,2,2,32,128]{4,3,2,1,0:T(8,128)S(1)}, u32[]{:S(2)}, u32[]{:S(2)}) %collective-permute-start.6) | collective-permute-done | bytes 131104 | tf_op jit(solution)/shard_map/ppermute | solution.py:128
  37.0 1.8 %fusion.37 = f32[2,2,16,32,128]{4,3,2,1,0:T(8,128)S(1)} fusion(f32[2,1,16,32,128]{4,3,2,1,0:T(8,128)S(1)} %get-tuple-element.83, f32[2,1,16,32,128]{4,3,2,1,0:T(8,128)S(1)} %get-tuple-element.82, f32[2,2,16,32,128]{4,3,2,1,0:T(8,128)S(1)} %convolution_bitcast_fusion.6, f32[2,2,16,2,128]{4,3,2,1,0:T(2,128)S(1)} %get-tuple-element.121, ...), kind=kLoop, calls=%fused_computation.152 | loop fusion | flops 9175040 | bytes 4063240 | tf_op jit(solution)/shard_map/mul | solution.py:161
  40.6 1.8 %collective-permute-start.11 = (f32[2,2,16,4,128]{4,3,2,1,0:T(4,128)S(1)}, f32[2,2,16,4,128]{4,3,2,1,0:T(4,128)S(1)}, u32[]{:S(2)}, u32[]{:S(2)}) collective-permute-start(f32[2,2,16,4,128]{4,3,2,1,0:T(4,128)S(1)} %pad_maximum_fusion.37), channel_id=1, source_target_pairs={{0,1},{1,0},{2,3},{3,2},{4,5},{5,4},{6,7},{7,6},{8,9},{9,8},{10,11... | collective-permute-start | bytes 393224 | tf_op jit(solution)/shard_map/ppermute | solution.py:124
  42.5 2.6 %collective-permute-start.10 = (f32[2,2,2,32,128]{4,3,2,1,0:T(8,128)S(1)}, f32[2,2,2,32,128]{4,3,2,1,0:T(8,128)S(1)}, u32[]{:S(2)}, u32[]{:S(2)}) collective-permute-start(f32[2,2,2,32,128]{4,3,2,1,0:T(8,128)S(1)} %get-tuple-element.71), channel_id=1, source_target_pairs={{16,0},{18,16},{2,18},{4,2},{20,4},{22,20},{6,22},{8,6},{24,8},{26... | collective-permute-start | bytes 393224 | tf_op jit(solution)/shard_map/ppermute | solution.py:129
  45.7 1.9 %collective-permute-done.10 = f32[2,2,2,32,128]{4,3,2,1,0:T(8,128)S(1)} collective-permute-done((f32[2,2,2,32,128]{4,3,2,1,0:T(8,128)S(1)}, f32[2,2,2,32,128]{4,3,2,1,0:T(8,128)S(1)}, u32[]{:S(2)}, u32[]{:S(2)}) %collective-permute-start.10) | collective-permute-done | bytes 131104 | tf_op jit(solution)/shard_map/ppermute | solution.py:129
  47.6 3.7 %collective-permute-done.9 = f32[2,2,2,32,128]{4,3,2,1,0:T(8,128)S(1)} collective-permute-done((f32[2,2,2,32,128]{4,3,2,1,0:T(8,128)S(1)}, f32[2,2,2,32,128]{4,3,2,1,0:T(8,128)S(1)}, u32[]{:S(2)}, u32[]{:S(2)}) %collective-permute-start.9) | collective-permute-done | bytes 131104 | tf_op jit(solution)/shard_map/ppermute | solution.py:128
  51.2 1.8 %fusion.41 = f32[2,2,16,32,128]{4,3,2,1,0:T(8,128)S(1)} fusion(f32[2,1,16,32,128]{4,3,2,1,0:T(8,128)S(1)} %get-tuple-element.75, f32[2,1,16,32,128]{4,3,2,1,0:T(8,128)S(1)} %get-tuple-element.74, f32[2,2,16,32,128]{4,3,2,1,0:T(8,128)S(1)} %convolution_bitcast_fusion.5, f32[2,2,16,2,128]{4,3,2,1,0:T(2,128)S(1)} %get-tuple-element.119, ...), kind=kLoop, calls=%fused_computation.157 | loop fusion | flops 9175040 | bytes 4063240 | tf_op jit(solution)/shard_map/mul | solution.py:161
  55.4 3.5 %collective-permute-start.13 = (f32[2,2,2,32,128]{4,3,2,1,0:T(8,128)S(1)}, f32[2,2,2,32,128]{4,3,2,1,0:T(8,128)S(1)}, u32[]{:S(2)}, u32[]{:S(2)}) collective-permute-start(f32[2,2,2,32,128]{4,3,2,1,0:T(8,128)S(1)} %get-tuple-element.63), channel_id=1, source_target_pairs={{16,0},{18,16},{2,18},{4,2},{20,4},{22,20},{6,22},{8,6},{24,8},{26... | collective-permute-start | bytes 393224 | tf_op jit(solution)/shard_map/ppermute | solution.py:129
  61.5 1.8 %fusion.45 = f32[2,2,16,32,128]{4,3,2,1,0:T(8,128)S(1)} fusion(f32[2,1,16,32,128]{4,3,2,1,0:T(8,128)S(1)} %get-tuple-element.67, f32[2,1,16,32,128]{4,3,2,1,0:T(8,128)S(1)} %get-tuple-element.66, f32[2,2,16,32,128]{4,3,2,1,0:T(8,128)S(1)} %convolution_bitcast_fusion.4, f32[2,2,16,2,128]{4,3,2,1,0:T(2,128)S(1)} %get-tuple-element.117, ...), kind=kLoop, calls=%fused_computation.162 | loop fusion | flops 9175040 | bytes 4063240 | tf_op jit(solution)/shard_map/mul | solution.py:161
  65.2 1.8 %collective-permute-start.17 = (f32[2,2,16,4,128]{4,3,2,1,0:T(4,128)S(1)}, f32[2,2,16,4,128]{4,3,2,1,0:T(4,128)S(1)}, u32[]{:S(2)}, u32[]{:S(2)}) collective-permute-start(f32[2,2,16,4,128]{4,3,2,1,0:T(4,128)S(1)} %pad_maximum_fusion.39), channel_id=1, source_target_pairs={{0,1},{1,0},{2,3},{3,2},{4,5},{5,4},{6,7},{7,6},{8,9},{9,8},{10,11... | collective-permute-start | bytes 393224 | tf_op jit(solution)/shard_map/ppermute | solution.py:124
  67.1 3.5 %collective-permute-start.16 = (f32[2,2,2,32,128]{4,3,2,1,0:T(8,128)S(1)}, f32[2,2,2,32,128]{4,3,2,1,0:T(8,128)S(1)}, u32[]{:S(2)}, u32[]{:S(2)}) collective-permute-start(f32[2,2,2,32,128]{4,3,2,1,0:T(8,128)S(1)} %get-tuple-element.55), channel_id=1, source_target_pairs={{16,0},{18,16},{2,18},{4,2},{20,4},{22,20},{6,22},{8,6},{24,8},{26... | collective-permute-start | bytes 393224 | tf_op jit(solution)/shard_map/ppermute | solution.py:129
  70.7 2.6 %collective-permute-done.15 = f32[2,2,2,32,128]{4,3,2,1,0:T(8,128)S(1)} collective-permute-done((f32[2,2,2,32,128]{4,3,2,1,0:T(8,128)S(1)}, f32[2,2,2,32,128]{4,3,2,1,0:T(8,128)S(1)}, u32[]{:S(2)}, u32[]{:S(2)}) %collective-permute-start.15) | collective-permute-done | bytes 131104 | tf_op jit(solution)/shard_map/ppermute | solution.py:128
  73.3 1.8 %fusion.49 = f32[2,2,16,32,128]{4,3,2,1,0:T(8,128)S(1)} fusion(f32[2,1,16,32,128]{4,3,2,1,0:T(8,128)S(1)} %get-tuple-element.59, f32[2,1,16,32,128]{4,3,2,1,0:T(8,128)S(1)} %get-tuple-element.58, f32[2,2,16,32,128]{4,3,2,1,0:T(8,128)S(1)} %convolution_bitcast_fusion.3, f32[2,2,16,2,128]{4,3,2,1,0:T(2,128)S(1)} %get-tuple-element.115, ...), kind=kLoop, calls=%fused_computation.167 | loop fusion | flops 9175040 | bytes 4063240 | tf_op jit(solution)/shard_map/mul | solution.py:161
  77.4 3.5 %collective-permute-start.19 = (f32[2,2,2,32,128]{4,3,2,1,0:T(8,128)S(1)}, f32[2,2,2,32,128]{4,3,2,1,0:T(8,128)S(1)}, u32[]{:S(2)}, u32[]{:S(2)}) collective-permute-start(f32[2,2,2,32,128]{4,3,2,1,0:T(8,128)S(1)} %get-tuple-element.47), channel_id=1, source_target_pairs={{16,0},{18,16},{2,18},{4,2},{20,4},{22,20},{6,22},{8,6},{24,8},{26... | collective-permute-start | bytes 393224 | tf_op jit(solution)/shard_map/ppermute | solution.py:129
  83.6 1.8 %fusion.53 = f32[2,2,16,32,128]{4,3,2,1,0:T(8,128)S(1)} fusion(f32[2,1,16,32,128]{4,3,2,1,0:T(8,128)S(1)} %get-tuple-element.51, f32[2,1,16,32,128]{4,3,2,1,0:T(8,128)S(1)} %get-tuple-element.50, f32[2,2,16,32,128]{4,3,2,1,0:T(8,128)S(1)} %convolution_bitcast_fusion.2, f32[2,2,16,2,128]{4,3,2,1,0:T(2,128)S(1)} %get-tuple-element.113, ...), kind=kLoop, calls=%fused_computation.172 | loop fusion | flops 9175040 | bytes 4063240 | tf_op jit(solution)/shard_map/mul | solution.py:161
  87.3 1.8 %collective-permute-start.23 = (f32[2,2,16,4,128]{4,3,2,1,0:T(4,128)S(1)}, f32[2,2,16,4,128]{4,3,2,1,0:T(4,128)S(1)}, u32[]{:S(2)}, u32[]{:S(2)}) collective-permute-start(f32[2,2,16,4,128]{4,3,2,1,0:T(4,128)S(1)} %pad_maximum_fusion.41), channel_id=1, source_target_pairs={{0,1},{1,0},{2,3},{3,2},{4,5},{5,4},{6,7},{7,6},{8,9},{9,8},{10,11... | collective-permute-start | bytes 393224 | tf_op jit(solution)/shard_map/ppermute | solution.py:124
  89.2 3.5 %collective-permute-start.22 = (f32[2,2,2,32,128]{4,3,2,1,0:T(8,128)S(1)}, f32[2,2,2,32,128]{4,3,2,1,0:T(8,128)S(1)}, u32[]{:S(2)}, u32[]{:S(2)}) collective-permute-start(f32[2,2,2,32,128]{4,3,2,1,0:T(8,128)S(1)} %get-tuple-element.39), channel_id=1, source_target_pairs={{16,0},{18,16},{2,18},{4,2},{20,4},{22,20},{6,22},{8,6},{24,8},{26... | collective-permute-start | bytes 393224 | tf_op jit(solution)/shard_map/ppermute | solution.py:129
  92.8 2.6 %collective-permute-done.21 = f32[2,2,2,32,128]{4,3,2,1,0:T(8,128)S(1)} collective-permute-done((f32[2,2,2,32,128]{4,3,2,1,0:T(8,128)S(1)}, f32[2,2,2,32,128]{4,3,2,1,0:T(8,128)S(1)}, u32[]{:S(2)}, u32[]{:S(2)}) %collective-permute-start.21) | collective-permute-done | bytes 131104 | tf_op jit(solution)/shard_map/ppermute | solution.py:128
  95.4 1.8 %fusion.57 = f32[2,2,16,32,128]{4,3,2,1,0:T(8,128)S(1)} fusion(f32[2,1,16,32,128]{4,3,2,1,0:T(8,128)S(1)} %get-tuple-element.43, f32[2,1,16,32,128]{4,3,2,1,0:T(8,128)S(1)} %get-tuple-element.42, f32[2,2,16,32,128]{4,3,2,1,0:T(8,128)S(1)} %convolution_bitcast_fusion.1, f32[2,2,16,2,128]{4,3,2,1,0:T(2,128)S(1)} %get-tuple-element.111, ...), kind=kLoop, calls=%fused_computation.177 | loop fusion | flops 9175040 | bytes 4063240 | tf_op jit(solution)/shard_map/mul | solution.py:161
  99.5 3.5 %collective-permute-start.25 = (f32[2,2,2,32,128]{4,3,2,1,0:T(8,128)S(1)}, f32[2,2,2,32,128]{4,3,2,1,0:T(8,128)S(1)}, u32[]{:S(2)}, u32[]{:S(2)}) collective-permute-start(f32[2,2,2,32,128]{4,3,2,1,0:T(8,128)S(1)} %get-tuple-element.31), channel_id=1, source_target_pairs={{16,0},{18,16},{2,18},{4,2},{20,4},{22,20},{6,22},{8,6},{24,8},{26... | collective-permute-start | bytes 393224 | tf_op jit(solution)/shard_map/ppermute | solution.py:129
  104.1 1.5 %collective-permute-done.24 = f32[2,2,2,32,128]{4,3,2,1,0:T(8,128)S(1)} collective-permute-done((f32[2,2,2,32,128]{4,3,2,1,0:T(8,128)S(1)}, f32[2,2,2,32,128]{4,3,2,1,0:T(8,128)S(1)}, u32[]{:S(2)}, u32[]{:S(2)}) %collective-permute-start.24) | collective-permute-done | bytes 131104 | tf_op jit(solution)/shard_map/ppermute | solution.py:128
  105.7 1.8 %fusion.61 = f32[2,2,16,32,128]{4,3,2,1,0:T(8,128)S(1)} fusion(f32[2,1,16,32,128]{4,3,2,1,0:T(8,128)S(1)} %get-tuple-element.35, f32[2,1,16,32,128]{4,3,2,1,0:T(8,128)S(1)} %get-tuple-element.34, f32[2,2,16,32,128]{4,3,2,1,0:T(8,128)S(1)} %convolution_bitcast_fusion, f32[2,2,16,2,128]{4,3,2,1,0:T(2,128)S(1)} %get-tuple-element.109, ...), kind=kLoop, calls=%fused_computation.182 | loop fusion | flops 9175040 | bytes 4063240 | tf_op jit(solution)/shard_map/mul | solution.py:161
  110.0 2.0 %collective-permute-start.28 = (f32[1,2,16,16,128]{4,3,2,1,0:T(8,128)S(1)}, f32[1,2,16,16,128]{4,3,2,1,0:T(8,128)S(1)}, u32[]{:S(2)}, u32[]{:S(2)}) collective-permute-start(f32[1,2,16,16,128]{4,3,2,1,0:T(8,128)S(1)} %get-tuple-element.97), channel_id=1, source_target_pairs={{0,16},{16,0},{1,17},{17,1},{2,18},{18,2},{3,19},{19,3},{4,20},{20... | collective-permute-start | bytes 786440 | tf_op jit(solution)/shard_map/ppermute | solution.py:232
  112.0 4.3 %collective-permute-done.27 = f32[1,2,16,16,128]{4,3,2,1,0:T(8,128)S(1)} collective-permute-done((f32[1,2,16,16,128]{4,3,2,1,0:T(8,128)S(1)}, f32[1,2,16,16,128]{4,3,2,1,0:T(8,128)S(1)}, u32[]{:S(2)}, u32[]{:S(2)}) %collective-permute-start.27) | collective-permute-done | bytes 262176 | tf_op jit(solution)/shard_map/ppermute | solution.py:231
  116.3 2.8 %collective-permute-done.28 = f32[1,2,16,16,128]{4,3,2,1,0:T(8,128)S(1)} collective-permute-done((f32[1,2,16,16,128]{4,3,2,1,0:T(8,128)S(1)}, f32[1,2,16,16,128]{4,3,2,1,0:T(8,128)S(1)}, u32[]{:S(2)}, u32[]{:S(2)}) %collective-permute-start.28) | collective-permute-done | bytes 262176 | tf_op jit(solution)/shard_map/ppermute | solution.py:232
  (140 shorter events, 34.6 us)
Async XLA Ops:
  1.2 13.9 %collective-permute-start.2 = (f32[1,2,16,4,128]{4,3,2,1,0:T(4,128)S(1)}, f32[1,2,16,4,128]{4,3,2,1,0:T(4,128)S(1)}, u32[]{:S(2)}, u32[]{:S(2)}) collective-permute-start(f32[1,2,16,4,128]{4,3,2,1,0:T(4,128)S(1)} %pad_maximum_fusion.43), channel_id=1, source_target_pairs={{0,1},{1,0},{2,3},{3,2},{4,5},{5,4},{6,7},{7,6},{8,9},{9,8},{10,11... | collective-permute-start | bytes 196616 | tf_op jit(solution)/shard_map/ppermute | solution.py:124
  4.2 10.9 %collective-permute-start = (f32[1,2,2,32,128]{4,3,2,1,0:T(8,128)S(1)}, f32[1,2,2,32,128]{4,3,2,1,0:T(8,128)S(1)}, u32[]{:S(2)}, u32[]{:S(2)}) collective-permute-start(f32[1,2,2,32,128]{4,3,2,1,0:T(8,128)S(1)} %get-tuple-element.102), channel_id=1, source_target_pairs={{0,16},{16,18},{18,2},{2,4},{4,20},{20,22},{22,6},{6,8},{8,24},{24... | collective-permute-start | bytes 196616 | tf_op jit(solution)/shard_map/ppermute | solution.py:128
  5.8 9.4 %collective-permute-start.1 = (f32[1,2,2,32,128]{4,3,2,1,0:T(8,128)S(1)}, f32[1,2,2,32,128]{4,3,2,1,0:T(8,128)S(1)}, u32[]{:S(2)}, u32[]{:S(2)}) collective-permute-start(f32[1,2,2,32,128]{4,3,2,1,0:T(8,128)S(1)} %get-tuple-element.103), channel_id=1, source_target_pairs={{16,0},{18,16},{2,18},{4,2},{20,4},{22,20},{6,22},{8,6},{24,8},{26... | collective-permute-start | bytes 196616 | tf_op jit(solution)/shard_map/ppermute | solution.py:129
  7.9 7.2 %copy-start.2 = (f32[2,32,32,128]{3,2,1,0:T(8,128)S(1)}, f32[2,32,32,128]{3,2,1,0:T(8,128)}, u32[]{:S(2)}) copy-start(f32[2,32,32,128]{3,2,1,0:T(8,128)} %param.12) | copy-start | bytes 3145732
  16.8 9.0 %collective-permute-start.3 = (f32[2,2,2,32,128]{4,3,2,1,0:T(8,128)S(1)}, f32[2,2,2,32,128]{4,3,2,1,0:T(8,128)S(1)}, u32[]{:S(2)}, u32[]{:S(2)}) collective-permute-start(f32[2,2,2,32,128]{4,3,2,1,0:T(8,128)S(1)} %get-tuple-element.87), channel_id=1, source_target_pairs={{0,16},{16,18},{18,2},{2,4},{4,20},{20,22},{22,6},{6,8},{8,24},{24... | collective-permute-start | bytes 393224 | tf_op jit(solution)/shard_map/ppermute | solution.py:128
  16.9 9.0 %collective-permute-start.4 = (f32[2,2,2,32,128]{4,3,2,1,0:T(8,128)S(1)}, f32[2,2,2,32,128]{4,3,2,1,0:T(8,128)S(1)}, u32[]{:S(2)}, u32[]{:S(2)}) collective-permute-start(f32[2,2,2,32,128]{4,3,2,1,0:T(8,128)S(1)} %get-tuple-element.86), channel_id=1, source_target_pairs={{16,0},{18,16},{2,18},{4,2},{20,4},{22,20},{6,22},{8,6},{24,8},{26... | collective-permute-start | bytes 393224 | tf_op jit(solution)/shard_map/ppermute | solution.py:129
  20.4 5.0 %collective-permute-start.5 = (f32[2,2,16,4,128]{4,3,2,1,0:T(4,128)S(1)}, f32[2,2,16,4,128]{4,3,2,1,0:T(4,128)S(1)}, u32[]{:S(2)}, u32[]{:S(2)}) collective-permute-start(f32[2,2,16,4,128]{4,3,2,1,0:T(4,128)S(1)} %pad_maximum_fusion.35), channel_id=1, source_target_pairs={{0,1},{1,0},{2,3},{3,2},{4,5},{5,4},{6,7},{7,6},{8,9},{9,8},{10,11... | collective-permute-start | bytes 393224 | tf_op jit(solution)/shard_map/ppermute | solution.py:124
  29.7 5.0 %collective-permute-start.8 = (f32[2,2,16,4,128]{4,3,2,1,0:T(4,128)S(1)}, f32[2,2,16,4,128]{4,3,2,1,0:T(4,128)S(1)}, u32[]{:S(2)}, u32[]{:S(2)}) collective-permute-start(f32[2,2,16,4,128]{4,3,2,1,0:T(4,128)S(1)} %pad_maximum_fusion.36), channel_id=1, source_target_pairs={{0,1},{1,0},{2,3},{3,2},{4,5},{5,4},{6,7},{7,6},{8,9},{9,8},{10,11... | collective-permute-start | bytes 393224 | tf_op jit(solution)/shard_map/ppermute | solution.py:124
  29.8 7.2 %collective-permute-start.6 = (f32[2,2,2,32,128]{4,3,2,1,0:T(8,128)S(1)}, f32[2,2,2,32,128]{4,3,2,1,0:T(8,128)S(1)}, u32[]{:S(2)}, u32[]{:S(2)}) collective-permute-start(f32[2,2,2,32,128]{4,3,2,1,0:T(8,128)S(1)} %get-tuple-element.78), channel_id=1, source_target_pairs={{0,16},{16,18},{18,2},{2,4},{4,20},{20,22},{22,6},{6,8},{8,24},{24... | collective-permute-start | bytes 393224 | tf_op jit(solution)/shard_map/ppermute | solution.py:128
  29.8 7.2 %collective-permute-start.7 = (f32[2,2,2,32,128]{4,3,2,1,0:T(8,128)S(1)}, f32[2,2,2,32,128]{4,3,2,1,0:T(8,128)S(1)}, u32[]{:S(2)}, u32[]{:S(2)}) collective-permute-start(f32[2,2,2,32,128]{4,3,2,1,0:T(8,128)S(1)} %get-tuple-element.79), channel_id=1, source_target_pairs={{16,0},{18,16},{2,18},{4,2},{20,4},{22,20},{6,22},{8,6},{24,8},{26... | collective-permute-start | bytes 393224 | tf_op jit(solution)/shard_map/ppermute | solution.py:129
  40.6 5.0 %collective-permute-start.11 = (f32[2,2,16,4,128]{4,3,2,1,0:T(4,128)S(1)}, f32[2,2,16,4,128]{4,3,2,1,0:T(4,128)S(1)}, u32[]{:S(2)}, u32[]{:S(2)}) collective-permute-start(f32[2,2,16,4,128]{4,3,2,1,0:T(4,128)S(1)} %pad_maximum_fusion.37), channel_id=1, source_target_pairs={{0,1},{1,0},{2,3},{3,2},{4,5},{5,4},{6,7},{7,6},{8,9},{9,8},{10,11... | collective-permute-start | bytes 393224 | tf_op jit(solution)/shard_map/ppermute | solution.py:124
  42.5 5.1 %collective-permute-start.10 = (f32[2,2,2,32,128]{4,3,2,1,0:T(8,128)S(1)}, f32[2,2,2,32,128]{4,3,2,1,0:T(8,128)S(1)}, u32[]{:S(2)}, u32[]{:S(2)}) collective-permute-start(f32[2,2,2,32,128]{4,3,2,1,0:T(8,128)S(1)} %get-tuple-element.71), channel_id=1, source_target_pairs={{16,0},{18,16},{2,18},{4,2},{20,4},{22,20},{6,22},{8,6},{24,8},{26... | collective-permute-start | bytes 393224 | tf_op jit(solution)/shard_map/ppermute | solution.py:129
  45.1 6.2 %collective-permute-start.9 = (f32[2,2,2,32,128]{4,3,2,1,0:T(8,128)S(1)}, f32[2,2,2,32,128]{4,3,2,1,0:T(8,128)S(1)}, u32[]{:S(2)}, u32[]{:S(2)}) collective-permute-start(f32[2,2,2,32,128]{4,3,2,1,0:T(8,128)S(1)} %get-tuple-element.70), channel_id=1, source_target_pairs={{0,16},{16,18},{18,2},{2,4},{4,20},{20,22},{22,6},{6,8},{8,24},{24... | collective-permute-start | bytes 393224 | tf_op jit(solution)/shard_map/ppermute | solution.py:128
  54.9 5.0 %collective-permute-start.14 = (f32[2,2,16,4,128]{4,3,2,1,0:T(4,128)S(1)}, f32[2,2,16,4,128]{4,3,2,1,0:T(4,128)S(1)}, u32[]{:S(2)}, u32[]{:S(2)}) collective-permute-start(f32[2,2,16,4,128]{4,3,2,1,0:T(4,128)S(1)} %pad_maximum_fusion.38), channel_id=1, source_target_pairs={{0,1},{1,0},{2,3},{3,2},{4,5},{5,4},{6,7},{7,6},{8,9},{9,8},{10,11... | collective-permute-start | bytes 393224 | tf_op jit(solution)/shard_map/ppermute | solution.py:124
  55.3 6.3 %collective-permute-start.12 = (f32[2,2,2,32,128]{4,3,2,1,0:T(8,128)S(1)}, f32[2,2,2,32,128]{4,3,2,1,0:T(8,128)S(1)}, u32[]{:S(2)}, u32[]{:S(2)}) collective-permute-start(f32[2,2,2,32,128]{4,3,2,1,0:T(8,128)S(1)} %get-tuple-element.62), channel_id=1, source_target_pairs={{0,16},{16,18},{18,2},{2,4},{4,20},{20,22},{22,6},{6,8},{8,24},{24... | collective-permute-start | bytes 393224 | tf_op jit(solution)/shard_map/ppermute | solution.py:128
  55.4 6.2 %collective-permute-start.13 = (f32[2,2,2,32,128]{4,3,2,1,0:T(8,128)S(1)}, f32[2,2,2,32,128]{4,3,2,1,0:T(8,128)S(1)}, u32[]{:S(2)}, u32[]{:S(2)}) collective-permute-start(f32[2,2,2,32,128]{4,3,2,1,0:T(8,128)S(1)} %get-tuple-element.63), channel_id=1, source_target_pairs={{16,0},{18,16},{2,18},{4,2},{20,4},{22,20},{6,22},{8,6},{24,8},{26... | collective-permute-start | bytes 393224 | tf_op jit(solution)/shard_map/ppermute | solution.py:129
  65.2 5.4 %collective-permute-start.17 = (f32[2,2,16,4,128]{4,3,2,1,0:T(4,128)S(1)}, f32[2,2,16,4,128]{4,3,2,1,0:T(4,128)S(1)}, u32[]{:S(2)}, u32[]{:S(2)}) collective-permute-start(f32[2,2,16,4,128]{4,3,2,1,0:T(4,128)S(1)} %pad_maximum_fusion.39), channel_id=1, source_target_pairs={{0,1},{1,0},{2,3},{3,2},{4,5},{5,4},{6,7},{7,6},{8,9},{9,8},{10,11... | collective-permute-start | bytes 393224 | tf_op jit(solution)/shard_map/ppermute | solution.py:124
  67.0 6.3 %collective-permute-start.15 = (f32[2,2,2,32,128]{4,3,2,1,0:T(8,128)S(1)}, f32[2,2,2,32,128]{4,3,2,1,0:T(8,128)S(1)}, u32[]{:S(2)}, u32[]{:S(2)}) collective-permute-start(f32[2,2,2,32,128]{4,3,2,1,0:T(8,128)S(1)} %get-tuple-element.54), channel_id=1, source_target_pairs={{0,16},{16,18},{18,2},{2,4},{4,20},{20,22},{22,6},{6,8},{8,24},{24... | collective-permute-start | bytes 393224 | tf_op jit(solution)/shard_map/ppermute | solution.py:128
  67.1 6.2 %collective-permute-start.16 = (f32[2,2,2,32,128]{4,3,2,1,0:T(8,128)S(1)}, f32[2,2,2,32,128]{4,3,2,1,0:T(8,128)S(1)}, u32[]{:S(2)}, u32[]{:S(2)}) collective-permute-start(f32[2,2,2,32,128]{4,3,2,1,0:T(8,128)S(1)} %get-tuple-element.55), channel_id=1, source_target_pairs={{16,0},{18,16},{2,18},{4,2},{20,4},{22,20},{6,22},{8,6},{24,8},{26... | collective-permute-start | bytes 393224 | tf_op jit(solution)/shard_map/ppermute | solution.py:129
  77.0 5.0 %collective-permute-start.20 = (f32[2,2,16,4,128]{4,3,2,1,0:T(4,128)S(1)}, f32[2,2,16,4,128]{4,3,2,1,0:T(4,128)S(1)}, u32[]{:S(2)}, u32[]{:S(2)}) collective-permute-start(f32[2,2,16,4,128]{4,3,2,1,0:T(4,128)S(1)} %pad_maximum_fusion.40), channel_id=1, source_target_pairs={{0,1},{1,0},{2,3},{3,2},{4,5},{5,4},{6,7},{7,6},{8,9},{9,8},{10,11... | collective-permute-start | bytes 393224 | tf_op jit(solution)/shard_map/ppermute | solution.py:124
  77.4 6.3 %collective-permute-start.18 = (f32[2,2,2,32,128]{4,3,2,1,0:T(8,128)S(1)}, f32[2,2,2,32,128]{4,3,2,1,0:T(8,128)S(1)}, u32[]{:S(2)}, u32[]{:S(2)}) collective-permute-start(f32[2,2,2,32,128]{4,3,2,1,0:T(8,128)S(1)} %get-tuple-element.46), channel_id=1, source_target_pairs={{0,16},{16,18},{18,2},{2,4},{4,20},{20,22},{22,6},{6,8},{8,24},{24... | collective-permute-start | bytes 393224 | tf_op jit(solution)/shard_map/ppermute | solution.py:128
  77.4 6.2 %collective-permute-start.19 = (f32[2,2,2,32,128]{4,3,2,1,0:T(8,128)S(1)}, f32[2,2,2,32,128]{4,3,2,1,0:T(8,128)S(1)}, u32[]{:S(2)}, u32[]{:S(2)}) collective-permute-start(f32[2,2,2,32,128]{4,3,2,1,0:T(8,128)S(1)} %get-tuple-element.47), channel_id=1, source_target_pairs={{16,0},{18,16},{2,18},{4,2},{20,4},{22,20},{6,22},{8,6},{24,8},{26... | collective-permute-start | bytes 393224 | tf_op jit(solution)/shard_map/ppermute | solution.py:129
  87.3 5.4 %collective-permute-start.23 = (f32[2,2,16,4,128]{4,3,2,1,0:T(4,128)S(1)}, f32[2,2,16,4,128]{4,3,2,1,0:T(4,128)S(1)}, u32[]{:S(2)}, u32[]{:S(2)}) collective-permute-start(f32[2,2,16,4,128]{4,3,2,1,0:T(4,128)S(1)} %pad_maximum_fusion.41), channel_id=1, source_target_pairs={{0,1},{1,0},{2,3},{3,2},{4,5},{5,4},{6,7},{7,6},{8,9},{9,8},{10,11... | collective-permute-start | bytes 393224 | tf_op jit(solution)/shard_map/ppermute | solution.py:124
  89.1 6.3 %collective-permute-start.21 = (f32[2,2,2,32,128]{4,3,2,1,0:T(8,128)S(1)}, f32[2,2,2,32,128]{4,3,2,1,0:T(8,128)S(1)}, u32[]{:S(2)}, u32[]{:S(2)}) collective-permute-start(f32[2,2,2,32,128]{4,3,2,1,0:T(8,128)S(1)} %get-tuple-element.38), channel_id=1, source_target_pairs={{0,16},{16,18},{18,2},{2,4},{4,20},{20,22},{22,6},{6,8},{8,24},{24... | collective-permute-start | bytes 393224 | tf_op jit(solution)/shard_map/ppermute | solution.py:128
  89.2 6.2 %collective-permute-start.22 = (f32[2,2,2,32,128]{4,3,2,1,0:T(8,128)S(1)}, f32[2,2,2,32,128]{4,3,2,1,0:T(8,128)S(1)}, u32[]{:S(2)}, u32[]{:S(2)}) collective-permute-start(f32[2,2,2,32,128]{4,3,2,1,0:T(8,128)S(1)} %get-tuple-element.39), channel_id=1, source_target_pairs={{16,0},{18,16},{2,18},{4,2},{20,4},{22,20},{6,22},{8,6},{24,8},{26... | collective-permute-start | bytes 393224 | tf_op jit(solution)/shard_map/ppermute | solution.py:129
  98.6 9.0 %copy-start = (f32[2,2,16,32,128]{4,3,2,1,0:T(8,128)}, f32[2,2,16,32,128]{4,3,2,1,0:T(8,128)S(1)}, u32[]{:S(2)}) copy-start(f32[2,2,16,32,128]{4,3,2,1,0:T(8,128)S(1)} %convolution_bitcast_fusion) | copy-start | bytes 3145732
  99.1 5.0 %collective-permute-start.26 = (f32[2,2,16,4,128]{4,3,2,1,0:T(4,128)S(1)}, f32[2,2,16,4,128]{4,3,2,1,0:T(4,128)S(1)}, u32[]{:S(2)}, u32[]{:S(2)}) collective-permute-start(f32[2,2,16,4,128]{4,3,2,1,0:T(4,128)S(1)} %pad_maximum_fusion.42), channel_id=1, source_target_pairs={{0,1},{1,0},{2,3},{3,2},{4,5},{5,4},{6,7},{7,6},{8,9},{9,8},{10,11... | collective-permute-start | bytes 393224 | tf_op jit(solution)/shard_map/ppermute | solution.py:124
  99.4 6.3 %collective-permute-start.24 = (f32[2,2,2,32,128]{4,3,2,1,0:T(8,128)S(1)}, f32[2,2,2,32,128]{4,3,2,1,0:T(8,128)S(1)}, u32[]{:S(2)}, u32[]{:S(2)}) collective-permute-start(f32[2,2,2,32,128]{4,3,2,1,0:T(8,128)S(1)} %get-tuple-element.30), channel_id=1, source_target_pairs={{0,16},{16,18},{18,2},{2,4},{4,20},{20,22},{22,6},{6,8},{8,24},{24... | collective-permute-start | bytes 393224 | tf_op jit(solution)/shard_map/ppermute | solution.py:128
  99.5 6.2 %collective-permute-start.25 = (f32[2,2,2,32,128]{4,3,2,1,0:T(8,128)S(1)}, f32[2,2,2,32,128]{4,3,2,1,0:T(8,128)S(1)}, u32[]{:S(2)}, u32[]{:S(2)}) collective-permute-start(f32[2,2,2,32,128]{4,3,2,1,0:T(8,128)S(1)} %get-tuple-element.31), channel_id=1, source_target_pairs={{16,0},{18,16},{2,18},{4,2},{20,4},{22,20},{6,22},{8,6},{24,8},{26... | collective-permute-start | bytes 393224 | tf_op jit(solution)/shard_map/ppermute | solution.py:129
  109.8 9.3 %copy-start.3 = (f32[1,2,32,32,128]{4,3,2,1,0:T(8,128)}, f32[1,2,32,32,128]{4,3,2,1,0:T(8,128)S(1)}, u32[]{:S(2)}) copy-start(f32[1,2,32,32,128]{4,3,2,1,0:T(8,128)S(1)} %get-tuple-element.27) | copy-start | bytes 3145732
  109.9 6.4 %collective-permute-start.27 = (f32[1,2,16,16,128]{4,3,2,1,0:T(8,128)S(1)}, f32[1,2,16,16,128]{4,3,2,1,0:T(8,128)S(1)}, u32[]{:S(2)}, u32[]{:S(2)}) collective-permute-start(f32[1,2,16,16,128]{4,3,2,1,0:T(8,128)S(1)} %get-tuple-element.96), channel_id=1, source_target_pairs={{0,16},{16,0},{1,17},{17,1},{2,18},{18,2},{3,19},{19,3},{4,20},{20... | collective-permute-start | bytes 786440 | tf_op jit(solution)/shard_map/ppermute | solution.py:231
  110.0 9.2 %collective-permute-start.28 = (f32[1,2,16,16,128]{4,3,2,1,0:T(8,128)S(1)}, f32[1,2,16,16,128]{4,3,2,1,0:T(8,128)S(1)}, u32[]{:S(2)}, u32[]{:S(2)}) collective-permute-start(f32[1,2,16,16,128]{4,3,2,1,0:T(8,128)S(1)} %get-tuple-element.97), channel_id=1, source_target_pairs={{0,16},{16,0},{1,17},{17,1},{2,18},{18,2},{3,19},{19,3},{4,20},{20... | collective-permute-start | bytes 786440 | tf_op jit(solution)/shard_map/ppermute | solution.py:232
  (8 other events, 13.2 us)

commit v6 on v4

--- a/solution.py
+++ b/solution.py
@@ -59,7 +59,7 @@
         d_ref[j] = d
         return c, d
 
-    lax.fori_loop(0, n, forward, (zero, zero))
+    lax.fori_loop(0, n, forward, (zero, zero), unroll=8)
 
     def backward(i, x):
         j = n - 1 - i
@@ -67,7 +67,7 @@
         out_ref[j] = x
         return x
 
-    lax.fori_loop(0, n, backward, zero)
+    lax.fori_loop(0, n, backward, zero, unroll=8)
 
 
 def vertical(diffusion):
@@ -217,23 +217,17 @@
         solved = column_solve(jnp.stack(rhs, 0), inverse)
         for i, l in enumerate(moving):
             states[l] = solved[i]
-    result = jnp.stack(states, 0)
     out = jnp.zeros((1,) + own_fields.shape[:1] + fields.shape[1:], jnp.float32)
     out = lax.dynamic_update_slice_in_dim(
-        out, lax.dynamic_index_in_dim(result, me, 0), start, 2
+        out, jnp.stack(states, 0)[me][None], start, 2
     )
     for shift in range(1, depth):
-        pairs = [(c, (c + shift) % depth) for c in range(depth)]
-        sent = lax.dynamic_index_in_dim(result, (me + shift) % depth, 0)
-        half = sent.shape[3] // 2
-        got = jnp.concatenate(
-            [
-                lax.ppermute(sent[:, :, :, :half], "corr", pairs),
-                lax.ppermute(sent[:, :, :, half:], "corr", pairs),
-            ],
-            3,
-        )
         origin = (me - shift) % depth
+        got = None
+        for level in range(depth):
+            pairs = [((level + shift) % depth, level)]
+            arrived = lax.ppermute(states[level][None], "corr", pairs)
+            got = arrived if got is None else jnp.where(me == level, arrived, got)
         out = lax.dynamic_update_slice_in_dim(
             out, got, slab_of(origin, tile, depth) * slab, 2
         )

time: 124 us -> 122 us (0.984)
  starting transfers between devices: 43.2 us -> 45.4 us
  waiting for transfers between devices: 34.6 us -> 32.8 us
    ppermute x2, starting transfers between devices: 2.08 us -> 4.33 us  [on_device(): arrived = lax.ppermute(states[level][None], 'corr', pairs)]
  transfers between devices with their start and end apart: 29 -> 29, of which waited for: 16 -> 16; matrix products, arithmetic and copies ran while one was open for 3% -> 6% of each run, Pallas kernels for 3% -> 2%
where the time goes in v6:
time: 122 us
  starting transfers between devices  45.4 us (37%)
  waiting for transfers between devices  32.8 us (27%)
  other arithmetic  25.5 us (21%)
  matrix products  9 us (7%)
  local copies, waits for them, and re-layouts  5.31 us (4%)
  Pallas kernels  2.94 us (2%)
    ppermute x9, starting transfers between devices, ring_halo(): after = lax.ppermute(first, axes, down)  29.4 us
    ppermute x9, waiting for transfers between devices, ring_halo(): before = lax.ppermute(last, axes, up)  15.5 us
    mul x9, other arithmetic, tendency(): return DT * (flow + kappa * laplace + react)  14.4 us
    ppermute x9, starting transfers between devices, ring_halo(): got = lax.ppermute(jnp.concatenate([first, last], dim), axes, up)  9.68 us
    dot_general x9, matrix products, column_solve(): jnp.einsum('lsxyk,sjk->lsxyj', rhs, inverse, precision=lax.Precision.HIGH...  9 us
    ppermute x9, waiting for transfers between devices, ring_halo(): got = lax.ppermute(jnp.concatenate([first, last], dim), axes, up)  8.78 us
    ppermute x2, waiting for transfers between devices, on_device(): arrived = lax.ppermute(states[level][None], 'corr', pairs)  6.35 us
    ppermute x2, starting transfers between devices, on_device(): arrived = lax.ppermute(states[level][None], 'corr', pairs)  4.33 us
  transfers between devices with their start and end apart: 29, of which 16 were waited for; matrix products, arithmetic and copies ran while one was open for 6% of the time, Pallas kernels for 2%

profile of v6, /device:TPU:0, one launch (start us, length us, event | category | flops | bytes accessed | tf_op | source)
XLA Modules:
  0.0 121.8 jit_solution(3123545586986462944)
XLA Ops:
  1.2 3.0 %collective-permute-start.2 = (f32[1,2,16,4,128]{4,3,2,1,0:T(4,128)S(1)}, f32[1,2,16,4,128]{4,3,2,1,0:T(4,128)S(1)}, u32[]{:S(2)}, u32[]{:S(2)}) collective-permute-start(f32[1,2,16,4,128]{4,3,2,1,0:T(4,128)S(1)} %pad_maximum_fusion.43), channel_id=1, source_target_pairs={{0,1},{1,0},{2,3},{3,2},{4,5},{5,4},{6,7},{7,6},{8,9},{9,8},{10,11... | collective-permute-start | bytes 196616 | tf_op jit(solution)/shard_map/ppermute | solution.py:124
  5.8 2.1 %collective-permute-start.1 = (f32[1,2,2,32,128]{4,3,2,1,0:T(8,128)S(1)}, f32[1,2,2,32,128]{4,3,2,1,0:T(8,128)S(1)}, u32[]{:S(2)}, u32[]{:S(2)}) collective-permute-start(f32[1,2,2,32,128]{4,3,2,1,0:T(8,128)S(1)} %get-tuple-element.99), channel_id=1, source_target_pairs={{16,0},{18,16},{2,18},{4,2},{20,4},{22,20},{6,22},{8,6},{24,8},{26... | collective-permute-start | bytes 196616 | tf_op jit(solution)/shard_map/ppermute | solution.py:129
  9.9 2.9 %shard_map.118 = f32[128,2,128]{2,1,0:T(2,128)} custom-call(f32[2,128]{1,0:T(2,128)} %copy-done.3, f32[2,128]{1,0:T(2,128)} %get-tuple-element.123.low_ref), custom_call_target="tpu_custom_call" | custom-call | flops 393216 | bytes 262144 | tf_op jit(solution)/shard_map/pallas_call | solution.py:78
  15.9 3.5 %collective-permute-start.4 = (f32[2,2,2,32,128]{4,3,2,1,0:T(8,128)S(1)}, f32[2,2,2,32,128]{4,3,2,1,0:T(8,128)S(1)}, u32[]{:S(2)}, u32[]{:S(2)}) collective-permute-start(f32[2,2,2,32,128]{4,3,2,1,0:T(8,128)S(1)} %get-tuple-element.84), channel_id=1, source_target_pairs={{16,0},{18,16},{2,18},{4,2},{20,4},{22,20},{6,22},{8,6},{24,8},{26... | collective-permute-start | bytes 393224 | tf_op jit(solution)/shard_map/ppermute | solution.py:129
  19.7 4.8 %collective-permute-done.5 = f32[2,2,16,4,128]{4,3,2,1,0:T(4,128)S(1)} collective-permute-done((f32[2,2,16,4,128]{4,3,2,1,0:T(4,128)S(1)}, f32[2,2,16,4,128]{4,3,2,1,0:T(4,128)S(1)}, u32[]{:S(2)}, u32[]{:S(2)}) %collective-permute-start.5) | collective-permute-done | bytes 131104 | tf_op jit(solution)/shard_map/ppermute | solution.py:124
  29.2 3.5 %collective-permute-start.7 = (f32[2,2,2,32,128]{4,3,2,1,0:T(8,128)S(1)}, f32[2,2,2,32,128]{4,3,2,1,0:T(8,128)S(1)}, u32[]{:S(2)}, u32[]{:S(2)}) collective-permute-start(f32[2,2,2,32,128]{4,3,2,1,0:T(8,128)S(1)} %get-tuple-element.77), channel_id=1, source_target_pairs={{16,0},{18,16},{2,18},{4,2},{20,4},{22,20},{6,22},{8,6},{24,8},{26... | collective-permute-start | bytes 393224 | tf_op jit(solution)/shard_map/ppermute | solution.py:129
  34.1 2.3 %collective-permute-done.6 = f32[2,2,2,32,128]{4,3,2,1,0:T(8,128)S(1)} collective-permute-done((f32[2,2,2,32,128]{4,3,2,1,0:T(8,128)S(1)}, f32[2,2,2,32,128]{4,3,2,1,0:T(8,128)S(1)}, u32[]{:S(2)}, u32[]{:S(2)}) %collective-permute-start.6) | collective-permute-done | bytes 131104 | tf_op jit(solution)/shard_map/ppermute | solution.py:128
  36.4 1.8 %fusion.37 = f32[2,2,16,32,128]{4,3,2,1,0:T(8,128)S(1)} fusion(f32[2,1,16,32,128]{4,3,2,1,0:T(8,128)S(1)} %get-tuple-element.81, f32[2,1,16,32,128]{4,3,2,1,0:T(8,128)S(1)} %get-tuple-element.80, f32[2,2,16,32,128]{4,3,2,1,0:T(8,128)S(1)} %convolution_bitcast_fusion.6, f32[2,2,16,2,128]{4,3,2,1,0:T(2,128)S(1)} %get-tuple-element.117, ...), kind=kLoop, calls=%fused_computation.148 | loop fusion | flops 9175040 | bytes 4063240 | tf_op jit(solution)/shard_map/mul | solution.py:161
  40.5 1.8 %collective-permute-start.11 = (f32[2,2,16,4,128]{4,3,2,1,0:T(4,128)S(1)}, f32[2,2,16,4,128]{4,3,2,1,0:T(4,128)S(1)}, u32[]{:S(2)}, u32[]{:S(2)}) collective-permute-start(f32[2,2,16,4,128]{4,3,2,1,0:T(4,128)S(1)} %pad_maximum_fusion.37), channel_id=1, source_target_pairs={{0,1},{1,0},{2,3},{3,2},{4,5},{5,4},{6,7},{7,6},{8,9},{9,8},{10,11... | collective-permute-start | bytes 393224 | tf_op jit(solution)/shard_map/ppermute | solution.py:124
  42.3 2.6 %collective-permute-start.10 = (f32[2,2,2,32,128]{4,3,2,1,0:T(8,128)S(1)}, f32[2,2,2,32,128]{4,3,2,1,0:T(8,128)S(1)}, u32[]{:S(2)}, u32[]{:S(2)}) collective-permute-start(f32[2,2,2,32,128]{4,3,2,1,0:T(8,128)S(1)} %get-tuple-element.69), channel_id=1, source_target_pairs={{16,0},{18,16},{2,18},{4,2},{20,4},{22,20},{6,22},{8,6},{24,8},{26... | collective-permute-start | bytes 393224 | tf_op jit(solution)/shard_map/ppermute | solution.py:129
  45.6 1.8 %collective-permute-done.10 = f32[2,2,2,32,128]{4,3,2,1,0:T(8,128)S(1)} collective-permute-done((f32[2,2,2,32,128]{4,3,2,1,0:T(8,128)S(1)}, f32[2,2,2,32,128]{4,3,2,1,0:T(8,128)S(1)}, u32[]{:S(2)}, u32[]{:S(2)}) %collective-permute-start.10) | collective-permute-done | bytes 131104 | tf_op jit(solution)/shard_map/ppermute | solution.py:129
  47.4 3.7 %collective-permute-done.9 = f32[2,2,2,32,128]{4,3,2,1,0:T(8,128)S(1)} collective-permute-done((f32[2,2,2,32,128]{4,3,2,1,0:T(8,128)S(1)}, f32[2,2,2,32,128]{4,3,2,1,0:T(8,128)S(1)}, u32[]{:S(2)}, u32[]{:S(2)}) %collective-permute-start.9) | collective-permute-done | bytes 131104 | tf_op jit(solution)/shard_map/ppermute | solution.py:128
  51.1 1.8 %fusion.41 = f32[2,2,16,32,128]{4,3,2,1,0:T(8,128)S(1)} fusion(f32[2,1,16,32,128]{4,3,2,1,0:T(8,128)S(1)} %get-tuple-element.73, f32[2,1,16,32,128]{4,3,2,1,0:T(8,128)S(1)} %get-tuple-element.72, f32[2,2,16,32,128]{4,3,2,1,0:T(8,128)S(1)} %convolution_bitcast_fusion.5, f32[2,2,16,2,128]{4,3,2,1,0:T(2,128)S(1)} %get-tuple-element.115, ...), kind=kLoop, calls=%fused_computation.153 | loop fusion | flops 9175040 | bytes 4063240 | tf_op jit(solution)/shard_map/mul | solution.py:161
  55.7 3.5 %collective-permute-start.13 = (f32[2,2,2,32,128]{4,3,2,1,0:T(8,128)S(1)}, f32[2,2,2,32,128]{4,3,2,1,0:T(8,128)S(1)}, u32[]{:S(2)}, u32[]{:S(2)}) collective-permute-start(f32[2,2,2,32,128]{4,3,2,1,0:T(8,128)S(1)} %get-tuple-element.61), channel_id=1, source_target_pairs={{16,0},{18,16},{2,18},{4,2},{20,4},{22,20},{6,22},{8,6},{24,8},{26... | collective-permute-start | bytes 393224 | tf_op jit(solution)/shard_map/ppermute | solution.py:129
  60.3 1.6 %collective-permute-done.12 = f32[2,2,2,32,128]{4,3,2,1,0:T(8,128)S(1)} collective-permute-done((f32[2,2,2,32,128]{4,3,2,1,0:T(8,128)S(1)}, f32[2,2,2,32,128]{4,3,2,1,0:T(8,128)S(1)}, u32[]{:S(2)}, u32[]{:S(2)}) %collective-permute-start.12) | collective-permute-done | bytes 131104 | tf_op jit(solution)/shard_map/ppermute | solution.py:128
  61.8 1.8 %fusion.45 = f32[2,2,16,32,128]{4,3,2,1,0:T(8,128)S(1)} fusion(f32[2,1,16,32,128]{4,3,2,1,0:T(8,128)S(1)} %get-tuple-element.65, f32[2,1,16,32,128]{4,3,2,1,0:T(8,128)S(1)} %get-tuple-element.64, f32[2,2,16,32,128]{4,3,2,1,0:T(8,128)S(1)} %convolution_bitcast_fusion.4, f32[2,2,16,2,128]{4,3,2,1,0:T(2,128)S(1)} %get-tuple-element.113, ...), kind=kLoop, calls=%fused_computation.158 | loop fusion | flops 9175040 | bytes 4063240 | tf_op jit(solution)/shard_map/mul | solution.py:161
  66.0 1.8 %collective-permute-start.17 = (f32[2,2,16,4,128]{4,3,2,1,0:T(4,128)S(1)}, f32[2,2,16,4,128]{4,3,2,1,0:T(4,128)S(1)}, u32[]{:S(2)}, u32[]{:S(2)}) collective-permute-start(f32[2,2,16,4,128]{4,3,2,1,0:T(4,128)S(1)} %pad_maximum_fusion.39), channel_id=1, source_target_pairs={{0,1},{1,0},{2,3},{3,2},{4,5},{5,4},{6,7},{7,6},{8,9},{9,8},{10,11... | collective-permute-start | bytes 393224 | tf_op jit(solution)/shard_map/ppermute | solution.py:124
  67.9 3.5 %collective-permute-start.16 = (f32[2,2,2,32,128]{4,3,2,1,0:T(8,128)S(1)}, f32[2,2,2,32,128]{4,3,2,1,0:T(8,128)S(1)}, u32[]{:S(2)}, u32[]{:S(2)}) collective-permute-start(f32[2,2,2,32,128]{4,3,2,1,0:T(8,128)S(1)} %get-tuple-element.53), channel_id=1, source_target_pairs={{16,0},{18,16},{2,18},{4,2},{20,4},{22,20},{6,22},{8,6},{24,8},{26... | collective-permute-start | bytes 393224 | tf_op jit(solution)/shard_map/ppermute | solution.py:129
  71.5 2.6 %collective-permute-done.15 = f32[2,2,2,32,128]{4,3,2,1,0:T(8,128)S(1)} collective-permute-done((f32[2,2,2,32,128]{4,3,2,1,0:T(8,128)S(1)}, f32[2,2,2,32,128]{4,3,2,1,0:T(8,128)S(1)}, u32[]{:S(2)}, u32[]{:S(2)}) %collective-permute-start.15) | collective-permute-done | bytes 131104 | tf_op jit(solution)/shard_map/ppermute | solution.py:128
  74.1 1.8 %fusion.49 = f32[2,2,16,32,128]{4,3,2,1,0:T(8,128)S(1)} fusion(f32[2,1,16,32,128]{4,3,2,1,0:T(8,128)S(1)} %get-tuple-element.57, f32[2,1,16,32,128]{4,3,2,1,0:T(8,128)S(1)} %get-tuple-element.56, f32[2,2,16,32,128]{4,3,2,1,0:T(8,128)S(1)} %convolution_bitcast_fusion.3, f32[2,2,16,2,128]{4,3,2,1,0:T(2,128)S(1)} %get-tuple-element.111, ...), kind=kLoop, calls=%fused_computation.163 | loop fusion | flops 9175040 | bytes 4063240 | tf_op jit(solution)/shard_map/mul | solution.py:161
  78.6 3.6 %collective-permute-start.19 = (f32[2,2,2,32,128]{4,3,2,1,0:T(8,128)S(1)}, f32[2,2,2,32,128]{4,3,2,1,0:T(8,128)S(1)}, u32[]{:S(2)}, u32[]{:S(2)}) collective-permute-start(f32[2,2,2,32,128]{4,3,2,1,0:T(8,128)S(1)} %get-tuple-element.45), channel_id=1, source_target_pairs={{16,0},{18,16},{2,18},{4,2},{20,4},{22,20},{6,22},{8,6},{24,8},{26... | collective-permute-start | bytes 393224 | tf_op jit(solution)/shard_map/ppermute | solution.py:129
  83.3 1.6 %collective-permute-done.18 = f32[2,2,2,32,128]{4,3,2,1,0:T(8,128)S(1)} collective-permute-done((f32[2,2,2,32,128]{4,3,2,1,0:T(8,128)S(1)}, f32[2,2,2,32,128]{4,3,2,1,0:T(8,128)S(1)}, u32[]{:S(2)}, u32[]{:S(2)}) %collective-permute-start.18) | collective-permute-done | bytes 131104 | tf_op jit(solution)/shard_map/ppermute | solution.py:128
  84.8 1.8 %fusion.53 = f32[2,2,16,32,128]{4,3,2,1,0:T(8,128)S(1)} fusion(f32[2,1,16,32,128]{4,3,2,1,0:T(8,128)S(1)} %get-tuple-element.49, f32[2,1,16,32,128]{4,3,2,1,0:T(8,128)S(1)} %get-tuple-element.48, f32[2,2,16,32,128]{4,3,2,1,0:T(8,128)S(1)} %convolution_bitcast_fusion.2, f32[2,2,16,2,128]{4,3,2,1,0:T(2,128)S(1)} %get-tuple-element.109, ...), kind=kLoop, calls=%fused_computation.168 | loop fusion | flops 9175040 | bytes 4063240 | tf_op jit(solution)/shard_map/mul | solution.py:161
  88.9 1.8 %collective-permute-start.23 = (f32[2,2,16,4,128]{4,3,2,1,0:T(4,128)S(1)}, f32[2,2,16,4,128]{4,3,2,1,0:T(4,128)S(1)}, u32[]{:S(2)}, u32[]{:S(2)}) collective-permute-start(f32[2,2,16,4,128]{4,3,2,1,0:T(4,128)S(1)} %pad_maximum_fusion.41), channel_id=1, source_target_pairs={{0,1},{1,0},{2,3},{3,2},{4,5},{5,4},{6,7},{7,6},{8,9},{9,8},{10,11... | collective-permute-start | bytes 393224 | tf_op jit(solution)/shard_map/ppermute | solution.py:124
  90.8 3.5 %collective-permute-start.22 = (f32[2,2,2,32,128]{4,3,2,1,0:T(8,128)S(1)}, f32[2,2,2,32,128]{4,3,2,1,0:T(8,128)S(1)}, u32[]{:S(2)}, u32[]{:S(2)}) collective-permute-start(f32[2,2,2,32,128]{4,3,2,1,0:T(8,128)S(1)} %get-tuple-element.37), channel_id=1, source_target_pairs={{16,0},{18,16},{2,18},{4,2},{20,4},{22,20},{6,22},{8,6},{24,8},{26... | collective-permute-start | bytes 393224 | tf_op jit(solution)/shard_map/ppermute | solution.py:129
  94.4 2.6 %collective-permute-done.21 = f32[2,2,2,32,128]{4,3,2,1,0:T(8,128)S(1)} collective-permute-done((f32[2,2,2,32,128]{4,3,2,1,0:T(8,128)S(1)}, f32[2,2,2,32,128]{4,3,2,1,0:T(8,128)S(1)}, u32[]{:S(2)}, u32[]{:S(2)}) %collective-permute-start.21) | collective-permute-done | bytes 131104 | tf_op jit(solution)/shard_map/ppermute | solution.py:128
  97.0 1.8 %fusion.57 = f32[2,2,16,32,128]{4,3,2,1,0:T(8,128)S(1)} fusion(f32[2,1,16,32,128]{4,3,2,1,0:T(8,128)S(1)} %get-tuple-element.41, f32[2,1,16,32,128]{4,3,2,1,0:T(8,128)S(1)} %get-tuple-element.40, f32[2,2,16,32,128]{4,3,2,1,0:T(8,128)S(1)} %convolution_bitcast_fusion.1, f32[2,2,16,2,128]{4,3,2,1,0:T(2,128)S(1)} %get-tuple-element.107, ...), kind=kLoop, calls=%fused_computation.173 | loop fusion | flops 9175040 | bytes 4063240 | tf_op jit(solution)/shard_map/mul | solution.py:161
  101.7 3.5 %collective-permute-start.25 = (f32[2,2,2,32,128]{4,3,2,1,0:T(8,128)S(1)}, f32[2,2,2,32,128]{4,3,2,1,0:T(8,128)S(1)}, u32[]{:S(2)}, u32[]{:S(2)}) collective-permute-start(f32[2,2,2,32,128]{4,3,2,1,0:T(8,128)S(1)} %get-tuple-element.29), channel_id=1, source_target_pairs={{16,0},{18,16},{2,18},{4,2},{20,4},{22,20},{6,22},{8,6},{24,8},{26... | collective-permute-start | bytes 393224 | tf_op jit(solution)/shard_map/ppermute | solution.py:129
  108.2 1.8 %fusion.61 = f32[2,2,16,32,128]{4,3,2,1,0:T(8,128)S(1)} fusion(f32[2,1,16,32,128]{4,3,2,1,0:T(8,128)S(1)} %get-tuple-element.33, f32[2,1,16,32,128]{4,3,2,1,0:T(8,128)S(1)} %get-tuple-element.32, f32[2,2,16,32,128]{4,3,2,1,0:T(8,128)S(1)} %convolution_bitcast_fusion, f32[2,2,16,2,128]{4,3,2,1,0:T(2,128)S(1)} %get-tuple-element.105, ...), kind=kLoop, calls=%fused_computation.178 | loop fusion | flops 9175040 | bytes 4063240 | tf_op jit(solution)/shard_map/mul | solution.py:161
  111.2 3.1 %collective-permute-start.27 = (f32[1,2,16,32,128]{4,3,2,1,0:T(8,128)S(1)}, f32[1,2,16,32,128]{4,3,2,1,0:T(8,128)S(1)}, u32[]{:S(2)}, u32[]{:S(2)}) collective-permute-start(f32[1,2,16,32,128]{4,3,2,1,0:T(8,128)S(1)} %convolution_bitcast_fusion.7), channel_id=1, source_target_pairs={{0,16},{1,17},{2,18},{3,19},{4,20},{5,21},{6,22},{7,23},{8,24},{9,... | collective-permute-start | bytes 1572872 | tf_op jit(solution)/shard_map/ppermute | solution.py:229
  114.6 1.7 %collective-permute-done.28 = f32[1,2,16,32,128]{4,3,2,1,0:T(8,128)S(1)} collective-permute-done((f32[1,2,16,32,128]{4,3,2,1,0:T(8,128)S(1)}, f32[1,2,16,32,128]{4,3,2,1,0:T(8,128)S(1)}, u32[]{:S(2)}, u32[]{:S(2)}) %collective-permute-start.28) | collective-permute-done | bytes 524320 | tf_op jit(solution)/shard_map/ppermute | solution.py:229
  116.2 4.7 %collective-permute-done.27 = f32[1,2,16,32,128]{4,3,2,1,0:T(8,128)S(1)} collective-permute-done((f32[1,2,16,32,128]{4,3,2,1,0:T(8,128)S(1)}, f32[1,2,16,32,128]{4,3,2,1,0:T(8,128)S(1)}, u32[]{:S(2)}, u32[]{:S(2)}) %collective-permute-start.27) | collective-permute-done | bytes 524320 | tf_op jit(solution)/shard_map/ppermute | solution.py:229
  (136 shorter events, 37.4 us)
Async XLA Ops:
  1.2 12.8 %collective-permute-start.2 = (f32[1,2,16,4,128]{4,3,2,1,0:T(4,128)S(1)}, f32[1,2,16,4,128]{4,3,2,1,0:T(4,128)S(1)}, u32[]{:S(2)}, u32[]{:S(2)}) collective-permute-start(f32[1,2,16,4,128]{4,3,2,1,0:T(4,128)S(1)} %pad_maximum_fusion.43), channel_id=1, source_target_pairs={{0,1},{1,0},{2,3},{3,2},{4,5},{5,4},{6,7},{7,6},{8,9},{9,8},{10,11... | collective-permute-start | bytes 196616 | tf_op jit(solution)/shard_map/ppermute | solution.py:124
  4.2 9.8 %collective-permute-start = (f32[1,2,2,32,128]{4,3,2,1,0:T(8,128)S(1)}, f32[1,2,2,32,128]{4,3,2,1,0:T(8,128)S(1)}, u32[]{:S(2)}, u32[]{:S(2)}) collective-permute-start(f32[1,2,2,32,128]{4,3,2,1,0:T(8,128)S(1)} %get-tuple-element.98), channel_id=1, source_target_pairs={{0,16},{16,18},{18,2},{2,4},{4,20},{20,22},{22,6},{6,8},{8,24},{24... | collective-permute-start | bytes 196616 | tf_op jit(solution)/shard_map/ppermute | solution.py:128
  5.8 8.2 %collective-permute-start.1 = (f32[1,2,2,32,128]{4,3,2,1,0:T(8,128)S(1)}, f32[1,2,2,32,128]{4,3,2,1,0:T(8,128)S(1)}, u32[]{:S(2)}, u32[]{:S(2)}) collective-permute-start(f32[1,2,2,32,128]{4,3,2,1,0:T(8,128)S(1)} %get-tuple-element.99), channel_id=1, source_target_pairs={{16,0},{18,16},{2,18},{4,2},{20,4},{22,20},{6,22},{8,6},{24,8},{26... | collective-permute-start | bytes 196616 | tf_op jit(solution)/shard_map/ppermute | solution.py:129
  7.9 6.1 %copy-start.1 = (f32[2,32,32,128]{3,2,1,0:T(8,128)S(1)}, f32[2,32,32,128]{3,2,1,0:T(8,128)}, u32[]{:S(2)}) copy-start(f32[2,32,32,128]{3,2,1,0:T(8,128)} %param.12) | copy-start | bytes 3145732
  7.9 6.1 %copy-start.6 = (f32[2]{0:T(128)S(1)}, f32[2]{0:T(128)}, u32[]{:S(2)}) copy-start(f32[2]{0:T(128)} %constant.134) | copy-start | bytes 28
  15.8 9.0 %collective-permute-start.3 = (f32[2,2,2,32,128]{4,3,2,1,0:T(8,128)S(1)}, f32[2,2,2,32,128]{4,3,2,1,0:T(8,128)S(1)}, u32[]{:S(2)}, u32[]{:S(2)}) collective-permute-start(f32[2,2,2,32,128]{4,3,2,1,0:T(8,128)S(1)} %get-tuple-element.85), channel_id=1, source_target_pairs={{0,16},{16,18},{18,2},{2,4},{4,20},{20,22},{22,6},{6,8},{8,24},{24... | collective-permute-start | bytes 393224 | tf_op jit(solution)/shard_map/ppermute | solution.py:128
  15.9 9.0 %collective-permute-start.4 = (f32[2,2,2,32,128]{4,3,2,1,0:T(8,128)S(1)}, f32[2,2,2,32,128]{4,3,2,1,0:T(8,128)S(1)}, u32[]{:S(2)}, u32[]{:S(2)}) collective-permute-start(f32[2,2,2,32,128]{4,3,2,1,0:T(8,128)S(1)} %get-tuple-element.84), channel_id=1, source_target_pairs={{16,0},{18,16},{2,18},{4,2},{20,4},{22,20},{6,22},{8,6},{24,8},{26... | collective-permute-start | bytes 393224 | tf_op jit(solution)/shard_map/ppermute | solution.py:129
  19.5 5.0 %collective-permute-start.5 = (f32[2,2,16,4,128]{4,3,2,1,0:T(4,128)S(1)}, f32[2,2,16,4,128]{4,3,2,1,0:T(4,128)S(1)}, u32[]{:S(2)}, u32[]{:S(2)}) collective-permute-start(f32[2,2,16,4,128]{4,3,2,1,0:T(4,128)S(1)} %pad_maximum_fusion.35), channel_id=1, source_target_pairs={{0,1},{1,0},{2,3},{3,2},{4,5},{5,4},{6,7},{7,6},{8,9},{9,8},{10,11... | collective-permute-start | bytes 393224 | tf_op jit(solution)/shard_map/ppermute | solution.py:124
  29.1 5.0 %collective-permute-start.8 = (f32[2,2,16,4,128]{4,3,2,1,0:T(4,128)S(1)}, f32[2,2,16,4,128]{4,3,2,1,0:T(4,128)S(1)}, u32[]{:S(2)}, u32[]{:S(2)}) collective-permute-start(f32[2,2,16,4,128]{4,3,2,1,0:T(4,128)S(1)} %pad_maximum_fusion.36), channel_id=1, source_target_pairs={{0,1},{1,0},{2,3},{3,2},{4,5},{5,4},{6,7},{7,6},{8,9},{9,8},{10,11... | collective-permute-start | bytes 393224 | tf_op jit(solution)/shard_map/ppermute | solution.py:124
  29.2 7.3 %collective-permute-start.6 = (f32[2,2,2,32,128]{4,3,2,1,0:T(8,128)S(1)}, f32[2,2,2,32,128]{4,3,2,1,0:T(8,128)S(1)}, u32[]{:S(2)}, u32[]{:S(2)}) collective-permute-start(f32[2,2,2,32,128]{4,3,2,1,0:T(8,128)S(1)} %get-tuple-element.76), channel_id=1, source_target_pairs={{0,16},{16,18},{18,2},{2,4},{4,20},{20,22},{22,6},{6,8},{8,24},{24... | collective-permute-start | bytes 393224 | tf_op jit(solution)/shard_map/ppermute | solution.py:128
  29.2 7.2 %collective-permute-start.7 = (f32[2,2,2,32,128]{4,3,2,1,0:T(8,128)S(1)}, f32[2,2,2,32,128]{4,3,2,1,0:T(8,128)S(1)}, u32[]{:S(2)}, u32[]{:S(2)}) collective-permute-start(f32[2,2,2,32,128]{4,3,2,1,0:T(8,128)S(1)} %get-tuple-element.77), channel_id=1, source_target_pairs={{16,0},{18,16},{2,18},{4,2},{20,4},{22,20},{6,22},{8,6},{24,8},{26... | collective-permute-start | bytes 393224 | tf_op jit(solution)/shard_map/ppermute | solution.py:129
  40.5 5.0 %collective-permute-start.11 = (f32[2,2,16,4,128]{4,3,2,1,0:T(4,128)S(1)}, f32[2,2,16,4,128]{4,3,2,1,0:T(4,128)S(1)}, u32[]{:S(2)}, u32[]{:S(2)}) collective-permute-start(f32[2,2,16,4,128]{4,3,2,1,0:T(4,128)S(1)} %pad_maximum_fusion.37), channel_id=1, source_target_pairs={{0,1},{1,0},{2,3},{3,2},{4,5},{5,4},{6,7},{7,6},{8,9},{9,8},{10,11... | collective-permute-start | bytes 393224 | tf_op jit(solution)/shard_map/ppermute | solution.py:124
  42.3 5.1 %collective-permute-start.10 = (f32[2,2,2,32,128]{4,3,2,1,0:T(8,128)S(1)}, f32[2,2,2,32,128]{4,3,2,1,0:T(8,128)S(1)}, u32[]{:S(2)}, u32[]{:S(2)}) collective-permute-start(f32[2,2,2,32,128]{4,3,2,1,0:T(8,128)S(1)} %get-tuple-element.69), channel_id=1, source_target_pairs={{16,0},{18,16},{2,18},{4,2},{20,4},{22,20},{6,22},{8,6},{24,8},{26... | collective-permute-start | bytes 393224 | tf_op jit(solution)/shard_map/ppermute | solution.py:129
  44.9 6.2 %collective-permute-start.9 = (f32[2,2,2,32,128]{4,3,2,1,0:T(8,128)S(1)}, f32[2,2,2,32,128]{4,3,2,1,0:T(8,128)S(1)}, u32[]{:S(2)}, u32[]{:S(2)}) collective-permute-start(f32[2,2,2,32,128]{4,3,2,1,0:T(8,128)S(1)} %get-tuple-element.68), channel_id=1, source_target_pairs={{0,16},{16,18},{18,2},{2,4},{4,20},{20,22},{22,6},{6,8},{8,24},{24... | collective-permute-start | bytes 393224 | tf_op jit(solution)/shard_map/ppermute | solution.py:128
  55.2 5.0 %collective-permute-start.14 = (f32[2,2,16,4,128]{4,3,2,1,0:T(4,128)S(1)}, f32[2,2,16,4,128]{4,3,2,1,0:T(4,128)S(1)}, u32[]{:S(2)}, u32[]{:S(2)}) collective-permute-start(f32[2,2,16,4,128]{4,3,2,1,0:T(4,128)S(1)} %pad_maximum_fusion.38), channel_id=1, source_target_pairs={{0,1},{1,0},{2,3},{3,2},{4,5},{5,4},{6,7},{7,6},{8,9},{9,8},{10,11... | collective-permute-start | bytes 393224 | tf_op jit(solution)/shard_map/ppermute | solution.py:124
  55.6 6.3 %collective-permute-start.12 = (f32[2,2,2,32,128]{4,3,2,1,0:T(8,128)S(1)}, f32[2,2,2,32,128]{4,3,2,1,0:T(8,128)S(1)}, u32[]{:S(2)}, u32[]{:S(2)}) collective-permute-start(f32[2,2,2,32,128]{4,3,2,1,0:T(8,128)S(1)} %get-tuple-element.60), channel_id=1, source_target_pairs={{0,16},{16,18},{18,2},{2,4},{4,20},{20,22},{22,6},{6,8},{8,24},{24... | collective-permute-start | bytes 393224 | tf_op jit(solution)/shard_map/ppermute | solution.py:128
  55.7 6.2 %collective-permute-start.13 = (f32[2,2,2,32,128]{4,3,2,1,0:T(8,128)S(1)}, f32[2,2,2,32,128]{4,3,2,1,0:T(8,128)S(1)}, u32[]{:S(2)}, u32[]{:S(2)}) collective-permute-start(f32[2,2,2,32,128]{4,3,2,1,0:T(8,128)S(1)} %get-tuple-element.61), channel_id=1, source_target_pairs={{16,0},{18,16},{2,18},{4,2},{20,4},{22,20},{6,22},{8,6},{24,8},{26... | collective-permute-start | bytes 393224 | tf_op jit(solution)/shard_map/ppermute | solution.py:129
  66.0 5.4 %collective-permute-start.17 = (f32[2,2,16,4,128]{4,3,2,1,0:T(4,128)S(1)}, f32[2,2,16,4,128]{4,3,2,1,0:T(4,128)S(1)}, u32[]{:S(2)}, u32[]{:S(2)}) collective-permute-start(f32[2,2,16,4,128]{4,3,2,1,0:T(4,128)S(1)} %pad_maximum_fusion.39), channel_id=1, source_target_pairs={{0,1},{1,0},{2,3},{3,2},{4,5},{5,4},{6,7},{7,6},{8,9},{9,8},{10,11... | collective-permute-start | bytes 393224 | tf_op jit(solution)/shard_map/ppermute | solution.py:124
  67.8 6.3 %collective-permute-start.15 = (f32[2,2,2,32,128]{4,3,2,1,0:T(8,128)S(1)}, f32[2,2,2,32,128]{4,3,2,1,0:T(8,128)S(1)}, u32[]{:S(2)}, u32[]{:S(2)}) collective-permute-start(f32[2,2,2,32,128]{4,3,2,1,0:T(8,128)S(1)} %get-tuple-element.52), channel_id=1, source_target_pairs={{0,16},{16,18},{18,2},{2,4},{4,20},{20,22},{22,6},{6,8},{8,24},{24... | collective-permute-start | bytes 393224 | tf_op jit(solution)/shard_map/ppermute | solution.py:128
  67.9 6.2 %collective-permute-start.16 = (f32[2,2,2,32,128]{4,3,2,1,0:T(8,128)S(1)}, f32[2,2,2,32,128]{4,3,2,1,0:T(8,128)S(1)}, u32[]{:S(2)}, u32[]{:S(2)}) collective-permute-start(f32[2,2,2,32,128]{4,3,2,1,0:T(8,128)S(1)} %get-tuple-element.53), channel_id=1, source_target_pairs={{16,0},{18,16},{2,18},{4,2},{20,4},{22,20},{6,22},{8,6},{24,8},{26... | collective-permute-start | bytes 393224 | tf_op jit(solution)/shard_map/ppermute | solution.py:129
  78.2 5.0 %collective-permute-start.20 = (f32[2,2,16,4,128]{4,3,2,1,0:T(4,128)S(1)}, f32[2,2,16,4,128]{4,3,2,1,0:T(4,128)S(1)}, u32[]{:S(2)}, u32[]{:S(2)}) collective-permute-start(f32[2,2,16,4,128]{4,3,2,1,0:T(4,128)S(1)} %pad_maximum_fusion.40), channel_id=1, source_target_pairs={{0,1},{1,0},{2,3},{3,2},{4,5},{5,4},{6,7},{7,6},{8,9},{9,8},{10,11... | collective-permute-start | bytes 393224 | tf_op jit(solution)/shard_map/ppermute | solution.py:124
  78.6 6.3 %collective-permute-start.18 = (f32[2,2,2,32,128]{4,3,2,1,0:T(8,128)S(1)}, f32[2,2,2,32,128]{4,3,2,1,0:T(8,128)S(1)}, u32[]{:S(2)}, u32[]{:S(2)}) collective-permute-start(f32[2,2,2,32,128]{4,3,2,1,0:T(8,128)S(1)} %get-tuple-element.44), channel_id=1, source_target_pairs={{0,16},{16,18},{18,2},{2,4},{4,20},{20,22},{22,6},{6,8},{8,24},{24... | collective-permute-start | bytes 393224 | tf_op jit(solution)/shard_map/ppermute | solution.py:128
  78.6 6.2 %collective-permute-start.19 = (f32[2,2,2,32,128]{4,3,2,1,0:T(8,128)S(1)}, f32[2,2,2,32,128]{4,3,2,1,0:T(8,128)S(1)}, u32[]{:S(2)}, u32[]{:S(2)}) collective-permute-start(f32[2,2,2,32,128]{4,3,2,1,0:T(8,128)S(1)} %get-tuple-element.45), channel_id=1, source_target_pairs={{16,0},{18,16},{2,18},{4,2},{20,4},{22,20},{6,22},{8,6},{24,8},{26... | collective-permute-start | bytes 393224 | tf_op jit(solution)/shard_map/ppermute | solution.py:129
  88.9 5.4 %collective-permute-start.23 = (f32[2,2,16,4,128]{4,3,2,1,0:T(4,128)S(1)}, f32[2,2,16,4,128]{4,3,2,1,0:T(4,128)S(1)}, u32[]{:S(2)}, u32[]{:S(2)}) collective-permute-start(f32[2,2,16,4,128]{4,3,2,1,0:T(4,128)S(1)} %pad_maximum_fusion.41), channel_id=1, source_target_pairs={{0,1},{1,0},{2,3},{3,2},{4,5},{5,4},{6,7},{7,6},{8,9},{9,8},{10,11... | collective-permute-start | bytes 393224 | tf_op jit(solution)/shard_map/ppermute | solution.py:124
  90.7 6.3 %collective-permute-start.21 = (f32[2,2,2,32,128]{4,3,2,1,0:T(8,128)S(1)}, f32[2,2,2,32,128]{4,3,2,1,0:T(8,128)S(1)}, u32[]{:S(2)}, u32[]{:S(2)}) collective-permute-start(f32[2,2,2,32,128]{4,3,2,1,0:T(8,128)S(1)} %get-tuple-element.36), channel_id=1, source_target_pairs={{0,16},{16,18},{18,2},{2,4},{4,20},{20,22},{22,6},{6,8},{8,24},{24... | collective-permute-start | bytes 393224 | tf_op jit(solution)/shard_map/ppermute | solution.py:128
  90.8 6.2 %collective-permute-start.22 = (f32[2,2,2,32,128]{4,3,2,1,0:T(8,128)S(1)}, f32[2,2,2,32,128]{4,3,2,1,0:T(8,128)S(1)}, u32[]{:S(2)}, u32[]{:S(2)}) collective-permute-start(f32[2,2,2,32,128]{4,3,2,1,0:T(8,128)S(1)} %get-tuple-element.37), channel_id=1, source_target_pairs={{16,0},{18,16},{2,18},{4,2},{20,4},{22,20},{6,22},{8,6},{24,8},{26... | collective-permute-start | bytes 393224 | tf_op jit(solution)/shard_map/ppermute | solution.py:129
  101.2 5.3 %collective-permute-start.26 = (f32[2,2,16,4,128]{4,3,2,1,0:T(4,128)S(1)}, f32[2,2,16,4,128]{4,3,2,1,0:T(4,128)S(1)}, u32[]{:S(2)}, u32[]{:S(2)}) collective-permute-start(f32[2,2,16,4,128]{4,3,2,1,0:T(4,128)S(1)} %pad_maximum_fusion.42), channel_id=1, source_target_pairs={{0,1},{1,0},{2,3},{3,2},{4,5},{5,4},{6,7},{7,6},{8,9},{9,8},{10,11... | collective-permute-start | bytes 393224 | tf_op jit(solution)/shard_map/ppermute | solution.py:124
  101.6 6.3 %collective-permute-start.24 = (f32[2,2,2,32,128]{4,3,2,1,0:T(8,128)S(1)}, f32[2,2,2,32,128]{4,3,2,1,0:T(8,128)S(1)}, u32[]{:S(2)}, u32[]{:S(2)}) collective-permute-start(f32[2,2,2,32,128]{4,3,2,1,0:T(8,128)S(1)} %get-tuple-element.28), channel_id=1, source_target_pairs={{0,16},{16,18},{18,2},{2,4},{4,20},{20,22},{22,6},{6,8},{8,24},{24... | collective-permute-start | bytes 393224 | tf_op jit(solution)/shard_map/ppermute | solution.py:128
  101.7 6.5 %collective-permute-start.25 = (f32[2,2,2,32,128]{4,3,2,1,0:T(8,128)S(1)}, f32[2,2,2,32,128]{4,3,2,1,0:T(8,128)S(1)}, u32[]{:S(2)}, u32[]{:S(2)}) collective-permute-start(f32[2,2,2,32,128]{4,3,2,1,0:T(8,128)S(1)} %get-tuple-element.29), channel_id=1, source_target_pairs={{16,0},{18,16},{2,18},{4,2},{20,4},{22,20},{6,22},{8,6},{24,8},{26... | collective-permute-start | bytes 393224 | tf_op jit(solution)/shard_map/ppermute | solution.py:129
  105.2 11.1 %collective-permute-start.28 = (f32[1,2,16,32,128]{4,3,2,1,0:T(8,128)S(1)}, f32[1,2,16,32,128]{4,3,2,1,0:T(8,128)S(1)}, u32[]{:S(2)}, u32[]{:S(2)}) collective-permute-start(f32[1,2,16,32,128]{4,3,2,1,0:T(8,128)S(1)} %slice.1158), channel_id=1, source_target_pairs={{16,0},{17,1},{18,2},{19,3},{20,4},{21,5},{22,6},{23,7},{24,8},{25... | collective-permute-start | bytes 1572872 | tf_op jit(solution)/shard_map/ppermute | solution.py:229
  111.2 9.7 %collective-permute-start.27 = (f32[1,2,16,32,128]{4,3,2,1,0:T(8,128)S(1)}, f32[1,2,16,32,128]{4,3,2,1,0:T(8,128)S(1)}, u32[]{:S(2)}, u32[]{:S(2)}) collective-permute-start(f32[1,2,16,32,128]{4,3,2,1,0:T(8,128)S(1)} %convolution_bitcast_fusion.7), channel_id=1, source_target_pairs={{0,16},{1,17},{2,18},{3,19},{4,20},{5,21},{6,22},{7,23},{8,24},{9,... | collective-permute-start | bytes 1572872 | tf_op jit(solution)/shard_map/ppermute | solution.py:229
  114.6 6.4 %copy-start.2 = (f32[1,2,32,32,128]{4,3,2,1,0:T(8,128)}, f32[1,2,32,32,128]{4,3,2,1,0:T(8,128)S(1)}, u32[]{:S(2)}) copy-start(f32[1,2,32,32,128]{4,3,2,1,0:T(8,128)S(1)} %fusion.67) | copy-start | bytes 3145732
  (6 other events, 4.8 us)

commit v7 on v6

--- a/solution.py
+++ b/solution.py
@@ -35,23 +35,23 @@
     return table
 
 
-def thomas_kernel(up_ref, low_ref, out_ref, c_ref, d_ref):
+def thomas_kernel(diff_ref, out_ref, c_ref, d_ref):
     n = out_ref.shape[0]
     shape = out_ref.shape[1:]
     lanes = lax.broadcasted_iota(jnp.int32, shape, 1)
     species = lax.broadcasted_iota(jnp.int32, shape, 0)
     zero = jnp.zeros(shape, jnp.float32)
 
-    def column(ref, j):
-        value = jnp.full(shape, ref[0, j], jnp.float32)
+    def column(j):
+        value = jnp.full(shape, diff_ref[0, j], jnp.float32)
         for s in range(1, shape[0]):
-            value = jnp.where(species == s, ref[s, j], value)
+            value = jnp.where(species == s, diff_ref[s, j], value)
         return value
 
     def forward(j, carry):
         cprev, dprev = carry
-        up = column(up_ref, j)
-        low = column(low_ref, j)
+        up = jnp.where(j < n - 1, column(j), 0.0)
+        low = jnp.where(j > 0, column(jnp.maximum(j - 1, 0)), 0.0)
         inv = 1.0 / ((1.0 + low + up) + low * cprev)
         c = -up * inv
         d = (jnp.where(lanes == j, 1.0, 0.0) + low * dprev) * inv
@@ -78,14 +78,14 @@
     rows = pl.pallas_call(
         thomas_kernel,
         out_shape=jax.ShapeDtypeStruct((depth, species, depth), jnp.float32),
-        in_specs=[pl.BlockSpec(memory_space=pltpu.SMEM)] * 2,
+        in_specs=[pl.BlockSpec(memory_space=pltpu.SMEM)],
         scratch_shapes=[pltpu.VMEM((depth, species, depth), jnp.float32)] * 2,
         cost_estimate=pl.CostEstimate(
             flops=12 * depth * species * depth,
             transcendentals=0,
             bytes_accessed=4 * 2 * depth * species * depth,
         ),
-    )(upper, lower)
+    )(diffusion)
     inverse = jnp.transpose(rows, (1, 0, 2))
     return (inverse, upper, lower)
 
@@ -136,7 +136,6 @@
     px = jnp.concatenate([west, state, east], 2)
     py = jnp.concatenate([south, state, north], 3)
     center = state
-    twelfth = 1.0 / 12.0
     far_x = px[:, :, :-4] - px[:, :, 4:]
     near_x = px[:, :, 3:-1] - px[:, :, 1:-3]
     far_sum_x = px[:, :, :-4] + px[:, :, 4:]
@@ -145,20 +144,18 @@
     near_y = py[:, :, :, 3:-1] - py[:, :, :, 1:-3]
     far_sum_y = py[:, :, :, :-4] + py[:, :, :, 4:]
     near_sum_y = py[:, :, :, 3:-1] + py[:, :, :, 1:-3]
-    dx1 = (far_x + 8.0 * near_x) * twelfth
-    dy1 = (far_y + 8.0 * near_y) * twelfth
-    laplace = (
-        16.0 * (near_sum_x + near_sum_y) - (far_sum_x + far_sum_y) - 60.0 * center
-    ) * twelfth
-    kappa = jnp.array([0.5, 1.0], jnp.float32)[None, :, None, None, None]
+    laplace = 16.0 * (near_sum_x + near_sum_y) - (far_sum_x + far_sum_y) - 60.0 * center
+    scale = jnp.array([0.5, 1.0], jnp.float32)[None, :, None, None, None] * (DT / 12.0)
     first = center[:, 0]
     second = center[:, 1]
     square_term = first * first * second
     react = jnp.stack(
         [A_RATE - (B_RATE + 1.0) * first + square_term, B_RATE * first - square_term], 1
     )
-    flow = -(wind[0][None, None] * dx1 + wind[1][None, None] * dy1)
-    return DT * (flow + kappa * laplace + react)
+    flow = wind[0][None, None] * (far_x + 8.0 * near_x) + wind[1][None, None] * (
+        far_y + 8.0 * near_y
+    )
+    return flow + scale * laplace + DT * react
 
 
 def column_solve(rhs, inverse):
@@ -176,7 +173,7 @@
     tile = lax.axis_index("tx")
     start = slab_of(me, tile, depth) * slab
     own_fields = lax.dynamic_slice_in_dim(fields, start, slab, 1)
-    own_wind = lax.dynamic_slice_in_dim(wind, start, slab, 1)
+    own_wind = lax.dynamic_slice_in_dim(wind, start, slab, 1) * (-DT / 12.0)
 
     states = [own_fields] * depth
     e_hist = [dict() for _ in range(depth)]

time: 122 us -> 124 us (1.016)
  local copies, waits for them, and re-layouts: 5.31 us -> 7.27 us
    mul x10 -> x1, other arithmetic: 15.5 us -> 0.05 us  [on_device(): own_wind = lax.dynamic_slice_in_dim(wind, start, slab, 1) * (-DT / 12.0)]
    add x0 -> x9, other arithmetic: none -> 15.3 us  [tendency(): return flow + scale * laplace + DT * react]
where the time goes in v7:
time: 124 us
  starting transfers between devices  45.3 us (37%)
  waiting for transfers between devices  32.8 us (26%)
  other arithmetic  25.6 us (21%)
  matrix products  9.1 us (7%)
  local copies, waits for them, and re-layouts  7.27 us (6%)
  Pallas kernels  2.97 us (2%)
    ppermute x9, starting transfers between devices, ring_halo(): after = lax.ppermute(first, axes, down)  29.4 us
    ppermute x9, waiting for transfers between devices, ring_halo(): before = lax.ppermute(last, axes, up)  15.5 us
    add x9, other arithmetic, tendency(): return flow + scale * laplace + DT * react  15.3 us
    ppermute x9, starting transfers between devices, ring_halo(): got = lax.ppermute(jnp.concatenate([first, last], dim), axes, up)  9.59 us
    dot_general x9, matrix products, column_solve(): jnp.einsum('lsxyk,sjk->lsxyj', rhs, inverse, precision=lax.Precision.HIGH...  9.1 us
    ppermute x9, waiting for transfers between devices, ring_halo(): got = lax.ppermute(jnp.concatenate([first, last], dim), axes, up)  8.8 us
    ppermute x2, waiting for transfers between devices, on_device(): arrived = lax.ppermute(states[level][None], 'corr', pairs)  6.35 us
    ppermute x2, starting transfers between devices, on_device(): arrived = lax.ppermute(states[level][None], 'corr', pairs)  4.33 us
  transfers between devices with their start and end apart: 29, of which 16 were waited for; matrix products, arithmetic and copies ran while one was open for 6% of the time, Pallas kernels for 2%

profile of v7, /device:TPU:0, one launch (start us, length us, event | category | flops | bytes accessed | tf_op | source)
XLA Modules:
  0.0 123.7 jit_solution(14718591971472270895)
XLA Ops:
  1.8 3.0 %collective-permute-start.2 = (f32[1,2,16,4,128]{4,3,2,1,0:T(4,128)}, f32[1,2,16,4,128]{4,3,2,1,0:T(4,128)}, u32[]{:S(2)}, u32[]{:S(2)}) collective-permute-start(f32[1,2,16,4,128]{4,3,2,1,0:T(4,128)} %pad_maximum_fusion.43), channel_id=1, source_target_pairs={{0,1},{1,0},{2,3},{3,2},{4,5},{5,4},{6,7},{7,6},{8,9},{9,8},{10,11... | collective-permute-start | bytes 196616 | tf_op jit(solution)/shard_map/ppermute | solution.py:124
  6.9 2.1 %collective-permute-start.1 = (f32[1,2,2,32,128]{4,3,2,1,0:T(8,128)}, f32[1,2,2,32,128]{4,3,2,1,0:T(8,128)S(1)}, u32[]{:S(2)}, u32[]{:S(2)}) collective-permute-start(f32[1,2,2,32,128]{4,3,2,1,0:T(8,128)} %get-tuple-element.99), channel_id=1, source_target_pairs={{16,0},{18,16},{2,18},{4,2},{20,4},{22,20},{6,22},{8,6},{24,8},{26... | collective-permute-start | bytes 196616 | tf_op jit(solution)/shard_map/ppermute | solution.py:129
  11.1 3.0 %shard_map.118 = f32[128,2,128]{2,1,0:T(2,128)} custom-call(f32[2,128]{1,0:T(2,128)} %diff_ref.1), custom_call_target="tpu_custom_call" | custom-call | flops 393216 | bytes 262144 | tf_op jit(solution)/shard_map/pallas_call | solution.py:78
  15.8 1.6 %fusion.87 = f32[1,2,16,32,128]{4,3,2,1,0:T(8,128)S(1)} fusion(f32[1,1,16,32,128]{4,3,2,1,0:T(8,128)} %get-tuple-element.103, f32[1,1,16,32,128]{4,3,2,1,0:T(8,128)S(1)} %get-tuple-element.102, f32[1,2,16,2,128]{4,3,2,1,0:T(2,128)S(1)} %get-tuple-element.121, f32[1,2,16,32,128]{4,3,2,1,0:T(8,128)S(1)} %dynamic-slice_bitcast_fusion, ...), kind=kLoop, calls=%fused_computation.235 | loop fusion | flops 4456448 | bytes 2818060 | tf_op jit(solution)/shard_map/add | solution.py:158
  18.4 3.5 %collective-permute-start.4 = (f32[2,2,2,32,128]{4,3,2,1,0:T(8,128)S(1)}, f32[2,2,2,32,128]{4,3,2,1,0:T(8,128)S(1)}, u32[]{:S(2)}, u32[]{:S(2)}) collective-permute-start(f32[2,2,2,32,128]{4,3,2,1,0:T(8,128)S(1)} %get-tuple-element.84), channel_id=1, source_target_pairs={{16,0},{18,16},{2,18},{4,2},{20,4},{22,20},{6,22},{8,6},{24,8},{26... | collective-permute-start | bytes 393224 | tf_op jit(solution)/shard_map/ppermute | solution.py:129
  22.2 4.8 %collective-permute-done.5 = f32[2,2,16,4,128]{4,3,2,1,0:T(4,128)S(1)} collective-permute-done((f32[2,2,16,4,128]{4,3,2,1,0:T(4,128)S(1)}, f32[2,2,16,4,128]{4,3,2,1,0:T(4,128)S(1)}, u32[]{:S(2)}, u32[]{:S(2)}) %collective-permute-start.5) | collective-permute-done | bytes 131104 | tf_op jit(solution)/shard_map/ppermute | solution.py:124
  31.2 3.5 %collective-permute-start.7 = (f32[2,2,2,32,128]{4,3,2,1,0:T(8,128)S(1)}, f32[2,2,2,32,128]{4,3,2,1,0:T(8,128)S(1)}, u32[]{:S(2)}, u32[]{:S(2)}) collective-permute-start(f32[2,2,2,32,128]{4,3,2,1,0:T(8,128)S(1)} %get-tuple-element.77), channel_id=1, source_target_pairs={{16,0},{18,16},{2,18},{4,2},{20,4},{22,20},{6,22},{8,6},{24,8},{26... | collective-permute-start | bytes 393224 | tf_op jit(solution)/shard_map/ppermute | solution.py:129
  36.1 2.3 %collective-permute-done.6 = f32[2,2,2,32,128]{4,3,2,1,0:T(8,128)S(1)} collective-permute-done((f32[2,2,2,32,128]{4,3,2,1,0:T(8,128)S(1)}, f32[2,2,2,32,128]{4,3,2,1,0:T(8,128)S(1)}, u32[]{:S(2)}, u32[]{:S(2)}) %collective-permute-start.6) | collective-permute-done | bytes 131104 | tf_op jit(solution)/shard_map/ppermute | solution.py:128
  38.4 1.8 %fusion.36 = f32[2,2,16,32,128]{4,3,2,1,0:T(8,128)S(1)} fusion(f32[2,1,16,32,128]{4,3,2,1,0:T(8,128)S(1)} %get-tuple-element.81, f32[2,1,16,32,128]{4,3,2,1,0:T(8,128)S(1)} %get-tuple-element.80, f32[2,2,16,32,128]{4,3,2,1,0:T(8,128)S(1)} %convolution_bitcast_fusion.6, f32[2,2,16,2,128]{4,3,2,1,0:T(2,128)S(1)} %get-tuple-element.117, ...), kind=kLoop, calls=%fused_computation.148 | loop fusion | flops 8912896 | bytes 4063240 | tf_op jit(solution)/shard_map/add | solution.py:158
  42.4 1.8 %collective-permute-start.11 = (f32[2,2,16,4,128]{4,3,2,1,0:T(4,128)S(1)}, f32[2,2,16,4,128]{4,3,2,1,0:T(4,128)S(1)}, u32[]{:S(2)}, u32[]{:S(2)}) collective-permute-start(f32[2,2,16,4,128]{4,3,2,1,0:T(4,128)S(1)} %pad_maximum_fusion.37), channel_id=1, source_target_pairs={{0,1},{1,0},{2,3},{3,2},{4,5},{5,4},{6,7},{7,6},{8,9},{9,8},{10,11... | collective-permute-start | bytes 393224 | tf_op jit(solution)/shard_map/ppermute | solution.py:124
  44.3 2.6 %collective-permute-start.10 = (f32[2,2,2,32,128]{4,3,2,1,0:T(8,128)S(1)}, f32[2,2,2,32,128]{4,3,2,1,0:T(8,128)S(1)}, u32[]{:S(2)}, u32[]{:S(2)}) collective-permute-start(f32[2,2,2,32,128]{4,3,2,1,0:T(8,128)S(1)} %get-tuple-element.69), channel_id=1, source_target_pairs={{16,0},{18,16},{2,18},{4,2},{20,4},{22,20},{6,22},{8,6},{24,8},{26... | collective-permute-start | bytes 393224 | tf_op jit(solution)/shard_map/ppermute | solution.py:129
  47.5 1.8 %collective-permute-done.10 = f32[2,2,2,32,128]{4,3,2,1,0:T(8,128)S(1)} collective-permute-done((f32[2,2,2,32,128]{4,3,2,1,0:T(8,128)S(1)}, f32[2,2,2,32,128]{4,3,2,1,0:T(8,128)S(1)}, u32[]{:S(2)}, u32[]{:S(2)}) %collective-permute-start.10) | collective-permute-done | bytes 131104 | tf_op jit(solution)/shard_map/ppermute | solution.py:129
  49.4 3.7 %collective-permute-done.9 = f32[2,2,2,32,128]{4,3,2,1,0:T(8,128)S(1)} collective-permute-done((f32[2,2,2,32,128]{4,3,2,1,0:T(8,128)S(1)}, f32[2,2,2,32,128]{4,3,2,1,0:T(8,128)S(1)}, u32[]{:S(2)}, u32[]{:S(2)}) %collective-permute-start.9) | collective-permute-done | bytes 131104 | tf_op jit(solution)/shard_map/ppermute | solution.py:128
  53.0 1.8 %fusion.40 = f32[2,2,16,32,128]{4,3,2,1,0:T(8,128)S(1)} fusion(f32[2,1,16,32,128]{4,3,2,1,0:T(8,128)S(1)} %get-tuple-element.73, f32[2,1,16,32,128]{4,3,2,1,0:T(8,128)S(1)} %get-tuple-element.72, f32[2,2,16,32,128]{4,3,2,1,0:T(8,128)S(1)} %convolution_bitcast_fusion.5, f32[2,2,16,2,128]{4,3,2,1,0:T(2,128)S(1)} %get-tuple-element.115, ...), kind=kLoop, calls=%fused_computation.153 | loop fusion | flops 8912896 | bytes 4063240 | tf_op jit(solution)/shard_map/add | solution.py:158
  57.6 3.5 %collective-permute-start.13 = (f32[2,2,2,32,128]{4,3,2,1,0:T(8,128)S(1)}, f32[2,2,2,32,128]{4,3,2,1,0:T(8,128)S(1)}, u32[]{:S(2)}, u32[]{:S(2)}) collective-permute-start(f32[2,2,2,32,128]{4,3,2,1,0:T(8,128)S(1)} %get-tuple-element.61), channel_id=1, source_target_pairs={{16,0},{18,16},{2,18},{4,2},{20,4},{22,20},{6,22},{8,6},{24,8},{26... | collective-permute-start | bytes 393224 | tf_op jit(solution)/shard_map/ppermute | solution.py:129
  62.2 1.6 %collective-permute-done.12 = f32[2,2,2,32,128]{4,3,2,1,0:T(8,128)S(1)} collective-permute-done((f32[2,2,2,32,128]{4,3,2,1,0:T(8,128)S(1)}, f32[2,2,2,32,128]{4,3,2,1,0:T(8,128)S(1)}, u32[]{:S(2)}, u32[]{:S(2)}) %collective-permute-start.12) | collective-permute-done | bytes 131104 | tf_op jit(solution)/shard_map/ppermute | solution.py:128
  63.8 1.8 %fusion.44 = f32[2,2,16,32,128]{4,3,2,1,0:T(8,128)S(1)} fusion(f32[2,1,16,32,128]{4,3,2,1,0:T(8,128)S(1)} %get-tuple-element.65, f32[2,1,16,32,128]{4,3,2,1,0:T(8,128)S(1)} %get-tuple-element.64, f32[2,2,16,32,128]{4,3,2,1,0:T(8,128)S(1)} %convolution_bitcast_fusion.4, f32[2,2,16,2,128]{4,3,2,1,0:T(2,128)S(1)} %get-tuple-element.113, ...), kind=kLoop, calls=%fused_computation.158 | loop fusion | flops 8912896 | bytes 4063240 | tf_op jit(solution)/shard_map/add | solution.py:158
  68.0 1.8 %collective-permute-start.17 = (f32[2,2,16,4,128]{4,3,2,1,0:T(4,128)S(1)}, f32[2,2,16,4,128]{4,3,2,1,0:T(4,128)S(1)}, u32[]{:S(2)}, u32[]{:S(2)}) collective-permute-start(f32[2,2,16,4,128]{4,3,2,1,0:T(4,128)S(1)} %pad_maximum_fusion.39), channel_id=1, source_target_pairs={{0,1},{1,0},{2,3},{3,2},{4,5},{5,4},{6,7},{7,6},{8,9},{9,8},{10,11... | collective-permute-start | bytes 393224 | tf_op jit(solution)/shard_map/ppermute | solution.py:124
  69.8 3.5 %collective-permute-start.16 = (f32[2,2,2,32,128]{4,3,2,1,0:T(8,128)S(1)}, f32[2,2,2,32,128]{4,3,2,1,0:T(8,128)S(1)}, u32[]{:S(2)}, u32[]{:S(2)}) collective-permute-start(f32[2,2,2,32,128]{4,3,2,1,0:T(8,128)S(1)} %get-tuple-element.53), channel_id=1, source_target_pairs={{16,0},{18,16},{2,18},{4,2},{20,4},{22,20},{6,22},{8,6},{24,8},{26... | collective-permute-start | bytes 393224 | tf_op jit(solution)/shard_map/ppermute | solution.py:129
  73.4 2.6 %collective-permute-done.15 = f32[2,2,2,32,128]{4,3,2,1,0:T(8,128)S(1)} collective-permute-done((f32[2,2,2,32,128]{4,3,2,1,0:T(8,128)S(1)}, f32[2,2,2,32,128]{4,3,2,1,0:T(8,128)S(1)}, u32[]{:S(2)}, u32[]{:S(2)}) %collective-permute-start.15) | collective-permute-done | bytes 131104 | tf_op jit(solution)/shard_map/ppermute | solution.py:128
  76.0 1.8 %fusion.48 = f32[2,2,16,32,128]{4,3,2,1,0:T(8,128)S(1)} fusion(f32[2,1,16,32,128]{4,3,2,1,0:T(8,128)S(1)} %get-tuple-element.57, f32[2,1,16,32,128]{4,3,2,1,0:T(8,128)S(1)} %get-tuple-element.56, f32[2,2,16,32,128]{4,3,2,1,0:T(8,128)S(1)} %convolution_bitcast_fusion.3, f32[2,2,16,2,128]{4,3,2,1,0:T(2,128)S(1)} %get-tuple-element.111, ...), kind=kLoop, calls=%fused_computation.163 | loop fusion | flops 8912896 | bytes 4063240 | tf_op jit(solution)/shard_map/add | solution.py:158
  80.6 3.5 %collective-permute-start.19 = (f32[2,2,2,32,128]{4,3,2,1,0:T(8,128)S(1)}, f32[2,2,2,32,128]{4,3,2,1,0:T(8,128)S(1)}, u32[]{:S(2)}, u32[]{:S(2)}) collective-permute-start(f32[2,2,2,32,128]{4,3,2,1,0:T(8,128)S(1)} %get-tuple-element.45), channel_id=1, source_target_pairs={{16,0},{18,16},{2,18},{4,2},{20,4},{22,20},{6,22},{8,6},{24,8},{26... | collective-permute-start | bytes 393224 | tf_op jit(solution)/shard_map/ppermute | solution.py:129
  86.8 1.8 %fusion.52 = f32[2,2,16,32,128]{4,3,2,1,0:T(8,128)S(1)} fusion(f32[2,1,16,32,128]{4,3,2,1,0:T(8,128)S(1)} %get-tuple-element.49, f32[2,1,16,32,128]{4,3,2,1,0:T(8,128)S(1)} %get-tuple-element.48, f32[2,2,16,32,128]{4,3,2,1,0:T(8,128)S(1)} %convolution_bitcast_fusion.2, f32[2,2,16,2,128]{4,3,2,1,0:T(2,128)S(1)} %get-tuple-element.109, ...), kind=kLoop, calls=%fused_computation.168 | loop fusion | flops 8912896 | bytes 4063240 | tf_op jit(solution)/shard_map/add | solution.py:158
  90.9 1.8 %collective-permute-start.23 = (f32[2,2,16,4,128]{4,3,2,1,0:T(4,128)S(1)}, f32[2,2,16,4,128]{4,3,2,1,0:T(4,128)S(1)}, u32[]{:S(2)}, u32[]{:S(2)}) collective-permute-start(f32[2,2,16,4,128]{4,3,2,1,0:T(4,128)S(1)} %pad_maximum_fusion.41), channel_id=1, source_target_pairs={{0,1},{1,0},{2,3},{3,2},{4,5},{5,4},{6,7},{7,6},{8,9},{9,8},{10,11... | collective-permute-start | bytes 393224 | tf_op jit(solution)/shard_map/ppermute | solution.py:124
  92.8 3.5 %collective-permute-start.22 = (f32[2,2,2,32,128]{4,3,2,1,0:T(8,128)S(1)}, f32[2,2,2,32,128]{4,3,2,1,0:T(8,128)S(1)}, u32[]{:S(2)}, u32[]{:S(2)}) collective-permute-start(f32[2,2,2,32,128]{4,3,2,1,0:T(8,128)S(1)} %get-tuple-element.37), channel_id=1, source_target_pairs={{16,0},{18,16},{2,18},{4,2},{20,4},{22,20},{6,22},{8,6},{24,8},{26... | collective-permute-start | bytes 393224 | tf_op jit(solution)/shard_map/ppermute | solution.py:129
  96.3 2.6 %collective-permute-done.21 = f32[2,2,2,32,128]{4,3,2,1,0:T(8,128)S(1)} collective-permute-done((f32[2,2,2,32,128]{4,3,2,1,0:T(8,128)S(1)}, f32[2,2,2,32,128]{4,3,2,1,0:T(8,128)S(1)}, u32[]{:S(2)}, u32[]{:S(2)}) %collective-permute-start.21) | collective-permute-done | bytes 131104 | tf_op jit(solution)/shard_map/ppermute | solution.py:128
  98.9 1.8 %fusion.56 = f32[2,2,16,32,128]{4,3,2,1,0:T(8,128)S(1)} fusion(f32[2,1,16,32,128]{4,3,2,1,0:T(8,128)S(1)} %get-tuple-element.41, f32[2,1,16,32,128]{4,3,2,1,0:T(8,128)S(1)} %get-tuple-element.40, f32[2,2,16,32,128]{4,3,2,1,0:T(8,128)S(1)} %convolution_bitcast_fusion.1, f32[2,2,16,2,128]{4,3,2,1,0:T(2,128)S(1)} %get-tuple-element.107, ...), kind=kLoop, calls=%fused_computation.173 | loop fusion | flops 8912896 | bytes 4063240 | tf_op jit(solution)/shard_map/add | solution.py:158
  103.6 3.5 %collective-permute-start.25 = (f32[2,2,2,32,128]{4,3,2,1,0:T(8,128)S(1)}, f32[2,2,2,32,128]{4,3,2,1,0:T(8,128)S(1)}, u32[]{:S(2)}, u32[]{:S(2)}) collective-permute-start(f32[2,2,2,32,128]{4,3,2,1,0:T(8,128)S(1)} %get-tuple-element.29), channel_id=1, source_target_pairs={{16,0},{18,16},{2,18},{4,2},{20,4},{22,20},{6,22},{8,6},{24,8},{26... | collective-permute-start | bytes 393224 | tf_op jit(solution)/shard_map/ppermute | solution.py:129
  110.1 1.8 %fusion.60 = f32[2,2,16,32,128]{4,3,2,1,0:T(8,128)S(1)} fusion(f32[2,1,16,32,128]{4,3,2,1,0:T(8,128)S(1)} %get-tuple-element.33, f32[2,1,16,32,128]{4,3,2,1,0:T(8,128)S(1)} %get-tuple-element.32, f32[2,2,16,32,128]{4,3,2,1,0:T(8,128)S(1)} %convolution_bitcast_fusion, f32[2,2,16,2,128]{4,3,2,1,0:T(2,128)S(1)} %get-tuple-element.105, ...), kind=kLoop, calls=%fused_computation.178 | loop fusion | flops 8912896 | bytes 4063240 | tf_op jit(solution)/shard_map/add | solution.py:158
  113.2 3.0 %collective-permute-start.27 = (f32[1,2,16,32,128]{4,3,2,1,0:T(8,128)S(1)}, f32[1,2,16,32,128]{4,3,2,1,0:T(8,128)S(1)}, u32[]{:S(2)}, u32[]{:S(2)}) collective-permute-start(f32[1,2,16,32,128]{4,3,2,1,0:T(8,128)S(1)} %convolution_bitcast_fusion.7), channel_id=1, source_target_pairs={{0,16},{1,17},{2,18},{3,19},{4,20},{5,21},{6,22},{7,23},{8,24},{9,... | collective-permute-start | bytes 1572872 | tf_op jit(solution)/shard_map/ppermute | solution.py:226
  116.5 1.7 %collective-permute-done.28 = f32[1,2,16,32,128]{4,3,2,1,0:T(8,128)S(1)} collective-permute-done((f32[1,2,16,32,128]{4,3,2,1,0:T(8,128)S(1)}, f32[1,2,16,32,128]{4,3,2,1,0:T(8,128)S(1)}, u32[]{:S(2)}, u32[]{:S(2)}) %collective-permute-start.28) | collective-permute-done | bytes 524320 | tf_op jit(solution)/shard_map/ppermute | solution.py:226
  118.2 4.7 %collective-permute-done.27 = f32[1,2,16,32,128]{4,3,2,1,0:T(8,128)S(1)} collective-permute-done((f32[1,2,16,32,128]{4,3,2,1,0:T(8,128)S(1)}, f32[1,2,16,32,128]{4,3,2,1,0:T(8,128)S(1)}, u32[]{:S(2)}, u32[]{:S(2)}) %collective-permute-start.27) | collective-permute-done | bytes 524320 | tf_op jit(solution)/shard_map/ppermute | solution.py:226
  (135 shorter events, 39.4 us)
Async XLA Ops:
  1.8 12.4 %collective-permute-start.2 = (f32[1,2,16,4,128]{4,3,2,1,0:T(4,128)}, f32[1,2,16,4,128]{4,3,2,1,0:T(4,128)}, u32[]{:S(2)}, u32[]{:S(2)}) collective-permute-start(f32[1,2,16,4,128]{4,3,2,1,0:T(4,128)} %pad_maximum_fusion.43), channel_id=1, source_target_pairs={{0,1},{1,0},{2,3},{3,2},{4,5},{5,4},{6,7},{7,6},{8,9},{9,8},{10,11... | collective-permute-start | bytes 196616 | tf_op jit(solution)/shard_map/ppermute | solution.py:124
  5.4 9.7 %collective-permute-start = (f32[1,2,2,32,128]{4,3,2,1,0:T(8,128)}, f32[1,2,2,32,128]{4,3,2,1,0:T(8,128)S(1)}, u32[]{:S(2)}, u32[]{:S(2)}) collective-permute-start(f32[1,2,2,32,128]{4,3,2,1,0:T(8,128)} %get-tuple-element.98), channel_id=1, source_target_pairs={{0,16},{16,18},{18,2},{2,4},{4,20},{20,22},{22,6},{6,8},{8,24},{24... | collective-permute-start | bytes 196616 | tf_op jit(solution)/shard_map/ppermute | solution.py:128
  6.9 8.2 %collective-permute-start.1 = (f32[1,2,2,32,128]{4,3,2,1,0:T(8,128)}, f32[1,2,2,32,128]{4,3,2,1,0:T(8,128)S(1)}, u32[]{:S(2)}, u32[]{:S(2)}) collective-permute-start(f32[1,2,2,32,128]{4,3,2,1,0:T(8,128)} %get-tuple-element.99), channel_id=1, source_target_pairs={{16,0},{18,16},{2,18},{4,2},{20,4},{22,20},{6,22},{8,6},{24,8},{26... | collective-permute-start | bytes 196616 | tf_op jit(solution)/shard_map/ppermute | solution.py:129
  9.9 5.8 %copy-start.1 = (f32[2,32,32,128]{3,2,1,0:T(8,128)S(1)}, f32[2,32,32,128]{3,2,1,0:T(8,128)}, u32[]{:S(2)}) copy-start(f32[2,32,32,128]{3,2,1,0:T(8,128)} %param.12) | copy-start | bytes 3145732
  10.0 5.8 %copy-start.6 = (f32[2]{0:T(128)S(1)}, f32[2]{0:T(128)}, u32[]{:S(2)}) copy-start(f32[2]{0:T(128)} %constant.135) | copy-start | bytes 28
  18.3 9.0 %collective-permute-start.3 = (f32[2,2,2,32,128]{4,3,2,1,0:T(8,128)S(1)}, f32[2,2,2,32,128]{4,3,2,1,0:T(8,128)S(1)}, u32[]{:S(2)}, u32[]{:S(2)}) collective-permute-start(f32[2,2,2,32,128]{4,3,2,1,0:T(8,128)S(1)} %get-tuple-element.85), channel_id=1, source_target_pairs={{0,16},{16,18},{18,2},{2,4},{4,20},{20,22},{22,6},{6,8},{8,24},{24... | collective-permute-start | bytes 393224 | tf_op jit(solution)/shard_map/ppermute | solution.py:128
  18.4 8.9 %collective-permute-start.4 = (f32[2,2,2,32,128]{4,3,2,1,0:T(8,128)S(1)}, f32[2,2,2,32,128]{4,3,2,1,0:T(8,128)S(1)}, u32[]{:S(2)}, u32[]{:S(2)}) collective-permute-start(f32[2,2,2,32,128]{4,3,2,1,0:T(8,128)S(1)} %get-tuple-element.84), channel_id=1, source_target_pairs={{16,0},{18,16},{2,18},{4,2},{20,4},{22,20},{6,22},{8,6},{24,8},{26... | collective-permute-start | bytes 393224 | tf_op jit(solution)/shard_map/ppermute | solution.py:129
  22.0 5.0 %collective-permute-start.5 = (f32[2,2,16,4,128]{4,3,2,1,0:T(4,128)S(1)}, f32[2,2,16,4,128]{4,3,2,1,0:T(4,128)S(1)}, u32[]{:S(2)}, u32[]{:S(2)}) collective-permute-start(f32[2,2,16,4,128]{4,3,2,1,0:T(4,128)S(1)} %pad_maximum_fusion.35), channel_id=1, source_target_pairs={{0,1},{1,0},{2,3},{3,2},{4,5},{5,4},{6,7},{7,6},{8,9},{9,8},{10,11... | collective-permute-start | bytes 393224 | tf_op jit(solution)/shard_map/ppermute | solution.py:124
  31.0 5.0 %collective-permute-start.8 = (f32[2,2,16,4,128]{4,3,2,1,0:T(4,128)S(1)}, f32[2,2,16,4,128]{4,3,2,1,0:T(4,128)S(1)}, u32[]{:S(2)}, u32[]{:S(2)}) collective-permute-start(f32[2,2,16,4,128]{4,3,2,1,0:T(4,128)S(1)} %pad_maximum_fusion.36), channel_id=1, source_target_pairs={{0,1},{1,0},{2,3},{3,2},{4,5},{5,4},{6,7},{7,6},{8,9},{9,8},{10,11... | collective-permute-start | bytes 393224 | tf_op jit(solution)/shard_map/ppermute | solution.py:124
  31.1 7.3 %collective-permute-start.6 = (f32[2,2,2,32,128]{4,3,2,1,0:T(8,128)S(1)}, f32[2,2,2,32,128]{4,3,2,1,0:T(8,128)S(1)}, u32[]{:S(2)}, u32[]{:S(2)}) collective-permute-start(f32[2,2,2,32,128]{4,3,2,1,0:T(8,128)S(1)} %get-tuple-element.76), channel_id=1, source_target_pairs={{0,16},{16,18},{18,2},{2,4},{4,20},{20,22},{22,6},{6,8},{8,24},{24... | collective-permute-start | bytes 393224 | tf_op jit(solution)/shard_map/ppermute | solution.py:128
  31.2 7.2 %collective-permute-start.7 = (f32[2,2,2,32,128]{4,3,2,1,0:T(8,128)S(1)}, f32[2,2,2,32,128]{4,3,2,1,0:T(8,128)S(1)}, u32[]{:S(2)}, u32[]{:S(2)}) collective-permute-start(f32[2,2,2,32,128]{4,3,2,1,0:T(8,128)S(1)} %get-tuple-element.77), channel_id=1, source_target_pairs={{16,0},{18,16},{2,18},{4,2},{20,4},{22,20},{6,22},{8,6},{24,8},{26... | collective-permute-start | bytes 393224 | tf_op jit(solution)/shard_map/ppermute | solution.py:129
  42.4 5.0 %collective-permute-start.11 = (f32[2,2,16,4,128]{4,3,2,1,0:T(4,128)S(1)}, f32[2,2,16,4,128]{4,3,2,1,0:T(4,128)S(1)}, u32[]{:S(2)}, u32[]{:S(2)}) collective-permute-start(f32[2,2,16,4,128]{4,3,2,1,0:T(4,128)S(1)} %pad_maximum_fusion.37), channel_id=1, source_target_pairs={{0,1},{1,0},{2,3},{3,2},{4,5},{5,4},{6,7},{7,6},{8,9},{9,8},{10,11... | collective-permute-start | bytes 393224 | tf_op jit(solution)/shard_map/ppermute | solution.py:124
  44.3 5.1 %collective-permute-start.10 = (f32[2,2,2,32,128]{4,3,2,1,0:T(8,128)S(1)}, f32[2,2,2,32,128]{4,3,2,1,0:T(8,128)S(1)}, u32[]{:S(2)}, u32[]{:S(2)}) collective-permute-start(f32[2,2,2,32,128]{4,3,2,1,0:T(8,128)S(1)} %get-tuple-element.69), channel_id=1, source_target_pairs={{16,0},{18,16},{2,18},{4,2},{20,4},{22,20},{6,22},{8,6},{24,8},{26... | collective-permute-start | bytes 393224 | tf_op jit(solution)/shard_map/ppermute | solution.py:129
  46.9 6.2 %collective-permute-start.9 = (f32[2,2,2,32,128]{4,3,2,1,0:T(8,128)S(1)}, f32[2,2,2,32,128]{4,3,2,1,0:T(8,128)S(1)}, u32[]{:S(2)}, u32[]{:S(2)}) collective-permute-start(f32[2,2,2,32,128]{4,3,2,1,0:T(8,128)S(1)} %get-tuple-element.68), channel_id=1, source_target_pairs={{0,16},{16,18},{18,2},{2,4},{4,20},{20,22},{22,6},{6,8},{8,24},{24... | collective-permute-start | bytes 393224 | tf_op jit(solution)/shard_map/ppermute | solution.py:128
  57.1 5.0 %collective-permute-start.14 = (f32[2,2,16,4,128]{4,3,2,1,0:T(4,128)S(1)}, f32[2,2,16,4,128]{4,3,2,1,0:T(4,128)S(1)}, u32[]{:S(2)}, u32[]{:S(2)}) collective-permute-start(f32[2,2,16,4,128]{4,3,2,1,0:T(4,128)S(1)} %pad_maximum_fusion.38), channel_id=1, source_target_pairs={{0,1},{1,0},{2,3},{3,2},{4,5},{5,4},{6,7},{7,6},{8,9},{9,8},{10,11... | collective-permute-start | bytes 393224 | tf_op jit(solution)/shard_map/ppermute | solution.py:124
  57.5 6.3 %collective-permute-start.12 = (f32[2,2,2,32,128]{4,3,2,1,0:T(8,128)S(1)}, f32[2,2,2,32,128]{4,3,2,1,0:T(8,128)S(1)}, u32[]{:S(2)}, u32[]{:S(2)}) collective-permute-start(f32[2,2,2,32,128]{4,3,2,1,0:T(8,128)S(1)} %get-tuple-element.60), channel_id=1, source_target_pairs={{0,16},{16,18},{18,2},{2,4},{4,20},{20,22},{22,6},{6,8},{8,24},{24... | collective-permute-start | bytes 393224 | tf_op jit(solution)/shard_map/ppermute | solution.py:128
  57.6 6.2 %collective-permute-start.13 = (f32[2,2,2,32,128]{4,3,2,1,0:T(8,128)S(1)}, f32[2,2,2,32,128]{4,3,2,1,0:T(8,128)S(1)}, u32[]{:S(2)}, u32[]{:S(2)}) collective-permute-start(f32[2,2,2,32,128]{4,3,2,1,0:T(8,128)S(1)} %get-tuple-element.61), channel_id=1, source_target_pairs={{16,0},{18,16},{2,18},{4,2},{20,4},{22,20},{6,22},{8,6},{24,8},{26... | collective-permute-start | bytes 393224 | tf_op jit(solution)/shard_map/ppermute | solution.py:129
  68.0 5.4 %collective-permute-start.17 = (f32[2,2,16,4,128]{4,3,2,1,0:T(4,128)S(1)}, f32[2,2,16,4,128]{4,3,2,1,0:T(4,128)S(1)}, u32[]{:S(2)}, u32[]{:S(2)}) collective-permute-start(f32[2,2,16,4,128]{4,3,2,1,0:T(4,128)S(1)} %pad_maximum_fusion.39), channel_id=1, source_target_pairs={{0,1},{1,0},{2,3},{3,2},{4,5},{5,4},{6,7},{7,6},{8,9},{9,8},{10,11... | collective-permute-start | bytes 393224 | tf_op jit(solution)/shard_map/ppermute | solution.py:124
  69.8 6.3 %collective-permute-start.15 = (f32[2,2,2,32,128]{4,3,2,1,0:T(8,128)S(1)}, f32[2,2,2,32,128]{4,3,2,1,0:T(8,128)S(1)}, u32[]{:S(2)}, u32[]{:S(2)}) collective-permute-start(f32[2,2,2,32,128]{4,3,2,1,0:T(8,128)S(1)} %get-tuple-element.52), channel_id=1, source_target_pairs={{0,16},{16,18},{18,2},{2,4},{4,20},{20,22},{22,6},{6,8},{8,24},{24... | collective-permute-start | bytes 393224 | tf_op jit(solution)/shard_map/ppermute | solution.py:128
  69.8 6.2 %collective-permute-start.16 = (f32[2,2,2,32,128]{4,3,2,1,0:T(8,128)S(1)}, f32[2,2,2,32,128]{4,3,2,1,0:T(8,128)S(1)}, u32[]{:S(2)}, u32[]{:S(2)}) collective-permute-start(f32[2,2,2,32,128]{4,3,2,1,0:T(8,128)S(1)} %get-tuple-element.53), channel_id=1, source_target_pairs={{16,0},{18,16},{2,18},{4,2},{20,4},{22,20},{6,22},{8,6},{24,8},{26... | collective-permute-start | bytes 393224 | tf_op jit(solution)/shard_map/ppermute | solution.py:129
  80.1 5.0 %collective-permute-start.20 = (f32[2,2,16,4,128]{4,3,2,1,0:T(4,128)S(1)}, f32[2,2,16,4,128]{4,3,2,1,0:T(4,128)S(1)}, u32[]{:S(2)}, u32[]{:S(2)}) collective-permute-start(f32[2,2,16,4,128]{4,3,2,1,0:T(4,128)S(1)} %pad_maximum_fusion.40), channel_id=1, source_target_pairs={{0,1},{1,0},{2,3},{3,2},{4,5},{5,4},{6,7},{7,6},{8,9},{9,8},{10,11... | collective-permute-start | bytes 393224 | tf_op jit(solution)/shard_map/ppermute | solution.py:124
  80.5 6.3 %collective-permute-start.18 = (f32[2,2,2,32,128]{4,3,2,1,0:T(8,128)S(1)}, f32[2,2,2,32,128]{4,3,2,1,0:T(8,128)S(1)}, u32[]{:S(2)}, u32[]{:S(2)}) collective-permute-start(f32[2,2,2,32,128]{4,3,2,1,0:T(8,128)S(1)} %get-tuple-element.44), channel_id=1, source_target_pairs={{0,16},{16,18},{18,2},{2,4},{4,20},{20,22},{22,6},{6,8},{8,24},{24... | collective-permute-start | bytes 393224 | tf_op jit(solution)/shard_map/ppermute | solution.py:128
  80.6 6.2 %collective-permute-start.19 = (f32[2,2,2,32,128]{4,3,2,1,0:T(8,128)S(1)}, f32[2,2,2,32,128]{4,3,2,1,0:T(8,128)S(1)}, u32[]{:S(2)}, u32[]{:S(2)}) collective-permute-start(f32[2,2,2,32,128]{4,3,2,1,0:T(8,128)S(1)} %get-tuple-element.45), channel_id=1, source_target_pairs={{16,0},{18,16},{2,18},{4,2},{20,4},{22,20},{6,22},{8,6},{24,8},{26... | collective-permute-start | bytes 393224 | tf_op jit(solution)/shard_map/ppermute | solution.py:129
  90.9 5.4 %collective-permute-start.23 = (f32[2,2,16,4,128]{4,3,2,1,0:T(4,128)S(1)}, f32[2,2,16,4,128]{4,3,2,1,0:T(4,128)S(1)}, u32[]{:S(2)}, u32[]{:S(2)}) collective-permute-start(f32[2,2,16,4,128]{4,3,2,1,0:T(4,128)S(1)} %pad_maximum_fusion.41), channel_id=1, source_target_pairs={{0,1},{1,0},{2,3},{3,2},{4,5},{5,4},{6,7},{7,6},{8,9},{9,8},{10,11... | collective-permute-start | bytes 393224 | tf_op jit(solution)/shard_map/ppermute | solution.py:124
  92.7 6.3 %collective-permute-start.21 = (f32[2,2,2,32,128]{4,3,2,1,0:T(8,128)S(1)}, f32[2,2,2,32,128]{4,3,2,1,0:T(8,128)S(1)}, u32[]{:S(2)}, u32[]{:S(2)}) collective-permute-start(f32[2,2,2,32,128]{4,3,2,1,0:T(8,128)S(1)} %get-tuple-element.36), channel_id=1, source_target_pairs={{0,16},{16,18},{18,2},{2,4},{4,20},{20,22},{22,6},{6,8},{8,24},{24... | collective-permute-start | bytes 393224 | tf_op jit(solution)/shard_map/ppermute | solution.py:128
  92.8 6.2 %collective-permute-start.22 = (f32[2,2,2,32,128]{4,3,2,1,0:T(8,128)S(1)}, f32[2,2,2,32,128]{4,3,2,1,0:T(8,128)S(1)}, u32[]{:S(2)}, u32[]{:S(2)}) collective-permute-start(f32[2,2,2,32,128]{4,3,2,1,0:T(8,128)S(1)} %get-tuple-element.37), channel_id=1, source_target_pairs={{16,0},{18,16},{2,18},{4,2},{20,4},{22,20},{6,22},{8,6},{24,8},{26... | collective-permute-start | bytes 393224 | tf_op jit(solution)/shard_map/ppermute | solution.py:129
  103.2 5.3 %collective-permute-start.26 = (f32[2,2,16,4,128]{4,3,2,1,0:T(4,128)S(1)}, f32[2,2,16,4,128]{4,3,2,1,0:T(4,128)S(1)}, u32[]{:S(2)}, u32[]{:S(2)}) collective-permute-start(f32[2,2,16,4,128]{4,3,2,1,0:T(4,128)S(1)} %pad_maximum_fusion.42), channel_id=1, source_target_pairs={{0,1},{1,0},{2,3},{3,2},{4,5},{5,4},{6,7},{7,6},{8,9},{9,8},{10,11... | collective-permute-start | bytes 393224 | tf_op jit(solution)/shard_map/ppermute | solution.py:124
  103.5 6.3 %collective-permute-start.24 = (f32[2,2,2,32,128]{4,3,2,1,0:T(8,128)S(1)}, f32[2,2,2,32,128]{4,3,2,1,0:T(8,128)S(1)}, u32[]{:S(2)}, u32[]{:S(2)}) collective-permute-start(f32[2,2,2,32,128]{4,3,2,1,0:T(8,128)S(1)} %get-tuple-element.28), channel_id=1, source_target_pairs={{0,16},{16,18},{18,2},{2,4},{4,20},{20,22},{22,6},{6,8},{8,24},{24... | collective-permute-start | bytes 393224 | tf_op jit(solution)/shard_map/ppermute | solution.py:128
  103.6 6.5 %collective-permute-start.25 = (f32[2,2,2,32,128]{4,3,2,1,0:T(8,128)S(1)}, f32[2,2,2,32,128]{4,3,2,1,0:T(8,128)S(1)}, u32[]{:S(2)}, u32[]{:S(2)}) collective-permute-start(f32[2,2,2,32,128]{4,3,2,1,0:T(8,128)S(1)} %get-tuple-element.29), channel_id=1, source_target_pairs={{16,0},{18,16},{2,18},{4,2},{20,4},{22,20},{6,22},{8,6},{24,8},{26... | collective-permute-start | bytes 393224 | tf_op jit(solution)/shard_map/ppermute | solution.py:129
  107.1 11.1 %collective-permute-start.28 = (f32[1,2,16,32,128]{4,3,2,1,0:T(8,128)S(1)}, f32[1,2,16,32,128]{4,3,2,1,0:T(8,128)S(1)}, u32[]{:S(2)}, u32[]{:S(2)}) collective-permute-start(f32[1,2,16,32,128]{4,3,2,1,0:T(8,128)S(1)} %slice.1160), channel_id=1, source_target_pairs={{16,0},{17,1},{18,2},{19,3},{20,4},{21,5},{22,6},{23,7},{24,8},{25... | collective-permute-start | bytes 1572872 | tf_op jit(solution)/shard_map/ppermute | solution.py:226
  113.2 9.7 %collective-permute-start.27 = (f32[1,2,16,32,128]{4,3,2,1,0:T(8,128)S(1)}, f32[1,2,16,32,128]{4,3,2,1,0:T(8,128)S(1)}, u32[]{:S(2)}, u32[]{:S(2)}) collective-permute-start(f32[1,2,16,32,128]{4,3,2,1,0:T(8,128)S(1)} %convolution_bitcast_fusion.7), channel_id=1, source_target_pairs={{0,16},{1,17},{2,18},{3,19},{4,20},{5,21},{6,22},{7,23},{8,24},{9,... | collective-permute-start | bytes 1572872 | tf_op jit(solution)/shard_map/ppermute | solution.py:226
  116.5 6.4 %copy-start.2 = (f32[1,2,32,32,128]{4,3,2,1,0:T(8,128)}, f32[1,2,32,32,128]{4,3,2,1,0:T(8,128)S(1)}, u32[]{:S(2)}) copy-start(f32[1,2,32,32,128]{4,3,2,1,0:T(8,128)S(1)} %fusion.66) | copy-start | bytes 3145732
  (5 other events, 5.2 us)

commit v8 on v6

--- a/solution.py
+++ b/solution.py
@@ -120,11 +120,6 @@
     down = [(j, i) for i, j in up]
     last = lax.slice_in_dim(block, length - width, length, axis=dim)
     first = lax.slice_in_dim(block, 0, width, axis=dim)
-    if size == 2:
-        got = lax.ppermute(jnp.concatenate([first, last], dim), axes, up)
-        after = lax.slice_in_dim(got, 0, width, axis=dim)
-        before = lax.slice_in_dim(got, width, 2 * width, axis=dim)
-        return before, after
     before = lax.ppermute(last, axes, up)
     after = lax.ppermute(first, axes, down)
     return before, after

time: 122 us -> 131 us (1.074)
  starting transfers between devices: 45.4 us -> 55.9 us
  waiting for transfers between devices: 32.8 us -> 30.4 us
    ppermute x9 -> x18, starting transfers between devices: 2.03 us -> 16.4 us  [ring_halo(): before = lax.ppermute(last, axes, up)]
    ppermute x9 -> x0, starting transfers between devices: 9.68 us -> none  [ring_halo(): got = lax.ppermute(jnp.concatenate([first, last], dim), axes, up)]
    ppermute x9 -> x0, waiting for transfers between devices: 8.78 us -> none  [ring_halo(): got = lax.ppermute(jnp.concatenate([first, last], dim), axes, up)]
    ppermute x9 -> x18, waiting for transfers between devices: 2.19 us -> 8.68 us  [ring_halo(): after = lax.ppermute(first, axes, down)]
    ppermute x9 -> x18, starting transfers between devices: 29.4 us -> 35.6 us  [ring_halo(): after = lax.ppermute(first, axes, down)]
    slice x8 -> x16, local copies, waits for them, and re-layouts: 0.13 us -> 1.79 us  [ring_halo(): last = lax.slice_in_dim(block, length - width, length, axis=dim)]
    ppermute x9 -> x18, waiting for transfers between devices: 15.5 us -> 15.4 us  [ring_halo(): before = lax.ppermute(last, axes, up)]
  transfers between devices with their start and end apart: 29 -> 38, of which waited for: 16 -> 18; matrix products, arithmetic and copies ran while one was open for 6% -> 6% of each run, Pallas kernels for 2% -> 2%
where the time goes in v8:
time: 131 us
  starting transfers between devices  55.9 us (43%)
  waiting for transfers between devices  30.4 us (23%)
  other arithmetic  26.3 us (20%)
  matrix products  8.9 us (7%)
  local copies, waits for them, and re-layouts  5.93 us (5%)
  Pallas kernels  2.93 us (2%)
    ppermute x18, starting transfers between devices, ring_halo(): after = lax.ppermute(first, axes, down)  35.6 us
    ppermute x18, starting transfers between devices, ring_halo(): before = lax.ppermute(last, axes, up)  16.4 us
    mul x9, other arithmetic, tendency(): return DT * (flow + kappa * laplace + react)  15.6 us
    ppermute x18, waiting for transfers between devices, ring_halo(): before = lax.ppermute(last, axes, up)  15.4 us
    dot_general x9, matrix products, column_solve(): jnp.einsum('lsxyk,sjk->lsxyj', rhs, inverse, precision=lax.Precision.HIGH...  8.9 us
    ppermute x18, waiting for transfers between devices, ring_halo(): after = lax.ppermute(first, axes, down)  8.68 us
    ppermute x2, waiting for transfers between devices, on_device(): arrived = lax.ppermute(states[level][None], 'corr', pairs)  6.35 us
    ppermute x2, starting transfers between devices, on_device(): arrived = lax.ppermute(states[level][None], 'corr', pairs)  3.94 us
  transfers between devices with their start and end apart: 38, of which 18 were waited for; matrix products, arithmetic and copies ran while one was open for 6% of the time, Pallas kernels for 2%

profile of v8, /device:TPU:0, one launch (start us, length us, event | category | flops | bytes accessed | tf_op | source)
XLA Modules:
  0.0 131.0 jit_solution(3094337682487899876)
XLA Ops:
  1.7 2.9 %collective-permute-start = (f32[1,2,2,32,128]{4,3,2,1,0:T(8,128)}, f32[1,2,2,32,128]{4,3,2,1,0:T(8,128)S(1)}, u32[]{:S(2)}, u32[]{:S(2)}) collective-permute-start(f32[1,2,2,32,128]{4,3,2,1,0:T(8,128)} %get-tuple-element.98), channel_id=1, source_target_pairs={{0,16},{16,18},{18,2},{2,4},{4,20},{20,22},{22,6},{6,8},{8,24},{24... | collective-permute-start | bytes 196616 | tf_op jit(solution)/shard_map/ppermute | solution.py:123
  6.9 2.0 %collective-permute-start.2 = (f32[1,2,16,2,128]{4,3,2,1,0:T(2,128)}, f32[1,2,16,2,128]{4,3,2,1,0:T(2,128)}, u32[]{:S(2)}, u32[]{:S(2)}) collective-permute-start(f32[1,2,16,2,128]{4,3,2,1,0:T(2,128)} %get-tuple-element.100), channel_id=1, source_target_pairs={{0,1},{1,0},{2,3},{3,2},{4,5},{5,4},{6,7},{7,6},{8,9},{9,8},{10,11... | collective-permute-start | bytes 98312 | tf_op jit(solution)/shard_map/ppermute | solution.py:123
  12.2 2.9 %shard_map.118 = f32[128,2,128]{2,1,0:T(2,128)} custom-call(f32[2,128]{1,0:T(2,128)} %copy-done.3, f32[2,128]{1,0:T(2,128)} %get-tuple-element.105.low_ref), custom_call_target="tpu_custom_call" | custom-call | flops 393216 | bytes 262144 | tf_op jit(solution)/shard_map/pallas_call | solution.py:78
  15.1 1.7 %fusion.88 = f32[1,2,16,32,128]{4,3,2,1,0:T(8,128)S(1)} fusion(f32[1,1,16,32,128]{4,3,2,1,0:T(8,128)} %get-tuple-element.103, f32[1,1,16,32,128]{4,3,2,1,0:T(8,128)S(1)} %get-tuple-element.102, f32[1,2,16,2,128]{4,3,2,1,0:T(2,128)} %collective-permute-done.3, f32[1,2,16,32,128]{4,3,2,1,0:T(8,128)S(1)} %dynamic-slice_bitcast_fusion, ...), kind=kLoop, calls=%fused_computation.235 | loop fusion | flops 4587520 | bytes 2818060 | tf_op jit(solution)/shard_map/mul | solution.py:156
  17.9 2.1 %collective-permute-start.6 = (f32[2,2,16,2,128]{4,3,2,1,0:T(2,128)S(1)}, f32[2,2,16,2,128]{4,3,2,1,0:T(2,128)S(1)}, u32[]{:S(2)}, u32[]{:S(2)}) collective-permute-start(f32[2,2,16,2,128]{4,3,2,1,0:T(2,128)S(1)} %get-tuple-element.89), channel_id=1, source_target_pairs={{0,1},{1,0},{2,3},{3,2},{4,5},{5,4},{6,7},{7,6},{8,9},{9,8},{10,11... | collective-permute-start | bytes 196616 | tf_op jit(solution)/shard_map/ppermute | solution.py:123
  20.5 3.1 %collective-permute-start.5 = (f32[2,2,2,32,128]{4,3,2,1,0:T(8,128)S(1)}, f32[2,2,2,32,128]{4,3,2,1,0:T(8,128)S(1)}, u32[]{:S(2)}, u32[]{:S(2)}) collective-permute-start(f32[2,2,2,32,128]{4,3,2,1,0:T(8,128)S(1)} %get-tuple-element.84), channel_id=1, source_target_pairs={{16,0},{18,16},{2,18},{4,2},{20,4},{22,20},{6,22},{8,6},{24,8},{26... | collective-permute-start | bytes 393224 | tf_op jit(solution)/shard_map/ppermute | solution.py:124
  24.4 2.5 %collective-permute-done.4 = f32[2,2,2,32,128]{4,3,2,1,0:T(8,128)S(1)} collective-permute-done((f32[2,2,2,32,128]{4,3,2,1,0:T(8,128)S(1)}, f32[2,2,2,32,128]{4,3,2,1,0:T(8,128)S(1)}, u32[]{:S(2)}, u32[]{:S(2)}) %collective-permute-start.4) | collective-permute-done | bytes 131104 | tf_op jit(solution)/shard_map/ppermute | solution.py:123
  31.0 3.5 %collective-permute-start.9 = (f32[2,2,2,32,128]{4,3,2,1,0:T(8,128)S(1)}, f32[2,2,2,32,128]{4,3,2,1,0:T(8,128)S(1)}, u32[]{:S(2)}, u32[]{:S(2)}) collective-permute-start(f32[2,2,2,32,128]{4,3,2,1,0:T(8,128)S(1)} %get-tuple-element.77), channel_id=1, source_target_pairs={{16,0},{18,16},{2,18},{4,2},{20,4},{22,20},{6,22},{8,6},{24,8},{26... | collective-permute-start | bytes 393224 | tf_op jit(solution)/shard_map/ppermute | solution.py:124
  34.6 2.3 %collective-permute-start.10 = (f32[2,2,16,2,128]{4,3,2,1,0:T(2,128)S(1)}, f32[2,2,16,2,128]{4,3,2,1,0:T(2,128)S(1)}, u32[]{:S(2)}, u32[]{:S(2)}) collective-permute-start(f32[2,2,16,2,128]{4,3,2,1,0:T(2,128)S(1)} %get-tuple-element.78), channel_id=1, source_target_pairs={{0,1},{1,0},{2,3},{3,2},{4,5},{5,4},{6,7},{7,6},{8,9},{9,8},{10,11... | collective-permute-start | bytes 196616 | tf_op jit(solution)/shard_map/ppermute | solution.py:123
  37.2 2.0 %collective-permute-done.10 = f32[2,2,16,2,128]{4,3,2,1,0:T(2,128)S(1)} collective-permute-done((f32[2,2,16,2,128]{4,3,2,1,0:T(2,128)S(1)}, f32[2,2,16,2,128]{4,3,2,1,0:T(2,128)S(1)}, u32[]{:S(2)}, u32[]{:S(2)}) %collective-permute-start.10) | collective-permute-done | bytes 65568 | tf_op jit(solution)/shard_map/ppermute | solution.py:123
  39.2 2.0 %collective-permute-done.11 = f32[2,2,16,2,128]{4,3,2,1,0:T(2,128)S(1)} collective-permute-done((f32[2,2,16,2,128]{4,3,2,1,0:T(2,128)S(1)}, f32[2,2,16,2,128]{4,3,2,1,0:T(2,128)S(1)}, u32[]{:S(2)}, u32[]{:S(2)}) %collective-permute-start.11) | collective-permute-done | bytes 65568 | tf_op jit(solution)/shard_map/ppermute | solution.py:124
  41.2 1.8 %fusion.37 = f32[2,2,16,32,128]{4,3,2,1,0:T(8,128)S(1)} fusion(f32[2,1,16,32,128]{4,3,2,1,0:T(8,128)S(1)} %get-tuple-element.81, f32[2,1,16,32,128]{4,3,2,1,0:T(8,128)S(1)} %get-tuple-element.80, f32[2,2,16,32,128]{4,3,2,1,0:T(8,128)S(1)} %convolution_bitcast_fusion.6, f32[2,2,16,2,128]{4,3,2,1,0:T(2,128)S(1)} %collective-permute-done.11, ...), kind=kLoop, calls=%fused_computation.148 | loop fusion | flops 9175040 | bytes 4063240 | tf_op jit(solution)/shard_map/mul | solution.py:156
  45.1 3.5 %collective-permute-start.13 = (f32[2,2,2,32,128]{4,3,2,1,0:T(8,128)S(1)}, f32[2,2,2,32,128]{4,3,2,1,0:T(8,128)S(1)}, u32[]{:S(2)}, u32[]{:S(2)}) collective-permute-start(f32[2,2,2,32,128]{4,3,2,1,0:T(8,128)S(1)} %get-tuple-element.69), channel_id=1, source_target_pairs={{16,0},{18,16},{2,18},{4,2},{20,4},{22,20},{6,22},{8,6},{24,8},{26... | collective-permute-start | bytes 393224 | tf_op jit(solution)/shard_map/ppermute | solution.py:124
  50.8 2.0 %collective-permute-done.14 = f32[2,2,16,2,128]{4,3,2,1,0:T(2,128)S(1)} collective-permute-done((f32[2,2,16,2,128]{4,3,2,1,0:T(2,128)S(1)}, f32[2,2,16,2,128]{4,3,2,1,0:T(2,128)S(1)}, u32[]{:S(2)}, u32[]{:S(2)}) %collective-permute-start.14) | collective-permute-done | bytes 65568 | tf_op jit(solution)/shard_map/ppermute | solution.py:123
  53.6 1.8 %fusion.41 = f32[2,2,16,32,128]{4,3,2,1,0:T(8,128)S(1)} fusion(f32[2,1,16,32,128]{4,3,2,1,0:T(8,128)S(1)} %get-tuple-element.73, f32[2,1,16,32,128]{4,3,2,1,0:T(8,128)S(1)} %get-tuple-element.72, f32[2,2,16,32,128]{4,3,2,1,0:T(8,128)S(1)} %convolution_bitcast_fusion.5, f32[2,2,16,2,128]{4,3,2,1,0:T(2,128)S(1)} %collective-permute-done.15, ...), kind=kLoop, calls=%fused_computation.153 | loop fusion | flops 9175040 | bytes 4063240 | tf_op jit(solution)/shard_map/mul | solution.py:156
  57.5 3.5 %collective-permute-start.17 = (f32[2,2,2,32,128]{4,3,2,1,0:T(8,128)S(1)}, f32[2,2,2,32,128]{4,3,2,1,0:T(8,128)S(1)}, u32[]{:S(2)}, u32[]{:S(2)}) collective-permute-start(f32[2,2,2,32,128]{4,3,2,1,0:T(8,128)S(1)} %get-tuple-element.61), channel_id=1, source_target_pairs={{16,0},{18,16},{2,18},{4,2},{20,4},{22,20},{6,22},{8,6},{24,8},{26... | collective-permute-start | bytes 393224 | tf_op jit(solution)/shard_map/ppermute | solution.py:124
  63.3 2.0 %collective-permute-done.18 = f32[2,2,16,2,128]{4,3,2,1,0:T(2,128)S(1)} collective-permute-done((f32[2,2,16,2,128]{4,3,2,1,0:T(2,128)S(1)}, f32[2,2,16,2,128]{4,3,2,1,0:T(2,128)S(1)}, u32[]{:S(2)}, u32[]{:S(2)}) %collective-permute-start.18) | collective-permute-done | bytes 65568 | tf_op jit(solution)/shard_map/ppermute | solution.py:123
  66.6 1.8 %fusion.45 = f32[2,2,16,32,128]{4,3,2,1,0:T(8,128)S(1)} fusion(f32[2,1,16,32,128]{4,3,2,1,0:T(8,128)S(1)} %get-tuple-element.65, f32[2,1,16,32,128]{4,3,2,1,0:T(8,128)S(1)} %get-tuple-element.64, f32[2,2,16,32,128]{4,3,2,1,0:T(8,128)S(1)} %convolution_bitcast_fusion.4, f32[2,2,16,2,128]{4,3,2,1,0:T(2,128)S(1)} %collective-permute-done.19, ...), kind=kLoop, calls=%fused_computation.158 | loop fusion | flops 9175040 | bytes 4063240 | tf_op jit(solution)/shard_map/mul | solution.py:156
  70.6 3.5 %collective-permute-start.21 = (f32[2,2,2,32,128]{4,3,2,1,0:T(8,128)S(1)}, f32[2,2,2,32,128]{4,3,2,1,0:T(8,128)S(1)}, u32[]{:S(2)}, u32[]{:S(2)}) collective-permute-start(f32[2,2,2,32,128]{4,3,2,1,0:T(8,128)S(1)} %get-tuple-element.53), channel_id=1, source_target_pairs={{16,0},{18,16},{2,18},{4,2},{20,4},{22,20},{6,22},{8,6},{24,8},{26... | collective-permute-start | bytes 393224 | tf_op jit(solution)/shard_map/ppermute | solution.py:124
  76.4 2.0 %collective-permute-done.22 = f32[2,2,16,2,128]{4,3,2,1,0:T(2,128)S(1)} collective-permute-done((f32[2,2,16,2,128]{4,3,2,1,0:T(2,128)S(1)}, f32[2,2,16,2,128]{4,3,2,1,0:T(2,128)S(1)}, u32[]{:S(2)}, u32[]{:S(2)}) %collective-permute-start.22) | collective-permute-done | bytes 65568 | tf_op jit(solution)/shard_map/ppermute | solution.py:123
  79.1 1.8 %fusion.49 = f32[2,2,16,32,128]{4,3,2,1,0:T(8,128)S(1)} fusion(f32[2,1,16,32,128]{4,3,2,1,0:T(8,128)S(1)} %get-tuple-element.57, f32[2,1,16,32,128]{4,3,2,1,0:T(8,128)S(1)} %get-tuple-element.56, f32[2,2,16,32,128]{4,3,2,1,0:T(8,128)S(1)} %convolution_bitcast_fusion.3, f32[2,2,16,2,128]{4,3,2,1,0:T(2,128)S(1)} %collective-permute-done.23, ...), kind=kLoop, calls=%fused_computation.163 | loop fusion | flops 9175040 | bytes 4063240 | tf_op jit(solution)/shard_map/mul | solution.py:156
  83.0 3.5 %collective-permute-start.25 = (f32[2,2,2,32,128]{4,3,2,1,0:T(8,128)S(1)}, f32[2,2,2,32,128]{4,3,2,1,0:T(8,128)S(1)}, u32[]{:S(2)}, u32[]{:S(2)}) collective-permute-start(f32[2,2,2,32,128]{4,3,2,1,0:T(8,128)S(1)} %get-tuple-element.45), channel_id=1, source_target_pairs={{16,0},{18,16},{2,18},{4,2},{20,4},{22,20},{6,22},{8,6},{24,8},{26... | collective-permute-start | bytes 393224 | tf_op jit(solution)/shard_map/ppermute | solution.py:124
  88.8 2.0 %collective-permute-done.26 = f32[2,2,16,2,128]{4,3,2,1,0:T(2,128)S(1)} collective-permute-done((f32[2,2,16,2,128]{4,3,2,1,0:T(2,128)S(1)}, f32[2,2,16,2,128]{4,3,2,1,0:T(2,128)S(1)}, u32[]{:S(2)}, u32[]{:S(2)}) %collective-permute-start.26) | collective-permute-done | bytes 65568 | tf_op jit(solution)/shard_map/ppermute | solution.py:123
  92.2 1.8 %fusion.53 = f32[2,2,16,32,128]{4,3,2,1,0:T(8,128)S(1)} fusion(f32[2,1,16,32,128]{4,3,2,1,0:T(8,128)S(1)} %get-tuple-element.49, f32[2,1,16,32,128]{4,3,2,1,0:T(8,128)S(1)} %get-tuple-element.48, f32[2,2,16,32,128]{4,3,2,1,0:T(8,128)S(1)} %convolution_bitcast_fusion.2, f32[2,2,16,2,128]{4,3,2,1,0:T(2,128)S(1)} %collective-permute-done.27, ...), kind=kLoop, calls=%fused_computation.168 | loop fusion | flops 9175040 | bytes 4063240 | tf_op jit(solution)/shard_map/mul | solution.py:156
  96.1 3.5 %collective-permute-start.29 = (f32[2,2,2,32,128]{4,3,2,1,0:T(8,128)S(1)}, f32[2,2,2,32,128]{4,3,2,1,0:T(8,128)S(1)}, u32[]{:S(2)}, u32[]{:S(2)}) collective-permute-start(f32[2,2,2,32,128]{4,3,2,1,0:T(8,128)S(1)} %get-tuple-element.37), channel_id=1, source_target_pairs={{16,0},{18,16},{2,18},{4,2},{20,4},{22,20},{6,22},{8,6},{24,8},{26... | collective-permute-start | bytes 393224 | tf_op jit(solution)/shard_map/ppermute | solution.py:124
  101.9 2.0 %collective-permute-done.30 = f32[2,2,16,2,128]{4,3,2,1,0:T(2,128)S(1)} collective-permute-done((f32[2,2,16,2,128]{4,3,2,1,0:T(2,128)S(1)}, f32[2,2,16,2,128]{4,3,2,1,0:T(2,128)S(1)}, u32[]{:S(2)}, u32[]{:S(2)}) %collective-permute-start.30) | collective-permute-done | bytes 65568 | tf_op jit(solution)/shard_map/ppermute | solution.py:123
  104.6 1.8 %fusion.57 = f32[2,2,16,32,128]{4,3,2,1,0:T(8,128)S(1)} fusion(f32[2,1,16,32,128]{4,3,2,1,0:T(8,128)S(1)} %get-tuple-element.41, f32[2,1,16,32,128]{4,3,2,1,0:T(8,128)S(1)} %get-tuple-element.40, f32[2,2,16,32,128]{4,3,2,1,0:T(8,128)S(1)} %convolution_bitcast_fusion.1, f32[2,2,16,2,128]{4,3,2,1,0:T(2,128)S(1)} %collective-permute-done.31, ...), kind=kLoop, calls=%fused_computation.173 | loop fusion | flops 9175040 | bytes 4063240 | tf_op jit(solution)/shard_map/mul | solution.py:156
  108.6 3.5 %collective-permute-start.33 = (f32[2,2,2,32,128]{4,3,2,1,0:T(8,128)S(1)}, f32[2,2,2,32,128]{4,3,2,1,0:T(8,128)S(1)}, u32[]{:S(2)}, u32[]{:S(2)}) collective-permute-start(f32[2,2,2,32,128]{4,3,2,1,0:T(8,128)S(1)} %get-tuple-element.29), channel_id=1, source_target_pairs={{16,0},{18,16},{2,18},{4,2},{20,4},{22,20},{6,22},{8,6},{24,8},{26... | collective-permute-start | bytes 393224 | tf_op jit(solution)/shard_map/ppermute | solution.py:124
  117.7 1.8 %fusion.61 = f32[2,2,16,32,128]{4,3,2,1,0:T(8,128)S(1)} fusion(f32[2,1,16,32,128]{4,3,2,1,0:T(8,128)S(1)} %get-tuple-element.33, f32[2,1,16,32,128]{4,3,2,1,0:T(8,128)S(1)} %get-tuple-element.32, f32[2,2,16,32,128]{4,3,2,1,0:T(8,128)S(1)} %convolution_bitcast_fusion, f32[2,2,16,2,128]{4,3,2,1,0:T(2,128)S(1)} %collective-permute-done.35, ...), kind=kLoop, calls=%fused_computation.178 | loop fusion | flops 9175040 | bytes 4063240 | tf_op jit(solution)/shard_map/mul | solution.py:156
  120.8 2.7 %collective-permute-start.36 = (f32[1,2,16,32,128]{4,3,2,1,0:T(8,128)S(1)}, f32[1,2,16,32,128]{4,3,2,1,0:T(8,128)S(1)}, u32[]{:S(2)}, u32[]{:S(2)}) collective-permute-start(f32[1,2,16,32,128]{4,3,2,1,0:T(8,128)S(1)} %convolution_bitcast_fusion.7), channel_id=1, source_target_pairs={{0,16},{1,17},{2,18},{3,19},{4,20},{5,21},{6,22},{7,23},{8,24},{9,... | collective-permute-start | bytes 1572872 | tf_op jit(solution)/shard_map/ppermute | solution.py:224
  123.8 1.7 %collective-permute-done.37 = f32[1,2,16,32,128]{4,3,2,1,0:T(8,128)S(1)} collective-permute-done((f32[1,2,16,32,128]{4,3,2,1,0:T(8,128)S(1)}, f32[1,2,16,32,128]{4,3,2,1,0:T(8,128)S(1)}, u32[]{:S(2)}, u32[]{:S(2)}) %collective-permute-start.37) | collective-permute-done | bytes 524320 | tf_op jit(solution)/shard_map/ppermute | solution.py:224
  125.5 4.7 %collective-permute-done.36 = f32[1,2,16,32,128]{4,3,2,1,0:T(8,128)S(1)} collective-permute-done((f32[1,2,16,32,128]{4,3,2,1,0:T(8,128)S(1)}, f32[1,2,16,32,128]{4,3,2,1,0:T(8,128)S(1)}, u32[]{:S(2)}, u32[]{:S(2)}) %collective-permute-start.36) | collective-permute-done | bytes 524320 | tf_op jit(solution)/shard_map/ppermute | solution.py:224
  (134 shorter events, 50.1 us)
Async XLA Ops:
  1.7 13.4 %collective-permute-start = (f32[1,2,2,32,128]{4,3,2,1,0:T(8,128)}, f32[1,2,2,32,128]{4,3,2,1,0:T(8,128)S(1)}, u32[]{:S(2)}, u32[]{:S(2)}) collective-permute-start(f32[1,2,2,32,128]{4,3,2,1,0:T(8,128)} %get-tuple-element.98), channel_id=1, source_target_pairs={{0,16},{16,18},{18,2},{2,4},{4,20},{20,22},{22,6},{6,8},{8,24},{24... | collective-permute-start | bytes 196616 | tf_op jit(solution)/shard_map/ppermute | solution.py:123
  4.7 10.4 %collective-permute-start.1 = (f32[1,2,2,32,128]{4,3,2,1,0:T(8,128)}, f32[1,2,2,32,128]{4,3,2,1,0:T(8,128)S(1)}, u32[]{:S(2)}, u32[]{:S(2)}) collective-permute-start(f32[1,2,2,32,128]{4,3,2,1,0:T(8,128)} %get-tuple-element.99), channel_id=1, source_target_pairs={{16,0},{18,16},{2,18},{4,2},{20,4},{22,20},{6,22},{8,6},{24,8},{26... | collective-permute-start | bytes 196616 | tf_op jit(solution)/shard_map/ppermute | solution.py:124
  6.9 8.2 %collective-permute-start.2 = (f32[1,2,16,2,128]{4,3,2,1,0:T(2,128)}, f32[1,2,16,2,128]{4,3,2,1,0:T(2,128)}, u32[]{:S(2)}, u32[]{:S(2)}) collective-permute-start(f32[1,2,16,2,128]{4,3,2,1,0:T(2,128)} %get-tuple-element.100), channel_id=1, source_target_pairs={{0,1},{1,0},{2,3},{3,2},{4,5},{5,4},{6,7},{7,6},{8,9},{9,8},{10,11... | collective-permute-start | bytes 98312 | tf_op jit(solution)/shard_map/ppermute | solution.py:123
  8.9 6.2 %collective-permute-start.3 = (f32[1,2,16,2,128]{4,3,2,1,0:T(2,128)}, f32[1,2,16,2,128]{4,3,2,1,0:T(2,128)}, u32[]{:S(2)}, u32[]{:S(2)}) collective-permute-start(f32[1,2,16,2,128]{4,3,2,1,0:T(2,128)} %get-tuple-element.101), channel_id=1, source_target_pairs={{1,0},{0,1},{3,2},{2,3},{5,4},{4,5},{7,6},{6,7},{9,8},{8,9},{11,10... | collective-permute-start | bytes 98312 | tf_op jit(solution)/shard_map/ppermute | solution.py:124
  17.9 5.8 %collective-permute-start.6 = (f32[2,2,16,2,128]{4,3,2,1,0:T(2,128)S(1)}, f32[2,2,16,2,128]{4,3,2,1,0:T(2,128)S(1)}, u32[]{:S(2)}, u32[]{:S(2)}) collective-permute-start(f32[2,2,16,2,128]{4,3,2,1,0:T(2,128)S(1)} %get-tuple-element.89), channel_id=1, source_target_pairs={{0,1},{1,0},{2,3},{3,2},{4,5},{5,4},{6,7},{7,6},{8,9},{9,8},{10,11... | collective-permute-start | bytes 196616 | tf_op jit(solution)/shard_map/ppermute | solution.py:123
  19.9 4.3 %collective-permute-start.7 = (f32[2,2,16,2,128]{4,3,2,1,0:T(2,128)S(1)}, f32[2,2,16,2,128]{4,3,2,1,0:T(2,128)S(1)}, u32[]{:S(2)}, u32[]{:S(2)}) collective-permute-start(f32[2,2,16,2,128]{4,3,2,1,0:T(2,128)S(1)} %get-tuple-element.88), channel_id=1, source_target_pairs={{1,0},{0,1},{3,2},{2,3},{5,4},{4,5},{7,6},{6,7},{9,8},{8,9},{11,10... | collective-permute-start | bytes 196616 | tf_op jit(solution)/shard_map/ppermute | solution.py:124
  20.0 6.9 %collective-permute-start.4 = (f32[2,2,2,32,128]{4,3,2,1,0:T(8,128)S(1)}, f32[2,2,2,32,128]{4,3,2,1,0:T(8,128)S(1)}, u32[]{:S(2)}, u32[]{:S(2)}) collective-permute-start(f32[2,2,2,32,128]{4,3,2,1,0:T(8,128)S(1)} %get-tuple-element.85), channel_id=1, source_target_pairs={{0,16},{16,18},{18,2},{2,4},{4,20},{20,22},{22,6},{6,8},{8,24},{24... | collective-permute-start | bytes 393224 | tf_op jit(solution)/shard_map/ppermute | solution.py:123
  20.5 6.5 %collective-permute-start.5 = (f32[2,2,2,32,128]{4,3,2,1,0:T(8,128)S(1)}, f32[2,2,2,32,128]{4,3,2,1,0:T(8,128)S(1)}, u32[]{:S(2)}, u32[]{:S(2)}) collective-permute-start(f32[2,2,2,32,128]{4,3,2,1,0:T(8,128)S(1)} %get-tuple-element.84), channel_id=1, source_target_pairs={{16,0},{18,16},{2,18},{4,2},{20,4},{22,20},{6,22},{8,6},{24,8},{26... | collective-permute-start | bytes 393224 | tf_op jit(solution)/shard_map/ppermute | solution.py:124
  31.0 10.2 %collective-permute-start.8 = (f32[2,2,2,32,128]{4,3,2,1,0:T(8,128)S(1)}, f32[2,2,2,32,128]{4,3,2,1,0:T(8,128)S(1)}, u32[]{:S(2)}, u32[]{:S(2)}) collective-permute-start(f32[2,2,2,32,128]{4,3,2,1,0:T(8,128)S(1)} %get-tuple-element.76), channel_id=1, source_target_pairs={{0,16},{16,18},{18,2},{2,4},{4,20},{20,22},{22,6},{6,8},{8,24},{24... | collective-permute-start | bytes 393224 | tf_op jit(solution)/shard_map/ppermute | solution.py:123
  31.0 10.1 %collective-permute-start.9 = (f32[2,2,2,32,128]{4,3,2,1,0:T(8,128)S(1)}, f32[2,2,2,32,128]{4,3,2,1,0:T(8,128)S(1)}, u32[]{:S(2)}, u32[]{:S(2)}) collective-permute-start(f32[2,2,2,32,128]{4,3,2,1,0:T(8,128)S(1)} %get-tuple-element.77), channel_id=1, source_target_pairs={{16,0},{18,16},{2,18},{4,2},{20,4},{22,20},{6,22},{8,6},{24,8},{26... | collective-permute-start | bytes 393224 | tf_op jit(solution)/shard_map/ppermute | solution.py:124
  34.6 4.6 %collective-permute-start.10 = (f32[2,2,16,2,128]{4,3,2,1,0:T(2,128)S(1)}, f32[2,2,16,2,128]{4,3,2,1,0:T(2,128)S(1)}, u32[]{:S(2)}, u32[]{:S(2)}) collective-permute-start(f32[2,2,16,2,128]{4,3,2,1,0:T(2,128)S(1)} %get-tuple-element.78), channel_id=1, source_target_pairs={{0,1},{1,0},{2,3},{3,2},{4,5},{5,4},{6,7},{7,6},{8,9},{9,8},{10,11... | collective-permute-start | bytes 196616 | tf_op jit(solution)/shard_map/ppermute | solution.py:123
  36.9 4.3 %collective-permute-start.11 = (f32[2,2,16,2,128]{4,3,2,1,0:T(2,128)S(1)}, f32[2,2,16,2,128]{4,3,2,1,0:T(2,128)S(1)}, u32[]{:S(2)}, u32[]{:S(2)}) collective-permute-start(f32[2,2,16,2,128]{4,3,2,1,0:T(2,128)S(1)} %get-tuple-element.79), channel_id=1, source_target_pairs={{1,0},{0,1},{3,2},{2,3},{5,4},{4,5},{7,6},{6,7},{9,8},{8,9},{11,10... | collective-permute-start | bytes 196616 | tf_op jit(solution)/shard_map/ppermute | solution.py:124
  45.0 8.6 %collective-permute-start.12 = (f32[2,2,2,32,128]{4,3,2,1,0:T(8,128)S(1)}, f32[2,2,2,32,128]{4,3,2,1,0:T(8,128)S(1)}, u32[]{:S(2)}, u32[]{:S(2)}) collective-permute-start(f32[2,2,2,32,128]{4,3,2,1,0:T(8,128)S(1)} %get-tuple-element.68), channel_id=1, source_target_pairs={{0,16},{16,18},{18,2},{2,4},{4,20},{20,22},{22,6},{6,8},{8,24},{24... | collective-permute-start | bytes 393224 | tf_op jit(solution)/shard_map/ppermute | solution.py:123
  45.1 8.5 %collective-permute-start.13 = (f32[2,2,2,32,128]{4,3,2,1,0:T(8,128)S(1)}, f32[2,2,2,32,128]{4,3,2,1,0:T(8,128)S(1)}, u32[]{:S(2)}, u32[]{:S(2)}) collective-permute-start(f32[2,2,2,32,128]{4,3,2,1,0:T(8,128)S(1)} %get-tuple-element.69), channel_id=1, source_target_pairs={{16,0},{18,16},{2,18},{4,2},{20,4},{22,20},{6,22},{8,6},{24,8},{26... | collective-permute-start | bytes 393224 | tf_op jit(solution)/shard_map/ppermute | solution.py:124
  48.6 4.3 %collective-permute-start.14 = (f32[2,2,16,2,128]{4,3,2,1,0:T(2,128)S(1)}, f32[2,2,16,2,128]{4,3,2,1,0:T(2,128)S(1)}, u32[]{:S(2)}, u32[]{:S(2)}) collective-permute-start(f32[2,2,16,2,128]{4,3,2,1,0:T(2,128)S(1)} %get-tuple-element.70), channel_id=1, source_target_pairs={{0,1},{1,0},{2,3},{3,2},{4,5},{5,4},{6,7},{7,6},{8,9},{9,8},{10,11... | collective-permute-start | bytes 196616 | tf_op jit(solution)/shard_map/ppermute | solution.py:123
  49.3 4.3 %collective-permute-start.15 = (f32[2,2,16,2,128]{4,3,2,1,0:T(2,128)S(1)}, f32[2,2,16,2,128]{4,3,2,1,0:T(2,128)S(1)}, u32[]{:S(2)}, u32[]{:S(2)}) collective-permute-start(f32[2,2,16,2,128]{4,3,2,1,0:T(2,128)S(1)} %get-tuple-element.71), channel_id=1, source_target_pairs={{1,0},{0,1},{3,2},{2,3},{5,4},{4,5},{7,6},{6,7},{9,8},{8,9},{11,10... | collective-permute-start | bytes 196616 | tf_op jit(solution)/shard_map/ppermute | solution.py:124
  57.4 9.2 %collective-permute-start.16 = (f32[2,2,2,32,128]{4,3,2,1,0:T(8,128)S(1)}, f32[2,2,2,32,128]{4,3,2,1,0:T(8,128)S(1)}, u32[]{:S(2)}, u32[]{:S(2)}) collective-permute-start(f32[2,2,2,32,128]{4,3,2,1,0:T(8,128)S(1)} %get-tuple-element.60), channel_id=1, source_target_pairs={{0,16},{16,18},{18,2},{2,4},{4,20},{20,22},{22,6},{6,8},{8,24},{24... | collective-permute-start | bytes 393224 | tf_op jit(solution)/shard_map/ppermute | solution.py:123
  57.5 9.1 %collective-permute-start.17 = (f32[2,2,2,32,128]{4,3,2,1,0:T(8,128)S(1)}, f32[2,2,2,32,128]{4,3,2,1,0:T(8,128)S(1)}, u32[]{:S(2)}, u32[]{:S(2)}) collective-permute-start(f32[2,2,2,32,128]{4,3,2,1,0:T(8,128)S(1)} %get-tuple-element.61), channel_id=1, source_target_pairs={{16,0},{18,16},{2,18},{4,2},{20,4},{22,20},{6,22},{8,6},{24,8},{26... | collective-permute-start | bytes 393224 | tf_op jit(solution)/shard_map/ppermute | solution.py:124
  61.0 4.3 %collective-permute-start.18 = (f32[2,2,16,2,128]{4,3,2,1,0:T(2,128)S(1)}, f32[2,2,16,2,128]{4,3,2,1,0:T(2,128)S(1)}, u32[]{:S(2)}, u32[]{:S(2)}) collective-permute-start(f32[2,2,16,2,128]{4,3,2,1,0:T(2,128)S(1)} %get-tuple-element.62), channel_id=1, source_target_pairs={{0,1},{1,0},{2,3},{3,2},{4,5},{5,4},{6,7},{7,6},{8,9},{9,8},{10,11... | collective-permute-start | bytes 196616 | tf_op jit(solution)/shard_map/ppermute | solution.py:123
  70.5 8.6 %collective-permute-start.20 = (f32[2,2,2,32,128]{4,3,2,1,0:T(8,128)S(1)}, f32[2,2,2,32,128]{4,3,2,1,0:T(8,128)S(1)}, u32[]{:S(2)}, u32[]{:S(2)}) collective-permute-start(f32[2,2,2,32,128]{4,3,2,1,0:T(8,128)S(1)} %get-tuple-element.52), channel_id=1, source_target_pairs={{0,16},{16,18},{18,2},{2,4},{4,20},{20,22},{22,6},{6,8},{8,24},{24... | collective-permute-start | bytes 393224 | tf_op jit(solution)/shard_map/ppermute | solution.py:123
  70.6 8.5 %collective-permute-start.21 = (f32[2,2,2,32,128]{4,3,2,1,0:T(8,128)S(1)}, f32[2,2,2,32,128]{4,3,2,1,0:T(8,128)S(1)}, u32[]{:S(2)}, u32[]{:S(2)}) collective-permute-start(f32[2,2,2,32,128]{4,3,2,1,0:T(8,128)S(1)} %get-tuple-element.53), channel_id=1, source_target_pairs={{16,0},{18,16},{2,18},{4,2},{20,4},{22,20},{6,22},{8,6},{24,8},{26... | collective-permute-start | bytes 393224 | tf_op jit(solution)/shard_map/ppermute | solution.py:124
  83.0 9.2 %collective-permute-start.24 = (f32[2,2,2,32,128]{4,3,2,1,0:T(8,128)S(1)}, f32[2,2,2,32,128]{4,3,2,1,0:T(8,128)S(1)}, u32[]{:S(2)}, u32[]{:S(2)}) collective-permute-start(f32[2,2,2,32,128]{4,3,2,1,0:T(8,128)S(1)} %get-tuple-element.44), channel_id=1, source_target_pairs={{0,16},{16,18},{18,2},{2,4},{4,20},{20,22},{22,6},{6,8},{8,24},{24... | collective-permute-start | bytes 393224 | tf_op jit(solution)/shard_map/ppermute | solution.py:123
  83.0 9.1 %collective-permute-start.25 = (f32[2,2,2,32,128]{4,3,2,1,0:T(8,128)S(1)}, f32[2,2,2,32,128]{4,3,2,1,0:T(8,128)S(1)}, u32[]{:S(2)}, u32[]{:S(2)}) collective-permute-start(f32[2,2,2,32,128]{4,3,2,1,0:T(8,128)S(1)} %get-tuple-element.45), channel_id=1, source_target_pairs={{16,0},{18,16},{2,18},{4,2},{20,4},{22,20},{6,22},{8,6},{24,8},{26... | collective-permute-start | bytes 393224 | tf_op jit(solution)/shard_map/ppermute | solution.py:124
  96.0 8.6 %collective-permute-start.28 = (f32[2,2,2,32,128]{4,3,2,1,0:T(8,128)S(1)}, f32[2,2,2,32,128]{4,3,2,1,0:T(8,128)S(1)}, u32[]{:S(2)}, u32[]{:S(2)}) collective-permute-start(f32[2,2,2,32,128]{4,3,2,1,0:T(8,128)S(1)} %get-tuple-element.36), channel_id=1, source_target_pairs={{0,16},{16,18},{18,2},{2,4},{4,20},{20,22},{22,6},{6,8},{8,24},{24... | collective-permute-start | bytes 393224 | tf_op jit(solution)/shard_map/ppermute | solution.py:123
  96.1 8.5 %collective-permute-start.29 = (f32[2,2,2,32,128]{4,3,2,1,0:T(8,128)S(1)}, f32[2,2,2,32,128]{4,3,2,1,0:T(8,128)S(1)}, u32[]{:S(2)}, u32[]{:S(2)}) collective-permute-start(f32[2,2,2,32,128]{4,3,2,1,0:T(8,128)S(1)} %get-tuple-element.37), channel_id=1, source_target_pairs={{16,0},{18,16},{2,18},{4,2},{20,4},{22,20},{6,22},{8,6},{24,8},{26... | collective-permute-start | bytes 393224 | tf_op jit(solution)/shard_map/ppermute | solution.py:124
  99.6 4.3 %collective-permute-start.30 = (f32[2,2,16,2,128]{4,3,2,1,0:T(2,128)S(1)}, f32[2,2,16,2,128]{4,3,2,1,0:T(2,128)S(1)}, u32[]{:S(2)}, u32[]{:S(2)}) collective-permute-start(f32[2,2,16,2,128]{4,3,2,1,0:T(2,128)S(1)} %get-tuple-element.38), channel_id=1, source_target_pairs={{0,1},{1,0},{2,3},{3,2},{4,5},{5,4},{6,7},{7,6},{8,9},{9,8},{10,11... | collective-permute-start | bytes 196616 | tf_op jit(solution)/shard_map/ppermute | solution.py:123
  100.3 4.3 %collective-permute-start.31 = (f32[2,2,16,2,128]{4,3,2,1,0:T(2,128)S(1)}, f32[2,2,16,2,128]{4,3,2,1,0:T(2,128)S(1)}, u32[]{:S(2)}, u32[]{:S(2)}) collective-permute-start(f32[2,2,16,2,128]{4,3,2,1,0:T(2,128)S(1)} %get-tuple-element.39), channel_id=1, source_target_pairs={{1,0},{0,1},{3,2},{2,3},{5,4},{4,5},{7,6},{6,7},{9,8},{8,9},{11,10... | collective-permute-start | bytes 196616 | tf_op jit(solution)/shard_map/ppermute | solution.py:124
  108.5 9.2 %collective-permute-start.32 = (f32[2,2,2,32,128]{4,3,2,1,0:T(8,128)S(1)}, f32[2,2,2,32,128]{4,3,2,1,0:T(8,128)S(1)}, u32[]{:S(2)}, u32[]{:S(2)}) collective-permute-start(f32[2,2,2,32,128]{4,3,2,1,0:T(8,128)S(1)} %get-tuple-element.28), channel_id=1, source_target_pairs={{0,16},{16,18},{18,2},{2,4},{4,20},{20,22},{22,6},{6,8},{8,24},{24... | collective-permute-start | bytes 393224 | tf_op jit(solution)/shard_map/ppermute | solution.py:123
  108.6 9.1 %collective-permute-start.33 = (f32[2,2,2,32,128]{4,3,2,1,0:T(8,128)S(1)}, f32[2,2,2,32,128]{4,3,2,1,0:T(8,128)S(1)}, u32[]{:S(2)}, u32[]{:S(2)}) collective-permute-start(f32[2,2,2,32,128]{4,3,2,1,0:T(8,128)S(1)} %get-tuple-element.29), channel_id=1, source_target_pairs={{16,0},{18,16},{2,18},{4,2},{20,4},{22,20},{6,22},{8,6},{24,8},{26... | collective-permute-start | bytes 393224 | tf_op jit(solution)/shard_map/ppermute | solution.py:124
  113.5 4.3 %collective-permute-start.35 = (f32[2,2,16,2,128]{4,3,2,1,0:T(2,128)S(1)}, f32[2,2,16,2,128]{4,3,2,1,0:T(2,128)S(1)}, u32[]{:S(2)}, u32[]{:S(2)}) collective-permute-start(f32[2,2,16,2,128]{4,3,2,1,0:T(2,128)S(1)} %get-tuple-element.31), channel_id=1, source_target_pairs={{1,0},{0,1},{3,2},{2,3},{5,4},{4,5},{7,6},{6,7},{9,8},{8,9},{11,10... | collective-permute-start | bytes 196616 | tf_op jit(solution)/shard_map/ppermute | solution.py:124
  114.4 11.1 %collective-permute-start.37 = (f32[1,2,16,32,128]{4,3,2,1,0:T(8,128)S(1)}, f32[1,2,16,32,128]{4,3,2,1,0:T(8,128)S(1)}, u32[]{:S(2)}, u32[]{:S(2)}) collective-permute-start(f32[1,2,16,32,128]{4,3,2,1,0:T(8,128)S(1)} %slice.1070), channel_id=1, source_target_pairs={{16,0},{17,1},{18,2},{19,3},{20,4},{21,5},{22,6},{23,7},{24,8},{25... | collective-permute-start | bytes 1572872 | tf_op jit(solution)/shard_map/ppermute | solution.py:224
  120.8 9.3 %collective-permute-start.36 = (f32[1,2,16,32,128]{4,3,2,1,0:T(8,128)S(1)}, f32[1,2,16,32,128]{4,3,2,1,0:T(8,128)S(1)}, u32[]{:S(2)}, u32[]{:S(2)}) collective-permute-start(f32[1,2,16,32,128]{4,3,2,1,0:T(8,128)S(1)} %convolution_bitcast_fusion.7), channel_id=1, source_target_pairs={{0,16},{1,17},{2,18},{3,19},{4,20},{5,21},{6,22},{7,23},{8,24},{9,... | collective-permute-start | bytes 1572872 | tf_op jit(solution)/shard_map/ppermute | solution.py:224
  (14 other events, 48.2 us)

commit v9 on v6

--- a/solution.py
+++ b/solution.py
@@ -130,8 +130,29 @@
     return before, after
 
 
-def tendency(state, wind):
-    west, east = ring_halo(state, ("corr", "tx"), x_ring(), 2, 2)
+def swap_halo(block, axes, order, parity, dim, width):
+    size = len(order)
+    length = block.shape[dim]
+    last = lax.slice_in_dim(block, length - width, length, axis=dim)
+    first = lax.slice_in_dim(block, 0, width, axis=dim)
+    got = []
+    for offset in range(2):
+        pairs = []
+        for g in range(offset, size, 2):
+            pairs += [(order[g], order[(g + 1) % size]), (order[(g + 1) % size], order[g])]
+        sent = jnp.where(parity == offset, last, first)
+        got.append(lax.ppermute(sent, axes, pairs))
+    before = jnp.where(parity == 0, got[1], got[0])
+    after = jnp.where(parity == 0, got[0], got[1])
+    return before, after
+
+
+def tendency(state, wind, parity):
+    ring = x_ring()
+    if len(ring) % 2 == 0:
+        west, east = swap_halo(state, ("corr", "tx"), ring, parity, 2, 2)
+    else:
+        west, east = ring_halo(state, ("corr", "tx"), ring, 2, 2)
     south, north = ring_halo(state, ("ty",), list(range(lax.axis_size("ty"))), 3, 2)
     px = jnp.concatenate([west, state, east], 2)
     py = jnp.concatenate([south, state, north], 3)
@@ -175,6 +196,7 @@
     me = lax.axis_index("corr")
     tile = lax.axis_index("tx")
     start = slab_of(me, tile, depth) * slab
+    parity = (tile * depth + slab_of(me, tile, depth)) % 2
     own_fields = lax.dynamic_slice_in_dim(fields, start, slab, 1)
     own_wind = lax.dynamic_slice_in_dim(wind, start, slab, 1)
 
@@ -188,7 +210,7 @@
             if 0 <= k - l < STEPS or (k - l == STEPS and l < depth - 1)
         ]
         stacked = jnp.stack([states[l] for l in active], 0)
-        own_e = tendency(stacked, own_wind)
+        own_e = tendency(stacked, own_wind, parity)
         feeds = [l for l in active if l < depth - 1]
         if feeds:
             lows = [active.index(l) for l in feeds]

time: 122 us -> 120 us (0.984)
  starting transfers between devices: 45.4 us -> 26.1 us
  waiting for transfers between devices: 32.8 us -> 49.4 us
    ppermute x18, starting transfers between devices: 31.4 us -> 14.1 us  [swap_halo(): got.append(lax.ppermute(sent, axes, pairs))]
    ppermute x9, waiting for transfers between devices: 8.78 us -> 20.2 us  [ring_halo(): got = lax.ppermute(jnp.concatenate([first, last], dim), axes, up)]
    ppermute x18, waiting for transfers between devices: 17.7 us -> 20.8 us  [swap_halo(): got.append(lax.ppermute(sent, axes, pairs))]
    ppermute x2, waiting for transfers between devices: 6.35 us -> 8.34 us  [on_device(): arrived = lax.ppermute(states[level][None], 'corr', pairs)]
    ppermute x2, starting transfers between devices: 4.33 us -> 2.76 us  [on_device(): arrived = lax.ppermute(states[level][None], 'corr', pairs)]
  transfers between devices with their start and end apart: 29 -> 29, of which waited for: 16 -> 21; matrix products, arithmetic and copies ran while one was open for 6% -> 6% of each run, Pallas kernels for 2% -> 2%
where the time goes in v9:
time: 120 us
  waiting for transfers between devices  49.4 us (41%)
  other arithmetic  26.5 us (22%)
  starting transfers between devices  26.1 us (22%)
  matrix products  9.01 us (8%)
  local copies, waits for them, and re-layouts  5.2 us (4%)
  Pallas kernels  2.94 us (2%)
    ppermute x18, waiting for transfers between devices, swap_halo(): got.append(lax.ppermute(sent, axes, pairs))  20.8 us
    ppermute x9, waiting for transfers between devices, ring_halo(): got = lax.ppermute(jnp.concatenate([first, last], dim), axes, up)  20.2 us
    mul x9, other arithmetic, tendency(): return DT * (flow + kappa * laplace + react)  15.1 us
    ppermute x18, starting transfers between devices, swap_halo(): got.append(lax.ppermute(sent, axes, pairs))  14.1 us
    ppermute x9, starting transfers between devices, ring_halo(): got = lax.ppermute(jnp.concatenate([first, last], dim), axes, up)  9.19 us
    dot_general x9, matrix products, column_solve(): jnp.einsum('lsxyk,sjk->lsxyj', rhs, inverse, precision=lax.Precision.HIGH...  9.01 us
    ppermute x2, waiting for transfers between devices, on_device(): arrived = lax.ppermute(states[level][None], 'corr', pairs)  8.34 us
    add x5, other arithmetic, on_device(): total = total + (quad + g_now[l - 1] - e_hist[l - 1][m])  3.65 us
  transfers between devices with their start and end apart: 29, of which 21 were waited for; matrix products, arithmetic and copies ran while one was open for 6% of the time, Pallas kernels for 2%

profile of v9, /device:TPU:0, one launch (start us, length us, event | category | flops | bytes accessed | tf_op | source)
XLA Modules:
  0.0 119.8 jit_solution(4777094418309617542)
XLA Ops:
  1.1 4.6 %collective-permute-start = (f32[1,2,2,32,128]{4,3,2,1,0:T(8,128)S(1)}, f32[1,2,2,32,128]{4,3,2,1,0:T(8,128)S(1)}, u32[]{:S(2)}, u32[]{:S(2)}) collective-permute-start(f32[1,2,2,32,128]{4,3,2,1,0:T(8,128)S(1)} %get-tuple-element.98), channel_id=1, source_target_pairs={{16,18},{18,16},{2,4},{4,2},{20,22},{22,20},{6,8},{8,6},{24,26},{2... | collective-permute-start | bytes 196616 | tf_op jit(solution)/shard_map/ppermute | solution.py:144
  5.7 1.6 %collective-permute-start.2 = (f32[1,2,16,4,128]{4,3,2,1,0:T(4,128)S(1)}, f32[1,2,16,4,128]{4,3,2,1,0:T(4,128)S(1)}, u32[]{:S(2)}, u32[]{:S(2)}) collective-permute-start(f32[1,2,16,4,128]{4,3,2,1,0:T(4,128)S(1)} %pad_maximum_fusion.43), channel_id=1, source_target_pairs={{0,1},{1,0},{2,3},{3,2},{4,5},{5,4},{6,7},{7,6},{8,9},{9,8},{10,11... | collective-permute-start | bytes 196616 | tf_op jit(solution)/shard_map/ppermute | solution.py:124
  9.4 2.9 %shard_map.118 = f32[128,2,128]{2,1,0:T(2,128)} custom-call(f32[2,128]{1,0:T(2,128)} %copy-done.3, f32[2,128]{1,0:T(2,128)} %get-tuple-element.141.low_ref), custom_call_target="tpu_custom_call" | custom-call | flops 393216 | bytes 262144 | tf_op jit(solution)/shard_map/pallas_call | solution.py:78
  15.3 1.7 %collective-permute-start.3 = (f32[2,2,2,32,128]{4,3,2,1,0:T(8,128)S(1)}, f32[2,2,2,32,128]{4,3,2,1,0:T(8,128)S(1)}, u32[]{:S(2)}, u32[]{:S(2)}) collective-permute-start(f32[2,2,2,32,128]{4,3,2,1,0:T(8,128)S(1)} %get-tuple-element.85), channel_id=1, source_target_pairs={{16,18},{18,16},{2,4},{4,2},{20,22},{22,20},{6,8},{8,6},{24,26},{2... | collective-permute-start | bytes 393224 | tf_op jit(solution)/shard_map/ppermute | solution.py:144
  18.3 3.6 %collective-permute-done.3 = f32[2,2,2,32,128]{4,3,2,1,0:T(8,128)S(1)} collective-permute-done((f32[2,2,2,32,128]{4,3,2,1,0:T(8,128)S(1)}, f32[2,2,2,32,128]{4,3,2,1,0:T(8,128)S(1)}, u32[]{:S(2)}, u32[]{:S(2)}) %collective-permute-start.3) | collective-permute-done | bytes 131104 | tf_op jit(solution)/shard_map/ppermute | solution.py:144
  29.1 3.4 %collective-permute-done.8 = f32[2,2,16,4,128]{4,3,2,1,0:T(4,128)S(1)} collective-permute-done((f32[2,2,16,4,128]{4,3,2,1,0:T(4,128)S(1)}, f32[2,2,16,4,128]{4,3,2,1,0:T(4,128)S(1)}, u32[]{:S(2)}, u32[]{:S(2)}) %collective-permute-start.8) | collective-permute-done | bytes 131104 | tf_op jit(solution)/shard_map/ppermute | solution.py:124
  32.5 1.8 %collective-permute-done.6 = f32[2,2,2,32,128]{4,3,2,1,0:T(8,128)S(1)} collective-permute-done((f32[2,2,2,32,128]{4,3,2,1,0:T(8,128)S(1)}, f32[2,2,2,32,128]{4,3,2,1,0:T(8,128)S(1)}, u32[]{:S(2)}, u32[]{:S(2)}) %collective-permute-start.6) | collective-permute-done | bytes 131104 | tf_op jit(solution)/shard_map/ppermute | solution.py:144
  34.3 1.8 %fusion.37 = f32[2,2,16,32,128]{4,3,2,1,0:T(8,128)S(1)} fusion(f32[2,1,16,32,128]{4,3,2,1,0:T(8,128)S(1)} %get-tuple-element.81, f32[2,1,16,32,128]{4,3,2,1,0:T(8,128)S(1)} %get-tuple-element.80, f32[2,2,16,32,128]{4,3,2,1,0:T(8,128)S(1)} %convolution_bitcast_fusion.6, f32[2,2,16,2,128]{4,3,2,1,0:T(2,128)S(1)} %get-tuple-element.133, ...), kind=kLoop, calls=%fused_computation.148 | loop fusion | flops 9175040 | bytes 4063240 | tf_op jit(solution)/shard_map/mul | solution.py:182
  38.4 1.6 %collective-permute-start.11 = (f32[2,2,16,4,128]{4,3,2,1,0:T(4,128)S(1)}, f32[2,2,16,4,128]{4,3,2,1,0:T(4,128)S(1)}, u32[]{:S(2)}, u32[]{:S(2)}) collective-permute-start(f32[2,2,16,4,128]{4,3,2,1,0:T(4,128)S(1)} %pad_maximum_fusion.37), channel_id=1, source_target_pairs={{0,1},{1,0},{2,3},{3,2},{4,5},{5,4},{6,7},{7,6},{8,9},{9,8},{10,11... | collective-permute-start | bytes 393224 | tf_op jit(solution)/shard_map/ppermute | solution.py:124
  41.8 1.7 %collective-permute-done.11 = f32[2,2,16,4,128]{4,3,2,1,0:T(4,128)S(1)} collective-permute-done((f32[2,2,16,4,128]{4,3,2,1,0:T(4,128)S(1)}, f32[2,2,16,4,128]{4,3,2,1,0:T(4,128)S(1)}, u32[]{:S(2)}, u32[]{:S(2)}) %collective-permute-start.11) | collective-permute-done | bytes 131104 | tf_op jit(solution)/shard_map/ppermute | solution.py:124
  43.5 1.5 %collective-permute-done.10 = f32[2,2,2,32,128]{4,3,2,1,0:T(8,128)S(1)} collective-permute-done((f32[2,2,2,32,128]{4,3,2,1,0:T(8,128)S(1)}, f32[2,2,2,32,128]{4,3,2,1,0:T(8,128)S(1)}, u32[]{:S(2)}, u32[]{:S(2)}) %collective-permute-start.10) | collective-permute-done | bytes 131104 | tf_op jit(solution)/shard_map/ppermute | solution.py:144
  45.1 1.9 %collective-permute-done.9 = f32[2,2,2,32,128]{4,3,2,1,0:T(8,128)S(1)} collective-permute-done((f32[2,2,2,32,128]{4,3,2,1,0:T(8,128)S(1)}, f32[2,2,2,32,128]{4,3,2,1,0:T(8,128)S(1)}, u32[]{:S(2)}, u32[]{:S(2)}) %collective-permute-start.9) | collective-permute-done | bytes 131104 | tf_op jit(solution)/shard_map/ppermute | solution.py:144
  47.0 2.0 %fusion.41 = f32[2,2,16,32,128]{4,3,2,1,0:T(8,128)S(1)} fusion(f32[2,1,16,32,128]{4,3,2,1,0:T(8,128)S(1)} %get-tuple-element.73, f32[2,1,16,32,128]{4,3,2,1,0:T(8,128)S(1)} %get-tuple-element.72, f32[2,2,16,32,128]{4,3,2,1,0:T(8,128)S(1)} %convolution_bitcast_fusion.5, f32[2,2,16,2,128]{4,3,2,1,0:T(2,128)S(1)} %get-tuple-element.131, ...), kind=kLoop, calls=%fused_computation.153 | loop fusion | flops 9175040 | bytes 4063240 | tf_op jit(solution)/shard_map/mul | solution.py:182
  52.7 3.6 %collective-permute-done.14 = f32[2,2,16,4,128]{4,3,2,1,0:T(4,128)S(1)} collective-permute-done((f32[2,2,16,4,128]{4,3,2,1,0:T(4,128)S(1)}, f32[2,2,16,4,128]{4,3,2,1,0:T(4,128)S(1)}, u32[]{:S(2)}, u32[]{:S(2)}) %collective-permute-start.14) | collective-permute-done | bytes 131104 | tf_op jit(solution)/shard_map/ppermute | solution.py:124
  56.4 1.8 %collective-permute-done.12 = f32[2,2,2,32,128]{4,3,2,1,0:T(8,128)S(1)} collective-permute-done((f32[2,2,2,32,128]{4,3,2,1,0:T(8,128)S(1)}, f32[2,2,2,32,128]{4,3,2,1,0:T(8,128)S(1)}, u32[]{:S(2)}, u32[]{:S(2)}) %collective-permute-start.12) | collective-permute-done | bytes 131104 | tf_op jit(solution)/shard_map/ppermute | solution.py:144
  58.2 1.8 %fusion.45 = f32[2,2,16,32,128]{4,3,2,1,0:T(8,128)S(1)} fusion(f32[2,1,16,32,128]{4,3,2,1,0:T(8,128)S(1)} %get-tuple-element.65, f32[2,1,16,32,128]{4,3,2,1,0:T(8,128)S(1)} %get-tuple-element.64, f32[2,2,16,32,128]{4,3,2,1,0:T(8,128)S(1)} %convolution_bitcast_fusion.4, f32[2,2,16,2,128]{4,3,2,1,0:T(2,128)S(1)} %get-tuple-element.129, ...), kind=kLoop, calls=%fused_computation.158 | loop fusion | flops 9175040 | bytes 4063240 | tf_op jit(solution)/shard_map/mul | solution.py:182
  62.4 1.6 %collective-permute-start.17 = (f32[2,2,16,4,128]{4,3,2,1,0:T(4,128)S(1)}, f32[2,2,16,4,128]{4,3,2,1,0:T(4,128)S(1)}, u32[]{:S(2)}, u32[]{:S(2)}) collective-permute-start(f32[2,2,16,4,128]{4,3,2,1,0:T(4,128)S(1)} %pad_maximum_fusion.39), channel_id=1, source_target_pairs={{0,1},{1,0},{2,3},{3,2},{4,5},{5,4},{6,7},{7,6},{8,9},{9,8},{10,11... | collective-permute-start | bytes 393224 | tf_op jit(solution)/shard_map/ppermute | solution.py:124
  64.9 2.5 %collective-permute-done.17 = f32[2,2,16,4,128]{4,3,2,1,0:T(4,128)S(1)} collective-permute-done((f32[2,2,16,4,128]{4,3,2,1,0:T(4,128)S(1)}, f32[2,2,16,4,128]{4,3,2,1,0:T(4,128)S(1)}, u32[]{:S(2)}, u32[]{:S(2)}) %collective-permute-start.17) | collective-permute-done | bytes 131104 | tf_op jit(solution)/shard_map/ppermute | solution.py:124
  67.5 2.8 %collective-permute-done.15 = f32[2,2,2,32,128]{4,3,2,1,0:T(8,128)S(1)} collective-permute-done((f32[2,2,2,32,128]{4,3,2,1,0:T(8,128)S(1)}, f32[2,2,2,32,128]{4,3,2,1,0:T(8,128)S(1)}, u32[]{:S(2)}, u32[]{:S(2)}) %collective-permute-start.15) | collective-permute-done | bytes 131104 | tf_op jit(solution)/shard_map/ppermute | solution.py:144
  70.3 1.8 %fusion.49 = f32[2,2,16,32,128]{4,3,2,1,0:T(8,128)S(1)} fusion(f32[2,1,16,32,128]{4,3,2,1,0:T(8,128)S(1)} %get-tuple-element.57, f32[2,1,16,32,128]{4,3,2,1,0:T(8,128)S(1)} %get-tuple-element.56, f32[2,2,16,32,128]{4,3,2,1,0:T(8,128)S(1)} %convolution_bitcast_fusion.3, f32[2,2,16,2,128]{4,3,2,1,0:T(2,128)S(1)} %get-tuple-element.127, ...), kind=kLoop, calls=%fused_computation.163 | loop fusion | flops 9175040 | bytes 4063240 | tf_op jit(solution)/shard_map/mul | solution.py:182
  76.0 3.5 %collective-permute-done.20 = f32[2,2,16,4,128]{4,3,2,1,0:T(4,128)S(1)} collective-permute-done((f32[2,2,16,4,128]{4,3,2,1,0:T(4,128)S(1)}, f32[2,2,16,4,128]{4,3,2,1,0:T(4,128)S(1)}, u32[]{:S(2)}, u32[]{:S(2)}) %collective-permute-start.20) | collective-permute-done | bytes 131104 | tf_op jit(solution)/shard_map/ppermute | solution.py:124
  79.5 1.8 %collective-permute-done.18 = f32[2,2,2,32,128]{4,3,2,1,0:T(8,128)S(1)} collective-permute-done((f32[2,2,2,32,128]{4,3,2,1,0:T(8,128)S(1)}, f32[2,2,2,32,128]{4,3,2,1,0:T(8,128)S(1)}, u32[]{:S(2)}, u32[]{:S(2)}) %collective-permute-start.18) | collective-permute-done | bytes 131104 | tf_op jit(solution)/shard_map/ppermute | solution.py:144
  81.3 2.1 %fusion.53 = f32[2,2,16,32,128]{4,3,2,1,0:T(8,128)S(1)} fusion(f32[2,1,16,32,128]{4,3,2,1,0:T(8,128)S(1)} %get-tuple-element.49, f32[2,1,16,32,128]{4,3,2,1,0:T(8,128)S(1)} %get-tuple-element.48, f32[2,2,16,32,128]{4,3,2,1,0:T(8,128)S(1)} %convolution_bitcast_fusion.2, f32[2,2,16,2,128]{4,3,2,1,0:T(2,128)S(1)} %get-tuple-element.125, ...), kind=kLoop, calls=%fused_computation.168 | loop fusion | flops 9175040 | bytes 4063240 | tf_op jit(solution)/shard_map/mul | solution.py:182
  85.7 1.6 %collective-permute-start.23 = (f32[2,2,16,4,128]{4,3,2,1,0:T(4,128)S(1)}, f32[2,2,16,4,128]{4,3,2,1,0:T(4,128)S(1)}, u32[]{:S(2)}, u32[]{:S(2)}) collective-permute-start(f32[2,2,16,4,128]{4,3,2,1,0:T(4,128)S(1)} %pad_maximum_fusion.41), channel_id=1, source_target_pairs={{0,1},{1,0},{2,3},{3,2},{4,5},{5,4},{6,7},{7,6},{8,9},{9,8},{10,11... | collective-permute-start | bytes 393224 | tf_op jit(solution)/shard_map/ppermute | solution.py:124
  88.2 2.5 %collective-permute-done.23 = f32[2,2,16,4,128]{4,3,2,1,0:T(4,128)S(1)} collective-permute-done((f32[2,2,16,4,128]{4,3,2,1,0:T(4,128)S(1)}, f32[2,2,16,4,128]{4,3,2,1,0:T(4,128)S(1)}, u32[]{:S(2)}, u32[]{:S(2)}) %collective-permute-start.23) | collective-permute-done | bytes 131104 | tf_op jit(solution)/shard_map/ppermute | solution.py:124
  90.7 2.8 %collective-permute-done.21 = f32[2,2,2,32,128]{4,3,2,1,0:T(8,128)S(1)} collective-permute-done((f32[2,2,2,32,128]{4,3,2,1,0:T(8,128)S(1)}, f32[2,2,2,32,128]{4,3,2,1,0:T(8,128)S(1)}, u32[]{:S(2)}, u32[]{:S(2)}) %collective-permute-start.21) | collective-permute-done | bytes 131104 | tf_op jit(solution)/shard_map/ppermute | solution.py:144
  93.6 1.8 %fusion.57 = f32[2,2,16,32,128]{4,3,2,1,0:T(8,128)S(1)} fusion(f32[2,1,16,32,128]{4,3,2,1,0:T(8,128)S(1)} %get-tuple-element.41, f32[2,1,16,32,128]{4,3,2,1,0:T(8,128)S(1)} %get-tuple-element.40, f32[2,2,16,32,128]{4,3,2,1,0:T(8,128)S(1)} %convolution_bitcast_fusion.1, f32[2,2,16,2,128]{4,3,2,1,0:T(2,128)S(1)} %get-tuple-element.123, ...), kind=kLoop, calls=%fused_computation.173 | loop fusion | flops 9175040 | bytes 4063240 | tf_op jit(solution)/shard_map/mul | solution.py:182
  100.6 2.2 %collective-permute-done.26 = f32[2,2,16,4,128]{4,3,2,1,0:T(4,128)S(1)} collective-permute-done((f32[2,2,16,4,128]{4,3,2,1,0:T(4,128)S(1)}, f32[2,2,16,4,128]{4,3,2,1,0:T(4,128)S(1)}, u32[]{:S(2)}, u32[]{:S(2)}) %collective-permute-start.26) | collective-permute-done | bytes 131104 | tf_op jit(solution)/shard_map/ppermute | solution.py:124
  102.9 1.8 %collective-permute-done.24 = f32[2,2,2,32,128]{4,3,2,1,0:T(8,128)S(1)} collective-permute-done((f32[2,2,2,32,128]{4,3,2,1,0:T(8,128)S(1)}, f32[2,2,2,32,128]{4,3,2,1,0:T(8,128)S(1)}, u32[]{:S(2)}, u32[]{:S(2)}) %collective-permute-start.24) | collective-permute-done | bytes 131104 | tf_op jit(solution)/shard_map/ppermute | solution.py:144
  105.7 1.8 %fusion.61 = f32[2,2,16,32,128]{4,3,2,1,0:T(8,128)S(1)} fusion(f32[2,1,16,32,128]{4,3,2,1,0:T(8,128)S(1)} %get-tuple-element.33, f32[2,1,16,32,128]{4,3,2,1,0:T(8,128)S(1)} %get-tuple-element.32, f32[2,2,16,32,128]{4,3,2,1,0:T(8,128)S(1)} %convolution_bitcast_fusion, f32[2,2,16,2,128]{4,3,2,1,0:T(2,128)S(1)} %get-tuple-element.121, ...), kind=kLoop, calls=%fused_computation.178 | loop fusion | flops 9175040 | bytes 4063240 | tf_op jit(solution)/shard_map/mul | solution.py:182
  110.6 4.9 %collective-permute-done.28 = f32[1,2,16,32,128]{4,3,2,1,0:T(8,128)S(1)} collective-permute-done((f32[1,2,16,32,128]{4,3,2,1,0:T(8,128)S(1)}, f32[1,2,16,32,128]{4,3,2,1,0:T(8,128)S(1)}, u32[]{:S(2)}, u32[]{:S(2)}) %collective-permute-start.28) | collective-permute-done | bytes 524320 | tf_op jit(solution)/shard_map/ppermute | solution.py:251
  115.5 3.5 %collective-permute-done.27 = f32[1,2,16,32,128]{4,3,2,1,0:T(8,128)S(1)} collective-permute-done((f32[1,2,16,32,128]{4,3,2,1,0:T(8,128)S(1)}, f32[1,2,16,32,128]{4,3,2,1,0:T(8,128)S(1)}, u32[]{:S(2)}, u32[]{:S(2)}) %collective-permute-start.27) | collective-permute-done | bytes 524320 | tf_op jit(solution)/shard_map/ppermute | solution.py:251
  (145 shorter events, 43.0 us)
Async XLA Ops:
  1.1 12.4 %collective-permute-start = (f32[1,2,2,32,128]{4,3,2,1,0:T(8,128)S(1)}, f32[1,2,2,32,128]{4,3,2,1,0:T(8,128)S(1)}, u32[]{:S(2)}, u32[]{:S(2)}) collective-permute-start(f32[1,2,2,32,128]{4,3,2,1,0:T(8,128)S(1)} %get-tuple-element.98), channel_id=1, source_target_pairs={{16,18},{18,16},{2,4},{4,2},{20,22},{22,20},{6,8},{8,6},{24,26},{2... | collective-permute-start | bytes 196616 | tf_op jit(solution)/shard_map/ppermute | solution.py:144
  5.7 7.8 %collective-permute-start.1 = (f32[1,2,2,32,128]{4,3,2,1,0:T(8,128)S(1)}, f32[1,2,2,32,128]{4,3,2,1,0:T(8,128)S(1)}, u32[]{:S(2)}, u32[]{:S(2)}) collective-permute-start(f32[1,2,2,32,128]{4,3,2,1,0:T(8,128)S(1)} %get-tuple-element.99), channel_id=1, source_target_pairs={{0,16},{16,0},{18,2},{2,18},{4,20},{20,4},{22,6},{6,22},{8,24},{24... | collective-permute-start | bytes 196616 | tf_op jit(solution)/shard_map/ppermute | solution.py:144
  5.7 7.7 %collective-permute-start.2 = (f32[1,2,16,4,128]{4,3,2,1,0:T(4,128)S(1)}, f32[1,2,16,4,128]{4,3,2,1,0:T(4,128)S(1)}, u32[]{:S(2)}, u32[]{:S(2)}) collective-permute-start(f32[1,2,16,4,128]{4,3,2,1,0:T(4,128)S(1)} %pad_maximum_fusion.43), channel_id=1, source_target_pairs={{0,1},{1,0},{2,3},{3,2},{4,5},{5,4},{6,7},{7,6},{8,9},{9,8},{10,11... | collective-permute-start | bytes 196616 | tf_op jit(solution)/shard_map/ppermute | solution.py:124
  7.6 5.9 %copy-start.1 = (f32[2,32,32,128]{3,2,1,0:T(8,128)S(1)}, f32[2,32,32,128]{3,2,1,0:T(8,128)}, u32[]{:S(2)}) copy-start(f32[2,32,32,128]{3,2,1,0:T(8,128)} %param.12) | copy-start | bytes 3145732
  7.7 5.9 %copy-start.6 = (f32[2]{0:T(128)S(1)}, f32[2]{0:T(128)}, u32[]{:S(2)}) copy-start(f32[2]{0:T(128)} %constant.140) | copy-start | bytes 28
  15.3 6.5 %collective-permute-start.3 = (f32[2,2,2,32,128]{4,3,2,1,0:T(8,128)S(1)}, f32[2,2,2,32,128]{4,3,2,1,0:T(8,128)S(1)}, u32[]{:S(2)}, u32[]{:S(2)}) collective-permute-start(f32[2,2,2,32,128]{4,3,2,1,0:T(8,128)S(1)} %get-tuple-element.85), channel_id=1, source_target_pairs={{16,18},{18,16},{2,4},{4,2},{20,22},{22,20},{6,8},{8,6},{24,26},{2... | collective-permute-start | bytes 393224 | tf_op jit(solution)/shard_map/ppermute | solution.py:144
  17.0 5.0 %collective-permute-start.4 = (f32[2,2,2,32,128]{4,3,2,1,0:T(8,128)S(1)}, f32[2,2,2,32,128]{4,3,2,1,0:T(8,128)S(1)}, u32[]{:S(2)}, u32[]{:S(2)}) collective-permute-start(f32[2,2,2,32,128]{4,3,2,1,0:T(8,128)S(1)} %get-tuple-element.84), channel_id=1, source_target_pairs={{0,16},{16,0},{18,2},{2,18},{4,20},{20,4},{22,6},{6,22},{8,24},{24... | collective-permute-start | bytes 393224 | tf_op jit(solution)/shard_map/ppermute | solution.py:144
  17.6 5.6 %collective-permute-start.5 = (f32[2,2,16,4,128]{4,3,2,1,0:T(4,128)S(1)}, f32[2,2,16,4,128]{4,3,2,1,0:T(4,128)S(1)}, u32[]{:S(2)}, u32[]{:S(2)}) collective-permute-start(f32[2,2,16,4,128]{4,3,2,1,0:T(4,128)S(1)} %pad_maximum_fusion.35), channel_id=1, source_target_pairs={{0,1},{1,0},{2,3},{3,2},{4,5},{5,4},{6,7},{7,6},{8,9},{9,8},{10,11... | collective-permute-start | bytes 393224 | tf_op jit(solution)/shard_map/ppermute | solution.py:124
  27.5 5.0 %collective-permute-start.8 = (f32[2,2,16,4,128]{4,3,2,1,0:T(4,128)S(1)}, f32[2,2,16,4,128]{4,3,2,1,0:T(4,128)S(1)}, u32[]{:S(2)}, u32[]{:S(2)}) collective-permute-start(f32[2,2,16,4,128]{4,3,2,1,0:T(4,128)S(1)} %pad_maximum_fusion.36), channel_id=1, source_target_pairs={{0,1},{1,0},{2,3},{3,2},{4,5},{5,4},{6,7},{7,6},{8,9},{9,8},{10,11... | collective-permute-start | bytes 393224 | tf_op jit(solution)/shard_map/ppermute | solution.py:124
  28.0 6.3 %collective-permute-start.6 = (f32[2,2,2,32,128]{4,3,2,1,0:T(8,128)S(1)}, f32[2,2,2,32,128]{4,3,2,1,0:T(8,128)S(1)}, u32[]{:S(2)}, u32[]{:S(2)}) collective-permute-start(f32[2,2,2,32,128]{4,3,2,1,0:T(8,128)S(1)} %get-tuple-element.76), channel_id=1, source_target_pairs={{16,18},{18,16},{2,4},{4,2},{20,22},{22,20},{6,8},{8,6},{24,26},{2... | collective-permute-start | bytes 393224 | tf_op jit(solution)/shard_map/ppermute | solution.py:144
  28.8 5.5 %collective-permute-start.7 = (f32[2,2,2,32,128]{4,3,2,1,0:T(8,128)S(1)}, f32[2,2,2,32,128]{4,3,2,1,0:T(8,128)S(1)}, u32[]{:S(2)}, u32[]{:S(2)}) collective-permute-start(f32[2,2,2,32,128]{4,3,2,1,0:T(8,128)S(1)} %get-tuple-element.77), channel_id=1, source_target_pairs={{0,16},{16,0},{18,2},{2,18},{4,20},{20,4},{22,6},{6,22},{8,24},{24... | collective-permute-start | bytes 393224 | tf_op jit(solution)/shard_map/ppermute | solution.py:144
  38.4 5.0 %collective-permute-start.11 = (f32[2,2,16,4,128]{4,3,2,1,0:T(4,128)S(1)}, f32[2,2,16,4,128]{4,3,2,1,0:T(4,128)S(1)}, u32[]{:S(2)}, u32[]{:S(2)}) collective-permute-start(f32[2,2,16,4,128]{4,3,2,1,0:T(4,128)S(1)} %pad_maximum_fusion.37), channel_id=1, source_target_pairs={{0,1},{1,0},{2,3},{3,2},{4,5},{5,4},{6,7},{7,6},{8,9},{9,8},{10,11... | collective-permute-start | bytes 393224 | tf_op jit(solution)/shard_map/ppermute | solution.py:124
  40.0 5.0 %collective-permute-start.10 = (f32[2,2,2,32,128]{4,3,2,1,0:T(8,128)S(1)}, f32[2,2,2,32,128]{4,3,2,1,0:T(8,128)S(1)}, u32[]{:S(2)}, u32[]{:S(2)}) collective-permute-start(f32[2,2,2,32,128]{4,3,2,1,0:T(8,128)S(1)} %get-tuple-element.69), channel_id=1, source_target_pairs={{0,16},{16,0},{18,2},{2,18},{4,20},{20,4},{22,6},{6,22},{8,24},{24... | collective-permute-start | bytes 393224 | tf_op jit(solution)/shard_map/ppermute | solution.py:144
  40.8 6.2 %collective-permute-start.9 = (f32[2,2,2,32,128]{4,3,2,1,0:T(8,128)S(1)}, f32[2,2,2,32,128]{4,3,2,1,0:T(8,128)S(1)}, u32[]{:S(2)}, u32[]{:S(2)}) collective-permute-start(f32[2,2,2,32,128]{4,3,2,1,0:T(8,128)S(1)} %get-tuple-element.68), channel_id=1, source_target_pairs={{16,18},{18,16},{2,4},{4,2},{20,22},{22,20},{6,8},{8,6},{24,26},{2... | collective-permute-start | bytes 393224 | tf_op jit(solution)/shard_map/ppermute | solution.py:144
  51.3 5.0 %collective-permute-start.14 = (f32[2,2,16,4,128]{4,3,2,1,0:T(4,128)S(1)}, f32[2,2,16,4,128]{4,3,2,1,0:T(4,128)S(1)}, u32[]{:S(2)}, u32[]{:S(2)}) collective-permute-start(f32[2,2,16,4,128]{4,3,2,1,0:T(4,128)S(1)} %pad_maximum_fusion.38), channel_id=1, source_target_pairs={{0,1},{1,0},{2,3},{3,2},{4,5},{5,4},{6,7},{7,6},{8,9},{9,8},{10,11... | collective-permute-start | bytes 393224 | tf_op jit(solution)/shard_map/ppermute | solution.py:124
  51.9 6.3 %collective-permute-start.12 = (f32[2,2,2,32,128]{4,3,2,1,0:T(8,128)S(1)}, f32[2,2,2,32,128]{4,3,2,1,0:T(8,128)S(1)}, u32[]{:S(2)}, u32[]{:S(2)}) collective-permute-start(f32[2,2,2,32,128]{4,3,2,1,0:T(8,128)S(1)} %get-tuple-element.60), channel_id=1, source_target_pairs={{16,18},{18,16},{2,4},{4,2},{20,22},{22,20},{6,8},{8,6},{24,26},{2... | collective-permute-start | bytes 393224 | tf_op jit(solution)/shard_map/ppermute | solution.py:144
  52.7 5.5 %collective-permute-start.13 = (f32[2,2,2,32,128]{4,3,2,1,0:T(8,128)S(1)}, f32[2,2,2,32,128]{4,3,2,1,0:T(8,128)S(1)}, u32[]{:S(2)}, u32[]{:S(2)}) collective-permute-start(f32[2,2,2,32,128]{4,3,2,1,0:T(8,128)S(1)} %get-tuple-element.61), channel_id=1, source_target_pairs={{0,16},{16,0},{18,2},{2,18},{4,20},{20,4},{22,6},{6,22},{8,24},{24... | collective-permute-start | bytes 393224 | tf_op jit(solution)/shard_map/ppermute | solution.py:144
  62.4 5.0 %collective-permute-start.17 = (f32[2,2,16,4,128]{4,3,2,1,0:T(4,128)S(1)}, f32[2,2,16,4,128]{4,3,2,1,0:T(4,128)S(1)}, u32[]{:S(2)}, u32[]{:S(2)}) collective-permute-start(f32[2,2,16,4,128]{4,3,2,1,0:T(4,128)S(1)} %pad_maximum_fusion.39), channel_id=1, source_target_pairs={{0,1},{1,0},{2,3},{3,2},{4,5},{5,4},{6,7},{7,6},{8,9},{9,8},{10,11... | collective-permute-start | bytes 393224 | tf_op jit(solution)/shard_map/ppermute | solution.py:124
  64.0 6.3 %collective-permute-start.15 = (f32[2,2,2,32,128]{4,3,2,1,0:T(8,128)S(1)}, f32[2,2,2,32,128]{4,3,2,1,0:T(8,128)S(1)}, u32[]{:S(2)}, u32[]{:S(2)}) collective-permute-start(f32[2,2,2,32,128]{4,3,2,1,0:T(8,128)S(1)} %get-tuple-element.52), channel_id=1, source_target_pairs={{16,18},{18,16},{2,4},{4,2},{20,22},{22,20},{6,8},{8,6},{24,26},{2... | collective-permute-start | bytes 393224 | tf_op jit(solution)/shard_map/ppermute | solution.py:144
  64.9 5.3 %collective-permute-start.16 = (f32[2,2,2,32,128]{4,3,2,1,0:T(8,128)S(1)}, f32[2,2,2,32,128]{4,3,2,1,0:T(8,128)S(1)}, u32[]{:S(2)}, u32[]{:S(2)}) collective-permute-start(f32[2,2,2,32,128]{4,3,2,1,0:T(8,128)S(1)} %get-tuple-element.53), channel_id=1, source_target_pairs={{0,16},{16,0},{18,2},{2,18},{4,20},{20,4},{22,6},{6,22},{8,24},{24... | collective-permute-start | bytes 393224 | tf_op jit(solution)/shard_map/ppermute | solution.py:144
  74.4 5.0 %collective-permute-start.20 = (f32[2,2,16,4,128]{4,3,2,1,0:T(4,128)S(1)}, f32[2,2,16,4,128]{4,3,2,1,0:T(4,128)S(1)}, u32[]{:S(2)}, u32[]{:S(2)}) collective-permute-start(f32[2,2,16,4,128]{4,3,2,1,0:T(4,128)S(1)} %pad_maximum_fusion.40), channel_id=1, source_target_pairs={{0,1},{1,0},{2,3},{3,2},{4,5},{5,4},{6,7},{7,6},{8,9},{9,8},{10,11... | collective-permute-start | bytes 393224 | tf_op jit(solution)/shard_map/ppermute | solution.py:124
  75.0 6.3 %collective-permute-start.18 = (f32[2,2,2,32,128]{4,3,2,1,0:T(8,128)S(1)}, f32[2,2,2,32,128]{4,3,2,1,0:T(8,128)S(1)}, u32[]{:S(2)}, u32[]{:S(2)}) collective-permute-start(f32[2,2,2,32,128]{4,3,2,1,0:T(8,128)S(1)} %get-tuple-element.44), channel_id=1, source_target_pairs={{16,18},{18,16},{2,4},{4,2},{20,22},{22,20},{6,8},{8,6},{24,26},{2... | collective-permute-start | bytes 393224 | tf_op jit(solution)/shard_map/ppermute | solution.py:144
  76.0 5.3 %collective-permute-start.19 = (f32[2,2,2,32,128]{4,3,2,1,0:T(8,128)S(1)}, f32[2,2,2,32,128]{4,3,2,1,0:T(8,128)S(1)}, u32[]{:S(2)}, u32[]{:S(2)}) collective-permute-start(f32[2,2,2,32,128]{4,3,2,1,0:T(8,128)S(1)} %get-tuple-element.45), channel_id=1, source_target_pairs={{0,16},{16,0},{18,2},{2,18},{4,20},{20,4},{22,6},{6,22},{8,24},{24... | collective-permute-start | bytes 393224 | tf_op jit(solution)/shard_map/ppermute | solution.py:144
  85.7 5.0 %collective-permute-start.23 = (f32[2,2,16,4,128]{4,3,2,1,0:T(4,128)S(1)}, f32[2,2,16,4,128]{4,3,2,1,0:T(4,128)S(1)}, u32[]{:S(2)}, u32[]{:S(2)}) collective-permute-start(f32[2,2,16,4,128]{4,3,2,1,0:T(4,128)S(1)} %pad_maximum_fusion.41), channel_id=1, source_target_pairs={{0,1},{1,0},{2,3},{3,2},{4,5},{5,4},{6,7},{7,6},{8,9},{9,8},{10,11... | collective-permute-start | bytes 393224 | tf_op jit(solution)/shard_map/ppermute | solution.py:124
  87.3 6.3 %collective-permute-start.21 = (f32[2,2,2,32,128]{4,3,2,1,0:T(8,128)S(1)}, f32[2,2,2,32,128]{4,3,2,1,0:T(8,128)S(1)}, u32[]{:S(2)}, u32[]{:S(2)}) collective-permute-start(f32[2,2,2,32,128]{4,3,2,1,0:T(8,128)S(1)} %get-tuple-element.36), channel_id=1, source_target_pairs={{16,18},{18,16},{2,4},{4,2},{20,22},{22,20},{6,8},{8,6},{24,26},{2... | collective-permute-start | bytes 393224 | tf_op jit(solution)/shard_map/ppermute | solution.py:144
  88.2 5.3 %collective-permute-start.22 = (f32[2,2,2,32,128]{4,3,2,1,0:T(8,128)S(1)}, f32[2,2,2,32,128]{4,3,2,1,0:T(8,128)S(1)}, u32[]{:S(2)}, u32[]{:S(2)}) collective-permute-start(f32[2,2,2,32,128]{4,3,2,1,0:T(8,128)S(1)} %get-tuple-element.37), channel_id=1, source_target_pairs={{0,16},{16,0},{18,2},{2,18},{4,20},{20,4},{22,6},{6,22},{8,24},{24... | collective-permute-start | bytes 393224 | tf_op jit(solution)/shard_map/ppermute | solution.py:144
  97.8 5.0 %collective-permute-start.26 = (f32[2,2,16,4,128]{4,3,2,1,0:T(4,128)S(1)}, f32[2,2,16,4,128]{4,3,2,1,0:T(4,128)S(1)}, u32[]{:S(2)}, u32[]{:S(2)}) collective-permute-start(f32[2,2,16,4,128]{4,3,2,1,0:T(4,128)S(1)} %pad_maximum_fusion.42), channel_id=1, source_target_pairs={{0,1},{1,0},{2,3},{3,2},{4,5},{5,4},{6,7},{7,6},{8,9},{9,8},{10,11... | collective-permute-start | bytes 393224 | tf_op jit(solution)/shard_map/ppermute | solution.py:124
  98.4 6.3 %collective-permute-start.24 = (f32[2,2,2,32,128]{4,3,2,1,0:T(8,128)S(1)}, f32[2,2,2,32,128]{4,3,2,1,0:T(8,128)S(1)}, u32[]{:S(2)}, u32[]{:S(2)}) collective-permute-start(f32[2,2,2,32,128]{4,3,2,1,0:T(8,128)S(1)} %get-tuple-element.28), channel_id=1, source_target_pairs={{16,18},{18,16},{2,4},{4,2},{20,22},{22,20},{6,8},{8,6},{24,26},{2... | collective-permute-start | bytes 393224 | tf_op jit(solution)/shard_map/ppermute | solution.py:144
  99.3 6.4 %collective-permute-start.25 = (f32[2,2,2,32,128]{4,3,2,1,0:T(8,128)S(1)}, f32[2,2,2,32,128]{4,3,2,1,0:T(8,128)S(1)}, u32[]{:S(2)}, u32[]{:S(2)}) collective-permute-start(f32[2,2,2,32,128]{4,3,2,1,0:T(8,128)S(1)} %get-tuple-element.29), channel_id=1, source_target_pairs={{0,16},{16,0},{18,2},{2,18},{4,20},{20,4},{22,6},{6,22},{8,24},{24... | collective-permute-start | bytes 393224 | tf_op jit(solution)/shard_map/ppermute | solution.py:144
  99.3 16.1 %collective-permute-start.28 = (f32[1,2,16,32,128]{4,3,2,1,0:T(8,128)S(1)}, f32[1,2,16,32,128]{4,3,2,1,0:T(8,128)S(1)}, u32[]{:S(2)}, u32[]{:S(2)}) collective-permute-start(f32[1,2,16,32,128]{4,3,2,1,0:T(8,128)S(1)} %slice.1158), channel_id=1, source_target_pairs={{16,0},{17,1},{18,2},{19,3},{20,4},{21,5},{22,6},{23,7},{24,8},{25... | collective-permute-start | bytes 1572872 | tf_op jit(solution)/shard_map/ppermute | solution.py:251
  108.8 10.1 %collective-permute-start.27 = (f32[1,2,16,32,128]{4,3,2,1,0:T(8,128)S(1)}, f32[1,2,16,32,128]{4,3,2,1,0:T(8,128)S(1)}, u32[]{:S(2)}, u32[]{:S(2)}) collective-permute-start(f32[1,2,16,32,128]{4,3,2,1,0:T(8,128)S(1)} %convolution_bitcast_fusion.7), channel_id=1, source_target_pairs={{0,16},{1,17},{2,18},{3,19},{4,20},{5,21},{6,22},{7,23},{8,24},{9,... | collective-permute-start | bytes 1572872 | tf_op jit(solution)/shard_map/ppermute | solution.py:251
  110.6 8.4 %copy-start.2 = (f32[1,2,32,32,128]{4,3,2,1,0:T(8,128)}, f32[1,2,32,32,128]{4,3,2,1,0:T(8,128)S(1)}, u32[]{:S(2)}) copy-start(f32[1,2,32,32,128]{4,3,2,1,0:T(8,128)S(1)} %fusion.67) | copy-start | bytes 3145732
  (6 other events, 4.9 us)

commit v10 on v9

--- a/solution.py
+++ b/solution.py
@@ -35,23 +35,23 @@
     return table
 
 
-def thomas_kernel(up_ref, low_ref, out_ref, c_ref, d_ref):
+def thomas_kernel(diff_ref, out_ref, c_ref, d_ref):
     n = out_ref.shape[0]
     shape = out_ref.shape[1:]
     lanes = lax.broadcasted_iota(jnp.int32, shape, 1)
     species = lax.broadcasted_iota(jnp.int32, shape, 0)
     zero = jnp.zeros(shape, jnp.float32)
 
-    def column(ref, j):
-        value = jnp.full(shape, ref[0, j], jnp.float32)
+    def column(j):
+        value = jnp.full(shape, diff_ref[0, j], jnp.float32)
         for s in range(1, shape[0]):
-            value = jnp.where(species == s, ref[s, j], value)
+            value = jnp.where(species == s, diff_ref[s, j], value)
         return value
 
     def forward(j, carry):
         cprev, dprev = carry
-        up = column(up_ref, j)
-        low = column(low_ref, j)
+        up = jnp.where(j < n - 1, column(j), 0.0)
+        low = jnp.where(j > 0, column(jnp.maximum(j - 1, 0)), 0.0)
         inv = 1.0 / ((1.0 + low + up) + low * cprev)
         c = -up * inv
         d = (jnp.where(lanes == j, 1.0, 0.0) + low * dprev) * inv
@@ -78,14 +78,14 @@
     rows = pl.pallas_call(
         thomas_kernel,
         out_shape=jax.ShapeDtypeStruct((depth, species, depth), jnp.float32),
-        in_specs=[pl.BlockSpec(memory_space=pltpu.SMEM)] * 2,
+        in_specs=[pl.BlockSpec(memory_space=pltpu.SMEM)],
         scratch_shapes=[pltpu.VMEM((depth, species, depth), jnp.float32)] * 2,
         cost_estimate=pl.CostEstimate(
             flops=12 * depth * species * depth,
             transcendentals=0,
             bytes_accessed=4 * 2 * depth * species * depth,
         ),
-    )(upper, lower)
+    )(diffusion)
     inverse = jnp.transpose(rows, (1, 0, 2))
     return (inverse, upper, lower)
 

time: 120 us -> 118 us (0.983)
    add x1, other arithmetic: 1.3 us -> 0.08 us  [vertical_apply(): return (lo + up) * w - lo * beneath - up * overhead]
  transfers between devices with their start and end apart: 29 -> 29, of which waited for: 21 -> 21; matrix products, arithmetic and copies ran while one was open for 6% -> 5% of each run, Pallas kernels for 2% -> 3%
where the time goes in v10:
time: 118 us
  waiting for transfers between devices  49.3 us (42%)
  starting transfers between devices  26.1 us (22%)
  other arithmetic  25.3 us (21%)
  matrix products  9.09 us (8%)
  local copies, waits for them, and re-layouts  4.17 us (4%)
  Pallas kernels  3.12 us (3%)
    ppermute x18, waiting for transfers between devices, swap_halo(): got.append(lax.ppermute(sent, axes, pairs))  20.8 us
    ppermute x9, waiting for transfers between devices, ring_halo(): got = lax.ppermute(jnp.concatenate([first, last], dim), axes, up)  20.2 us
    mul x9, other arithmetic, tendency(): return DT * (flow + kappa * laplace + react)  15.1 us
    ppermute x18, starting transfers between devices, swap_halo(): got.append(lax.ppermute(sent, axes, pairs))  14.1 us
    ppermute x9, starting transfers between devices, ring_halo(): got = lax.ppermute(jnp.concatenate([first, last], dim), axes, up)  9.2 us
    dot_general x9, matrix products, column_solve(): jnp.einsum('lsxyk,sjk->lsxyj', rhs, inverse, precision=lax.Precision.HIGH...  9.09 us
    ppermute x2, waiting for transfers between devices, on_device(): arrived = lax.ppermute(states[level][None], 'corr', pairs)  8.34 us
    add x5, other arithmetic, on_device(): total = total + (quad + g_now[l - 1] - e_hist[l - 1][m])  3.62 us
  transfers between devices with their start and end apart: 29, of which 21 were waited for; matrix products, arithmetic and copies ran while one was open for 5% of the time, Pallas kernels for 3%

profile of v10, /device:TPU:0, one launch (start us, length us, event | category | flops | bytes accessed | tf_op | source)
XLA Modules:
  0.0 117.8 jit_solution(17570093191813893756)
XLA Ops:
  1.1 4.6 %collective-permute-start = (f32[1,2,2,32,128]{4,3,2,1,0:T(8,128)S(1)}, f32[1,2,2,32,128]{4,3,2,1,0:T(8,128)S(1)}, u32[]{:S(2)}, u32[]{:S(2)}) collective-permute-start(f32[1,2,2,32,128]{4,3,2,1,0:T(8,128)S(1)} %get-tuple-element.98), channel_id=1, source_target_pairs={{16,18},{18,16},{2,4},{4,2},{20,22},{22,20},{6,8},{8,6},{24,26},{2... | collective-permute-start | bytes 196616 | tf_op jit(solution)/shard_map/ppermute | solution.py:144
  5.7 1.6 %collective-permute-start.2 = (f32[1,2,16,4,128]{4,3,2,1,0:T(4,128)S(1)}, f32[1,2,16,4,128]{4,3,2,1,0:T(4,128)S(1)}, u32[]{:S(2)}, u32[]{:S(2)}) collective-permute-start(f32[1,2,16,4,128]{4,3,2,1,0:T(4,128)S(1)} %pad_maximum_fusion.43), channel_id=1, source_target_pairs={{0,1},{1,0},{2,3},{3,2},{4,5},{5,4},{6,7},{7,6},{8,9},{9,8},{10,11... | collective-permute-start | bytes 196616 | tf_op jit(solution)/shard_map/ppermute | solution.py:124
  7.7 3.1 %shard_map.118 = f32[128,2,128]{2,1,0:T(2,128)} custom-call(f32[2,128]{1,0:T(2,128)} %diff_ref.1), custom_call_target="tpu_custom_call" | custom-call | flops 393216 | bytes 262144 | tf_op jit(solution)/shard_map/pallas_call | solution.py:78
  13.9 1.7 %collective-permute-start.3 = (f32[2,2,2,32,128]{4,3,2,1,0:T(8,128)S(1)}, f32[2,2,2,32,128]{4,3,2,1,0:T(8,128)S(1)}, u32[]{:S(2)}, u32[]{:S(2)}) collective-permute-start(f32[2,2,2,32,128]{4,3,2,1,0:T(8,128)S(1)} %get-tuple-element.85), channel_id=1, source_target_pairs={{16,18},{18,16},{2,4},{4,2},{20,22},{22,20},{6,8},{8,6},{24,26},{2... | collective-permute-start | bytes 393224 | tf_op jit(solution)/shard_map/ppermute | solution.py:144
  16.9 3.6 %collective-permute-done.3 = f32[2,2,2,32,128]{4,3,2,1,0:T(8,128)S(1)} collective-permute-done((f32[2,2,2,32,128]{4,3,2,1,0:T(8,128)S(1)}, f32[2,2,2,32,128]{4,3,2,1,0:T(8,128)S(1)}, u32[]{:S(2)}, u32[]{:S(2)}) %collective-permute-start.3) | collective-permute-done | bytes 131104 | tf_op jit(solution)/shard_map/ppermute | solution.py:144
  27.1 3.4 %collective-permute-done.8 = f32[2,2,16,4,128]{4,3,2,1,0:T(4,128)S(1)} collective-permute-done((f32[2,2,16,4,128]{4,3,2,1,0:T(4,128)S(1)}, f32[2,2,16,4,128]{4,3,2,1,0:T(4,128)S(1)}, u32[]{:S(2)}, u32[]{:S(2)}) %collective-permute-start.8) | collective-permute-done | bytes 131104 | tf_op jit(solution)/shard_map/ppermute | solution.py:124
  30.5 1.8 %collective-permute-done.6 = f32[2,2,2,32,128]{4,3,2,1,0:T(8,128)S(1)} collective-permute-done((f32[2,2,2,32,128]{4,3,2,1,0:T(8,128)S(1)}, f32[2,2,2,32,128]{4,3,2,1,0:T(8,128)S(1)}, u32[]{:S(2)}, u32[]{:S(2)}) %collective-permute-start.6) | collective-permute-done | bytes 131104 | tf_op jit(solution)/shard_map/ppermute | solution.py:144
  32.3 1.8 %fusion.37 = f32[2,2,16,32,128]{4,3,2,1,0:T(8,128)S(1)} fusion(f32[2,1,16,32,128]{4,3,2,1,0:T(8,128)S(1)} %get-tuple-element.81, f32[2,1,16,32,128]{4,3,2,1,0:T(8,128)S(1)} %get-tuple-element.80, f32[2,2,16,32,128]{4,3,2,1,0:T(8,128)S(1)} %convolution_bitcast_fusion.6, f32[2,2,16,2,128]{4,3,2,1,0:T(2,128)S(1)} %get-tuple-element.133, ...), kind=kLoop, calls=%fused_computation.148 | loop fusion | flops 9175040 | bytes 4063240 | tf_op jit(solution)/shard_map/mul | solution.py:182
  36.4 1.6 %collective-permute-start.11 = (f32[2,2,16,4,128]{4,3,2,1,0:T(4,128)S(1)}, f32[2,2,16,4,128]{4,3,2,1,0:T(4,128)S(1)}, u32[]{:S(2)}, u32[]{:S(2)}) collective-permute-start(f32[2,2,16,4,128]{4,3,2,1,0:T(4,128)S(1)} %pad_maximum_fusion.37), channel_id=1, source_target_pairs={{0,1},{1,0},{2,3},{3,2},{4,5},{5,4},{6,7},{7,6},{8,9},{9,8},{10,11... | collective-permute-start | bytes 393224 | tf_op jit(solution)/shard_map/ppermute | solution.py:124
  39.7 1.7 %collective-permute-done.11 = f32[2,2,16,4,128]{4,3,2,1,0:T(4,128)S(1)} collective-permute-done((f32[2,2,16,4,128]{4,3,2,1,0:T(4,128)S(1)}, f32[2,2,16,4,128]{4,3,2,1,0:T(4,128)S(1)}, u32[]{:S(2)}, u32[]{:S(2)}) %collective-permute-start.11) | collective-permute-done | bytes 131104 | tf_op jit(solution)/shard_map/ppermute | solution.py:124
  41.5 1.6 %collective-permute-done.10 = f32[2,2,2,32,128]{4,3,2,1,0:T(8,128)S(1)} collective-permute-done((f32[2,2,2,32,128]{4,3,2,1,0:T(8,128)S(1)}, f32[2,2,2,32,128]{4,3,2,1,0:T(8,128)S(1)}, u32[]{:S(2)}, u32[]{:S(2)}) %collective-permute-start.10) | collective-permute-done | bytes 131104 | tf_op jit(solution)/shard_map/ppermute | solution.py:144
  43.0 1.9 %collective-permute-done.9 = f32[2,2,2,32,128]{4,3,2,1,0:T(8,128)S(1)} collective-permute-done((f32[2,2,2,32,128]{4,3,2,1,0:T(8,128)S(1)}, f32[2,2,2,32,128]{4,3,2,1,0:T(8,128)S(1)}, u32[]{:S(2)}, u32[]{:S(2)}) %collective-permute-start.9) | collective-permute-done | bytes 131104 | tf_op jit(solution)/shard_map/ppermute | solution.py:144
  44.9 2.0 %fusion.41 = f32[2,2,16,32,128]{4,3,2,1,0:T(8,128)S(1)} fusion(f32[2,1,16,32,128]{4,3,2,1,0:T(8,128)S(1)} %get-tuple-element.73, f32[2,1,16,32,128]{4,3,2,1,0:T(8,128)S(1)} %get-tuple-element.72, f32[2,2,16,32,128]{4,3,2,1,0:T(8,128)S(1)} %convolution_bitcast_fusion.5, f32[2,2,16,2,128]{4,3,2,1,0:T(2,128)S(1)} %get-tuple-element.131, ...), kind=kLoop, calls=%fused_computation.153 | loop fusion | flops 9175040 | bytes 4063240 | tf_op jit(solution)/shard_map/mul | solution.py:182
  50.6 3.7 %collective-permute-done.14 = f32[2,2,16,4,128]{4,3,2,1,0:T(4,128)S(1)} collective-permute-done((f32[2,2,16,4,128]{4,3,2,1,0:T(4,128)S(1)}, f32[2,2,16,4,128]{4,3,2,1,0:T(4,128)S(1)}, u32[]{:S(2)}, u32[]{:S(2)}) %collective-permute-start.14) | collective-permute-done | bytes 131104 | tf_op jit(solution)/shard_map/ppermute | solution.py:124
  54.3 1.8 %collective-permute-done.12 = f32[2,2,2,32,128]{4,3,2,1,0:T(8,128)S(1)} collective-permute-done((f32[2,2,2,32,128]{4,3,2,1,0:T(8,128)S(1)}, f32[2,2,2,32,128]{4,3,2,1,0:T(8,128)S(1)}, u32[]{:S(2)}, u32[]{:S(2)}) %collective-permute-start.12) | collective-permute-done | bytes 131104 | tf_op jit(solution)/shard_map/ppermute | solution.py:144
  56.1 1.8 %fusion.45 = f32[2,2,16,32,128]{4,3,2,1,0:T(8,128)S(1)} fusion(f32[2,1,16,32,128]{4,3,2,1,0:T(8,128)S(1)} %get-tuple-element.65, f32[2,1,16,32,128]{4,3,2,1,0:T(8,128)S(1)} %get-tuple-element.64, f32[2,2,16,32,128]{4,3,2,1,0:T(8,128)S(1)} %convolution_bitcast_fusion.4, f32[2,2,16,2,128]{4,3,2,1,0:T(2,128)S(1)} %get-tuple-element.129, ...), kind=kLoop, calls=%fused_computation.158 | loop fusion | flops 9175040 | bytes 4063240 | tf_op jit(solution)/shard_map/mul | solution.py:182
  60.3 1.6 %collective-permute-start.17 = (f32[2,2,16,4,128]{4,3,2,1,0:T(4,128)S(1)}, f32[2,2,16,4,128]{4,3,2,1,0:T(4,128)S(1)}, u32[]{:S(2)}, u32[]{:S(2)}) collective-permute-start(f32[2,2,16,4,128]{4,3,2,1,0:T(4,128)S(1)} %pad_maximum_fusion.39), channel_id=1, source_target_pairs={{0,1},{1,0},{2,3},{3,2},{4,5},{5,4},{6,7},{7,6},{8,9},{9,8},{10,11... | collective-permute-start | bytes 393224 | tf_op jit(solution)/shard_map/ppermute | solution.py:124
  62.9 2.5 %collective-permute-done.17 = f32[2,2,16,4,128]{4,3,2,1,0:T(4,128)S(1)} collective-permute-done((f32[2,2,16,4,128]{4,3,2,1,0:T(4,128)S(1)}, f32[2,2,16,4,128]{4,3,2,1,0:T(4,128)S(1)}, u32[]{:S(2)}, u32[]{:S(2)}) %collective-permute-start.17) | collective-permute-done | bytes 131104 | tf_op jit(solution)/shard_map/ppermute | solution.py:124
  65.4 2.8 %collective-permute-done.15 = f32[2,2,2,32,128]{4,3,2,1,0:T(8,128)S(1)} collective-permute-done((f32[2,2,2,32,128]{4,3,2,1,0:T(8,128)S(1)}, f32[2,2,2,32,128]{4,3,2,1,0:T(8,128)S(1)}, u32[]{:S(2)}, u32[]{:S(2)}) %collective-permute-start.15) | collective-permute-done | bytes 131104 | tf_op jit(solution)/shard_map/ppermute | solution.py:144
  68.2 1.8 %fusion.49 = f32[2,2,16,32,128]{4,3,2,1,0:T(8,128)S(1)} fusion(f32[2,1,16,32,128]{4,3,2,1,0:T(8,128)S(1)} %get-tuple-element.57, f32[2,1,16,32,128]{4,3,2,1,0:T(8,128)S(1)} %get-tuple-element.56, f32[2,2,16,32,128]{4,3,2,1,0:T(8,128)S(1)} %convolution_bitcast_fusion.3, f32[2,2,16,2,128]{4,3,2,1,0:T(2,128)S(1)} %get-tuple-element.127, ...), kind=kLoop, calls=%fused_computation.163 | loop fusion | flops 9175040 | bytes 4063240 | tf_op jit(solution)/shard_map/mul | solution.py:182
  73.9 3.5 %collective-permute-done.20 = f32[2,2,16,4,128]{4,3,2,1,0:T(4,128)S(1)} collective-permute-done((f32[2,2,16,4,128]{4,3,2,1,0:T(4,128)S(1)}, f32[2,2,16,4,128]{4,3,2,1,0:T(4,128)S(1)}, u32[]{:S(2)}, u32[]{:S(2)}) %collective-permute-start.20) | collective-permute-done | bytes 131104 | tf_op jit(solution)/shard_map/ppermute | solution.py:124
  77.4 1.8 %collective-permute-done.18 = f32[2,2,2,32,128]{4,3,2,1,0:T(8,128)S(1)} collective-permute-done((f32[2,2,2,32,128]{4,3,2,1,0:T(8,128)S(1)}, f32[2,2,2,32,128]{4,3,2,1,0:T(8,128)S(1)}, u32[]{:S(2)}, u32[]{:S(2)}) %collective-permute-start.18) | collective-permute-done | bytes 131104 | tf_op jit(solution)/shard_map/ppermute | solution.py:144
  79.2 2.1 %fusion.53 = f32[2,2,16,32,128]{4,3,2,1,0:T(8,128)S(1)} fusion(f32[2,1,16,32,128]{4,3,2,1,0:T(8,128)S(1)} %get-tuple-element.49, f32[2,1,16,32,128]{4,3,2,1,0:T(8,128)S(1)} %get-tuple-element.48, f32[2,2,16,32,128]{4,3,2,1,0:T(8,128)S(1)} %convolution_bitcast_fusion.2, f32[2,2,16,2,128]{4,3,2,1,0:T(2,128)S(1)} %get-tuple-element.125, ...), kind=kLoop, calls=%fused_computation.168 | loop fusion | flops 9175040 | bytes 4063240 | tf_op jit(solution)/shard_map/mul | solution.py:182
  83.6 1.6 %collective-permute-start.23 = (f32[2,2,16,4,128]{4,3,2,1,0:T(4,128)S(1)}, f32[2,2,16,4,128]{4,3,2,1,0:T(4,128)S(1)}, u32[]{:S(2)}, u32[]{:S(2)}) collective-permute-start(f32[2,2,16,4,128]{4,3,2,1,0:T(4,128)S(1)} %pad_maximum_fusion.41), channel_id=1, source_target_pairs={{0,1},{1,0},{2,3},{3,2},{4,5},{5,4},{6,7},{7,6},{8,9},{9,8},{10,11... | collective-permute-start | bytes 393224 | tf_op jit(solution)/shard_map/ppermute | solution.py:124
  86.2 2.5 %collective-permute-done.23 = f32[2,2,16,4,128]{4,3,2,1,0:T(4,128)S(1)} collective-permute-done((f32[2,2,16,4,128]{4,3,2,1,0:T(4,128)S(1)}, f32[2,2,16,4,128]{4,3,2,1,0:T(4,128)S(1)}, u32[]{:S(2)}, u32[]{:S(2)}) %collective-permute-start.23) | collective-permute-done | bytes 131104 | tf_op jit(solution)/shard_map/ppermute | solution.py:124
  88.7 2.8 %collective-permute-done.21 = f32[2,2,2,32,128]{4,3,2,1,0:T(8,128)S(1)} collective-permute-done((f32[2,2,2,32,128]{4,3,2,1,0:T(8,128)S(1)}, f32[2,2,2,32,128]{4,3,2,1,0:T(8,128)S(1)}, u32[]{:S(2)}, u32[]{:S(2)}) %collective-permute-start.21) | collective-permute-done | bytes 131104 | tf_op jit(solution)/shard_map/ppermute | solution.py:144
  91.5 1.8 %fusion.57 = f32[2,2,16,32,128]{4,3,2,1,0:T(8,128)S(1)} fusion(f32[2,1,16,32,128]{4,3,2,1,0:T(8,128)S(1)} %get-tuple-element.41, f32[2,1,16,32,128]{4,3,2,1,0:T(8,128)S(1)} %get-tuple-element.40, f32[2,2,16,32,128]{4,3,2,1,0:T(8,128)S(1)} %convolution_bitcast_fusion.1, f32[2,2,16,2,128]{4,3,2,1,0:T(2,128)S(1)} %get-tuple-element.123, ...), kind=kLoop, calls=%fused_computation.173 | loop fusion | flops 9175040 | bytes 4063240 | tf_op jit(solution)/shard_map/mul | solution.py:182
  98.5 2.2 %collective-permute-done.26 = f32[2,2,16,4,128]{4,3,2,1,0:T(4,128)S(1)} collective-permute-done((f32[2,2,16,4,128]{4,3,2,1,0:T(4,128)S(1)}, f32[2,2,16,4,128]{4,3,2,1,0:T(4,128)S(1)}, u32[]{:S(2)}, u32[]{:S(2)}) %collective-permute-start.26) | collective-permute-done | bytes 131104 | tf_op jit(solution)/shard_map/ppermute | solution.py:124
  100.8 1.8 %collective-permute-done.24 = f32[2,2,2,32,128]{4,3,2,1,0:T(8,128)S(1)} collective-permute-done((f32[2,2,2,32,128]{4,3,2,1,0:T(8,128)S(1)}, f32[2,2,2,32,128]{4,3,2,1,0:T(8,128)S(1)}, u32[]{:S(2)}, u32[]{:S(2)}) %collective-permute-start.24) | collective-permute-done | bytes 131104 | tf_op jit(solution)/shard_map/ppermute | solution.py:144
  103.6 1.9 %fusion.61 = f32[2,2,16,32,128]{4,3,2,1,0:T(8,128)S(1)} fusion(f32[2,1,16,32,128]{4,3,2,1,0:T(8,128)S(1)} %get-tuple-element.33, f32[2,1,16,32,128]{4,3,2,1,0:T(8,128)S(1)} %get-tuple-element.32, f32[2,2,16,32,128]{4,3,2,1,0:T(8,128)S(1)} %convolution_bitcast_fusion, f32[2,2,16,2,128]{4,3,2,1,0:T(2,128)S(1)} %get-tuple-element.121, ...), kind=kLoop, calls=%fused_computation.178 | loop fusion | flops 9175040 | bytes 4063240 | tf_op jit(solution)/shard_map/mul | solution.py:182
  108.6 4.8 %collective-permute-done.28 = f32[1,2,16,32,128]{4,3,2,1,0:T(8,128)S(1)} collective-permute-done((f32[1,2,16,32,128]{4,3,2,1,0:T(8,128)S(1)}, f32[1,2,16,32,128]{4,3,2,1,0:T(8,128)S(1)}, u32[]{:S(2)}, u32[]{:S(2)}) %collective-permute-start.28) | collective-permute-done | bytes 524320 | tf_op jit(solution)/shard_map/ppermute | solution.py:251
  113.4 3.6 %collective-permute-done.27 = f32[1,2,16,32,128]{4,3,2,1,0:T(8,128)S(1)} collective-permute-done((f32[1,2,16,32,128]{4,3,2,1,0:T(8,128)S(1)}, f32[1,2,16,32,128]{4,3,2,1,0:T(8,128)S(1)}, u32[]{:S(2)}, u32[]{:S(2)}) %collective-permute-start.27) | collective-permute-done | bytes 524320 | tf_op jit(solution)/shard_map/ppermute | solution.py:251
  (137 shorter events, 40.8 us)
Async XLA Ops:
  1.1 10.9 %collective-permute-start = (f32[1,2,2,32,128]{4,3,2,1,0:T(8,128)S(1)}, f32[1,2,2,32,128]{4,3,2,1,0:T(8,128)S(1)}, u32[]{:S(2)}, u32[]{:S(2)}) collective-permute-start(f32[1,2,2,32,128]{4,3,2,1,0:T(8,128)S(1)} %get-tuple-element.98), channel_id=1, source_target_pairs={{16,18},{18,16},{2,4},{4,2},{20,22},{22,20},{6,8},{8,6},{24,26},{2... | collective-permute-start | bytes 196616 | tf_op jit(solution)/shard_map/ppermute | solution.py:144
  5.7 6.3 %collective-permute-start.1 = (f32[1,2,2,32,128]{4,3,2,1,0:T(8,128)S(1)}, f32[1,2,2,32,128]{4,3,2,1,0:T(8,128)S(1)}, u32[]{:S(2)}, u32[]{:S(2)}) collective-permute-start(f32[1,2,2,32,128]{4,3,2,1,0:T(8,128)S(1)} %get-tuple-element.99), channel_id=1, source_target_pairs={{0,16},{16,0},{18,2},{2,18},{4,20},{20,4},{22,6},{6,22},{8,24},{24... | collective-permute-start | bytes 196616 | tf_op jit(solution)/shard_map/ppermute | solution.py:144
  5.7 6.2 %collective-permute-start.2 = (f32[1,2,16,4,128]{4,3,2,1,0:T(4,128)S(1)}, f32[1,2,16,4,128]{4,3,2,1,0:T(4,128)S(1)}, u32[]{:S(2)}, u32[]{:S(2)}) collective-permute-start(f32[1,2,16,4,128]{4,3,2,1,0:T(4,128)S(1)} %pad_maximum_fusion.43), channel_id=1, source_target_pairs={{0,1},{1,0},{2,3},{3,2},{4,5},{5,4},{6,7},{7,6},{8,9},{9,8},{10,11... | collective-permute-start | bytes 196616 | tf_op jit(solution)/shard_map/ppermute | solution.py:124
  7.6 4.4 %copy-start.1 = (f32[2,32,32,128]{3,2,1,0:T(8,128)S(1)}, f32[2,32,32,128]{3,2,1,0:T(8,128)}, u32[]{:S(2)}) copy-start(f32[2,32,32,128]{3,2,1,0:T(8,128)} %param.12) | copy-start | bytes 3145732
  7.6 4.4 %copy-start.3 = (f32[2]{0:T(128)S(1)}, f32[2]{0:T(128)}, u32[]{:S(2)}) copy-start(f32[2]{0:T(128)} %constant.140) | copy-start | bytes 28
  13.9 6.5 %collective-permute-start.3 = (f32[2,2,2,32,128]{4,3,2,1,0:T(8,128)S(1)}, f32[2,2,2,32,128]{4,3,2,1,0:T(8,128)S(1)}, u32[]{:S(2)}, u32[]{:S(2)}) collective-permute-start(f32[2,2,2,32,128]{4,3,2,1,0:T(8,128)S(1)} %get-tuple-element.85), channel_id=1, source_target_pairs={{16,18},{18,16},{2,4},{4,2},{20,22},{22,20},{6,8},{8,6},{24,26},{2... | collective-permute-start | bytes 393224 | tf_op jit(solution)/shard_map/ppermute | solution.py:144
  15.6 5.0 %collective-permute-start.4 = (f32[2,2,2,32,128]{4,3,2,1,0:T(8,128)S(1)}, f32[2,2,2,32,128]{4,3,2,1,0:T(8,128)S(1)}, u32[]{:S(2)}, u32[]{:S(2)}) collective-permute-start(f32[2,2,2,32,128]{4,3,2,1,0:T(8,128)S(1)} %get-tuple-element.84), channel_id=1, source_target_pairs={{0,16},{16,0},{18,2},{2,18},{4,20},{20,4},{22,6},{6,22},{8,24},{24... | collective-permute-start | bytes 393224 | tf_op jit(solution)/shard_map/ppermute | solution.py:144
  16.1 5.6 %collective-permute-start.5 = (f32[2,2,16,4,128]{4,3,2,1,0:T(4,128)S(1)}, f32[2,2,16,4,128]{4,3,2,1,0:T(4,128)S(1)}, u32[]{:S(2)}, u32[]{:S(2)}) collective-permute-start(f32[2,2,16,4,128]{4,3,2,1,0:T(4,128)S(1)} %pad_maximum_fusion.35), channel_id=1, source_target_pairs={{0,1},{1,0},{2,3},{3,2},{4,5},{5,4},{6,7},{7,6},{8,9},{9,8},{10,11... | collective-permute-start | bytes 393224 | tf_op jit(solution)/shard_map/ppermute | solution.py:124
  25.4 5.0 %collective-permute-start.8 = (f32[2,2,16,4,128]{4,3,2,1,0:T(4,128)S(1)}, f32[2,2,16,4,128]{4,3,2,1,0:T(4,128)S(1)}, u32[]{:S(2)}, u32[]{:S(2)}) collective-permute-start(f32[2,2,16,4,128]{4,3,2,1,0:T(4,128)S(1)} %pad_maximum_fusion.36), channel_id=1, source_target_pairs={{0,1},{1,0},{2,3},{3,2},{4,5},{5,4},{6,7},{7,6},{8,9},{9,8},{10,11... | collective-permute-start | bytes 393224 | tf_op jit(solution)/shard_map/ppermute | solution.py:124
  26.0 6.3 %collective-permute-start.6 = (f32[2,2,2,32,128]{4,3,2,1,0:T(8,128)S(1)}, f32[2,2,2,32,128]{4,3,2,1,0:T(8,128)S(1)}, u32[]{:S(2)}, u32[]{:S(2)}) collective-permute-start(f32[2,2,2,32,128]{4,3,2,1,0:T(8,128)S(1)} %get-tuple-element.76), channel_id=1, source_target_pairs={{16,18},{18,16},{2,4},{4,2},{20,22},{22,20},{6,8},{8,6},{24,26},{2... | collective-permute-start | bytes 393224 | tf_op jit(solution)/shard_map/ppermute | solution.py:144
  26.7 5.5 %collective-permute-start.7 = (f32[2,2,2,32,128]{4,3,2,1,0:T(8,128)S(1)}, f32[2,2,2,32,128]{4,3,2,1,0:T(8,128)S(1)}, u32[]{:S(2)}, u32[]{:S(2)}) collective-permute-start(f32[2,2,2,32,128]{4,3,2,1,0:T(8,128)S(1)} %get-tuple-element.77), channel_id=1, source_target_pairs={{0,16},{16,0},{18,2},{2,18},{4,20},{20,4},{22,6},{6,22},{8,24},{24... | collective-permute-start | bytes 393224 | tf_op jit(solution)/shard_map/ppermute | solution.py:144
  36.4 5.0 %collective-permute-start.11 = (f32[2,2,16,4,128]{4,3,2,1,0:T(4,128)S(1)}, f32[2,2,16,4,128]{4,3,2,1,0:T(4,128)S(1)}, u32[]{:S(2)}, u32[]{:S(2)}) collective-permute-start(f32[2,2,16,4,128]{4,3,2,1,0:T(4,128)S(1)} %pad_maximum_fusion.37), channel_id=1, source_target_pairs={{0,1},{1,0},{2,3},{3,2},{4,5},{5,4},{6,7},{7,6},{8,9},{9,8},{10,11... | collective-permute-start | bytes 393224 | tf_op jit(solution)/shard_map/ppermute | solution.py:124
  38.0 5.0 %collective-permute-start.10 = (f32[2,2,2,32,128]{4,3,2,1,0:T(8,128)S(1)}, f32[2,2,2,32,128]{4,3,2,1,0:T(8,128)S(1)}, u32[]{:S(2)}, u32[]{:S(2)}) collective-permute-start(f32[2,2,2,32,128]{4,3,2,1,0:T(8,128)S(1)} %get-tuple-element.69), channel_id=1, source_target_pairs={{0,16},{16,0},{18,2},{2,18},{4,20},{20,4},{22,6},{6,22},{8,24},{24... | collective-permute-start | bytes 393224 | tf_op jit(solution)/shard_map/ppermute | solution.py:144
  38.7 6.2 %collective-permute-start.9 = (f32[2,2,2,32,128]{4,3,2,1,0:T(8,128)S(1)}, f32[2,2,2,32,128]{4,3,2,1,0:T(8,128)S(1)}, u32[]{:S(2)}, u32[]{:S(2)}) collective-permute-start(f32[2,2,2,32,128]{4,3,2,1,0:T(8,128)S(1)} %get-tuple-element.68), channel_id=1, source_target_pairs={{16,18},{18,16},{2,4},{4,2},{20,22},{22,20},{6,8},{8,6},{24,26},{2... | collective-permute-start | bytes 393224 | tf_op jit(solution)/shard_map/ppermute | solution.py:144
  49.3 5.0 %collective-permute-start.14 = (f32[2,2,16,4,128]{4,3,2,1,0:T(4,128)S(1)}, f32[2,2,16,4,128]{4,3,2,1,0:T(4,128)S(1)}, u32[]{:S(2)}, u32[]{:S(2)}) collective-permute-start(f32[2,2,16,4,128]{4,3,2,1,0:T(4,128)S(1)} %pad_maximum_fusion.38), channel_id=1, source_target_pairs={{0,1},{1,0},{2,3},{3,2},{4,5},{5,4},{6,7},{7,6},{8,9},{9,8},{10,11... | collective-permute-start | bytes 393224 | tf_op jit(solution)/shard_map/ppermute | solution.py:124
  49.9 6.3 %collective-permute-start.12 = (f32[2,2,2,32,128]{4,3,2,1,0:T(8,128)S(1)}, f32[2,2,2,32,128]{4,3,2,1,0:T(8,128)S(1)}, u32[]{:S(2)}, u32[]{:S(2)}) collective-permute-start(f32[2,2,2,32,128]{4,3,2,1,0:T(8,128)S(1)} %get-tuple-element.60), channel_id=1, source_target_pairs={{16,18},{18,16},{2,4},{4,2},{20,22},{22,20},{6,8},{8,6},{24,26},{2... | collective-permute-start | bytes 393224 | tf_op jit(solution)/shard_map/ppermute | solution.py:144
  50.6 5.5 %collective-permute-start.13 = (f32[2,2,2,32,128]{4,3,2,1,0:T(8,128)S(1)}, f32[2,2,2,32,128]{4,3,2,1,0:T(8,128)S(1)}, u32[]{:S(2)}, u32[]{:S(2)}) collective-permute-start(f32[2,2,2,32,128]{4,3,2,1,0:T(8,128)S(1)} %get-tuple-element.61), channel_id=1, source_target_pairs={{0,16},{16,0},{18,2},{2,18},{4,20},{20,4},{22,6},{6,22},{8,24},{24... | collective-permute-start | bytes 393224 | tf_op jit(solution)/shard_map/ppermute | solution.py:144
  60.3 5.0 %collective-permute-start.17 = (f32[2,2,16,4,128]{4,3,2,1,0:T(4,128)S(1)}, f32[2,2,16,4,128]{4,3,2,1,0:T(4,128)S(1)}, u32[]{:S(2)}, u32[]{:S(2)}) collective-permute-start(f32[2,2,16,4,128]{4,3,2,1,0:T(4,128)S(1)} %pad_maximum_fusion.39), channel_id=1, source_target_pairs={{0,1},{1,0},{2,3},{3,2},{4,5},{5,4},{6,7},{7,6},{8,9},{9,8},{10,11... | collective-permute-start | bytes 393224 | tf_op jit(solution)/shard_map/ppermute | solution.py:124
  61.9 6.3 %collective-permute-start.15 = (f32[2,2,2,32,128]{4,3,2,1,0:T(8,128)S(1)}, f32[2,2,2,32,128]{4,3,2,1,0:T(8,128)S(1)}, u32[]{:S(2)}, u32[]{:S(2)}) collective-permute-start(f32[2,2,2,32,128]{4,3,2,1,0:T(8,128)S(1)} %get-tuple-element.52), channel_id=1, source_target_pairs={{16,18},{18,16},{2,4},{4,2},{20,22},{22,20},{6,8},{8,6},{24,26},{2... | collective-permute-start | bytes 393224 | tf_op jit(solution)/shard_map/ppermute | solution.py:144
  62.9 5.3 %collective-permute-start.16 = (f32[2,2,2,32,128]{4,3,2,1,0:T(8,128)S(1)}, f32[2,2,2,32,128]{4,3,2,1,0:T(8,128)S(1)}, u32[]{:S(2)}, u32[]{:S(2)}) collective-permute-start(f32[2,2,2,32,128]{4,3,2,1,0:T(8,128)S(1)} %get-tuple-element.53), channel_id=1, source_target_pairs={{0,16},{16,0},{18,2},{2,18},{4,20},{20,4},{22,6},{6,22},{8,24},{24... | collective-permute-start | bytes 393224 | tf_op jit(solution)/shard_map/ppermute | solution.py:144
  72.3 5.0 %collective-permute-start.20 = (f32[2,2,16,4,128]{4,3,2,1,0:T(4,128)S(1)}, f32[2,2,16,4,128]{4,3,2,1,0:T(4,128)S(1)}, u32[]{:S(2)}, u32[]{:S(2)}) collective-permute-start(f32[2,2,16,4,128]{4,3,2,1,0:T(4,128)S(1)} %pad_maximum_fusion.40), channel_id=1, source_target_pairs={{0,1},{1,0},{2,3},{3,2},{4,5},{5,4},{6,7},{7,6},{8,9},{9,8},{10,11... | collective-permute-start | bytes 393224 | tf_op jit(solution)/shard_map/ppermute | solution.py:124
  72.9 6.3 %collective-permute-start.18 = (f32[2,2,2,32,128]{4,3,2,1,0:T(8,128)S(1)}, f32[2,2,2,32,128]{4,3,2,1,0:T(8,128)S(1)}, u32[]{:S(2)}, u32[]{:S(2)}) collective-permute-start(f32[2,2,2,32,128]{4,3,2,1,0:T(8,128)S(1)} %get-tuple-element.44), channel_id=1, source_target_pairs={{16,18},{18,16},{2,4},{4,2},{20,22},{22,20},{6,8},{8,6},{24,26},{2... | collective-permute-start | bytes 393224 | tf_op jit(solution)/shard_map/ppermute | solution.py:144
  73.9 5.3 %collective-permute-start.19 = (f32[2,2,2,32,128]{4,3,2,1,0:T(8,128)S(1)}, f32[2,2,2,32,128]{4,3,2,1,0:T(8,128)S(1)}, u32[]{:S(2)}, u32[]{:S(2)}) collective-permute-start(f32[2,2,2,32,128]{4,3,2,1,0:T(8,128)S(1)} %get-tuple-element.45), channel_id=1, source_target_pairs={{0,16},{16,0},{18,2},{2,18},{4,20},{20,4},{22,6},{6,22},{8,24},{24... | collective-permute-start | bytes 393224 | tf_op jit(solution)/shard_map/ppermute | solution.py:144
  83.6 5.0 %collective-permute-start.23 = (f32[2,2,16,4,128]{4,3,2,1,0:T(4,128)S(1)}, f32[2,2,16,4,128]{4,3,2,1,0:T(4,128)S(1)}, u32[]{:S(2)}, u32[]{:S(2)}) collective-permute-start(f32[2,2,16,4,128]{4,3,2,1,0:T(4,128)S(1)} %pad_maximum_fusion.41), channel_id=1, source_target_pairs={{0,1},{1,0},{2,3},{3,2},{4,5},{5,4},{6,7},{7,6},{8,9},{9,8},{10,11... | collective-permute-start | bytes 393224 | tf_op jit(solution)/shard_map/ppermute | solution.py:124
  85.2 6.3 %collective-permute-start.21 = (f32[2,2,2,32,128]{4,3,2,1,0:T(8,128)S(1)}, f32[2,2,2,32,128]{4,3,2,1,0:T(8,128)S(1)}, u32[]{:S(2)}, u32[]{:S(2)}) collective-permute-start(f32[2,2,2,32,128]{4,3,2,1,0:T(8,128)S(1)} %get-tuple-element.36), channel_id=1, source_target_pairs={{16,18},{18,16},{2,4},{4,2},{20,22},{22,20},{6,8},{8,6},{24,26},{2... | collective-permute-start | bytes 393224 | tf_op jit(solution)/shard_map/ppermute | solution.py:144
  86.2 5.3 %collective-permute-start.22 = (f32[2,2,2,32,128]{4,3,2,1,0:T(8,128)S(1)}, f32[2,2,2,32,128]{4,3,2,1,0:T(8,128)S(1)}, u32[]{:S(2)}, u32[]{:S(2)}) collective-permute-start(f32[2,2,2,32,128]{4,3,2,1,0:T(8,128)S(1)} %get-tuple-element.37), channel_id=1, source_target_pairs={{0,16},{16,0},{18,2},{2,18},{4,20},{20,4},{22,6},{6,22},{8,24},{24... | collective-permute-start | bytes 393224 | tf_op jit(solution)/shard_map/ppermute | solution.py:144
  95.7 5.0 %collective-permute-start.26 = (f32[2,2,16,4,128]{4,3,2,1,0:T(4,128)S(1)}, f32[2,2,16,4,128]{4,3,2,1,0:T(4,128)S(1)}, u32[]{:S(2)}, u32[]{:S(2)}) collective-permute-start(f32[2,2,16,4,128]{4,3,2,1,0:T(4,128)S(1)} %pad_maximum_fusion.42), channel_id=1, source_target_pairs={{0,1},{1,0},{2,3},{3,2},{4,5},{5,4},{6,7},{7,6},{8,9},{9,8},{10,11... | collective-permute-start | bytes 393224 | tf_op jit(solution)/shard_map/ppermute | solution.py:124
  96.3 6.3 %collective-permute-start.24 = (f32[2,2,2,32,128]{4,3,2,1,0:T(8,128)S(1)}, f32[2,2,2,32,128]{4,3,2,1,0:T(8,128)S(1)}, u32[]{:S(2)}, u32[]{:S(2)}) collective-permute-start(f32[2,2,2,32,128]{4,3,2,1,0:T(8,128)S(1)} %get-tuple-element.28), channel_id=1, source_target_pairs={{16,18},{18,16},{2,4},{4,2},{20,22},{22,20},{6,8},{8,6},{24,26},{2... | collective-permute-start | bytes 393224 | tf_op jit(solution)/shard_map/ppermute | solution.py:144
  97.3 6.4 %collective-permute-start.25 = (f32[2,2,2,32,128]{4,3,2,1,0:T(8,128)S(1)}, f32[2,2,2,32,128]{4,3,2,1,0:T(8,128)S(1)}, u32[]{:S(2)}, u32[]{:S(2)}) collective-permute-start(f32[2,2,2,32,128]{4,3,2,1,0:T(8,128)S(1)} %get-tuple-element.29), channel_id=1, source_target_pairs={{0,16},{16,0},{18,2},{2,18},{4,20},{20,4},{22,6},{6,22},{8,24},{24... | collective-permute-start | bytes 393224 | tf_op jit(solution)/shard_map/ppermute | solution.py:144
  97.3 16.1 %collective-permute-start.28 = (f32[1,2,16,32,128]{4,3,2,1,0:T(8,128)S(1)}, f32[1,2,16,32,128]{4,3,2,1,0:T(8,128)S(1)}, u32[]{:S(2)}, u32[]{:S(2)}) collective-permute-start(f32[1,2,16,32,128]{4,3,2,1,0:T(8,128)S(1)} %slice.1158), channel_id=1, source_target_pairs={{16,0},{17,1},{18,2},{19,3},{20,4},{21,5},{22,6},{23,7},{24,8},{25... | collective-permute-start | bytes 1572872 | tf_op jit(solution)/shard_map/ppermute | solution.py:251
  106.8 10.1 %collective-permute-start.27 = (f32[1,2,16,32,128]{4,3,2,1,0:T(8,128)S(1)}, f32[1,2,16,32,128]{4,3,2,1,0:T(8,128)S(1)}, u32[]{:S(2)}, u32[]{:S(2)}) collective-permute-start(f32[1,2,16,32,128]{4,3,2,1,0:T(8,128)S(1)} %convolution_bitcast_fusion.7), channel_id=1, source_target_pairs={{0,16},{1,17},{2,18},{3,19},{4,20},{5,21},{6,22},{7,23},{8,24},{9,... | collective-permute-start | bytes 1572872 | tf_op jit(solution)/shard_map/ppermute | solution.py:251
  108.6 8.4 %copy-start.2 = (f32[1,2,32,32,128]{4,3,2,1,0:T(8,128)}, f32[1,2,32,32,128]{4,3,2,1,0:T(8,128)S(1)}, u32[]{:S(2)}) copy-start(f32[1,2,32,32,128]{4,3,2,1,0:T(8,128)S(1)} %fusion.67) | copy-start | bytes 3145732
  (2 other events, 4.3 us)

commit v11 on v10

--- a/solution.py
+++ b/solution.py
@@ -59,7 +59,7 @@
         d_ref[j] = d
         return c, d
 
-    lax.fori_loop(0, n, forward, (zero, zero), unroll=8)
+    lax.fori_loop(0, n, forward, (zero, zero), unroll=16)
 
     def backward(i, x):
         j = n - 1 - i
@@ -67,7 +67,7 @@
         out_ref[j] = x
         return x
 
-    lax.fori_loop(0, n, backward, zero, unroll=8)
+    lax.fori_loop(0, n, backward, zero, unroll=16)
 
 
 def vertical(diffusion):

time: 118 us -> 118 us (level)
  no operation moved by 1% of the time
where the time goes in v11:
time: 118 us
  waiting for transfers between devices  49.3 us (42%)
  starting transfers between devices  26.1 us (22%)
  other arithmetic  25.3 us (21%)
  matrix products  9.09 us (8%)
  local copies, waits for them, and re-layouts  4.17 us (4%)
  Pallas kernels  3 us (3%)
    ppermute x18, waiting for transfers between devices, swap_halo(): got.append(lax.ppermute(sent, axes, pairs))  20.8 us
    ppermute x9, waiting for transfers between devices, ring_halo(): got = lax.ppermute(jnp.concatenate([first, last], dim), axes, up)  20.2 us
    mul x9, other arithmetic, tendency(): return DT * (flow + kappa * laplace + react)  15.1 us
    ppermute x18, starting transfers between devices, swap_halo(): got.append(lax.ppermute(sent, axes, pairs))  14.1 us
    ppermute x9, starting transfers between devices, ring_halo(): got = lax.ppermute(jnp.concatenate([first, last], dim), axes, up)  9.2 us
    dot_general x9, matrix products, column_solve(): jnp.einsum('lsxyk,sjk->lsxyj', rhs, inverse, precision=lax.Precision.HIGH...  9.09 us
    ppermute x2, waiting for transfers between devices, on_device(): arrived = lax.ppermute(states[level][None], 'corr', pairs)  8.34 us
    add x5, other arithmetic, on_device(): total = total + (quad + g_now[l - 1] - e_hist[l - 1][m])  3.62 us
  transfers between devices with their start and end apart: 29, of which 21 were waited for; matrix products, arithmetic and copies ran while one was open for 5% of the time, Pallas kernels for 3%

profile of v11, /device:TPU:0, one launch (start us, length us, event | category | flops | bytes accessed | tf_op | source)
XLA Modules:
  0.0 117.7 jit_solution(11183501596687992018)
XLA Ops:
  1.1 4.6 %collective-permute-start = (f32[1,2,2,32,128]{4,3,2,1,0:T(8,128)S(1)}, f32[1,2,2,32,128]{4,3,2,1,0:T(8,128)S(1)}, u32[]{:S(2)}, u32[]{:S(2)}) collective-permute-start(f32[1,2,2,32,128]{4,3,2,1,0:T(8,128)S(1)} %get-tuple-element.98), channel_id=1, source_target_pairs={{16,18},{18,16},{2,4},{4,2},{20,22},{22,20},{6,8},{8,6},{24,26},{2... | collective-permute-start | bytes 196616 | tf_op jit(solution)/shard_map/ppermute | solution.py:144
  5.7 1.6 %collective-permute-start.2 = (f32[1,2,16,4,128]{4,3,2,1,0:T(4,128)S(1)}, f32[1,2,16,4,128]{4,3,2,1,0:T(4,128)S(1)}, u32[]{:S(2)}, u32[]{:S(2)}) collective-permute-start(f32[1,2,16,4,128]{4,3,2,1,0:T(4,128)S(1)} %pad_maximum_fusion.43), channel_id=1, source_target_pairs={{0,1},{1,0},{2,3},{3,2},{4,5},{5,4},{6,7},{7,6},{8,9},{9,8},{10,11... | collective-permute-start | bytes 196616 | tf_op jit(solution)/shard_map/ppermute | solution.py:124
  7.7 3.0 %shard_map.118 = f32[128,2,128]{2,1,0:T(2,128)} custom-call(f32[2,128]{1,0:T(2,128)} %diff_ref.1), custom_call_target="tpu_custom_call" | custom-call | flops 393216 | bytes 262144 | tf_op jit(solution)/shard_map/pallas_call | solution.py:78
  13.8 1.7 %collective-permute-start.3 = (f32[2,2,2,32,128]{4,3,2,1,0:T(8,128)S(1)}, f32[2,2,2,32,128]{4,3,2,1,0:T(8,128)S(1)}, u32[]{:S(2)}, u32[]{:S(2)}) collective-permute-start(f32[2,2,2,32,128]{4,3,2,1,0:T(8,128)S(1)} %get-tuple-element.85), channel_id=1, source_target_pairs={{16,18},{18,16},{2,4},{4,2},{20,22},{22,20},{6,8},{8,6},{24,26},{2... | collective-permute-start | bytes 393224 | tf_op jit(solution)/shard_map/ppermute | solution.py:144
  16.7 3.6 %collective-permute-done.3 = f32[2,2,2,32,128]{4,3,2,1,0:T(8,128)S(1)} collective-permute-done((f32[2,2,2,32,128]{4,3,2,1,0:T(8,128)S(1)}, f32[2,2,2,32,128]{4,3,2,1,0:T(8,128)S(1)}, u32[]{:S(2)}, u32[]{:S(2)}) %collective-permute-start.3) | collective-permute-done | bytes 131104 | tf_op jit(solution)/shard_map/ppermute | solution.py:144
  27.0 3.4 %collective-permute-done.8 = f32[2,2,16,4,128]{4,3,2,1,0:T(4,128)S(1)} collective-permute-done((f32[2,2,16,4,128]{4,3,2,1,0:T(4,128)S(1)}, f32[2,2,16,4,128]{4,3,2,1,0:T(4,128)S(1)}, u32[]{:S(2)}, u32[]{:S(2)}) %collective-permute-start.8) | collective-permute-done | bytes 131104 | tf_op jit(solution)/shard_map/ppermute | solution.py:124
  30.4 1.8 %collective-permute-done.6 = f32[2,2,2,32,128]{4,3,2,1,0:T(8,128)S(1)} collective-permute-done((f32[2,2,2,32,128]{4,3,2,1,0:T(8,128)S(1)}, f32[2,2,2,32,128]{4,3,2,1,0:T(8,128)S(1)}, u32[]{:S(2)}, u32[]{:S(2)}) %collective-permute-start.6) | collective-permute-done | bytes 131104 | tf_op jit(solution)/shard_map/ppermute | solution.py:144
  32.2 1.8 %fusion.37 = f32[2,2,16,32,128]{4,3,2,1,0:T(8,128)S(1)} fusion(f32[2,1,16,32,128]{4,3,2,1,0:T(8,128)S(1)} %get-tuple-element.81, f32[2,1,16,32,128]{4,3,2,1,0:T(8,128)S(1)} %get-tuple-element.80, f32[2,2,16,32,128]{4,3,2,1,0:T(8,128)S(1)} %convolution_bitcast_fusion.6, f32[2,2,16,2,128]{4,3,2,1,0:T(2,128)S(1)} %get-tuple-element.133, ...), kind=kLoop, calls=%fused_computation.148 | loop fusion | flops 9175040 | bytes 4063240 | tf_op jit(solution)/shard_map/mul | solution.py:182
  36.3 1.6 %collective-permute-start.11 = (f32[2,2,16,4,128]{4,3,2,1,0:T(4,128)S(1)}, f32[2,2,16,4,128]{4,3,2,1,0:T(4,128)S(1)}, u32[]{:S(2)}, u32[]{:S(2)}) collective-permute-start(f32[2,2,16,4,128]{4,3,2,1,0:T(4,128)S(1)} %pad_maximum_fusion.37), channel_id=1, source_target_pairs={{0,1},{1,0},{2,3},{3,2},{4,5},{5,4},{6,7},{7,6},{8,9},{9,8},{10,11... | collective-permute-start | bytes 393224 | tf_op jit(solution)/shard_map/ppermute | solution.py:124
  39.6 1.7 %collective-permute-done.11 = f32[2,2,16,4,128]{4,3,2,1,0:T(4,128)S(1)} collective-permute-done((f32[2,2,16,4,128]{4,3,2,1,0:T(4,128)S(1)}, f32[2,2,16,4,128]{4,3,2,1,0:T(4,128)S(1)}, u32[]{:S(2)}, u32[]{:S(2)}) %collective-permute-start.11) | collective-permute-done | bytes 131104 | tf_op jit(solution)/shard_map/ppermute | solution.py:124
  41.4 1.6 %collective-permute-done.10 = f32[2,2,2,32,128]{4,3,2,1,0:T(8,128)S(1)} collective-permute-done((f32[2,2,2,32,128]{4,3,2,1,0:T(8,128)S(1)}, f32[2,2,2,32,128]{4,3,2,1,0:T(8,128)S(1)}, u32[]{:S(2)}, u32[]{:S(2)}) %collective-permute-start.10) | collective-permute-done | bytes 131104 | tf_op jit(solution)/shard_map/ppermute | solution.py:144
  42.9 1.9 %collective-permute-done.9 = f32[2,2,2,32,128]{4,3,2,1,0:T(8,128)S(1)} collective-permute-done((f32[2,2,2,32,128]{4,3,2,1,0:T(8,128)S(1)}, f32[2,2,2,32,128]{4,3,2,1,0:T(8,128)S(1)}, u32[]{:S(2)}, u32[]{:S(2)}) %collective-permute-start.9) | collective-permute-done | bytes 131104 | tf_op jit(solution)/shard_map/ppermute | solution.py:144
  44.8 2.0 %fusion.41 = f32[2,2,16,32,128]{4,3,2,1,0:T(8,128)S(1)} fusion(f32[2,1,16,32,128]{4,3,2,1,0:T(8,128)S(1)} %get-tuple-element.73, f32[2,1,16,32,128]{4,3,2,1,0:T(8,128)S(1)} %get-tuple-element.72, f32[2,2,16,32,128]{4,3,2,1,0:T(8,128)S(1)} %convolution_bitcast_fusion.5, f32[2,2,16,2,128]{4,3,2,1,0:T(2,128)S(1)} %get-tuple-element.131, ...), kind=kLoop, calls=%fused_computation.153 | loop fusion | flops 9175040 | bytes 4063240 | tf_op jit(solution)/shard_map/mul | solution.py:182
  50.5 3.7 %collective-permute-done.14 = f32[2,2,16,4,128]{4,3,2,1,0:T(4,128)S(1)} collective-permute-done((f32[2,2,16,4,128]{4,3,2,1,0:T(4,128)S(1)}, f32[2,2,16,4,128]{4,3,2,1,0:T(4,128)S(1)}, u32[]{:S(2)}, u32[]{:S(2)}) %collective-permute-start.14) | collective-permute-done | bytes 131104 | tf_op jit(solution)/shard_map/ppermute | solution.py:124
  54.2 1.8 %collective-permute-done.12 = f32[2,2,2,32,128]{4,3,2,1,0:T(8,128)S(1)} collective-permute-done((f32[2,2,2,32,128]{4,3,2,1,0:T(8,128)S(1)}, f32[2,2,2,32,128]{4,3,2,1,0:T(8,128)S(1)}, u32[]{:S(2)}, u32[]{:S(2)}) %collective-permute-start.12) | collective-permute-done | bytes 131104 | tf_op jit(solution)/shard_map/ppermute | solution.py:144
  56.0 1.8 %fusion.45 = f32[2,2,16,32,128]{4,3,2,1,0:T(8,128)S(1)} fusion(f32[2,1,16,32,128]{4,3,2,1,0:T(8,128)S(1)} %get-tuple-element.65, f32[2,1,16,32,128]{4,3,2,1,0:T(8,128)S(1)} %get-tuple-element.64, f32[2,2,16,32,128]{4,3,2,1,0:T(8,128)S(1)} %convolution_bitcast_fusion.4, f32[2,2,16,2,128]{4,3,2,1,0:T(2,128)S(1)} %get-tuple-element.129, ...), kind=kLoop, calls=%fused_computation.158 | loop fusion | flops 9175040 | bytes 4063240 | tf_op jit(solution)/shard_map/mul | solution.py:182
  60.2 1.6 %collective-permute-start.17 = (f32[2,2,16,4,128]{4,3,2,1,0:T(4,128)S(1)}, f32[2,2,16,4,128]{4,3,2,1,0:T(4,128)S(1)}, u32[]{:S(2)}, u32[]{:S(2)}) collective-permute-start(f32[2,2,16,4,128]{4,3,2,1,0:T(4,128)S(1)} %pad_maximum_fusion.39), channel_id=1, source_target_pairs={{0,1},{1,0},{2,3},{3,2},{4,5},{5,4},{6,7},{7,6},{8,9},{9,8},{10,11... | collective-permute-start | bytes 393224 | tf_op jit(solution)/shard_map/ppermute | solution.py:124
  62.8 2.5 %collective-permute-done.17 = f32[2,2,16,4,128]{4,3,2,1,0:T(4,128)S(1)} collective-permute-done((f32[2,2,16,4,128]{4,3,2,1,0:T(4,128)S(1)}, f32[2,2,16,4,128]{4,3,2,1,0:T(4,128)S(1)}, u32[]{:S(2)}, u32[]{:S(2)}) %collective-permute-start.17) | collective-permute-done | bytes 131104 | tf_op jit(solution)/shard_map/ppermute | solution.py:124
  65.3 2.8 %collective-permute-done.15 = f32[2,2,2,32,128]{4,3,2,1,0:T(8,128)S(1)} collective-permute-done((f32[2,2,2,32,128]{4,3,2,1,0:T(8,128)S(1)}, f32[2,2,2,32,128]{4,3,2,1,0:T(8,128)S(1)}, u32[]{:S(2)}, u32[]{:S(2)}) %collective-permute-start.15) | collective-permute-done | bytes 131104 | tf_op jit(solution)/shard_map/ppermute | solution.py:144
  68.1 1.8 %fusion.49 = f32[2,2,16,32,128]{4,3,2,1,0:T(8,128)S(1)} fusion(f32[2,1,16,32,128]{4,3,2,1,0:T(8,128)S(1)} %get-tuple-element.57, f32[2,1,16,32,128]{4,3,2,1,0:T(8,128)S(1)} %get-tuple-element.56, f32[2,2,16,32,128]{4,3,2,1,0:T(8,128)S(1)} %convolution_bitcast_fusion.3, f32[2,2,16,2,128]{4,3,2,1,0:T(2,128)S(1)} %get-tuple-element.127, ...), kind=kLoop, calls=%fused_computation.163 | loop fusion | flops 9175040 | bytes 4063240 | tf_op jit(solution)/shard_map/mul | solution.py:182
  73.8 3.5 %collective-permute-done.20 = f32[2,2,16,4,128]{4,3,2,1,0:T(4,128)S(1)} collective-permute-done((f32[2,2,16,4,128]{4,3,2,1,0:T(4,128)S(1)}, f32[2,2,16,4,128]{4,3,2,1,0:T(4,128)S(1)}, u32[]{:S(2)}, u32[]{:S(2)}) %collective-permute-start.20) | collective-permute-done | bytes 131104 | tf_op jit(solution)/shard_map/ppermute | solution.py:124
  77.3 1.8 %collective-permute-done.18 = f32[2,2,2,32,128]{4,3,2,1,0:T(8,128)S(1)} collective-permute-done((f32[2,2,2,32,128]{4,3,2,1,0:T(8,128)S(1)}, f32[2,2,2,32,128]{4,3,2,1,0:T(8,128)S(1)}, u32[]{:S(2)}, u32[]{:S(2)}) %collective-permute-start.18) | collective-permute-done | bytes 131104 | tf_op jit(solution)/shard_map/ppermute | solution.py:144
  79.1 2.1 %fusion.53 = f32[2,2,16,32,128]{4,3,2,1,0:T(8,128)S(1)} fusion(f32[2,1,16,32,128]{4,3,2,1,0:T(8,128)S(1)} %get-tuple-element.49, f32[2,1,16,32,128]{4,3,2,1,0:T(8,128)S(1)} %get-tuple-element.48, f32[2,2,16,32,128]{4,3,2,1,0:T(8,128)S(1)} %convolution_bitcast_fusion.2, f32[2,2,16,2,128]{4,3,2,1,0:T(2,128)S(1)} %get-tuple-element.125, ...), kind=kLoop, calls=%fused_computation.168 | loop fusion | flops 9175040 | bytes 4063240 | tf_op jit(solution)/shard_map/mul | solution.py:182
  83.5 1.6 %collective-permute-start.23 = (f32[2,2,16,4,128]{4,3,2,1,0:T(4,128)S(1)}, f32[2,2,16,4,128]{4,3,2,1,0:T(4,128)S(1)}, u32[]{:S(2)}, u32[]{:S(2)}) collective-permute-start(f32[2,2,16,4,128]{4,3,2,1,0:T(4,128)S(1)} %pad_maximum_fusion.41), channel_id=1, source_target_pairs={{0,1},{1,0},{2,3},{3,2},{4,5},{5,4},{6,7},{7,6},{8,9},{9,8},{10,11... | collective-permute-start | bytes 393224 | tf_op jit(solution)/shard_map/ppermute | solution.py:124
  86.0 2.5 %collective-permute-done.23 = f32[2,2,16,4,128]{4,3,2,1,0:T(4,128)S(1)} collective-permute-done((f32[2,2,16,4,128]{4,3,2,1,0:T(4,128)S(1)}, f32[2,2,16,4,128]{4,3,2,1,0:T(4,128)S(1)}, u32[]{:S(2)}, u32[]{:S(2)}) %collective-permute-start.23) | collective-permute-done | bytes 131104 | tf_op jit(solution)/shard_map/ppermute | solution.py:124
  88.6 2.8 %collective-permute-done.21 = f32[2,2,2,32,128]{4,3,2,1,0:T(8,128)S(1)} collective-permute-done((f32[2,2,2,32,128]{4,3,2,1,0:T(8,128)S(1)}, f32[2,2,2,32,128]{4,3,2,1,0:T(8,128)S(1)}, u32[]{:S(2)}, u32[]{:S(2)}) %collective-permute-start.21) | collective-permute-done | bytes 131104 | tf_op jit(solution)/shard_map/ppermute | solution.py:144
  91.4 1.8 %fusion.57 = f32[2,2,16,32,128]{4,3,2,1,0:T(8,128)S(1)} fusion(f32[2,1,16,32,128]{4,3,2,1,0:T(8,128)S(1)} %get-tuple-element.41, f32[2,1,16,32,128]{4,3,2,1,0:T(8,128)S(1)} %get-tuple-element.40, f32[2,2,16,32,128]{4,3,2,1,0:T(8,128)S(1)} %convolution_bitcast_fusion.1, f32[2,2,16,2,128]{4,3,2,1,0:T(2,128)S(1)} %get-tuple-element.123, ...), kind=kLoop, calls=%fused_computation.173 | loop fusion | flops 9175040 | bytes 4063240 | tf_op jit(solution)/shard_map/mul | solution.py:182
  98.4 2.2 %collective-permute-done.26 = f32[2,2,16,4,128]{4,3,2,1,0:T(4,128)S(1)} collective-permute-done((f32[2,2,16,4,128]{4,3,2,1,0:T(4,128)S(1)}, f32[2,2,16,4,128]{4,3,2,1,0:T(4,128)S(1)}, u32[]{:S(2)}, u32[]{:S(2)}) %collective-permute-start.26) | collective-permute-done | bytes 131104 | tf_op jit(solution)/shard_map/ppermute | solution.py:124
  100.7 1.8 %collective-permute-done.24 = f32[2,2,2,32,128]{4,3,2,1,0:T(8,128)S(1)} collective-permute-done((f32[2,2,2,32,128]{4,3,2,1,0:T(8,128)S(1)}, f32[2,2,2,32,128]{4,3,2,1,0:T(8,128)S(1)}, u32[]{:S(2)}, u32[]{:S(2)}) %collective-permute-start.24) | collective-permute-done | bytes 131104 | tf_op jit(solution)/shard_map/ppermute | solution.py:144
  103.5 1.9 %fusion.61 = f32[2,2,16,32,128]{4,3,2,1,0:T(8,128)S(1)} fusion(f32[2,1,16,32,128]{4,3,2,1,0:T(8,128)S(1)} %get-tuple-element.33, f32[2,1,16,32,128]{4,3,2,1,0:T(8,128)S(1)} %get-tuple-element.32, f32[2,2,16,32,128]{4,3,2,1,0:T(8,128)S(1)} %convolution_bitcast_fusion, f32[2,2,16,2,128]{4,3,2,1,0:T(2,128)S(1)} %get-tuple-element.121, ...), kind=kLoop, calls=%fused_computation.178 | loop fusion | flops 9175040 | bytes 4063240 | tf_op jit(solution)/shard_map/mul | solution.py:182
  108.5 4.8 %collective-permute-done.28 = f32[1,2,16,32,128]{4,3,2,1,0:T(8,128)S(1)} collective-permute-done((f32[1,2,16,32,128]{4,3,2,1,0:T(8,128)S(1)}, f32[1,2,16,32,128]{4,3,2,1,0:T(8,128)S(1)}, u32[]{:S(2)}, u32[]{:S(2)}) %collective-permute-start.28) | collective-permute-done | bytes 524320 | tf_op jit(solution)/shard_map/ppermute | solution.py:251
  113.3 3.6 %collective-permute-done.27 = f32[1,2,16,32,128]{4,3,2,1,0:T(8,128)S(1)} collective-permute-done((f32[1,2,16,32,128]{4,3,2,1,0:T(8,128)S(1)}, f32[1,2,16,32,128]{4,3,2,1,0:T(8,128)S(1)}, u32[]{:S(2)}, u32[]{:S(2)}) %collective-permute-start.27) | collective-permute-done | bytes 524320 | tf_op jit(solution)/shard_map/ppermute | solution.py:251
  (137 shorter events, 40.8 us)
Async XLA Ops:
  1.1 10.8 %collective-permute-start = (f32[1,2,2,32,128]{4,3,2,1,0:T(8,128)S(1)}, f32[1,2,2,32,128]{4,3,2,1,0:T(8,128)S(1)}, u32[]{:S(2)}, u32[]{:S(2)}) collective-permute-start(f32[1,2,2,32,128]{4,3,2,1,0:T(8,128)S(1)} %get-tuple-element.98), channel_id=1, source_target_pairs={{16,18},{18,16},{2,4},{4,2},{20,22},{22,20},{6,8},{8,6},{24,26},{2... | collective-permute-start | bytes 196616 | tf_op jit(solution)/shard_map/ppermute | solution.py:144
  5.7 6.2 %collective-permute-start.1 = (f32[1,2,2,32,128]{4,3,2,1,0:T(8,128)S(1)}, f32[1,2,2,32,128]{4,3,2,1,0:T(8,128)S(1)}, u32[]{:S(2)}, u32[]{:S(2)}) collective-permute-start(f32[1,2,2,32,128]{4,3,2,1,0:T(8,128)S(1)} %get-tuple-element.99), channel_id=1, source_target_pairs={{0,16},{16,0},{18,2},{2,18},{4,20},{20,4},{22,6},{6,22},{8,24},{24... | collective-permute-start | bytes 196616 | tf_op jit(solution)/shard_map/ppermute | solution.py:144
  5.7 6.1 %collective-permute-start.2 = (f32[1,2,16,4,128]{4,3,2,1,0:T(4,128)S(1)}, f32[1,2,16,4,128]{4,3,2,1,0:T(4,128)S(1)}, u32[]{:S(2)}, u32[]{:S(2)}) collective-permute-start(f32[1,2,16,4,128]{4,3,2,1,0:T(4,128)S(1)} %pad_maximum_fusion.43), channel_id=1, source_target_pairs={{0,1},{1,0},{2,3},{3,2},{4,5},{5,4},{6,7},{7,6},{8,9},{9,8},{10,11... | collective-permute-start | bytes 196616 | tf_op jit(solution)/shard_map/ppermute | solution.py:124
  7.6 4.3 %copy-start.1 = (f32[2,32,32,128]{3,2,1,0:T(8,128)S(1)}, f32[2,32,32,128]{3,2,1,0:T(8,128)}, u32[]{:S(2)}) copy-start(f32[2,32,32,128]{3,2,1,0:T(8,128)} %param.12) | copy-start | bytes 3145732
  7.6 4.3 %copy-start.3 = (f32[2]{0:T(128)S(1)}, f32[2]{0:T(128)}, u32[]{:S(2)}) copy-start(f32[2]{0:T(128)} %constant.140) | copy-start | bytes 28
  13.8 6.5 %collective-permute-start.3 = (f32[2,2,2,32,128]{4,3,2,1,0:T(8,128)S(1)}, f32[2,2,2,32,128]{4,3,2,1,0:T(8,128)S(1)}, u32[]{:S(2)}, u32[]{:S(2)}) collective-permute-start(f32[2,2,2,32,128]{4,3,2,1,0:T(8,128)S(1)} %get-tuple-element.85), channel_id=1, source_target_pairs={{16,18},{18,16},{2,4},{4,2},{20,22},{22,20},{6,8},{8,6},{24,26},{2... | collective-permute-start | bytes 393224 | tf_op jit(solution)/shard_map/ppermute | solution.py:144
  15.4 5.0 %collective-permute-start.4 = (f32[2,2,2,32,128]{4,3,2,1,0:T(8,128)S(1)}, f32[2,2,2,32,128]{4,3,2,1,0:T(8,128)S(1)}, u32[]{:S(2)}, u32[]{:S(2)}) collective-permute-start(f32[2,2,2,32,128]{4,3,2,1,0:T(8,128)S(1)} %get-tuple-element.84), channel_id=1, source_target_pairs={{0,16},{16,0},{18,2},{2,18},{4,20},{20,4},{22,6},{6,22},{8,24},{24... | collective-permute-start | bytes 393224 | tf_op jit(solution)/shard_map/ppermute | solution.py:144
  16.0 5.6 %collective-permute-start.5 = (f32[2,2,16,4,128]{4,3,2,1,0:T(4,128)S(1)}, f32[2,2,16,4,128]{4,3,2,1,0:T(4,128)S(1)}, u32[]{:S(2)}, u32[]{:S(2)}) collective-permute-start(f32[2,2,16,4,128]{4,3,2,1,0:T(4,128)S(1)} %pad_maximum_fusion.35), channel_id=1, source_target_pairs={{0,1},{1,0},{2,3},{3,2},{4,5},{5,4},{6,7},{7,6},{8,9},{9,8},{10,11... | collective-permute-start | bytes 393224 | tf_op jit(solution)/shard_map/ppermute | solution.py:124
  25.3 5.0 %collective-permute-start.8 = (f32[2,2,16,4,128]{4,3,2,1,0:T(4,128)S(1)}, f32[2,2,16,4,128]{4,3,2,1,0:T(4,128)S(1)}, u32[]{:S(2)}, u32[]{:S(2)}) collective-permute-start(f32[2,2,16,4,128]{4,3,2,1,0:T(4,128)S(1)} %pad_maximum_fusion.36), channel_id=1, source_target_pairs={{0,1},{1,0},{2,3},{3,2},{4,5},{5,4},{6,7},{7,6},{8,9},{9,8},{10,11... | collective-permute-start | bytes 393224 | tf_op jit(solution)/shard_map/ppermute | solution.py:124
  25.9 6.3 %collective-permute-start.6 = (f32[2,2,2,32,128]{4,3,2,1,0:T(8,128)S(1)}, f32[2,2,2,32,128]{4,3,2,1,0:T(8,128)S(1)}, u32[]{:S(2)}, u32[]{:S(2)}) collective-permute-start(f32[2,2,2,32,128]{4,3,2,1,0:T(8,128)S(1)} %get-tuple-element.76), channel_id=1, source_target_pairs={{16,18},{18,16},{2,4},{4,2},{20,22},{22,20},{6,8},{8,6},{24,26},{2... | collective-permute-start | bytes 393224 | tf_op jit(solution)/shard_map/ppermute | solution.py:144
  26.6 5.5 %collective-permute-start.7 = (f32[2,2,2,32,128]{4,3,2,1,0:T(8,128)S(1)}, f32[2,2,2,32,128]{4,3,2,1,0:T(8,128)S(1)}, u32[]{:S(2)}, u32[]{:S(2)}) collective-permute-start(f32[2,2,2,32,128]{4,3,2,1,0:T(8,128)S(1)} %get-tuple-element.77), channel_id=1, source_target_pairs={{0,16},{16,0},{18,2},{2,18},{4,20},{20,4},{22,6},{6,22},{8,24},{24... | collective-permute-start | bytes 393224 | tf_op jit(solution)/shard_map/ppermute | solution.py:144
  36.3 5.0 %collective-permute-start.11 = (f32[2,2,16,4,128]{4,3,2,1,0:T(4,128)S(1)}, f32[2,2,16,4,128]{4,3,2,1,0:T(4,128)S(1)}, u32[]{:S(2)}, u32[]{:S(2)}) collective-permute-start(f32[2,2,16,4,128]{4,3,2,1,0:T(4,128)S(1)} %pad_maximum_fusion.37), channel_id=1, source_target_pairs={{0,1},{1,0},{2,3},{3,2},{4,5},{5,4},{6,7},{7,6},{8,9},{9,8},{10,11... | collective-permute-start | bytes 393224 | tf_op jit(solution)/shard_map/ppermute | solution.py:124
  37.9 5.0 %collective-permute-start.10 = (f32[2,2,2,32,128]{4,3,2,1,0:T(8,128)S(1)}, f32[2,2,2,32,128]{4,3,2,1,0:T(8,128)S(1)}, u32[]{:S(2)}, u32[]{:S(2)}) collective-permute-start(f32[2,2,2,32,128]{4,3,2,1,0:T(8,128)S(1)} %get-tuple-element.69), channel_id=1, source_target_pairs={{0,16},{16,0},{18,2},{2,18},{4,20},{20,4},{22,6},{6,22},{8,24},{24... | collective-permute-start | bytes 393224 | tf_op jit(solution)/shard_map/ppermute | solution.py:144
  38.6 6.2 %collective-permute-start.9 = (f32[2,2,2,32,128]{4,3,2,1,0:T(8,128)S(1)}, f32[2,2,2,32,128]{4,3,2,1,0:T(8,128)S(1)}, u32[]{:S(2)}, u32[]{:S(2)}) collective-permute-start(f32[2,2,2,32,128]{4,3,2,1,0:T(8,128)S(1)} %get-tuple-element.68), channel_id=1, source_target_pairs={{16,18},{18,16},{2,4},{4,2},{20,22},{22,20},{6,8},{8,6},{24,26},{2... | collective-permute-start | bytes 393224 | tf_op jit(solution)/shard_map/ppermute | solution.py:144
  49.1 5.0 %collective-permute-start.14 = (f32[2,2,16,4,128]{4,3,2,1,0:T(4,128)S(1)}, f32[2,2,16,4,128]{4,3,2,1,0:T(4,128)S(1)}, u32[]{:S(2)}, u32[]{:S(2)}) collective-permute-start(f32[2,2,16,4,128]{4,3,2,1,0:T(4,128)S(1)} %pad_maximum_fusion.38), channel_id=1, source_target_pairs={{0,1},{1,0},{2,3},{3,2},{4,5},{5,4},{6,7},{7,6},{8,9},{9,8},{10,11... | collective-permute-start | bytes 393224 | tf_op jit(solution)/shard_map/ppermute | solution.py:124
  49.7 6.3 %collective-permute-start.12 = (f32[2,2,2,32,128]{4,3,2,1,0:T(8,128)S(1)}, f32[2,2,2,32,128]{4,3,2,1,0:T(8,128)S(1)}, u32[]{:S(2)}, u32[]{:S(2)}) collective-permute-start(f32[2,2,2,32,128]{4,3,2,1,0:T(8,128)S(1)} %get-tuple-element.60), channel_id=1, source_target_pairs={{16,18},{18,16},{2,4},{4,2},{20,22},{22,20},{6,8},{8,6},{24,26},{2... | collective-permute-start | bytes 393224 | tf_op jit(solution)/shard_map/ppermute | solution.py:144
  50.5 5.5 %collective-permute-start.13 = (f32[2,2,2,32,128]{4,3,2,1,0:T(8,128)S(1)}, f32[2,2,2,32,128]{4,3,2,1,0:T(8,128)S(1)}, u32[]{:S(2)}, u32[]{:S(2)}) collective-permute-start(f32[2,2,2,32,128]{4,3,2,1,0:T(8,128)S(1)} %get-tuple-element.61), channel_id=1, source_target_pairs={{0,16},{16,0},{18,2},{2,18},{4,20},{20,4},{22,6},{6,22},{8,24},{24... | collective-permute-start | bytes 393224 | tf_op jit(solution)/shard_map/ppermute | solution.py:144
  60.2 5.0 %collective-permute-start.17 = (f32[2,2,16,4,128]{4,3,2,1,0:T(4,128)S(1)}, f32[2,2,16,4,128]{4,3,2,1,0:T(4,128)S(1)}, u32[]{:S(2)}, u32[]{:S(2)}) collective-permute-start(f32[2,2,16,4,128]{4,3,2,1,0:T(4,128)S(1)} %pad_maximum_fusion.39), channel_id=1, source_target_pairs={{0,1},{1,0},{2,3},{3,2},{4,5},{5,4},{6,7},{7,6},{8,9},{9,8},{10,11... | collective-permute-start | bytes 393224 | tf_op jit(solution)/shard_map/ppermute | solution.py:124
  61.8 6.3 %collective-permute-start.15 = (f32[2,2,2,32,128]{4,3,2,1,0:T(8,128)S(1)}, f32[2,2,2,32,128]{4,3,2,1,0:T(8,128)S(1)}, u32[]{:S(2)}, u32[]{:S(2)}) collective-permute-start(f32[2,2,2,32,128]{4,3,2,1,0:T(8,128)S(1)} %get-tuple-element.52), channel_id=1, source_target_pairs={{16,18},{18,16},{2,4},{4,2},{20,22},{22,20},{6,8},{8,6},{24,26},{2... | collective-permute-start | bytes 393224 | tf_op jit(solution)/shard_map/ppermute | solution.py:144
  62.8 5.3 %collective-permute-start.16 = (f32[2,2,2,32,128]{4,3,2,1,0:T(8,128)S(1)}, f32[2,2,2,32,128]{4,3,2,1,0:T(8,128)S(1)}, u32[]{:S(2)}, u32[]{:S(2)}) collective-permute-start(f32[2,2,2,32,128]{4,3,2,1,0:T(8,128)S(1)} %get-tuple-element.53), channel_id=1, source_target_pairs={{0,16},{16,0},{18,2},{2,18},{4,20},{20,4},{22,6},{6,22},{8,24},{24... | collective-permute-start | bytes 393224 | tf_op jit(solution)/shard_map/ppermute | solution.py:144
  72.2 5.0 %collective-permute-start.20 = (f32[2,2,16,4,128]{4,3,2,1,0:T(4,128)S(1)}, f32[2,2,16,4,128]{4,3,2,1,0:T(4,128)S(1)}, u32[]{:S(2)}, u32[]{:S(2)}) collective-permute-start(f32[2,2,16,4,128]{4,3,2,1,0:T(4,128)S(1)} %pad_maximum_fusion.40), channel_id=1, source_target_pairs={{0,1},{1,0},{2,3},{3,2},{4,5},{5,4},{6,7},{7,6},{8,9},{9,8},{10,11... | collective-permute-start | bytes 393224 | tf_op jit(solution)/shard_map/ppermute | solution.py:124
  72.8 6.3 %collective-permute-start.18 = (f32[2,2,2,32,128]{4,3,2,1,0:T(8,128)S(1)}, f32[2,2,2,32,128]{4,3,2,1,0:T(8,128)S(1)}, u32[]{:S(2)}, u32[]{:S(2)}) collective-permute-start(f32[2,2,2,32,128]{4,3,2,1,0:T(8,128)S(1)} %get-tuple-element.44), channel_id=1, source_target_pairs={{16,18},{18,16},{2,4},{4,2},{20,22},{22,20},{6,8},{8,6},{24,26},{2... | collective-permute-start | bytes 393224 | tf_op jit(solution)/shard_map/ppermute | solution.py:144
  73.8 5.3 %collective-permute-start.19 = (f32[2,2,2,32,128]{4,3,2,1,0:T(8,128)S(1)}, f32[2,2,2,32,128]{4,3,2,1,0:T(8,128)S(1)}, u32[]{:S(2)}, u32[]{:S(2)}) collective-permute-start(f32[2,2,2,32,128]{4,3,2,1,0:T(8,128)S(1)} %get-tuple-element.45), channel_id=1, source_target_pairs={{0,16},{16,0},{18,2},{2,18},{4,20},{20,4},{22,6},{6,22},{8,24},{24... | collective-permute-start | bytes 393224 | tf_op jit(solution)/shard_map/ppermute | solution.py:144
  83.5 5.0 %collective-permute-start.23 = (f32[2,2,16,4,128]{4,3,2,1,0:T(4,128)S(1)}, f32[2,2,16,4,128]{4,3,2,1,0:T(4,128)S(1)}, u32[]{:S(2)}, u32[]{:S(2)}) collective-permute-start(f32[2,2,16,4,128]{4,3,2,1,0:T(4,128)S(1)} %pad_maximum_fusion.41), channel_id=1, source_target_pairs={{0,1},{1,0},{2,3},{3,2},{4,5},{5,4},{6,7},{7,6},{8,9},{9,8},{10,11... | collective-permute-start | bytes 393224 | tf_op jit(solution)/shard_map/ppermute | solution.py:124
  85.1 6.3 %collective-permute-start.21 = (f32[2,2,2,32,128]{4,3,2,1,0:T(8,128)S(1)}, f32[2,2,2,32,128]{4,3,2,1,0:T(8,128)S(1)}, u32[]{:S(2)}, u32[]{:S(2)}) collective-permute-start(f32[2,2,2,32,128]{4,3,2,1,0:T(8,128)S(1)} %get-tuple-element.36), channel_id=1, source_target_pairs={{16,18},{18,16},{2,4},{4,2},{20,22},{22,20},{6,8},{8,6},{24,26},{2... | collective-permute-start | bytes 393224 | tf_op jit(solution)/shard_map/ppermute | solution.py:144
  86.0 5.3 %collective-permute-start.22 = (f32[2,2,2,32,128]{4,3,2,1,0:T(8,128)S(1)}, f32[2,2,2,32,128]{4,3,2,1,0:T(8,128)S(1)}, u32[]{:S(2)}, u32[]{:S(2)}) collective-permute-start(f32[2,2,2,32,128]{4,3,2,1,0:T(8,128)S(1)} %get-tuple-element.37), channel_id=1, source_target_pairs={{0,16},{16,0},{18,2},{2,18},{4,20},{20,4},{22,6},{6,22},{8,24},{24... | collective-permute-start | bytes 393224 | tf_op jit(solution)/shard_map/ppermute | solution.py:144
  95.6 5.0 %collective-permute-start.26 = (f32[2,2,16,4,128]{4,3,2,1,0:T(4,128)S(1)}, f32[2,2,16,4,128]{4,3,2,1,0:T(4,128)S(1)}, u32[]{:S(2)}, u32[]{:S(2)}) collective-permute-start(f32[2,2,16,4,128]{4,3,2,1,0:T(4,128)S(1)} %pad_maximum_fusion.42), channel_id=1, source_target_pairs={{0,1},{1,0},{2,3},{3,2},{4,5},{5,4},{6,7},{7,6},{8,9},{9,8},{10,11... | collective-permute-start | bytes 393224 | tf_op jit(solution)/shard_map/ppermute | solution.py:124
  96.2 6.3 %collective-permute-start.24 = (f32[2,2,2,32,128]{4,3,2,1,0:T(8,128)S(1)}, f32[2,2,2,32,128]{4,3,2,1,0:T(8,128)S(1)}, u32[]{:S(2)}, u32[]{:S(2)}) collective-permute-start(f32[2,2,2,32,128]{4,3,2,1,0:T(8,128)S(1)} %get-tuple-element.28), channel_id=1, source_target_pairs={{16,18},{18,16},{2,4},{4,2},{20,22},{22,20},{6,8},{8,6},{24,26},{2... | collective-permute-start | bytes 393224 | tf_op jit(solution)/shard_map/ppermute | solution.py:144
  97.1 6.4 %collective-permute-start.25 = (f32[2,2,2,32,128]{4,3,2,1,0:T(8,128)S(1)}, f32[2,2,2,32,128]{4,3,2,1,0:T(8,128)S(1)}, u32[]{:S(2)}, u32[]{:S(2)}) collective-permute-start(f32[2,2,2,32,128]{4,3,2,1,0:T(8,128)S(1)} %get-tuple-element.29), channel_id=1, source_target_pairs={{0,16},{16,0},{18,2},{2,18},{4,20},{20,4},{22,6},{6,22},{8,24},{24... | collective-permute-start | bytes 393224 | tf_op jit(solution)/shard_map/ppermute | solution.py:144
  97.1 16.1 %collective-permute-start.28 = (f32[1,2,16,32,128]{4,3,2,1,0:T(8,128)S(1)}, f32[1,2,16,32,128]{4,3,2,1,0:T(8,128)S(1)}, u32[]{:S(2)}, u32[]{:S(2)}) collective-permute-start(f32[1,2,16,32,128]{4,3,2,1,0:T(8,128)S(1)} %slice.1158), channel_id=1, source_target_pairs={{16,0},{17,1},{18,2},{19,3},{20,4},{21,5},{22,6},{23,7},{24,8},{25... | collective-permute-start | bytes 1572872 | tf_op jit(solution)/shard_map/ppermute | solution.py:251
  106.7 10.1 %collective-permute-start.27 = (f32[1,2,16,32,128]{4,3,2,1,0:T(8,128)S(1)}, f32[1,2,16,32,128]{4,3,2,1,0:T(8,128)S(1)}, u32[]{:S(2)}, u32[]{:S(2)}) collective-permute-start(f32[1,2,16,32,128]{4,3,2,1,0:T(8,128)S(1)} %convolution_bitcast_fusion.7), channel_id=1, source_target_pairs={{0,16},{1,17},{2,18},{3,19},{4,20},{5,21},{6,22},{7,23},{8,24},{9,... | collective-permute-start | bytes 1572872 | tf_op jit(solution)/shard_map/ppermute | solution.py:251
  108.5 8.4 %copy-start.2 = (f32[1,2,32,32,128]{4,3,2,1,0:T(8,128)}, f32[1,2,32,32,128]{4,3,2,1,0:T(8,128)S(1)}, u32[]{:S(2)}) copy-start(f32[1,2,32,32,128]{4,3,2,1,0:T(8,128)S(1)} %fusion.67) | copy-start | bytes 3145732
  (2 other events, 4.2 us)

commit v12 on v11

--- a/solution.py
+++ b/solution.py
@@ -226,16 +226,16 @@
             m = k - l
             i = active.index(l)
             e_hist[l][m] = own_e[i]
-            total = states[l] + own_e[i]
+            total = states[l]
             if l > 0:
-                quad = None
-                for slot in range(5):
+                last = float(table[m, 4])
+                quad = (1.0 - last) * g_now[l - 1] - e_hist[l - 1][m]
+                for slot in range(4):
                     node = m - 3 + slot
                     if node >= 0:
-                        term = float(table[m, slot]) * d_hist[l - 1][node]
-                        quad = term if quad is None else quad + term
-                total = total + (quad + g_now[l - 1] - e_hist[l - 1][m])
-            rhs.append(total)
+                        quad = quad + float(table[m, slot]) * d_hist[l - 1][node]
+                total = (total + quad) + last * own_e[active.index(l - 1)]
+            rhs.append(total + own_e[i])
         solved = column_solve(jnp.stack(rhs, 0), inverse)
         for i, l in enumerate(moving):
             states[l] = solved[i]

time: 118 us -> 118 us (level)
  no operation moved by 1% of the time
where the time goes in v12:
time: 118 us
  waiting for transfers between devices  49.3 us (42%)
  starting transfers between devices  26.1 us (22%)
  other arithmetic  25.3 us (21%)
  matrix products  9.04 us (8%)
  local copies, waits for them, and re-layouts  4.17 us (4%)
  Pallas kernels  3 us (3%)
    ppermute x18, waiting for transfers between devices, swap_halo(): got.append(lax.ppermute(sent, axes, pairs))  20.8 us
    ppermute x9, waiting for transfers between devices, ring_halo(): got = lax.ppermute(jnp.concatenate([first, last], dim), axes, up)  20.2 us
    mul x9, other arithmetic, tendency(): return DT * (flow + kappa * laplace + react)  15.1 us
    ppermute x18, starting transfers between devices, swap_halo(): got.append(lax.ppermute(sent, axes, pairs))  14.1 us
    ppermute x9, starting transfers between devices, ring_halo(): got = lax.ppermute(jnp.concatenate([first, last], dim), axes, up)  9.19 us
    dot_general x9, matrix products, column_solve(): jnp.einsum('lsxyk,sjk->lsxyj', rhs, inverse, precision=lax.Precision.HIGH...  9.04 us
    ppermute x2, waiting for transfers between devices, on_device(): arrived = lax.ppermute(states[level][None], 'corr', pairs)  8.34 us
    add x7, other arithmetic, on_device(): rhs.append(total + own_e[i])  4.5 us
  transfers between devices with their start and end apart: 29, of which 21 were waited for; matrix products, arithmetic and copies ran while one was open for 5% of the time, Pallas kernels for 3%

profile of v12, /device:TPU:0, one launch (start us, length us, event | category | flops | bytes accessed | tf_op | source)
XLA Modules:
  0.0 117.7 jit_solution(18200237871359259281)
XLA Ops:
  1.1 4.6 %collective-permute-start = (f32[1,2,2,32,128]{4,3,2,1,0:T(8,128)S(1)}, f32[1,2,2,32,128]{4,3,2,1,0:T(8,128)S(1)}, u32[]{:S(2)}, u32[]{:S(2)}) collective-permute-start(f32[1,2,2,32,128]{4,3,2,1,0:T(8,128)S(1)} %get-tuple-element.101), channel_id=1, source_target_pairs={{16,18},{18,16},{2,4},{4,2},{20,22},{22,20},{6,8},{8,6},{24,26},{2... | collective-permute-start | bytes 196616 | tf_op jit(solution)/shard_map/ppermute | solution.py:144
  5.7 1.6 %collective-permute-start.2 = (f32[1,2,16,4,128]{4,3,2,1,0:T(4,128)S(1)}, f32[1,2,16,4,128]{4,3,2,1,0:T(4,128)S(1)}, u32[]{:S(2)}, u32[]{:S(2)}) collective-permute-start(f32[1,2,16,4,128]{4,3,2,1,0:T(4,128)S(1)} %pad_maximum_fusion.43), channel_id=1, source_target_pairs={{0,1},{1,0},{2,3},{3,2},{4,5},{5,4},{6,7},{7,6},{8,9},{9,8},{10,11... | collective-permute-start | bytes 196616 | tf_op jit(solution)/shard_map/ppermute | solution.py:124
  7.7 3.0 %shard_map.118 = f32[128,2,128]{2,1,0:T(2,128)} custom-call(f32[2,128]{1,0:T(2,128)} %diff_ref.1), custom_call_target="tpu_custom_call" | custom-call | flops 393216 | bytes 262144 | tf_op jit(solution)/shard_map/pallas_call | solution.py:78
  13.8 1.7 %collective-permute-start.3 = (f32[2,2,2,32,128]{4,3,2,1,0:T(8,128)S(1)}, f32[2,2,2,32,128]{4,3,2,1,0:T(8,128)S(1)}, u32[]{:S(2)}, u32[]{:S(2)}) collective-permute-start(f32[2,2,2,32,128]{4,3,2,1,0:T(8,128)S(1)} %get-tuple-element.88), channel_id=1, source_target_pairs={{16,18},{18,16},{2,4},{4,2},{20,22},{22,20},{6,8},{8,6},{24,26},{2... | collective-permute-start | bytes 393224 | tf_op jit(solution)/shard_map/ppermute | solution.py:144
  16.7 3.6 %collective-permute-done.3 = f32[2,2,2,32,128]{4,3,2,1,0:T(8,128)S(1)} collective-permute-done((f32[2,2,2,32,128]{4,3,2,1,0:T(8,128)S(1)}, f32[2,2,2,32,128]{4,3,2,1,0:T(8,128)S(1)}, u32[]{:S(2)}, u32[]{:S(2)}) %collective-permute-start.3) | collective-permute-done | bytes 131104 | tf_op jit(solution)/shard_map/ppermute | solution.py:144
  27.0 3.4 %collective-permute-done.8 = f32[2,2,16,4,128]{4,3,2,1,0:T(4,128)S(1)} collective-permute-done((f32[2,2,16,4,128]{4,3,2,1,0:T(4,128)S(1)}, f32[2,2,16,4,128]{4,3,2,1,0:T(4,128)S(1)}, u32[]{:S(2)}, u32[]{:S(2)}) %collective-permute-start.8) | collective-permute-done | bytes 131104 | tf_op jit(solution)/shard_map/ppermute | solution.py:124
  30.4 1.8 %collective-permute-done.6 = f32[2,2,2,32,128]{4,3,2,1,0:T(8,128)S(1)} collective-permute-done((f32[2,2,2,32,128]{4,3,2,1,0:T(8,128)S(1)}, f32[2,2,2,32,128]{4,3,2,1,0:T(8,128)S(1)}, u32[]{:S(2)}, u32[]{:S(2)}) %collective-permute-start.6) | collective-permute-done | bytes 131104 | tf_op jit(solution)/shard_map/ppermute | solution.py:144
  32.2 1.8 %fusion.37 = f32[2,2,16,32,128]{4,3,2,1,0:T(8,128)S(1)} fusion(f32[2,1,16,32,128]{4,3,2,1,0:T(8,128)S(1)} %get-tuple-element.84, f32[2,1,16,32,128]{4,3,2,1,0:T(8,128)S(1)} %get-tuple-element.83, f32[2,2,16,32,128]{4,3,2,1,0:T(8,128)S(1)} %convolution_bitcast_fusion.6, f32[2,2,16,2,128]{4,3,2,1,0:T(2,128)S(1)} %get-tuple-element.136, ...), kind=kLoop, calls=%fused_computation.148 | loop fusion | flops 9175040 | bytes 4063240 | tf_op jit(solution)/shard_map/mul | solution.py:182
  36.3 1.6 %collective-permute-start.11 = (f32[2,2,16,4,128]{4,3,2,1,0:T(4,128)S(1)}, f32[2,2,16,4,128]{4,3,2,1,0:T(4,128)S(1)}, u32[]{:S(2)}, u32[]{:S(2)}) collective-permute-start(f32[2,2,16,4,128]{4,3,2,1,0:T(4,128)S(1)} %pad_maximum_fusion.37), channel_id=1, source_target_pairs={{0,1},{1,0},{2,3},{3,2},{4,5},{5,4},{6,7},{7,6},{8,9},{9,8},{10,11... | collective-permute-start | bytes 393224 | tf_op jit(solution)/shard_map/ppermute | solution.py:124
  39.6 1.7 %collective-permute-done.11 = f32[2,2,16,4,128]{4,3,2,1,0:T(4,128)S(1)} collective-permute-done((f32[2,2,16,4,128]{4,3,2,1,0:T(4,128)S(1)}, f32[2,2,16,4,128]{4,3,2,1,0:T(4,128)S(1)}, u32[]{:S(2)}, u32[]{:S(2)}) %collective-permute-start.11) | collective-permute-done | bytes 131104 | tf_op jit(solution)/shard_map/ppermute | solution.py:124
  41.4 1.6 %collective-permute-done.10 = f32[2,2,2,32,128]{4,3,2,1,0:T(8,128)S(1)} collective-permute-done((f32[2,2,2,32,128]{4,3,2,1,0:T(8,128)S(1)}, f32[2,2,2,32,128]{4,3,2,1,0:T(8,128)S(1)}, u32[]{:S(2)}, u32[]{:S(2)}) %collective-permute-start.10) | collective-permute-done | bytes 131104 | tf_op jit(solution)/shard_map/ppermute | solution.py:144
  42.9 1.9 %collective-permute-done.9 = f32[2,2,2,32,128]{4,3,2,1,0:T(8,128)S(1)} collective-permute-done((f32[2,2,2,32,128]{4,3,2,1,0:T(8,128)S(1)}, f32[2,2,2,32,128]{4,3,2,1,0:T(8,128)S(1)}, u32[]{:S(2)}, u32[]{:S(2)}) %collective-permute-start.9) | collective-permute-done | bytes 131104 | tf_op jit(solution)/shard_map/ppermute | solution.py:144
  44.8 2.0 %fusion.41 = f32[2,2,16,32,128]{4,3,2,1,0:T(8,128)S(1)} fusion(f32[2,1,16,32,128]{4,3,2,1,0:T(8,128)S(1)} %get-tuple-element.76, f32[2,1,16,32,128]{4,3,2,1,0:T(8,128)S(1)} %get-tuple-element.75, f32[2,2,16,32,128]{4,3,2,1,0:T(8,128)S(1)} %convolution_bitcast_fusion.5, f32[2,2,16,2,128]{4,3,2,1,0:T(2,128)S(1)} %get-tuple-element.134, ...), kind=kLoop, calls=%fused_computation.153 | loop fusion | flops 9175040 | bytes 4063240 | tf_op jit(solution)/shard_map/mul | solution.py:182
  50.5 3.7 %collective-permute-done.14 = f32[2,2,16,4,128]{4,3,2,1,0:T(4,128)S(1)} collective-permute-done((f32[2,2,16,4,128]{4,3,2,1,0:T(4,128)S(1)}, f32[2,2,16,4,128]{4,3,2,1,0:T(4,128)S(1)}, u32[]{:S(2)}, u32[]{:S(2)}) %collective-permute-start.14) | collective-permute-done | bytes 131104 | tf_op jit(solution)/shard_map/ppermute | solution.py:124
  54.2 1.8 %collective-permute-done.12 = f32[2,2,2,32,128]{4,3,2,1,0:T(8,128)S(1)} collective-permute-done((f32[2,2,2,32,128]{4,3,2,1,0:T(8,128)S(1)}, f32[2,2,2,32,128]{4,3,2,1,0:T(8,128)S(1)}, u32[]{:S(2)}, u32[]{:S(2)}) %collective-permute-start.12) | collective-permute-done | bytes 131104 | tf_op jit(solution)/shard_map/ppermute | solution.py:144
  56.0 1.8 %fusion.45 = f32[2,2,16,32,128]{4,3,2,1,0:T(8,128)S(1)} fusion(f32[2,1,16,32,128]{4,3,2,1,0:T(8,128)S(1)} %get-tuple-element.68, f32[2,1,16,32,128]{4,3,2,1,0:T(8,128)S(1)} %get-tuple-element.67, f32[2,2,16,32,128]{4,3,2,1,0:T(8,128)S(1)} %convolution_bitcast_fusion.4, f32[2,2,16,2,128]{4,3,2,1,0:T(2,128)S(1)} %get-tuple-element.132, ...), kind=kLoop, calls=%fused_computation.158 | loop fusion | flops 9175040 | bytes 4063240 | tf_op jit(solution)/shard_map/mul | solution.py:182
  60.2 1.6 %collective-permute-start.17 = (f32[2,2,16,4,128]{4,3,2,1,0:T(4,128)S(1)}, f32[2,2,16,4,128]{4,3,2,1,0:T(4,128)S(1)}, u32[]{:S(2)}, u32[]{:S(2)}) collective-permute-start(f32[2,2,16,4,128]{4,3,2,1,0:T(4,128)S(1)} %pad_maximum_fusion.39), channel_id=1, source_target_pairs={{0,1},{1,0},{2,3},{3,2},{4,5},{5,4},{6,7},{7,6},{8,9},{9,8},{10,11... | collective-permute-start | bytes 393224 | tf_op jit(solution)/shard_map/ppermute | solution.py:124
  62.8 2.5 %collective-permute-done.17 = f32[2,2,16,4,128]{4,3,2,1,0:T(4,128)S(1)} collective-permute-done((f32[2,2,16,4,128]{4,3,2,1,0:T(4,128)S(1)}, f32[2,2,16,4,128]{4,3,2,1,0:T(4,128)S(1)}, u32[]{:S(2)}, u32[]{:S(2)}) %collective-permute-start.17) | collective-permute-done | bytes 131104 | tf_op jit(solution)/shard_map/ppermute | solution.py:124
  65.3 2.8 %collective-permute-done.15 = f32[2,2,2,32,128]{4,3,2,1,0:T(8,128)S(1)} collective-permute-done((f32[2,2,2,32,128]{4,3,2,1,0:T(8,128)S(1)}, f32[2,2,2,32,128]{4,3,2,1,0:T(8,128)S(1)}, u32[]{:S(2)}, u32[]{:S(2)}) %collective-permute-start.15) | collective-permute-done | bytes 131104 | tf_op jit(solution)/shard_map/ppermute | solution.py:144
  68.1 1.8 %fusion.49 = f32[2,2,16,32,128]{4,3,2,1,0:T(8,128)S(1)} fusion(f32[2,1,16,32,128]{4,3,2,1,0:T(8,128)S(1)} %get-tuple-element.60, f32[2,1,16,32,128]{4,3,2,1,0:T(8,128)S(1)} %get-tuple-element.59, f32[2,2,16,32,128]{4,3,2,1,0:T(8,128)S(1)} %convolution_bitcast_fusion.3, f32[2,2,16,2,128]{4,3,2,1,0:T(2,128)S(1)} %get-tuple-element.130, ...), kind=kLoop, calls=%fused_computation.163 | loop fusion | flops 9175040 | bytes 4063240 | tf_op jit(solution)/shard_map/mul | solution.py:182
  73.8 3.5 %collective-permute-done.20 = f32[2,2,16,4,128]{4,3,2,1,0:T(4,128)S(1)} collective-permute-done((f32[2,2,16,4,128]{4,3,2,1,0:T(4,128)S(1)}, f32[2,2,16,4,128]{4,3,2,1,0:T(4,128)S(1)}, u32[]{:S(2)}, u32[]{:S(2)}) %collective-permute-start.20) | collective-permute-done | bytes 131104 | tf_op jit(solution)/shard_map/ppermute | solution.py:124
  77.4 1.8 %collective-permute-done.18 = f32[2,2,2,32,128]{4,3,2,1,0:T(8,128)S(1)} collective-permute-done((f32[2,2,2,32,128]{4,3,2,1,0:T(8,128)S(1)}, f32[2,2,2,32,128]{4,3,2,1,0:T(8,128)S(1)}, u32[]{:S(2)}, u32[]{:S(2)}) %collective-permute-start.18) | collective-permute-done | bytes 131104 | tf_op jit(solution)/shard_map/ppermute | solution.py:144
  79.2 2.1 %fusion.53 = f32[2,2,16,32,128]{4,3,2,1,0:T(8,128)S(1)} fusion(f32[2,1,16,32,128]{4,3,2,1,0:T(8,128)S(1)} %get-tuple-element.52, f32[2,1,16,32,128]{4,3,2,1,0:T(8,128)S(1)} %get-tuple-element.51, f32[2,2,16,32,128]{4,3,2,1,0:T(8,128)S(1)} %convolution_bitcast_fusion.2, f32[2,2,16,2,128]{4,3,2,1,0:T(2,128)S(1)} %get-tuple-element.128, ...), kind=kLoop, calls=%fused_computation.168 | loop fusion | flops 9175040 | bytes 4063240 | tf_op jit(solution)/shard_map/mul | solution.py:182
  83.5 1.6 %collective-permute-start.23 = (f32[2,2,16,4,128]{4,3,2,1,0:T(4,128)S(1)}, f32[2,2,16,4,128]{4,3,2,1,0:T(4,128)S(1)}, u32[]{:S(2)}, u32[]{:S(2)}) collective-permute-start(f32[2,2,16,4,128]{4,3,2,1,0:T(4,128)S(1)} %pad_maximum_fusion.41), channel_id=1, source_target_pairs={{0,1},{1,0},{2,3},{3,2},{4,5},{5,4},{6,7},{7,6},{8,9},{9,8},{10,11... | collective-permute-start | bytes 393224 | tf_op jit(solution)/shard_map/ppermute | solution.py:124
  86.1 2.5 %collective-permute-done.23 = f32[2,2,16,4,128]{4,3,2,1,0:T(4,128)S(1)} collective-permute-done((f32[2,2,16,4,128]{4,3,2,1,0:T(4,128)S(1)}, f32[2,2,16,4,128]{4,3,2,1,0:T(4,128)S(1)}, u32[]{:S(2)}, u32[]{:S(2)}) %collective-permute-start.23) | collective-permute-done | bytes 131104 | tf_op jit(solution)/shard_map/ppermute | solution.py:124
  88.6 2.8 %collective-permute-done.21 = f32[2,2,2,32,128]{4,3,2,1,0:T(8,128)S(1)} collective-permute-done((f32[2,2,2,32,128]{4,3,2,1,0:T(8,128)S(1)}, f32[2,2,2,32,128]{4,3,2,1,0:T(8,128)S(1)}, u32[]{:S(2)}, u32[]{:S(2)}) %collective-permute-start.21) | collective-permute-done | bytes 131104 | tf_op jit(solution)/shard_map/ppermute | solution.py:144
  91.4 1.8 %fusion.57 = f32[2,2,16,32,128]{4,3,2,1,0:T(8,128)S(1)} fusion(f32[2,1,16,32,128]{4,3,2,1,0:T(8,128)S(1)} %get-tuple-element.44, f32[2,1,16,32,128]{4,3,2,1,0:T(8,128)S(1)} %get-tuple-element.43, f32[2,2,16,32,128]{4,3,2,1,0:T(8,128)S(1)} %convolution_bitcast_fusion.1, f32[2,2,16,2,128]{4,3,2,1,0:T(2,128)S(1)} %get-tuple-element.126, ...), kind=kLoop, calls=%fused_computation.173 | loop fusion | flops 9175040 | bytes 4063240 | tf_op jit(solution)/shard_map/mul | solution.py:182
  98.5 2.2 %collective-permute-done.26 = f32[2,2,16,4,128]{4,3,2,1,0:T(4,128)S(1)} collective-permute-done((f32[2,2,16,4,128]{4,3,2,1,0:T(4,128)S(1)}, f32[2,2,16,4,128]{4,3,2,1,0:T(4,128)S(1)}, u32[]{:S(2)}, u32[]{:S(2)}) %collective-permute-start.26) | collective-permute-done | bytes 131104 | tf_op jit(solution)/shard_map/ppermute | solution.py:124
  100.7 1.8 %collective-permute-done.24 = f32[2,2,2,32,128]{4,3,2,1,0:T(8,128)S(1)} collective-permute-done((f32[2,2,2,32,128]{4,3,2,1,0:T(8,128)S(1)}, f32[2,2,2,32,128]{4,3,2,1,0:T(8,128)S(1)}, u32[]{:S(2)}, u32[]{:S(2)}) %collective-permute-start.24) | collective-permute-done | bytes 131104 | tf_op jit(solution)/shard_map/ppermute | solution.py:144
  103.6 1.9 %fusion.61 = f32[2,2,16,32,128]{4,3,2,1,0:T(8,128)S(1)} fusion(f32[2,1,16,32,128]{4,3,2,1,0:T(8,128)S(1)} %get-tuple-element.36, f32[2,1,16,32,128]{4,3,2,1,0:T(8,128)S(1)} %get-tuple-element.35, f32[2,2,16,32,128]{4,3,2,1,0:T(8,128)S(1)} %convolution_bitcast_fusion, f32[2,2,16,2,128]{4,3,2,1,0:T(2,128)S(1)} %get-tuple-element.124, ...), kind=kLoop, calls=%fused_computation.178 | loop fusion | flops 9175040 | bytes 4063240 | tf_op jit(solution)/shard_map/mul | solution.py:182
  108.5 4.8 %collective-permute-done.28 = f32[1,2,16,32,128]{4,3,2,1,0:T(8,128)S(1)} collective-permute-done((f32[1,2,16,32,128]{4,3,2,1,0:T(8,128)S(1)}, f32[1,2,16,32,128]{4,3,2,1,0:T(8,128)S(1)}, u32[]{:S(2)}, u32[]{:S(2)}) %collective-permute-start.28) | collective-permute-done | bytes 524320 | tf_op jit(solution)/shard_map/ppermute | solution.py:251
  113.3 3.5 %collective-permute-done.27 = f32[1,2,16,32,128]{4,3,2,1,0:T(8,128)S(1)} collective-permute-done((f32[1,2,16,32,128]{4,3,2,1,0:T(8,128)S(1)}, f32[1,2,16,32,128]{4,3,2,1,0:T(8,128)S(1)}, u32[]{:S(2)}, u32[]{:S(2)}) %collective-permute-start.27) | collective-permute-done | bytes 524320 | tf_op jit(solution)/shard_map/ppermute | solution.py:251
  (137 shorter events, 40.8 us)
Async XLA Ops:
  1.1 10.8 %collective-permute-start = (f32[1,2,2,32,128]{4,3,2,1,0:T(8,128)S(1)}, f32[1,2,2,32,128]{4,3,2,1,0:T(8,128)S(1)}, u32[]{:S(2)}, u32[]{:S(2)}) collective-permute-start(f32[1,2,2,32,128]{4,3,2,1,0:T(8,128)S(1)} %get-tuple-element.101), channel_id=1, source_target_pairs={{16,18},{18,16},{2,4},{4,2},{20,22},{22,20},{6,8},{8,6},{24,26},{2... | collective-permute-start | bytes 196616 | tf_op jit(solution)/shard_map/ppermute | solution.py:144
  5.7 6.2 %collective-permute-start.1 = (f32[1,2,2,32,128]{4,3,2,1,0:T(8,128)S(1)}, f32[1,2,2,32,128]{4,3,2,1,0:T(8,128)S(1)}, u32[]{:S(2)}, u32[]{:S(2)}) collective-permute-start(f32[1,2,2,32,128]{4,3,2,1,0:T(8,128)S(1)} %get-tuple-element.102), channel_id=1, source_target_pairs={{0,16},{16,0},{18,2},{2,18},{4,20},{20,4},{22,6},{6,22},{8,24},{24... | collective-permute-start | bytes 196616 | tf_op jit(solution)/shard_map/ppermute | solution.py:144
  5.7 6.1 %collective-permute-start.2 = (f32[1,2,16,4,128]{4,3,2,1,0:T(4,128)S(1)}, f32[1,2,16,4,128]{4,3,2,1,0:T(4,128)S(1)}, u32[]{:S(2)}, u32[]{:S(2)}) collective-permute-start(f32[1,2,16,4,128]{4,3,2,1,0:T(4,128)S(1)} %pad_maximum_fusion.43), channel_id=1, source_target_pairs={{0,1},{1,0},{2,3},{3,2},{4,5},{5,4},{6,7},{7,6},{8,9},{9,8},{10,11... | collective-permute-start | bytes 196616 | tf_op jit(solution)/shard_map/ppermute | solution.py:124
  7.6 4.3 %copy-start.1 = (f32[2,32,32,128]{3,2,1,0:T(8,128)S(1)}, f32[2,32,32,128]{3,2,1,0:T(8,128)}, u32[]{:S(2)}) copy-start(f32[2,32,32,128]{3,2,1,0:T(8,128)} %param.12) | copy-start | bytes 3145732
  7.6 4.3 %copy-start.3 = (f32[2]{0:T(128)S(1)}, f32[2]{0:T(128)}, u32[]{:S(2)}) copy-start(f32[2]{0:T(128)} %constant.146) | copy-start | bytes 28
  13.8 6.5 %collective-permute-start.3 = (f32[2,2,2,32,128]{4,3,2,1,0:T(8,128)S(1)}, f32[2,2,2,32,128]{4,3,2,1,0:T(8,128)S(1)}, u32[]{:S(2)}, u32[]{:S(2)}) collective-permute-start(f32[2,2,2,32,128]{4,3,2,1,0:T(8,128)S(1)} %get-tuple-element.88), channel_id=1, source_target_pairs={{16,18},{18,16},{2,4},{4,2},{20,22},{22,20},{6,8},{8,6},{24,26},{2... | collective-permute-start | bytes 393224 | tf_op jit(solution)/shard_map/ppermute | solution.py:144
  15.4 5.0 %collective-permute-start.4 = (f32[2,2,2,32,128]{4,3,2,1,0:T(8,128)S(1)}, f32[2,2,2,32,128]{4,3,2,1,0:T(8,128)S(1)}, u32[]{:S(2)}, u32[]{:S(2)}) collective-permute-start(f32[2,2,2,32,128]{4,3,2,1,0:T(8,128)S(1)} %get-tuple-element.87), channel_id=1, source_target_pairs={{0,16},{16,0},{18,2},{2,18},{4,20},{20,4},{22,6},{6,22},{8,24},{24... | collective-permute-start | bytes 393224 | tf_op jit(solution)/shard_map/ppermute | solution.py:144
  16.0 5.6 %collective-permute-start.5 = (f32[2,2,16,4,128]{4,3,2,1,0:T(4,128)S(1)}, f32[2,2,16,4,128]{4,3,2,1,0:T(4,128)S(1)}, u32[]{:S(2)}, u32[]{:S(2)}) collective-permute-start(f32[2,2,16,4,128]{4,3,2,1,0:T(4,128)S(1)} %pad_maximum_fusion.35), channel_id=1, source_target_pairs={{0,1},{1,0},{2,3},{3,2},{4,5},{5,4},{6,7},{7,6},{8,9},{9,8},{10,11... | collective-permute-start | bytes 393224 | tf_op jit(solution)/shard_map/ppermute | solution.py:124
  25.3 5.0 %collective-permute-start.8 = (f32[2,2,16,4,128]{4,3,2,1,0:T(4,128)S(1)}, f32[2,2,16,4,128]{4,3,2,1,0:T(4,128)S(1)}, u32[]{:S(2)}, u32[]{:S(2)}) collective-permute-start(f32[2,2,16,4,128]{4,3,2,1,0:T(4,128)S(1)} %pad_maximum_fusion.36), channel_id=1, source_target_pairs={{0,1},{1,0},{2,3},{3,2},{4,5},{5,4},{6,7},{7,6},{8,9},{9,8},{10,11... | collective-permute-start | bytes 393224 | tf_op jit(solution)/shard_map/ppermute | solution.py:124
  25.9 6.3 %collective-permute-start.6 = (f32[2,2,2,32,128]{4,3,2,1,0:T(8,128)S(1)}, f32[2,2,2,32,128]{4,3,2,1,0:T(8,128)S(1)}, u32[]{:S(2)}, u32[]{:S(2)}) collective-permute-start(f32[2,2,2,32,128]{4,3,2,1,0:T(8,128)S(1)} %get-tuple-element.79), channel_id=1, source_target_pairs={{16,18},{18,16},{2,4},{4,2},{20,22},{22,20},{6,8},{8,6},{24,26},{2... | collective-permute-start | bytes 393224 | tf_op jit(solution)/shard_map/ppermute | solution.py:144
  26.6 5.5 %collective-permute-start.7 = (f32[2,2,2,32,128]{4,3,2,1,0:T(8,128)S(1)}, f32[2,2,2,32,128]{4,3,2,1,0:T(8,128)S(1)}, u32[]{:S(2)}, u32[]{:S(2)}) collective-permute-start(f32[2,2,2,32,128]{4,3,2,1,0:T(8,128)S(1)} %get-tuple-element.80), channel_id=1, source_target_pairs={{0,16},{16,0},{18,2},{2,18},{4,20},{20,4},{22,6},{6,22},{8,24},{24... | collective-permute-start | bytes 393224 | tf_op jit(solution)/shard_map/ppermute | solution.py:144
  36.3 5.0 %collective-permute-start.11 = (f32[2,2,16,4,128]{4,3,2,1,0:T(4,128)S(1)}, f32[2,2,16,4,128]{4,3,2,1,0:T(4,128)S(1)}, u32[]{:S(2)}, u32[]{:S(2)}) collective-permute-start(f32[2,2,16,4,128]{4,3,2,1,0:T(4,128)S(1)} %pad_maximum_fusion.37), channel_id=1, source_target_pairs={{0,1},{1,0},{2,3},{3,2},{4,5},{5,4},{6,7},{7,6},{8,9},{9,8},{10,11... | collective-permute-start | bytes 393224 | tf_op jit(solution)/shard_map/ppermute | solution.py:124
  37.9 5.0 %collective-permute-start.10 = (f32[2,2,2,32,128]{4,3,2,1,0:T(8,128)S(1)}, f32[2,2,2,32,128]{4,3,2,1,0:T(8,128)S(1)}, u32[]{:S(2)}, u32[]{:S(2)}) collective-permute-start(f32[2,2,2,32,128]{4,3,2,1,0:T(8,128)S(1)} %get-tuple-element.72), channel_id=1, source_target_pairs={{0,16},{16,0},{18,2},{2,18},{4,20},{20,4},{22,6},{6,22},{8,24},{24... | collective-permute-start | bytes 393224 | tf_op jit(solution)/shard_map/ppermute | solution.py:144
  38.6 6.2 %collective-permute-start.9 = (f32[2,2,2,32,128]{4,3,2,1,0:T(8,128)S(1)}, f32[2,2,2,32,128]{4,3,2,1,0:T(8,128)S(1)}, u32[]{:S(2)}, u32[]{:S(2)}) collective-permute-start(f32[2,2,2,32,128]{4,3,2,1,0:T(8,128)S(1)} %get-tuple-element.71), channel_id=1, source_target_pairs={{16,18},{18,16},{2,4},{4,2},{20,22},{22,20},{6,8},{8,6},{24,26},{2... | collective-permute-start | bytes 393224 | tf_op jit(solution)/shard_map/ppermute | solution.py:144
  49.2 5.0 %collective-permute-start.14 = (f32[2,2,16,4,128]{4,3,2,1,0:T(4,128)S(1)}, f32[2,2,16,4,128]{4,3,2,1,0:T(4,128)S(1)}, u32[]{:S(2)}, u32[]{:S(2)}) collective-permute-start(f32[2,2,16,4,128]{4,3,2,1,0:T(4,128)S(1)} %pad_maximum_fusion.38), channel_id=1, source_target_pairs={{0,1},{1,0},{2,3},{3,2},{4,5},{5,4},{6,7},{7,6},{8,9},{9,8},{10,11... | collective-permute-start | bytes 393224 | tf_op jit(solution)/shard_map/ppermute | solution.py:124
  49.8 6.3 %collective-permute-start.12 = (f32[2,2,2,32,128]{4,3,2,1,0:T(8,128)S(1)}, f32[2,2,2,32,128]{4,3,2,1,0:T(8,128)S(1)}, u32[]{:S(2)}, u32[]{:S(2)}) collective-permute-start(f32[2,2,2,32,128]{4,3,2,1,0:T(8,128)S(1)} %get-tuple-element.63), channel_id=1, source_target_pairs={{16,18},{18,16},{2,4},{4,2},{20,22},{22,20},{6,8},{8,6},{24,26},{2... | collective-permute-start | bytes 393224 | tf_op jit(solution)/shard_map/ppermute | solution.py:144
  50.5 5.5 %collective-permute-start.13 = (f32[2,2,2,32,128]{4,3,2,1,0:T(8,128)S(1)}, f32[2,2,2,32,128]{4,3,2,1,0:T(8,128)S(1)}, u32[]{:S(2)}, u32[]{:S(2)}) collective-permute-start(f32[2,2,2,32,128]{4,3,2,1,0:T(8,128)S(1)} %get-tuple-element.64), channel_id=1, source_target_pairs={{0,16},{16,0},{18,2},{2,18},{4,20},{20,4},{22,6},{6,22},{8,24},{24... | collective-permute-start | bytes 393224 | tf_op jit(solution)/shard_map/ppermute | solution.py:144
  60.2 5.0 %collective-permute-start.17 = (f32[2,2,16,4,128]{4,3,2,1,0:T(4,128)S(1)}, f32[2,2,16,4,128]{4,3,2,1,0:T(4,128)S(1)}, u32[]{:S(2)}, u32[]{:S(2)}) collective-permute-start(f32[2,2,16,4,128]{4,3,2,1,0:T(4,128)S(1)} %pad_maximum_fusion.39), channel_id=1, source_target_pairs={{0,1},{1,0},{2,3},{3,2},{4,5},{5,4},{6,7},{7,6},{8,9},{9,8},{10,11... | collective-permute-start | bytes 393224 | tf_op jit(solution)/shard_map/ppermute | solution.py:124
  61.9 6.3 %collective-permute-start.15 = (f32[2,2,2,32,128]{4,3,2,1,0:T(8,128)S(1)}, f32[2,2,2,32,128]{4,3,2,1,0:T(8,128)S(1)}, u32[]{:S(2)}, u32[]{:S(2)}) collective-permute-start(f32[2,2,2,32,128]{4,3,2,1,0:T(8,128)S(1)} %get-tuple-element.55), channel_id=1, source_target_pairs={{16,18},{18,16},{2,4},{4,2},{20,22},{22,20},{6,8},{8,6},{24,26},{2... | collective-permute-start | bytes 393224 | tf_op jit(solution)/shard_map/ppermute | solution.py:144
  62.8 5.3 %collective-permute-start.16 = (f32[2,2,2,32,128]{4,3,2,1,0:T(8,128)S(1)}, f32[2,2,2,32,128]{4,3,2,1,0:T(8,128)S(1)}, u32[]{:S(2)}, u32[]{:S(2)}) collective-permute-start(f32[2,2,2,32,128]{4,3,2,1,0:T(8,128)S(1)} %get-tuple-element.56), channel_id=1, source_target_pairs={{0,16},{16,0},{18,2},{2,18},{4,20},{20,4},{22,6},{6,22},{8,24},{24... | collective-permute-start | bytes 393224 | tf_op jit(solution)/shard_map/ppermute | solution.py:144
  72.3 5.0 %collective-permute-start.20 = (f32[2,2,16,4,128]{4,3,2,1,0:T(4,128)S(1)}, f32[2,2,16,4,128]{4,3,2,1,0:T(4,128)S(1)}, u32[]{:S(2)}, u32[]{:S(2)}) collective-permute-start(f32[2,2,16,4,128]{4,3,2,1,0:T(4,128)S(1)} %pad_maximum_fusion.40), channel_id=1, source_target_pairs={{0,1},{1,0},{2,3},{3,2},{4,5},{5,4},{6,7},{7,6},{8,9},{9,8},{10,11... | collective-permute-start | bytes 393224 | tf_op jit(solution)/shard_map/ppermute | solution.py:124
  72.9 6.3 %collective-permute-start.18 = (f32[2,2,2,32,128]{4,3,2,1,0:T(8,128)S(1)}, f32[2,2,2,32,128]{4,3,2,1,0:T(8,128)S(1)}, u32[]{:S(2)}, u32[]{:S(2)}) collective-permute-start(f32[2,2,2,32,128]{4,3,2,1,0:T(8,128)S(1)} %get-tuple-element.47), channel_id=1, source_target_pairs={{16,18},{18,16},{2,4},{4,2},{20,22},{22,20},{6,8},{8,6},{24,26},{2... | collective-permute-start | bytes 393224 | tf_op jit(solution)/shard_map/ppermute | solution.py:144
  73.8 5.3 %collective-permute-start.19 = (f32[2,2,2,32,128]{4,3,2,1,0:T(8,128)S(1)}, f32[2,2,2,32,128]{4,3,2,1,0:T(8,128)S(1)}, u32[]{:S(2)}, u32[]{:S(2)}) collective-permute-start(f32[2,2,2,32,128]{4,3,2,1,0:T(8,128)S(1)} %get-tuple-element.48), channel_id=1, source_target_pairs={{0,16},{16,0},{18,2},{2,18},{4,20},{20,4},{22,6},{6,22},{8,24},{24... | collective-permute-start | bytes 393224 | tf_op jit(solution)/shard_map/ppermute | solution.py:144
  83.5 5.0 %collective-permute-start.23 = (f32[2,2,16,4,128]{4,3,2,1,0:T(4,128)S(1)}, f32[2,2,16,4,128]{4,3,2,1,0:T(4,128)S(1)}, u32[]{:S(2)}, u32[]{:S(2)}) collective-permute-start(f32[2,2,16,4,128]{4,3,2,1,0:T(4,128)S(1)} %pad_maximum_fusion.41), channel_id=1, source_target_pairs={{0,1},{1,0},{2,3},{3,2},{4,5},{5,4},{6,7},{7,6},{8,9},{9,8},{10,11... | collective-permute-start | bytes 393224 | tf_op jit(solution)/shard_map/ppermute | solution.py:124
  85.1 6.3 %collective-permute-start.21 = (f32[2,2,2,32,128]{4,3,2,1,0:T(8,128)S(1)}, f32[2,2,2,32,128]{4,3,2,1,0:T(8,128)S(1)}, u32[]{:S(2)}, u32[]{:S(2)}) collective-permute-start(f32[2,2,2,32,128]{4,3,2,1,0:T(8,128)S(1)} %get-tuple-element.39), channel_id=1, source_target_pairs={{16,18},{18,16},{2,4},{4,2},{20,22},{22,20},{6,8},{8,6},{24,26},{2... | collective-permute-start | bytes 393224 | tf_op jit(solution)/shard_map/ppermute | solution.py:144
  86.1 5.3 %collective-permute-start.22 = (f32[2,2,2,32,128]{4,3,2,1,0:T(8,128)S(1)}, f32[2,2,2,32,128]{4,3,2,1,0:T(8,128)S(1)}, u32[]{:S(2)}, u32[]{:S(2)}) collective-permute-start(f32[2,2,2,32,128]{4,3,2,1,0:T(8,128)S(1)} %get-tuple-element.40), channel_id=1, source_target_pairs={{0,16},{16,0},{18,2},{2,18},{4,20},{20,4},{22,6},{6,22},{8,24},{24... | collective-permute-start | bytes 393224 | tf_op jit(solution)/shard_map/ppermute | solution.py:144
  95.6 5.0 %collective-permute-start.26 = (f32[2,2,16,4,128]{4,3,2,1,0:T(4,128)S(1)}, f32[2,2,16,4,128]{4,3,2,1,0:T(4,128)S(1)}, u32[]{:S(2)}, u32[]{:S(2)}) collective-permute-start(f32[2,2,16,4,128]{4,3,2,1,0:T(4,128)S(1)} %pad_maximum_fusion.42), channel_id=1, source_target_pairs={{0,1},{1,0},{2,3},{3,2},{4,5},{5,4},{6,7},{7,6},{8,9},{9,8},{10,11... | collective-permute-start | bytes 393224 | tf_op jit(solution)/shard_map/ppermute | solution.py:124
  96.2 6.3 %collective-permute-start.24 = (f32[2,2,2,32,128]{4,3,2,1,0:T(8,128)S(1)}, f32[2,2,2,32,128]{4,3,2,1,0:T(8,128)S(1)}, u32[]{:S(2)}, u32[]{:S(2)}) collective-permute-start(f32[2,2,2,32,128]{4,3,2,1,0:T(8,128)S(1)} %get-tuple-element.31), channel_id=1, source_target_pairs={{16,18},{18,16},{2,4},{4,2},{20,22},{22,20},{6,8},{8,6},{24,26},{2... | collective-permute-start | bytes 393224 | tf_op jit(solution)/shard_map/ppermute | solution.py:144
  97.2 6.4 %collective-permute-start.25 = (f32[2,2,2,32,128]{4,3,2,1,0:T(8,128)S(1)}, f32[2,2,2,32,128]{4,3,2,1,0:T(8,128)S(1)}, u32[]{:S(2)}, u32[]{:S(2)}) collective-permute-start(f32[2,2,2,32,128]{4,3,2,1,0:T(8,128)S(1)} %get-tuple-element.32), channel_id=1, source_target_pairs={{0,16},{16,0},{18,2},{2,18},{4,20},{20,4},{22,6},{6,22},{8,24},{24... | collective-permute-start | bytes 393224 | tf_op jit(solution)/shard_map/ppermute | solution.py:144
  97.2 16.1 %collective-permute-start.28 = (f32[1,2,16,32,128]{4,3,2,1,0:T(8,128)S(1)}, f32[1,2,16,32,128]{4,3,2,1,0:T(8,128)S(1)}, u32[]{:S(2)}, u32[]{:S(2)}) collective-permute-start(f32[1,2,16,32,128]{4,3,2,1,0:T(8,128)S(1)} %slice.1165), channel_id=1, source_target_pairs={{16,0},{17,1},{18,2},{19,3},{20,4},{21,5},{22,6},{23,7},{24,8},{25... | collective-permute-start | bytes 1572872 | tf_op jit(solution)/shard_map/ppermute | solution.py:251
  106.7 10.1 %collective-permute-start.27 = (f32[1,2,16,32,128]{4,3,2,1,0:T(8,128)S(1)}, f32[1,2,16,32,128]{4,3,2,1,0:T(8,128)S(1)}, u32[]{:S(2)}, u32[]{:S(2)}) collective-permute-start(f32[1,2,16,32,128]{4,3,2,1,0:T(8,128)S(1)} %convolution_bitcast_fusion.7), channel_id=1, source_target_pairs={{0,16},{1,17},{2,18},{3,19},{4,20},{5,21},{6,22},{7,23},{8,24},{9,... | collective-permute-start | bytes 1572872 | tf_op jit(solution)/shard_map/ppermute | solution.py:251
  108.4 8.4 %copy-start.2 = (f32[1,2,32,32,128]{4,3,2,1,0:T(8,128)}, f32[1,2,32,32,128]{4,3,2,1,0:T(8,128)S(1)}, u32[]{:S(2)}) copy-start(f32[1,2,32,32,128]{4,3,2,1,0:T(8,128)S(1)} %fusion.67) | copy-start | bytes 3145732
  (2 other events, 4.2 us)

commit v13 on v11

--- a/solution.py
+++ b/solution.py
@@ -133,14 +133,13 @@
 def swap_halo(block, axes, order, parity, dim, width):
     size = len(order)
     length = block.shape[dim]
-    last = lax.slice_in_dim(block, length - width, length, axis=dim)
-    first = lax.slice_in_dim(block, 0, width, axis=dim)
     got = []
     for offset in range(2):
         pairs = []
         for g in range(offset, size, 2):
             pairs += [(order[g], order[(g + 1) % size]), (order[(g + 1) % size], order[g])]
-        sent = jnp.where(parity == offset, last, first)
+        edge = jnp.where(parity == offset, length - width, 0)
+        sent = lax.dynamic_slice_in_dim(block, edge, width, dim)
         got.append(lax.ppermute(sent, axes, pairs))
     before = jnp.where(parity == 0, got[1], got[0])
     after = jnp.where(parity == 0, got[0], got[1])

time: 118 us -> 119 us (level)
    ppermute x18, waiting for transfers between devices: 20.8 us -> 22.4 us  [swap_halo(): got.append(lax.ppermute(sent, axes, pairs))]
    ppermute x9, waiting for transfers between devices: 20.2 us -> 18.6 us  [ring_halo(): got = lax.ppermute(jnp.concatenate([first, last], dim), axes, up)]
  transfers between devices with their start and end apart: 29 -> 29, of which waited for: 21 -> 21; matrix products, arithmetic and copies ran while one was open for 5% -> 7% of each run, Pallas kernels for 3% -> 3%
where the time goes in v13:
time: 119 us
  waiting for transfers between devices  49.2 us (41%)
  starting transfers between devices  26.1 us (22%)
  other arithmetic  25.2 us (21%)
  matrix products  9.12 us (8%)
  local copies, waits for them, and re-layouts  5.22 us (4%)
  Pallas kernels  3 us (3%)
    ppermute x18, waiting for transfers between devices, swap_halo(): got.append(lax.ppermute(sent, axes, pairs))  22.4 us
    ppermute x9, waiting for transfers between devices, ring_halo(): got = lax.ppermute(jnp.concatenate([first, last], dim), axes, up)  18.6 us
    mul x9, other arithmetic, tendency(): return DT * (flow + kappa * laplace + react)  15.1 us
    ppermute x18, starting transfers between devices, swap_halo(): got.append(lax.ppermute(sent, axes, pairs))  14.1 us
    ppermute x9, starting transfers between devices, ring_halo(): got = lax.ppermute(jnp.concatenate([first, last], dim), axes, up)  9.19 us
    dot_general x9, matrix products, column_solve(): jnp.einsum('lsxyk,sjk->lsxyj', rhs, inverse, precision=lax.Precision.HIGH...  9.12 us
    ppermute x2, waiting for transfers between devices, on_device(): arrived = lax.ppermute(states[level][None], 'corr', pairs)  8.2 us
    add x5, other arithmetic, on_device(): total = total + (quad + g_now[l - 1] - e_hist[l - 1][m])  3.63 us
  transfers between devices with their start and end apart: 29, of which 21 were waited for; matrix products, arithmetic and copies ran while one was open for 7% of the time, Pallas kernels for 3%

profile of v13, /device:TPU:0, one launch (start us, length us, event | category | flops | bytes accessed | tf_op | source)
XLA Modules:
  0.0 118.6 jit_solution(15768830344774146252)
XLA Ops:
  0.9 4.6 %collective-permute-start = (f32[1,2,2,32,128]{4,3,2,1,0:T(8,128)S(1)}, f32[1,2,2,32,128]{4,3,2,1,0:T(8,128)S(1)}, u32[]{:S(2)}, u32[]{:S(2)}) collective-permute-start(f32[1,2,2,32,128]{4,3,2,1,0:T(8,128)S(1)} %get-tuple-element.94), channel_id=1, source_target_pairs={{16,18},{18,16},{2,4},{4,2},{20,22},{22,20},{6,8},{8,6},{24,26},{2... | collective-permute-start | bytes 196616 | tf_op jit(solution)/shard_map/ppermute | solution.py:143
  6.6 1.6 %collective-permute-start.2 = (f32[1,2,16,4,128]{4,3,2,1,0:T(4,128)S(1)}, f32[1,2,16,4,128]{4,3,2,1,0:T(4,128)S(1)}, u32[]{:S(2)}, u32[]{:S(2)}) collective-permute-start(f32[1,2,16,4,128]{4,3,2,1,0:T(4,128)S(1)} %pad_maximum_fusion.43), channel_id=1, source_target_pairs={{0,1},{1,0},{2,3},{3,2},{4,5},{5,4},{6,7},{7,6},{8,9},{9,8},{10,11... | collective-permute-start | bytes 196616 | tf_op jit(solution)/shard_map/ppermute | solution.py:124
  8.5 3.0 %shard_map.118 = f32[128,2,128]{2,1,0:T(2,128)} custom-call(f32[2,128]{1,0:T(2,128)} %diff_ref.1), custom_call_target="tpu_custom_call" | custom-call | flops 393216 | bytes 262144 | tf_op jit(solution)/shard_map/pallas_call | solution.py:78
  14.6 1.7 %collective-permute-start.3 = (f32[2,2,2,32,128]{4,3,2,1,0:T(8,128)S(1)}, f32[2,2,2,32,128]{4,3,2,1,0:T(8,128)S(1)}, u32[]{:S(2)}, u32[]{:S(2)}) collective-permute-start(f32[2,2,2,32,128]{4,3,2,1,0:T(8,128)S(1)} %get-tuple-element.85), channel_id=1, source_target_pairs={{16,18},{18,16},{2,4},{4,2},{20,22},{22,20},{6,8},{8,6},{24,26},{2... | collective-permute-start | bytes 393224 | tf_op jit(solution)/shard_map/ppermute | solution.py:143
  17.6 3.6 %collective-permute-done.3 = f32[2,2,2,32,128]{4,3,2,1,0:T(8,128)S(1)} collective-permute-done((f32[2,2,2,32,128]{4,3,2,1,0:T(8,128)S(1)}, f32[2,2,2,32,128]{4,3,2,1,0:T(8,128)S(1)}, u32[]{:S(2)}, u32[]{:S(2)}) %collective-permute-start.3) | collective-permute-done | bytes 131104 | tf_op jit(solution)/shard_map/ppermute | solution.py:143
  27.9 3.1 %collective-permute-done.8 = f32[2,2,16,4,128]{4,3,2,1,0:T(4,128)S(1)} collective-permute-done((f32[2,2,16,4,128]{4,3,2,1,0:T(4,128)S(1)}, f32[2,2,16,4,128]{4,3,2,1,0:T(4,128)S(1)}, u32[]{:S(2)}, u32[]{:S(2)}) %collective-permute-start.8) | collective-permute-done | bytes 131104 | tf_op jit(solution)/shard_map/ppermute | solution.py:124
  31.0 2.0 %collective-permute-done.6 = f32[2,2,2,32,128]{4,3,2,1,0:T(8,128)S(1)} collective-permute-done((f32[2,2,2,32,128]{4,3,2,1,0:T(8,128)S(1)}, f32[2,2,2,32,128]{4,3,2,1,0:T(8,128)S(1)}, u32[]{:S(2)}, u32[]{:S(2)}) %collective-permute-start.6) | collective-permute-done | bytes 131104 | tf_op jit(solution)/shard_map/ppermute | solution.py:143
  33.1 1.8 %fusion.38 = f32[2,2,16,32,128]{4,3,2,1,0:T(8,128)S(1)} fusion(f32[2,1,16,32,128]{4,3,2,1,0:T(8,128)S(1)} %get-tuple-element.81, f32[2,1,16,32,128]{4,3,2,1,0:T(8,128)S(1)} %get-tuple-element.80, f32[2,2,16,32,128]{4,3,2,1,0:T(8,128)S(1)} %bitcast.134, f32[2,2,16,2,128]{4,3,2,1,0:T(2,128)S(1)} %get-tuple-element.133, ...), kind=kLoop, calls=%fused_computation.142 | loop fusion | flops 9175040 | bytes 4063240 | tf_op jit(solution)/shard_map/mul | solution.py:181
  36.9 1.6 %collective-permute-start.11 = (f32[2,2,16,4,128]{4,3,2,1,0:T(4,128)S(1)}, f32[2,2,16,4,128]{4,3,2,1,0:T(4,128)S(1)}, u32[]{:S(2)}, u32[]{:S(2)}) collective-permute-start(f32[2,2,16,4,128]{4,3,2,1,0:T(4,128)S(1)} %pad_maximum_fusion.37), channel_id=1, source_target_pairs={{0,1},{1,0},{2,3},{3,2},{4,5},{5,4},{6,7},{7,6},{8,9},{9,8},{10,11... | collective-permute-start | bytes 393224 | tf_op jit(solution)/shard_map/ppermute | solution.py:124
  42.0 1.8 %collective-permute-done.10 = f32[2,2,2,32,128]{4,3,2,1,0:T(8,128)S(1)} collective-permute-done((f32[2,2,2,32,128]{4,3,2,1,0:T(8,128)S(1)}, f32[2,2,2,32,128]{4,3,2,1,0:T(8,128)S(1)}, u32[]{:S(2)}, u32[]{:S(2)}) %collective-permute-start.10) | collective-permute-done | bytes 131104 | tf_op jit(solution)/shard_map/ppermute | solution.py:143
  43.8 1.9 %collective-permute-done.9 = f32[2,2,2,32,128]{4,3,2,1,0:T(8,128)S(1)} collective-permute-done((f32[2,2,2,32,128]{4,3,2,1,0:T(8,128)S(1)}, f32[2,2,2,32,128]{4,3,2,1,0:T(8,128)S(1)}, u32[]{:S(2)}, u32[]{:S(2)}) %collective-permute-start.9) | collective-permute-done | bytes 131104 | tf_op jit(solution)/shard_map/ppermute | solution.py:143
  45.7 2.0 %fusion.43 = f32[2,2,16,32,128]{4,3,2,1,0:T(8,128)S(1)} fusion(f32[2,1,16,32,128]{4,3,2,1,0:T(8,128)S(1)} %get-tuple-element.73, f32[2,1,16,32,128]{4,3,2,1,0:T(8,128)S(1)} %get-tuple-element.72, f32[2,2,16,32,128]{4,3,2,1,0:T(8,128)S(1)} %bitcast.149, f32[2,2,16,2,128]{4,3,2,1,0:T(2,128)S(1)} %get-tuple-element.131, ...), kind=kLoop, calls=%fused_computation.148 | loop fusion | flops 9175040 | bytes 4063240 | tf_op jit(solution)/shard_map/mul | solution.py:181
  51.4 3.4 %collective-permute-done.14 = f32[2,2,16,4,128]{4,3,2,1,0:T(4,128)S(1)} collective-permute-done((f32[2,2,16,4,128]{4,3,2,1,0:T(4,128)S(1)}, f32[2,2,16,4,128]{4,3,2,1,0:T(4,128)S(1)}, u32[]{:S(2)}, u32[]{:S(2)}) %collective-permute-start.14) | collective-permute-done | bytes 131104 | tf_op jit(solution)/shard_map/ppermute | solution.py:124
  54.9 2.0 %collective-permute-done.12 = f32[2,2,2,32,128]{4,3,2,1,0:T(8,128)S(1)} collective-permute-done((f32[2,2,2,32,128]{4,3,2,1,0:T(8,128)S(1)}, f32[2,2,2,32,128]{4,3,2,1,0:T(8,128)S(1)}, u32[]{:S(2)}, u32[]{:S(2)}) %collective-permute-start.12) | collective-permute-done | bytes 131104 | tf_op jit(solution)/shard_map/ppermute | solution.py:143
  56.9 1.8 %fusion.48 = f32[2,2,16,32,128]{4,3,2,1,0:T(8,128)S(1)} fusion(f32[2,1,16,32,128]{4,3,2,1,0:T(8,128)S(1)} %get-tuple-element.65, f32[2,1,16,32,128]{4,3,2,1,0:T(8,128)S(1)} %get-tuple-element.64, f32[2,2,16,32,128]{4,3,2,1,0:T(8,128)S(1)} %bitcast.139, f32[2,2,16,2,128]{4,3,2,1,0:T(2,128)S(1)} %get-tuple-element.129, ...), kind=kLoop, calls=%fused_computation.154 | loop fusion | flops 9175040 | bytes 4063240 | tf_op jit(solution)/shard_map/mul | solution.py:181
  60.9 1.6 %collective-permute-start.17 = (f32[2,2,16,4,128]{4,3,2,1,0:T(4,128)S(1)}, f32[2,2,16,4,128]{4,3,2,1,0:T(4,128)S(1)}, u32[]{:S(2)}, u32[]{:S(2)}) collective-permute-start(f32[2,2,16,4,128]{4,3,2,1,0:T(4,128)S(1)} %pad_maximum_fusion.39), channel_id=1, source_target_pairs={{0,1},{1,0},{2,3},{3,2},{4,5},{5,4},{6,7},{7,6},{8,9},{9,8},{10,11... | collective-permute-start | bytes 393224 | tf_op jit(solution)/shard_map/ppermute | solution.py:124
  63.7 2.2 %collective-permute-done.17 = f32[2,2,16,4,128]{4,3,2,1,0:T(4,128)S(1)} collective-permute-done((f32[2,2,16,4,128]{4,3,2,1,0:T(4,128)S(1)}, f32[2,2,16,4,128]{4,3,2,1,0:T(4,128)S(1)}, u32[]{:S(2)}, u32[]{:S(2)}) %collective-permute-start.17) | collective-permute-done | bytes 131104 | tf_op jit(solution)/shard_map/ppermute | solution.py:124
  66.0 3.0 %collective-permute-done.15 = f32[2,2,2,32,128]{4,3,2,1,0:T(8,128)S(1)} collective-permute-done((f32[2,2,2,32,128]{4,3,2,1,0:T(8,128)S(1)}, f32[2,2,2,32,128]{4,3,2,1,0:T(8,128)S(1)}, u32[]{:S(2)}, u32[]{:S(2)}) %collective-permute-start.15) | collective-permute-done | bytes 131104 | tf_op jit(solution)/shard_map/ppermute | solution.py:143
  69.0 1.8 %fusion.53 = f32[2,2,16,32,128]{4,3,2,1,0:T(8,128)S(1)} fusion(f32[2,1,16,32,128]{4,3,2,1,0:T(8,128)S(1)} %get-tuple-element.57, f32[2,1,16,32,128]{4,3,2,1,0:T(8,128)S(1)} %get-tuple-element.56, f32[2,2,16,32,128]{4,3,2,1,0:T(8,128)S(1)} %bitcast.144, f32[2,2,16,2,128]{4,3,2,1,0:T(2,128)S(1)} %get-tuple-element.127, ...), kind=kLoop, calls=%fused_computation.160 | loop fusion | flops 9175040 | bytes 4063240 | tf_op jit(solution)/shard_map/mul | solution.py:181
  74.7 3.3 %collective-permute-done.20 = f32[2,2,16,4,128]{4,3,2,1,0:T(4,128)S(1)} collective-permute-done((f32[2,2,16,4,128]{4,3,2,1,0:T(4,128)S(1)}, f32[2,2,16,4,128]{4,3,2,1,0:T(4,128)S(1)}, u32[]{:S(2)}, u32[]{:S(2)}) %collective-permute-start.20) | collective-permute-done | bytes 131104 | tf_op jit(solution)/shard_map/ppermute | solution.py:124
  78.0 2.0 %collective-permute-done.18 = f32[2,2,2,32,128]{4,3,2,1,0:T(8,128)S(1)} collective-permute-done((f32[2,2,2,32,128]{4,3,2,1,0:T(8,128)S(1)}, f32[2,2,2,32,128]{4,3,2,1,0:T(8,128)S(1)}, u32[]{:S(2)}, u32[]{:S(2)}) %collective-permute-start.18) | collective-permute-done | bytes 131104 | tf_op jit(solution)/shard_map/ppermute | solution.py:143
  80.0 2.1 %fusion.58 = f32[2,2,16,32,128]{4,3,2,1,0:T(8,128)S(1)} fusion(f32[2,1,16,32,128]{4,3,2,1,0:T(8,128)S(1)} %get-tuple-element.49, f32[2,1,16,32,128]{4,3,2,1,0:T(8,128)S(1)} %get-tuple-element.48, f32[2,2,16,32,128]{4,3,2,1,0:T(8,128)S(1)} %bitcast.154, f32[2,2,16,2,128]{4,3,2,1,0:T(2,128)S(1)} %get-tuple-element.125, ...), kind=kLoop, calls=%fused_computation.166 | loop fusion | flops 9175040 | bytes 4063240 | tf_op jit(solution)/shard_map/mul | solution.py:181
  84.2 1.6 %collective-permute-start.23 = (f32[2,2,16,4,128]{4,3,2,1,0:T(4,128)S(1)}, f32[2,2,16,4,128]{4,3,2,1,0:T(4,128)S(1)}, u32[]{:S(2)}, u32[]{:S(2)}) collective-permute-start(f32[2,2,16,4,128]{4,3,2,1,0:T(4,128)S(1)} %pad_maximum_fusion.41), channel_id=1, source_target_pairs={{0,1},{1,0},{2,3},{3,2},{4,5},{5,4},{6,7},{7,6},{8,9},{9,8},{10,11... | collective-permute-start | bytes 393224 | tf_op jit(solution)/shard_map/ppermute | solution.py:124
  87.0 2.2 %collective-permute-done.23 = f32[2,2,16,4,128]{4,3,2,1,0:T(4,128)S(1)} collective-permute-done((f32[2,2,16,4,128]{4,3,2,1,0:T(4,128)S(1)}, f32[2,2,16,4,128]{4,3,2,1,0:T(4,128)S(1)}, u32[]{:S(2)}, u32[]{:S(2)}) %collective-permute-start.23) | collective-permute-done | bytes 131104 | tf_op jit(solution)/shard_map/ppermute | solution.py:124
  89.3 3.0 %collective-permute-done.21 = f32[2,2,2,32,128]{4,3,2,1,0:T(8,128)S(1)} collective-permute-done((f32[2,2,2,32,128]{4,3,2,1,0:T(8,128)S(1)}, f32[2,2,2,32,128]{4,3,2,1,0:T(8,128)S(1)}, u32[]{:S(2)}, u32[]{:S(2)}) %collective-permute-start.21) | collective-permute-done | bytes 131104 | tf_op jit(solution)/shard_map/ppermute | solution.py:143
  92.3 1.8 %fusion.63 = f32[2,2,16,32,128]{4,3,2,1,0:T(8,128)S(1)} fusion(f32[2,1,16,32,128]{4,3,2,1,0:T(8,128)S(1)} %get-tuple-element.41, f32[2,1,16,32,128]{4,3,2,1,0:T(8,128)S(1)} %get-tuple-element.40, f32[2,2,16,32,128]{4,3,2,1,0:T(8,128)S(1)} %bitcast.122, f32[2,2,16,2,128]{4,3,2,1,0:T(2,128)S(1)} %get-tuple-element.123, ...), kind=kLoop, calls=%fused_computation.172 | loop fusion | flops 9175040 | bytes 4063240 | tf_op jit(solution)/shard_map/mul | solution.py:181
  99.4 1.9 %collective-permute-done.26 = f32[2,2,16,4,128]{4,3,2,1,0:T(4,128)S(1)} collective-permute-done((f32[2,2,16,4,128]{4,3,2,1,0:T(4,128)S(1)}, f32[2,2,16,4,128]{4,3,2,1,0:T(4,128)S(1)}, u32[]{:S(2)}, u32[]{:S(2)}) %collective-permute-start.26) | collective-permute-done | bytes 131104 | tf_op jit(solution)/shard_map/ppermute | solution.py:124
  101.4 2.0 %collective-permute-done.24 = f32[2,2,2,32,128]{4,3,2,1,0:T(8,128)S(1)} collective-permute-done((f32[2,2,2,32,128]{4,3,2,1,0:T(8,128)S(1)}, f32[2,2,2,32,128]{4,3,2,1,0:T(8,128)S(1)}, u32[]{:S(2)}, u32[]{:S(2)}) %collective-permute-start.24) | collective-permute-done | bytes 131104 | tf_op jit(solution)/shard_map/ppermute | solution.py:143
  104.5 1.8 %fusion.68 = f32[2,2,16,32,128]{4,3,2,1,0:T(8,128)S(1)} fusion(f32[2,1,16,32,128]{4,3,2,1,0:T(8,128)S(1)} %get-tuple-element.33, f32[2,1,16,32,128]{4,3,2,1,0:T(8,128)S(1)} %get-tuple-element.32, f32[2,2,16,32,128]{4,3,2,1,0:T(8,128)S(1)} %bitcast.129, f32[2,2,16,2,128]{4,3,2,1,0:T(2,128)S(1)} %get-tuple-element.121, ...), kind=kLoop, calls=%fused_computation.178 | loop fusion | flops 9175040 | bytes 4063240 | tf_op jit(solution)/shard_map/mul | solution.py:181
  107.7 1.5 %collective-permute-start.27 = (f32[1,2,16,32,128]{4,3,2,1,0:T(8,128)S(1)}, f32[1,2,16,32,128]{4,3,2,1,0:T(8,128)S(1)}, u32[]{:S(2)}, u32[]{:S(2)}) collective-permute-start(f32[1,2,16,32,128]{4,3,2,1,0:T(8,128)S(1)} %convolution_bitcast_fusion), channel_id=1, source_target_pairs={{0,16},{1,17},{2,18},{3,19},{4,20},{5,21},{6,22},{7,23},{8,24},{9,... | collective-permute-start | bytes 1572872 | tf_op jit(solution)/shard_map/ppermute | solution.py:250
  109.5 4.8 %collective-permute-done.28 = f32[1,2,16,32,128]{4,3,2,1,0:T(8,128)S(1)} collective-permute-done((f32[1,2,16,32,128]{4,3,2,1,0:T(8,128)S(1)}, f32[1,2,16,32,128]{4,3,2,1,0:T(8,128)S(1)}, u32[]{:S(2)}, u32[]{:S(2)}) %collective-permute-start.28) | collective-permute-done | bytes 524320 | tf_op jit(solution)/shard_map/ppermute | solution.py:250
  114.3 3.4 %collective-permute-done.27 = f32[1,2,16,32,128]{4,3,2,1,0:T(8,128)S(1)} collective-permute-done((f32[1,2,16,32,128]{4,3,2,1,0:T(8,128)S(1)}, f32[1,2,16,32,128]{4,3,2,1,0:T(8,128)S(1)}, u32[]{:S(2)}, u32[]{:S(2)}) %collective-permute-start.27) | collective-permute-done | bytes 524320 | tf_op jit(solution)/shard_map/ppermute | solution.py:250
  (137 shorter events, 41.8 us)
Async XLA Ops:
  0.9 11.9 %collective-permute-start = (f32[1,2,2,32,128]{4,3,2,1,0:T(8,128)S(1)}, f32[1,2,2,32,128]{4,3,2,1,0:T(8,128)S(1)}, u32[]{:S(2)}, u32[]{:S(2)}) collective-permute-start(f32[1,2,2,32,128]{4,3,2,1,0:T(8,128)S(1)} %get-tuple-element.94), channel_id=1, source_target_pairs={{16,18},{18,16},{2,4},{4,2},{20,22},{22,20},{6,8},{8,6},{24,26},{2... | collective-permute-start | bytes 196616 | tf_op jit(solution)/shard_map/ppermute | solution.py:143
  5.4 7.3 %collective-permute-start.1 = (f32[1,2,2,32,128]{4,3,2,1,0:T(8,128)S(1)}, f32[1,2,2,32,128]{4,3,2,1,0:T(8,128)S(1)}, u32[]{:S(2)}, u32[]{:S(2)}) collective-permute-start(f32[1,2,2,32,128]{4,3,2,1,0:T(8,128)S(1)} %get-tuple-element.95), channel_id=1, source_target_pairs={{0,16},{16,0},{18,2},{2,18},{4,20},{20,4},{22,6},{6,22},{8,24},{24... | collective-permute-start | bytes 196616 | tf_op jit(solution)/shard_map/ppermute | solution.py:143
  6.6 6.1 %collective-permute-start.2 = (f32[1,2,16,4,128]{4,3,2,1,0:T(4,128)S(1)}, f32[1,2,16,4,128]{4,3,2,1,0:T(4,128)S(1)}, u32[]{:S(2)}, u32[]{:S(2)}) collective-permute-start(f32[1,2,16,4,128]{4,3,2,1,0:T(4,128)S(1)} %pad_maximum_fusion.43), channel_id=1, source_target_pairs={{0,1},{1,0},{2,3},{3,2},{4,5},{5,4},{6,7},{7,6},{8,9},{9,8},{10,11... | collective-permute-start | bytes 196616 | tf_op jit(solution)/shard_map/ppermute | solution.py:124
  8.5 4.3 %copy-start.1 = (f32[2,32,32,128]{3,2,1,0:T(8,128)S(1)}, f32[2,32,32,128]{3,2,1,0:T(8,128)}, u32[]{:S(2)}) copy-start(f32[2,32,32,128]{3,2,1,0:T(8,128)} %param.12) | copy-start | bytes 3145732
  8.5 4.3 %copy-start.3 = (f32[2]{0:T(128)S(1)}, f32[2]{0:T(128)}, u32[]{:S(2)}) copy-start(f32[2]{0:T(128)} %constant.178) | copy-start | bytes 28
  14.6 6.5 %collective-permute-start.3 = (f32[2,2,2,32,128]{4,3,2,1,0:T(8,128)S(1)}, f32[2,2,2,32,128]{4,3,2,1,0:T(8,128)S(1)}, u32[]{:S(2)}, u32[]{:S(2)}) collective-permute-start(f32[2,2,2,32,128]{4,3,2,1,0:T(8,128)S(1)} %get-tuple-element.85), channel_id=1, source_target_pairs={{16,18},{18,16},{2,4},{4,2},{20,22},{22,20},{6,8},{8,6},{24,26},{2... | collective-permute-start | bytes 393224 | tf_op jit(solution)/shard_map/ppermute | solution.py:143
  16.3 5.0 %collective-permute-start.4 = (f32[2,2,2,32,128]{4,3,2,1,0:T(8,128)S(1)}, f32[2,2,2,32,128]{4,3,2,1,0:T(8,128)S(1)}, u32[]{:S(2)}, u32[]{:S(2)}) collective-permute-start(f32[2,2,2,32,128]{4,3,2,1,0:T(8,128)S(1)} %get-tuple-element.84), channel_id=1, source_target_pairs={{0,16},{16,0},{18,2},{2,18},{4,20},{20,4},{22,6},{6,22},{8,24},{24... | collective-permute-start | bytes 393224 | tf_op jit(solution)/shard_map/ppermute | solution.py:143
  16.9 5.6 %collective-permute-start.5 = (f32[2,2,16,4,128]{4,3,2,1,0:T(4,128)S(1)}, f32[2,2,16,4,128]{4,3,2,1,0:T(4,128)S(1)}, u32[]{:S(2)}, u32[]{:S(2)}) collective-permute-start(f32[2,2,16,4,128]{4,3,2,1,0:T(4,128)S(1)} %pad_maximum_fusion.35), channel_id=1, source_target_pairs={{0,1},{1,0},{2,3},{3,2},{4,5},{5,4},{6,7},{7,6},{8,9},{9,8},{10,11... | collective-permute-start | bytes 393224 | tf_op jit(solution)/shard_map/ppermute | solution.py:124
  26.0 5.0 %collective-permute-start.8 = (f32[2,2,16,4,128]{4,3,2,1,0:T(4,128)S(1)}, f32[2,2,16,4,128]{4,3,2,1,0:T(4,128)S(1)}, u32[]{:S(2)}, u32[]{:S(2)}) collective-permute-start(f32[2,2,16,4,128]{4,3,2,1,0:T(4,128)S(1)} %pad_maximum_fusion.36), channel_id=1, source_target_pairs={{0,1},{1,0},{2,3},{3,2},{4,5},{5,4},{6,7},{7,6},{8,9},{9,8},{10,11... | collective-permute-start | bytes 393224 | tf_op jit(solution)/shard_map/ppermute | solution.py:124
  26.8 6.3 %collective-permute-start.6 = (f32[2,2,2,32,128]{4,3,2,1,0:T(8,128)S(1)}, f32[2,2,2,32,128]{4,3,2,1,0:T(8,128)S(1)}, u32[]{:S(2)}, u32[]{:S(2)}) collective-permute-start(f32[2,2,2,32,128]{4,3,2,1,0:T(8,128)S(1)} %get-tuple-element.76), channel_id=1, source_target_pairs={{16,18},{18,16},{2,4},{4,2},{20,22},{22,20},{6,8},{8,6},{24,26},{2... | collective-permute-start | bytes 393224 | tf_op jit(solution)/shard_map/ppermute | solution.py:143
  27.5 5.5 %collective-permute-start.7 = (f32[2,2,2,32,128]{4,3,2,1,0:T(8,128)S(1)}, f32[2,2,2,32,128]{4,3,2,1,0:T(8,128)S(1)}, u32[]{:S(2)}, u32[]{:S(2)}) collective-permute-start(f32[2,2,2,32,128]{4,3,2,1,0:T(8,128)S(1)} %get-tuple-element.77), channel_id=1, source_target_pairs={{0,16},{16,0},{18,2},{2,18},{4,20},{20,4},{22,6},{6,22},{8,24},{24... | collective-permute-start | bytes 393224 | tf_op jit(solution)/shard_map/ppermute | solution.py:143
  36.9 5.0 %collective-permute-start.11 = (f32[2,2,16,4,128]{4,3,2,1,0:T(4,128)S(1)}, f32[2,2,16,4,128]{4,3,2,1,0:T(4,128)S(1)}, u32[]{:S(2)}, u32[]{:S(2)}) collective-permute-start(f32[2,2,16,4,128]{4,3,2,1,0:T(4,128)S(1)} %pad_maximum_fusion.37), channel_id=1, source_target_pairs={{0,1},{1,0},{2,3},{3,2},{4,5},{5,4},{6,7},{7,6},{8,9},{9,8},{10,11... | collective-permute-start | bytes 393224 | tf_op jit(solution)/shard_map/ppermute | solution.py:124
  38.8 5.0 %collective-permute-start.10 = (f32[2,2,2,32,128]{4,3,2,1,0:T(8,128)S(1)}, f32[2,2,2,32,128]{4,3,2,1,0:T(8,128)S(1)}, u32[]{:S(2)}, u32[]{:S(2)}) collective-permute-start(f32[2,2,2,32,128]{4,3,2,1,0:T(8,128)S(1)} %get-tuple-element.69), channel_id=1, source_target_pairs={{0,16},{16,0},{18,2},{2,18},{4,20},{20,4},{22,6},{6,22},{8,24},{24... | collective-permute-start | bytes 393224 | tf_op jit(solution)/shard_map/ppermute | solution.py:143
  39.5 6.2 %collective-permute-start.9 = (f32[2,2,2,32,128]{4,3,2,1,0:T(8,128)S(1)}, f32[2,2,2,32,128]{4,3,2,1,0:T(8,128)S(1)}, u32[]{:S(2)}, u32[]{:S(2)}) collective-permute-start(f32[2,2,2,32,128]{4,3,2,1,0:T(8,128)S(1)} %get-tuple-element.68), channel_id=1, source_target_pairs={{16,18},{18,16},{2,4},{4,2},{20,22},{22,20},{6,8},{8,6},{24,26},{2... | collective-permute-start | bytes 393224 | tf_op jit(solution)/shard_map/ppermute | solution.py:143
  49.8 5.0 %collective-permute-start.14 = (f32[2,2,16,4,128]{4,3,2,1,0:T(4,128)S(1)}, f32[2,2,16,4,128]{4,3,2,1,0:T(4,128)S(1)}, u32[]{:S(2)}, u32[]{:S(2)}) collective-permute-start(f32[2,2,16,4,128]{4,3,2,1,0:T(4,128)S(1)} %pad_maximum_fusion.38), channel_id=1, source_target_pairs={{0,1},{1,0},{2,3},{3,2},{4,5},{5,4},{6,7},{7,6},{8,9},{9,8},{10,11... | collective-permute-start | bytes 393224 | tf_op jit(solution)/shard_map/ppermute | solution.py:124
  50.6 6.3 %collective-permute-start.12 = (f32[2,2,2,32,128]{4,3,2,1,0:T(8,128)S(1)}, f32[2,2,2,32,128]{4,3,2,1,0:T(8,128)S(1)}, u32[]{:S(2)}, u32[]{:S(2)}) collective-permute-start(f32[2,2,2,32,128]{4,3,2,1,0:T(8,128)S(1)} %get-tuple-element.60), channel_id=1, source_target_pairs={{16,18},{18,16},{2,4},{4,2},{20,22},{22,20},{6,8},{8,6},{24,26},{2... | collective-permute-start | bytes 393224 | tf_op jit(solution)/shard_map/ppermute | solution.py:143
  51.4 5.5 %collective-permute-start.13 = (f32[2,2,2,32,128]{4,3,2,1,0:T(8,128)S(1)}, f32[2,2,2,32,128]{4,3,2,1,0:T(8,128)S(1)}, u32[]{:S(2)}, u32[]{:S(2)}) collective-permute-start(f32[2,2,2,32,128]{4,3,2,1,0:T(8,128)S(1)} %get-tuple-element.61), channel_id=1, source_target_pairs={{0,16},{16,0},{18,2},{2,18},{4,20},{20,4},{22,6},{6,22},{8,24},{24... | collective-permute-start | bytes 393224 | tf_op jit(solution)/shard_map/ppermute | solution.py:143
  60.9 5.0 %collective-permute-start.17 = (f32[2,2,16,4,128]{4,3,2,1,0:T(4,128)S(1)}, f32[2,2,16,4,128]{4,3,2,1,0:T(4,128)S(1)}, u32[]{:S(2)}, u32[]{:S(2)}) collective-permute-start(f32[2,2,16,4,128]{4,3,2,1,0:T(4,128)S(1)} %pad_maximum_fusion.39), channel_id=1, source_target_pairs={{0,1},{1,0},{2,3},{3,2},{4,5},{5,4},{6,7},{7,6},{8,9},{9,8},{10,11... | collective-permute-start | bytes 393224 | tf_op jit(solution)/shard_map/ppermute | solution.py:124
  62.7 6.3 %collective-permute-start.15 = (f32[2,2,2,32,128]{4,3,2,1,0:T(8,128)S(1)}, f32[2,2,2,32,128]{4,3,2,1,0:T(8,128)S(1)}, u32[]{:S(2)}, u32[]{:S(2)}) collective-permute-start(f32[2,2,2,32,128]{4,3,2,1,0:T(8,128)S(1)} %get-tuple-element.52), channel_id=1, source_target_pairs={{16,18},{18,16},{2,4},{4,2},{20,22},{22,20},{6,8},{8,6},{24,26},{2... | collective-permute-start | bytes 393224 | tf_op jit(solution)/shard_map/ppermute | solution.py:143
  63.7 5.3 %collective-permute-start.16 = (f32[2,2,2,32,128]{4,3,2,1,0:T(8,128)S(1)}, f32[2,2,2,32,128]{4,3,2,1,0:T(8,128)S(1)}, u32[]{:S(2)}, u32[]{:S(2)}) collective-permute-start(f32[2,2,2,32,128]{4,3,2,1,0:T(8,128)S(1)} %get-tuple-element.53), channel_id=1, source_target_pairs={{0,16},{16,0},{18,2},{2,18},{4,20},{20,4},{22,6},{6,22},{8,24},{24... | collective-permute-start | bytes 393224 | tf_op jit(solution)/shard_map/ppermute | solution.py:143
  72.9 5.0 %collective-permute-start.20 = (f32[2,2,16,4,128]{4,3,2,1,0:T(4,128)S(1)}, f32[2,2,16,4,128]{4,3,2,1,0:T(4,128)S(1)}, u32[]{:S(2)}, u32[]{:S(2)}) collective-permute-start(f32[2,2,16,4,128]{4,3,2,1,0:T(4,128)S(1)} %pad_maximum_fusion.40), channel_id=1, source_target_pairs={{0,1},{1,0},{2,3},{3,2},{4,5},{5,4},{6,7},{7,6},{8,9},{9,8},{10,11... | collective-permute-start | bytes 393224 | tf_op jit(solution)/shard_map/ppermute | solution.py:124
  73.8 6.3 %collective-permute-start.18 = (f32[2,2,2,32,128]{4,3,2,1,0:T(8,128)S(1)}, f32[2,2,2,32,128]{4,3,2,1,0:T(8,128)S(1)}, u32[]{:S(2)}, u32[]{:S(2)}) collective-permute-start(f32[2,2,2,32,128]{4,3,2,1,0:T(8,128)S(1)} %get-tuple-element.44), channel_id=1, source_target_pairs={{16,18},{18,16},{2,4},{4,2},{20,22},{22,20},{6,8},{8,6},{24,26},{2... | collective-permute-start | bytes 393224 | tf_op jit(solution)/shard_map/ppermute | solution.py:143
  74.7 5.3 %collective-permute-start.19 = (f32[2,2,2,32,128]{4,3,2,1,0:T(8,128)S(1)}, f32[2,2,2,32,128]{4,3,2,1,0:T(8,128)S(1)}, u32[]{:S(2)}, u32[]{:S(2)}) collective-permute-start(f32[2,2,2,32,128]{4,3,2,1,0:T(8,128)S(1)} %get-tuple-element.45), channel_id=1, source_target_pairs={{0,16},{16,0},{18,2},{2,18},{4,20},{20,4},{22,6},{6,22},{8,24},{24... | collective-permute-start | bytes 393224 | tf_op jit(solution)/shard_map/ppermute | solution.py:143
  84.2 5.0 %collective-permute-start.23 = (f32[2,2,16,4,128]{4,3,2,1,0:T(4,128)S(1)}, f32[2,2,16,4,128]{4,3,2,1,0:T(4,128)S(1)}, u32[]{:S(2)}, u32[]{:S(2)}) collective-permute-start(f32[2,2,16,4,128]{4,3,2,1,0:T(4,128)S(1)} %pad_maximum_fusion.41), channel_id=1, source_target_pairs={{0,1},{1,0},{2,3},{3,2},{4,5},{5,4},{6,7},{7,6},{8,9},{9,8},{10,11... | collective-permute-start | bytes 393224 | tf_op jit(solution)/shard_map/ppermute | solution.py:124
  86.0 6.3 %collective-permute-start.21 = (f32[2,2,2,32,128]{4,3,2,1,0:T(8,128)S(1)}, f32[2,2,2,32,128]{4,3,2,1,0:T(8,128)S(1)}, u32[]{:S(2)}, u32[]{:S(2)}) collective-permute-start(f32[2,2,2,32,128]{4,3,2,1,0:T(8,128)S(1)} %get-tuple-element.36), channel_id=1, source_target_pairs={{16,18},{18,16},{2,4},{4,2},{20,22},{22,20},{6,8},{8,6},{24,26},{2... | collective-permute-start | bytes 393224 | tf_op jit(solution)/shard_map/ppermute | solution.py:143
  87.0 5.3 %collective-permute-start.22 = (f32[2,2,2,32,128]{4,3,2,1,0:T(8,128)S(1)}, f32[2,2,2,32,128]{4,3,2,1,0:T(8,128)S(1)}, u32[]{:S(2)}, u32[]{:S(2)}) collective-permute-start(f32[2,2,2,32,128]{4,3,2,1,0:T(8,128)S(1)} %get-tuple-element.37), channel_id=1, source_target_pairs={{0,16},{16,0},{18,2},{2,18},{4,20},{20,4},{22,6},{6,22},{8,24},{24... | collective-permute-start | bytes 393224 | tf_op jit(solution)/shard_map/ppermute | solution.py:143
  96.3 5.0 %collective-permute-start.26 = (f32[2,2,16,4,128]{4,3,2,1,0:T(4,128)S(1)}, f32[2,2,16,4,128]{4,3,2,1,0:T(4,128)S(1)}, u32[]{:S(2)}, u32[]{:S(2)}) collective-permute-start(f32[2,2,16,4,128]{4,3,2,1,0:T(4,128)S(1)} %pad_maximum_fusion.42), channel_id=1, source_target_pairs={{0,1},{1,0},{2,3},{3,2},{4,5},{5,4},{6,7},{7,6},{8,9},{9,8},{10,11... | collective-permute-start | bytes 393224 | tf_op jit(solution)/shard_map/ppermute | solution.py:124
  97.2 6.3 %collective-permute-start.24 = (f32[2,2,2,32,128]{4,3,2,1,0:T(8,128)S(1)}, f32[2,2,2,32,128]{4,3,2,1,0:T(8,128)S(1)}, u32[]{:S(2)}, u32[]{:S(2)}) collective-permute-start(f32[2,2,2,32,128]{4,3,2,1,0:T(8,128)S(1)} %get-tuple-element.28), channel_id=1, source_target_pairs={{16,18},{18,16},{2,4},{4,2},{20,22},{22,20},{6,8},{8,6},{24,26},{2... | collective-permute-start | bytes 393224 | tf_op jit(solution)/shard_map/ppermute | solution.py:143
  98.1 6.4 %collective-permute-start.25 = (f32[2,2,2,32,128]{4,3,2,1,0:T(8,128)S(1)}, f32[2,2,2,32,128]{4,3,2,1,0:T(8,128)S(1)}, u32[]{:S(2)}, u32[]{:S(2)}) collective-permute-start(f32[2,2,2,32,128]{4,3,2,1,0:T(8,128)S(1)} %get-tuple-element.29), channel_id=1, source_target_pairs={{0,16},{16,0},{18,2},{2,18},{4,20},{20,4},{22,6},{6,22},{8,24},{24... | collective-permute-start | bytes 393224 | tf_op jit(solution)/shard_map/ppermute | solution.py:143
  98.1 16.1 %collective-permute-start.28 = (f32[1,2,16,32,128]{4,3,2,1,0:T(8,128)S(1)}, f32[1,2,16,32,128]{4,3,2,1,0:T(8,128)S(1)}, u32[]{:S(2)}, u32[]{:S(2)}) collective-permute-start(f32[1,2,16,32,128]{4,3,2,1,0:T(8,128)S(1)} %slice.1061), channel_id=1, source_target_pairs={{16,0},{17,1},{18,2},{19,3},{20,4},{21,5},{22,6},{23,7},{24,8},{25... | collective-permute-start | bytes 1572872 | tf_op jit(solution)/shard_map/ppermute | solution.py:250
  107.7 10.0 %collective-permute-start.27 = (f32[1,2,16,32,128]{4,3,2,1,0:T(8,128)S(1)}, f32[1,2,16,32,128]{4,3,2,1,0:T(8,128)S(1)}, u32[]{:S(2)}, u32[]{:S(2)}) collective-permute-start(f32[1,2,16,32,128]{4,3,2,1,0:T(8,128)S(1)} %convolution_bitcast_fusion), channel_id=1, source_target_pairs={{0,16},{1,17},{2,18},{3,19},{4,20},{5,21},{6,22},{7,23},{8,24},{9,... | collective-permute-start | bytes 1572872 | tf_op jit(solution)/shard_map/ppermute | solution.py:250
  109.5 8.2 %copy-start.2 = (f32[1,2,32,32,128]{4,3,2,1,0:T(8,128)}, f32[1,2,32,32,128]{4,3,2,1,0:T(8,128)S(1)}, u32[]{:S(2)}) copy-start(f32[1,2,32,32,128]{4,3,2,1,0:T(8,128)S(1)} %fusion.74) | copy-start | bytes 3145732
  (2 other events, 4.2 us)

commit v14 on v11

--- a/solution.py
+++ b/solution.py
@@ -121,10 +121,8 @@
     last = lax.slice_in_dim(block, length - width, length, axis=dim)
     first = lax.slice_in_dim(block, 0, width, axis=dim)
     if size == 2:
-        got = lax.ppermute(jnp.concatenate([first, last], dim), axes, up)
-        after = lax.slice_in_dim(got, 0, width, axis=dim)
-        before = lax.slice_in_dim(got, width, 2 * width, axis=dim)
-        return before, after
+        got = lax.ppermute(jnp.stack([first, last], 0), axes, up)
+        return got[1], got[0]
     before = lax.ppermute(last, axes, up)
     after = lax.ppermute(first, axes, down)
     return before, after

time: 118 us -> 118 us (level)
  no operation moved by 1% of the time
where the time goes in v14:
time: 118 us
  waiting for transfers between devices  49.6 us (42%)
  starting transfers between devices  26.1 us (22%)
  other arithmetic  25.4 us (22%)
  matrix products  9.09 us (8%)
  local copies, waits for them, and re-layouts  3.82 us (3%)
  Pallas kernels  3 us (3%)
    ppermute x18, waiting for transfers between devices, swap_halo(): got.append(lax.ppermute(sent, axes, pairs))  21.1 us
    ppermute x9, waiting for transfers between devices, ring_halo(): got = lax.ppermute(jnp.stack([first, last], 0), axes, up)  20.2 us
    mul x9, other arithmetic, tendency(): return DT * (flow + kappa * laplace + react)  15.1 us
    ppermute x18, starting transfers between devices, swap_halo(): got.append(lax.ppermute(sent, axes, pairs))  14.1 us
    ppermute x9, starting transfers between devices, ring_halo(): got = lax.ppermute(jnp.stack([first, last], 0), axes, up)  9.2 us
    dot_general x9, matrix products, column_solve(): jnp.einsum('lsxyk,sjk->lsxyj', rhs, inverse, precision=lax.Precision.HIGH...  9.09 us
    ppermute x2, waiting for transfers between devices, on_device(): arrived = lax.ppermute(states[level][None], 'corr', pairs)  8.34 us
    add x5, other arithmetic, on_device(): total = total + (quad + g_now[l - 1] - e_hist[l - 1][m])  3.62 us
  transfers between devices with their start and end apart: 29, of which 21 were waited for; matrix products, arithmetic and copies ran while one was open for 5% of the time, Pallas kernels for 3%

profile of v14, /device:TPU:0, one launch (start us, length us, event | category | flops | bytes accessed | tf_op | source)
XLA Modules:
  0.0 117.7 jit_solution(2035080514662267446)
XLA Ops:
  1.1 4.6 %collective-permute-start = (f32[1,2,2,32,128]{4,3,2,1,0:T(8,128)S(1)}, f32[1,2,2,32,128]{4,3,2,1,0:T(8,128)S(1)}, u32[]{:S(2)}, u32[]{:S(2)}) collective-permute-start(f32[1,2,2,32,128]{4,3,2,1,0:T(8,128)S(1)} %get-tuple-element.98), channel_id=1, source_target_pairs={{16,18},{18,16},{2,4},{4,2},{20,22},{22,20},{6,8},{8,6},{24,26},{2... | collective-permute-start | bytes 196616 | tf_op jit(solution)/shard_map/ppermute | solution.py:142
  5.7 1.6 %collective-permute-start.2 = (f32[2,1,2,16,2,128]{5,4,3,2,1,0:T(2,128)S(1)}, f32[2,1,2,16,2,128]{5,4,3,2,1,0:T(2,128)S(1)}, u32[]{:S(2)}, u32[]{:S(2)}) collective-permute-start(f32[2,1,2,16,2,128]{5,4,3,2,1,0:T(2,128)S(1)} %pad_maximum_fusion.43), channel_id=1, source_target_pairs={{0,1},{1,0},{2,3},{3,2},{4,5},{5,4},{6,7},{7,6},{8,9},{9,8},{10,11... | collective-permute-start | bytes 196616 | tf_op jit(solution)/shard_map/ppermute | solution.py:124
  7.7 3.0 %shard_map.118 = f32[128,2,128]{2,1,0:T(2,128)} custom-call(f32[2,128]{1,0:T(2,128)} %diff_ref.1), custom_call_target="tpu_custom_call" | custom-call | flops 393216 | bytes 262144 | tf_op jit(solution)/shard_map/pallas_call | solution.py:78
  13.7 1.7 %collective-permute-start.3 = (f32[2,2,2,32,128]{4,3,2,1,0:T(8,128)S(1)}, f32[2,2,2,32,128]{4,3,2,1,0:T(8,128)S(1)}, u32[]{:S(2)}, u32[]{:S(2)}) collective-permute-start(f32[2,2,2,32,128]{4,3,2,1,0:T(8,128)S(1)} %get-tuple-element.85), channel_id=1, source_target_pairs={{16,18},{18,16},{2,4},{4,2},{20,22},{22,20},{6,8},{8,6},{24,26},{2... | collective-permute-start | bytes 393224 | tf_op jit(solution)/shard_map/ppermute | solution.py:142
  16.7 3.6 %collective-permute-done.3 = f32[2,2,2,32,128]{4,3,2,1,0:T(8,128)S(1)} collective-permute-done((f32[2,2,2,32,128]{4,3,2,1,0:T(8,128)S(1)}, f32[2,2,2,32,128]{4,3,2,1,0:T(8,128)S(1)}, u32[]{:S(2)}, u32[]{:S(2)}) %collective-permute-start.3) | collective-permute-done | bytes 131104 | tf_op jit(solution)/shard_map/ppermute | solution.py:142
  26.9 3.4 %collective-permute-done.8 = f32[2,2,2,16,2,128]{5,4,3,2,1,0:T(2,128)S(1)} collective-permute-done((f32[2,2,2,16,2,128]{5,4,3,2,1,0:T(2,128)S(1)}, f32[2,2,2,16,2,128]{5,4,3,2,1,0:T(2,128)S(1)}, u32[]{:S(2)}, u32[]{:S(2)}) %collective-permute-start.8) | collective-permute-done | bytes 131104 | tf_op jit(solution)/shard_map/ppermute | solution.py:124
  30.3 1.8 %collective-permute-done.6 = f32[2,2,2,32,128]{4,3,2,1,0:T(8,128)S(1)} collective-permute-done((f32[2,2,2,32,128]{4,3,2,1,0:T(8,128)S(1)}, f32[2,2,2,32,128]{4,3,2,1,0:T(8,128)S(1)}, u32[]{:S(2)}, u32[]{:S(2)}) %collective-permute-start.6) | collective-permute-done | bytes 131104 | tf_op jit(solution)/shard_map/ppermute | solution.py:142
  32.1 1.8 %fusion.37 = f32[2,2,16,32,128]{4,3,2,1,0:T(8,128)S(1)} fusion(f32[2,1,16,32,128]{4,3,2,1,0:T(8,128)S(1)} %get-tuple-element.81, f32[2,1,16,32,128]{4,3,2,1,0:T(8,128)S(1)} %get-tuple-element.80, f32[2,2,16,32,128]{4,3,2,1,0:T(8,128)S(1)} %convolution_bitcast_fusion.6, f32[2,2,16,2,128]{4,3,2,1,0:T(2,128)S(1)} %get-tuple-element.133, ...), kind=kLoop, calls=%fused_computation.148 | loop fusion | flops 9175040 | bytes 4063240 | tf_op jit(solution)/shard_map/mul | solution.py:180
  36.2 1.6 %collective-permute-start.11 = (f32[2,2,2,16,2,128]{5,4,3,2,1,0:T(2,128)S(1)}, f32[2,2,2,16,2,128]{5,4,3,2,1,0:T(2,128)S(1)}, u32[]{:S(2)}, u32[]{:S(2)}) collective-permute-start(f32[2,2,2,16,2,128]{5,4,3,2,1,0:T(2,128)S(1)} %pad_maximum_fusion.37), channel_id=1, source_target_pairs={{0,1},{1,0},{2,3},{3,2},{4,5},{5,4},{6,7},{7,6},{8,9},{9,8},{10,11... | collective-permute-start | bytes 393224 | tf_op jit(solution)/shard_map/ppermute | solution.py:124
  39.6 1.7 %collective-permute-done.11 = f32[2,2,2,16,2,128]{5,4,3,2,1,0:T(2,128)S(1)} collective-permute-done((f32[2,2,2,16,2,128]{5,4,3,2,1,0:T(2,128)S(1)}, f32[2,2,2,16,2,128]{5,4,3,2,1,0:T(2,128)S(1)}, u32[]{:S(2)}, u32[]{:S(2)}) %collective-permute-start.11) | collective-permute-done | bytes 131104 | tf_op jit(solution)/shard_map/ppermute | solution.py:124
  41.3 1.6 %collective-permute-done.10 = f32[2,2,2,32,128]{4,3,2,1,0:T(8,128)S(1)} collective-permute-done((f32[2,2,2,32,128]{4,3,2,1,0:T(8,128)S(1)}, f32[2,2,2,32,128]{4,3,2,1,0:T(8,128)S(1)}, u32[]{:S(2)}, u32[]{:S(2)}) %collective-permute-start.10) | collective-permute-done | bytes 131104 | tf_op jit(solution)/shard_map/ppermute | solution.py:142
  42.9 1.9 %collective-permute-done.9 = f32[2,2,2,32,128]{4,3,2,1,0:T(8,128)S(1)} collective-permute-done((f32[2,2,2,32,128]{4,3,2,1,0:T(8,128)S(1)}, f32[2,2,2,32,128]{4,3,2,1,0:T(8,128)S(1)}, u32[]{:S(2)}, u32[]{:S(2)}) %collective-permute-start.9) | collective-permute-done | bytes 131104 | tf_op jit(solution)/shard_map/ppermute | solution.py:142
  44.8 2.0 %fusion.41 = f32[2,2,16,32,128]{4,3,2,1,0:T(8,128)S(1)} fusion(f32[2,1,16,32,128]{4,3,2,1,0:T(8,128)S(1)} %get-tuple-element.73, f32[2,1,16,32,128]{4,3,2,1,0:T(8,128)S(1)} %get-tuple-element.72, f32[2,2,16,32,128]{4,3,2,1,0:T(8,128)S(1)} %convolution_bitcast_fusion.5, f32[2,2,16,2,128]{4,3,2,1,0:T(2,128)S(1)} %get-tuple-element.131, ...), kind=kLoop, calls=%fused_computation.153 | loop fusion | flops 9175040 | bytes 4063240 | tf_op jit(solution)/shard_map/mul | solution.py:180
  50.5 3.7 %collective-permute-done.14 = f32[2,2,2,16,2,128]{5,4,3,2,1,0:T(2,128)S(1)} collective-permute-done((f32[2,2,2,16,2,128]{5,4,3,2,1,0:T(2,128)S(1)}, f32[2,2,2,16,2,128]{5,4,3,2,1,0:T(2,128)S(1)}, u32[]{:S(2)}, u32[]{:S(2)}) %collective-permute-start.14) | collective-permute-done | bytes 131104 | tf_op jit(solution)/shard_map/ppermute | solution.py:124
  54.1 1.8 %collective-permute-done.12 = f32[2,2,2,32,128]{4,3,2,1,0:T(8,128)S(1)} collective-permute-done((f32[2,2,2,32,128]{4,3,2,1,0:T(8,128)S(1)}, f32[2,2,2,32,128]{4,3,2,1,0:T(8,128)S(1)}, u32[]{:S(2)}, u32[]{:S(2)}) %collective-permute-start.12) | collective-permute-done | bytes 131104 | tf_op jit(solution)/shard_map/ppermute | solution.py:142
  56.0 1.8 %fusion.45 = f32[2,2,16,32,128]{4,3,2,1,0:T(8,128)S(1)} fusion(f32[2,1,16,32,128]{4,3,2,1,0:T(8,128)S(1)} %get-tuple-element.65, f32[2,1,16,32,128]{4,3,2,1,0:T(8,128)S(1)} %get-tuple-element.64, f32[2,2,16,32,128]{4,3,2,1,0:T(8,128)S(1)} %convolution_bitcast_fusion.4, f32[2,2,16,2,128]{4,3,2,1,0:T(2,128)S(1)} %get-tuple-element.129, ...), kind=kLoop, calls=%fused_computation.158 | loop fusion | flops 9175040 | bytes 4063240 | tf_op jit(solution)/shard_map/mul | solution.py:180
  60.2 1.6 %collective-permute-start.17 = (f32[2,2,2,16,2,128]{5,4,3,2,1,0:T(2,128)S(1)}, f32[2,2,2,16,2,128]{5,4,3,2,1,0:T(2,128)S(1)}, u32[]{:S(2)}, u32[]{:S(2)}) collective-permute-start(f32[2,2,2,16,2,128]{5,4,3,2,1,0:T(2,128)S(1)} %pad_maximum_fusion.39), channel_id=1, source_target_pairs={{0,1},{1,0},{2,3},{3,2},{4,5},{5,4},{6,7},{7,6},{8,9},{9,8},{10,11... | collective-permute-start | bytes 393224 | tf_op jit(solution)/shard_map/ppermute | solution.py:124
  62.7 2.5 %collective-permute-done.17 = f32[2,2,2,16,2,128]{5,4,3,2,1,0:T(2,128)S(1)} collective-permute-done((f32[2,2,2,16,2,128]{5,4,3,2,1,0:T(2,128)S(1)}, f32[2,2,2,16,2,128]{5,4,3,2,1,0:T(2,128)S(1)}, u32[]{:S(2)}, u32[]{:S(2)}) %collective-permute-start.17) | collective-permute-done | bytes 131104 | tf_op jit(solution)/shard_map/ppermute | solution.py:124
  65.2 2.8 %collective-permute-done.15 = f32[2,2,2,32,128]{4,3,2,1,0:T(8,128)S(1)} collective-permute-done((f32[2,2,2,32,128]{4,3,2,1,0:T(8,128)S(1)}, f32[2,2,2,32,128]{4,3,2,1,0:T(8,128)S(1)}, u32[]{:S(2)}, u32[]{:S(2)}) %collective-permute-start.15) | collective-permute-done | bytes 131104 | tf_op jit(solution)/shard_map/ppermute | solution.py:142
  68.1 1.8 %fusion.49 = f32[2,2,16,32,128]{4,3,2,1,0:T(8,128)S(1)} fusion(f32[2,1,16,32,128]{4,3,2,1,0:T(8,128)S(1)} %get-tuple-element.57, f32[2,1,16,32,128]{4,3,2,1,0:T(8,128)S(1)} %get-tuple-element.56, f32[2,2,16,32,128]{4,3,2,1,0:T(8,128)S(1)} %convolution_bitcast_fusion.3, f32[2,2,16,2,128]{4,3,2,1,0:T(2,128)S(1)} %get-tuple-element.127, ...), kind=kLoop, calls=%fused_computation.163 | loop fusion | flops 9175040 | bytes 4063240 | tf_op jit(solution)/shard_map/mul | solution.py:180
  73.7 3.5 %collective-permute-done.20 = f32[2,2,2,16,2,128]{5,4,3,2,1,0:T(2,128)S(1)} collective-permute-done((f32[2,2,2,16,2,128]{5,4,3,2,1,0:T(2,128)S(1)}, f32[2,2,2,16,2,128]{5,4,3,2,1,0:T(2,128)S(1)}, u32[]{:S(2)}, u32[]{:S(2)}) %collective-permute-start.20) | collective-permute-done | bytes 131104 | tf_op jit(solution)/shard_map/ppermute | solution.py:124
  77.2 1.8 %collective-permute-done.18 = f32[2,2,2,32,128]{4,3,2,1,0:T(8,128)S(1)} collective-permute-done((f32[2,2,2,32,128]{4,3,2,1,0:T(8,128)S(1)}, f32[2,2,2,32,128]{4,3,2,1,0:T(8,128)S(1)}, u32[]{:S(2)}, u32[]{:S(2)}) %collective-permute-start.18) | collective-permute-done | bytes 131104 | tf_op jit(solution)/shard_map/ppermute | solution.py:142
  79.1 2.1 %fusion.53 = f32[2,2,16,32,128]{4,3,2,1,0:T(8,128)S(1)} fusion(f32[2,1,16,32,128]{4,3,2,1,0:T(8,128)S(1)} %get-tuple-element.49, f32[2,1,16,32,128]{4,3,2,1,0:T(8,128)S(1)} %get-tuple-element.48, f32[2,2,16,32,128]{4,3,2,1,0:T(8,128)S(1)} %convolution_bitcast_fusion.2, f32[2,2,16,2,128]{4,3,2,1,0:T(2,128)S(1)} %get-tuple-element.125, ...), kind=kLoop, calls=%fused_computation.168 | loop fusion | flops 9175040 | bytes 4063240 | tf_op jit(solution)/shard_map/mul | solution.py:180
  83.4 1.6 %collective-permute-start.23 = (f32[2,2,2,16,2,128]{5,4,3,2,1,0:T(2,128)S(1)}, f32[2,2,2,16,2,128]{5,4,3,2,1,0:T(2,128)S(1)}, u32[]{:S(2)}, u32[]{:S(2)}) collective-permute-start(f32[2,2,2,16,2,128]{5,4,3,2,1,0:T(2,128)S(1)} %pad_maximum_fusion.41), channel_id=1, source_target_pairs={{0,1},{1,0},{2,3},{3,2},{4,5},{5,4},{6,7},{7,6},{8,9},{9,8},{10,11... | collective-permute-start | bytes 393224 | tf_op jit(solution)/shard_map/ppermute | solution.py:124
  86.0 2.5 %collective-permute-done.23 = f32[2,2,2,16,2,128]{5,4,3,2,1,0:T(2,128)S(1)} collective-permute-done((f32[2,2,2,16,2,128]{5,4,3,2,1,0:T(2,128)S(1)}, f32[2,2,2,16,2,128]{5,4,3,2,1,0:T(2,128)S(1)}, u32[]{:S(2)}, u32[]{:S(2)}) %collective-permute-start.23) | collective-permute-done | bytes 131104 | tf_op jit(solution)/shard_map/ppermute | solution.py:124
  88.5 2.8 %collective-permute-done.21 = f32[2,2,2,32,128]{4,3,2,1,0:T(8,128)S(1)} collective-permute-done((f32[2,2,2,32,128]{4,3,2,1,0:T(8,128)S(1)}, f32[2,2,2,32,128]{4,3,2,1,0:T(8,128)S(1)}, u32[]{:S(2)}, u32[]{:S(2)}) %collective-permute-start.21) | collective-permute-done | bytes 131104 | tf_op jit(solution)/shard_map/ppermute | solution.py:142
  91.3 1.8 %fusion.57 = f32[2,2,16,32,128]{4,3,2,1,0:T(8,128)S(1)} fusion(f32[2,1,16,32,128]{4,3,2,1,0:T(8,128)S(1)} %get-tuple-element.41, f32[2,1,16,32,128]{4,3,2,1,0:T(8,128)S(1)} %get-tuple-element.40, f32[2,2,16,32,128]{4,3,2,1,0:T(8,128)S(1)} %convolution_bitcast_fusion.1, f32[2,2,16,2,128]{4,3,2,1,0:T(2,128)S(1)} %get-tuple-element.123, ...), kind=kLoop, calls=%fused_computation.173 | loop fusion | flops 9175040 | bytes 4063240 | tf_op jit(solution)/shard_map/mul | solution.py:180
  98.4 2.2 %collective-permute-done.26 = f32[2,2,2,16,2,128]{5,4,3,2,1,0:T(2,128)S(1)} collective-permute-done((f32[2,2,2,16,2,128]{5,4,3,2,1,0:T(2,128)S(1)}, f32[2,2,2,16,2,128]{5,4,3,2,1,0:T(2,128)S(1)}, u32[]{:S(2)}, u32[]{:S(2)}) %collective-permute-start.26) | collective-permute-done | bytes 131104 | tf_op jit(solution)/shard_map/ppermute | solution.py:124
  100.6 1.8 %collective-permute-done.24 = f32[2,2,2,32,128]{4,3,2,1,0:T(8,128)S(1)} collective-permute-done((f32[2,2,2,32,128]{4,3,2,1,0:T(8,128)S(1)}, f32[2,2,2,32,128]{4,3,2,1,0:T(8,128)S(1)}, u32[]{:S(2)}, u32[]{:S(2)}) %collective-permute-start.24) | collective-permute-done | bytes 131104 | tf_op jit(solution)/shard_map/ppermute | solution.py:142
  103.5 1.9 %fusion.61 = f32[2,2,16,32,128]{4,3,2,1,0:T(8,128)S(1)} fusion(f32[2,1,16,32,128]{4,3,2,1,0:T(8,128)S(1)} %get-tuple-element.33, f32[2,1,16,32,128]{4,3,2,1,0:T(8,128)S(1)} %get-tuple-element.32, f32[2,2,16,32,128]{4,3,2,1,0:T(8,128)S(1)} %convolution_bitcast_fusion, f32[2,2,16,2,128]{4,3,2,1,0:T(2,128)S(1)} %get-tuple-element.121, ...), kind=kLoop, calls=%fused_computation.178 | loop fusion | flops 9175040 | bytes 4063240 | tf_op jit(solution)/shard_map/mul | solution.py:180
  108.5 4.8 %collective-permute-done.28 = f32[1,2,16,32,128]{4,3,2,1,0:T(8,128)S(1)} collective-permute-done((f32[1,2,16,32,128]{4,3,2,1,0:T(8,128)S(1)}, f32[1,2,16,32,128]{4,3,2,1,0:T(8,128)S(1)}, u32[]{:S(2)}, u32[]{:S(2)}) %collective-permute-start.28) | collective-permute-done | bytes 524320 | tf_op jit(solution)/shard_map/ppermute | solution.py:249
  113.2 3.6 %collective-permute-done.27 = f32[1,2,16,32,128]{4,3,2,1,0:T(8,128)S(1)} collective-permute-done((f32[1,2,16,32,128]{4,3,2,1,0:T(8,128)S(1)}, f32[1,2,16,32,128]{4,3,2,1,0:T(8,128)S(1)}, u32[]{:S(2)}, u32[]{:S(2)}) %collective-permute-start.27) | collective-permute-done | bytes 524320 | tf_op jit(solution)/shard_map/ppermute | solution.py:249
  (137 shorter events, 40.5 us)
Async XLA Ops:
  1.1 10.7 %collective-permute-start = (f32[1,2,2,32,128]{4,3,2,1,0:T(8,128)S(1)}, f32[1,2,2,32,128]{4,3,2,1,0:T(8,128)S(1)}, u32[]{:S(2)}, u32[]{:S(2)}) collective-permute-start(f32[1,2,2,32,128]{4,3,2,1,0:T(8,128)S(1)} %get-tuple-element.98), channel_id=1, source_target_pairs={{16,18},{18,16},{2,4},{4,2},{20,22},{22,20},{6,8},{8,6},{24,26},{2... | collective-permute-start | bytes 196616 | tf_op jit(solution)/shard_map/ppermute | solution.py:142
  5.7 6.2 %collective-permute-start.1 = (f32[1,2,2,32,128]{4,3,2,1,0:T(8,128)S(1)}, f32[1,2,2,32,128]{4,3,2,1,0:T(8,128)S(1)}, u32[]{:S(2)}, u32[]{:S(2)}) collective-permute-start(f32[1,2,2,32,128]{4,3,2,1,0:T(8,128)S(1)} %get-tuple-element.99), channel_id=1, source_target_pairs={{0,16},{16,0},{18,2},{2,18},{4,20},{20,4},{22,6},{6,22},{8,24},{24... | collective-permute-start | bytes 196616 | tf_op jit(solution)/shard_map/ppermute | solution.py:142
  5.7 6.1 %collective-permute-start.2 = (f32[2,1,2,16,2,128]{5,4,3,2,1,0:T(2,128)S(1)}, f32[2,1,2,16,2,128]{5,4,3,2,1,0:T(2,128)S(1)}, u32[]{:S(2)}, u32[]{:S(2)}) collective-permute-start(f32[2,1,2,16,2,128]{5,4,3,2,1,0:T(2,128)S(1)} %pad_maximum_fusion.43), channel_id=1, source_target_pairs={{0,1},{1,0},{2,3},{3,2},{4,5},{5,4},{6,7},{7,6},{8,9},{9,8},{10,11... | collective-permute-start | bytes 196616 | tf_op jit(solution)/shard_map/ppermute | solution.py:124
  7.6 4.3 %copy-start.1 = (f32[2,32,32,128]{3,2,1,0:T(8,128)S(1)}, f32[2,32,32,128]{3,2,1,0:T(8,128)}, u32[]{:S(2)}) copy-start(f32[2,32,32,128]{3,2,1,0:T(8,128)} %param.12) | copy-start | bytes 3145732
  7.6 4.3 %copy-start.3 = (f32[2]{0:T(128)S(1)}, f32[2]{0:T(128)}, u32[]{:S(2)}) copy-start(f32[2]{0:T(128)} %constant.140) | copy-start | bytes 28
  13.7 6.5 %collective-permute-start.3 = (f32[2,2,2,32,128]{4,3,2,1,0:T(8,128)S(1)}, f32[2,2,2,32,128]{4,3,2,1,0:T(8,128)S(1)}, u32[]{:S(2)}, u32[]{:S(2)}) collective-permute-start(f32[2,2,2,32,128]{4,3,2,1,0:T(8,128)S(1)} %get-tuple-element.85), channel_id=1, source_target_pairs={{16,18},{18,16},{2,4},{4,2},{20,22},{22,20},{6,8},{8,6},{24,26},{2... | collective-permute-start | bytes 393224 | tf_op jit(solution)/shard_map/ppermute | solution.py:142
  15.4 5.0 %collective-permute-start.4 = (f32[2,2,2,32,128]{4,3,2,1,0:T(8,128)S(1)}, f32[2,2,2,32,128]{4,3,2,1,0:T(8,128)S(1)}, u32[]{:S(2)}, u32[]{:S(2)}) collective-permute-start(f32[2,2,2,32,128]{4,3,2,1,0:T(8,128)S(1)} %get-tuple-element.84), channel_id=1, source_target_pairs={{0,16},{16,0},{18,2},{2,18},{4,20},{20,4},{22,6},{6,22},{8,24},{24... | collective-permute-start | bytes 393224 | tf_op jit(solution)/shard_map/ppermute | solution.py:142
  16.0 5.6 %collective-permute-start.5 = (f32[2,2,2,16,2,128]{5,4,3,2,1,0:T(2,128)S(1)}, f32[2,2,2,16,2,128]{5,4,3,2,1,0:T(2,128)S(1)}, u32[]{:S(2)}, u32[]{:S(2)}) collective-permute-start(f32[2,2,2,16,2,128]{5,4,3,2,1,0:T(2,128)S(1)} %pad_maximum_fusion.35), channel_id=1, source_target_pairs={{0,1},{1,0},{2,3},{3,2},{4,5},{5,4},{6,7},{7,6},{8,9},{9,8},{10,11... | collective-permute-start | bytes 393224 | tf_op jit(solution)/shard_map/ppermute | solution.py:124
  25.2 5.0 %collective-permute-start.8 = (f32[2,2,2,16,2,128]{5,4,3,2,1,0:T(2,128)S(1)}, f32[2,2,2,16,2,128]{5,4,3,2,1,0:T(2,128)S(1)}, u32[]{:S(2)}, u32[]{:S(2)}) collective-permute-start(f32[2,2,2,16,2,128]{5,4,3,2,1,0:T(2,128)S(1)} %pad_maximum_fusion.36), channel_id=1, source_target_pairs={{0,1},{1,0},{2,3},{3,2},{4,5},{5,4},{6,7},{7,6},{8,9},{9,8},{10,11... | collective-permute-start | bytes 393224 | tf_op jit(solution)/shard_map/ppermute | solution.py:124
  25.8 6.3 %collective-permute-start.6 = (f32[2,2,2,32,128]{4,3,2,1,0:T(8,128)S(1)}, f32[2,2,2,32,128]{4,3,2,1,0:T(8,128)S(1)}, u32[]{:S(2)}, u32[]{:S(2)}) collective-permute-start(f32[2,2,2,32,128]{4,3,2,1,0:T(8,128)S(1)} %get-tuple-element.76), channel_id=1, source_target_pairs={{16,18},{18,16},{2,4},{4,2},{20,22},{22,20},{6,8},{8,6},{24,26},{2... | collective-permute-start | bytes 393224 | tf_op jit(solution)/shard_map/ppermute | solution.py:142
  26.6 5.5 %collective-permute-start.7 = (f32[2,2,2,32,128]{4,3,2,1,0:T(8,128)S(1)}, f32[2,2,2,32,128]{4,3,2,1,0:T(8,128)S(1)}, u32[]{:S(2)}, u32[]{:S(2)}) collective-permute-start(f32[2,2,2,32,128]{4,3,2,1,0:T(8,128)S(1)} %get-tuple-element.77), channel_id=1, source_target_pairs={{0,16},{16,0},{18,2},{2,18},{4,20},{20,4},{22,6},{6,22},{8,24},{24... | collective-permute-start | bytes 393224 | tf_op jit(solution)/shard_map/ppermute | solution.py:142
  36.2 5.0 %collective-permute-start.11 = (f32[2,2,2,16,2,128]{5,4,3,2,1,0:T(2,128)S(1)}, f32[2,2,2,16,2,128]{5,4,3,2,1,0:T(2,128)S(1)}, u32[]{:S(2)}, u32[]{:S(2)}) collective-permute-start(f32[2,2,2,16,2,128]{5,4,3,2,1,0:T(2,128)S(1)} %pad_maximum_fusion.37), channel_id=1, source_target_pairs={{0,1},{1,0},{2,3},{3,2},{4,5},{5,4},{6,7},{7,6},{8,9},{9,8},{10,11... | collective-permute-start | bytes 393224 | tf_op jit(solution)/shard_map/ppermute | solution.py:124
  37.8 5.0 %collective-permute-start.10 = (f32[2,2,2,32,128]{4,3,2,1,0:T(8,128)S(1)}, f32[2,2,2,32,128]{4,3,2,1,0:T(8,128)S(1)}, u32[]{:S(2)}, u32[]{:S(2)}) collective-permute-start(f32[2,2,2,32,128]{4,3,2,1,0:T(8,128)S(1)} %get-tuple-element.69), channel_id=1, source_target_pairs={{0,16},{16,0},{18,2},{2,18},{4,20},{20,4},{22,6},{6,22},{8,24},{24... | collective-permute-start | bytes 393224 | tf_op jit(solution)/shard_map/ppermute | solution.py:142
  38.6 6.2 %collective-permute-start.9 = (f32[2,2,2,32,128]{4,3,2,1,0:T(8,128)S(1)}, f32[2,2,2,32,128]{4,3,2,1,0:T(8,128)S(1)}, u32[]{:S(2)}, u32[]{:S(2)}) collective-permute-start(f32[2,2,2,32,128]{4,3,2,1,0:T(8,128)S(1)} %get-tuple-element.68), channel_id=1, source_target_pairs={{16,18},{18,16},{2,4},{4,2},{20,22},{22,20},{6,8},{8,6},{24,26},{2... | collective-permute-start | bytes 393224 | tf_op jit(solution)/shard_map/ppermute | solution.py:142
  49.1 5.0 %collective-permute-start.14 = (f32[2,2,2,16,2,128]{5,4,3,2,1,0:T(2,128)S(1)}, f32[2,2,2,16,2,128]{5,4,3,2,1,0:T(2,128)S(1)}, u32[]{:S(2)}, u32[]{:S(2)}) collective-permute-start(f32[2,2,2,16,2,128]{5,4,3,2,1,0:T(2,128)S(1)} %pad_maximum_fusion.38), channel_id=1, source_target_pairs={{0,1},{1,0},{2,3},{3,2},{4,5},{5,4},{6,7},{7,6},{8,9},{9,8},{10,11... | collective-permute-start | bytes 393224 | tf_op jit(solution)/shard_map/ppermute | solution.py:124
  49.7 6.3 %collective-permute-start.12 = (f32[2,2,2,32,128]{4,3,2,1,0:T(8,128)S(1)}, f32[2,2,2,32,128]{4,3,2,1,0:T(8,128)S(1)}, u32[]{:S(2)}, u32[]{:S(2)}) collective-permute-start(f32[2,2,2,32,128]{4,3,2,1,0:T(8,128)S(1)} %get-tuple-element.60), channel_id=1, source_target_pairs={{16,18},{18,16},{2,4},{4,2},{20,22},{22,20},{6,8},{8,6},{24,26},{2... | collective-permute-start | bytes 393224 | tf_op jit(solution)/shard_map/ppermute | solution.py:142
  50.5 5.5 %collective-permute-start.13 = (f32[2,2,2,32,128]{4,3,2,1,0:T(8,128)S(1)}, f32[2,2,2,32,128]{4,3,2,1,0:T(8,128)S(1)}, u32[]{:S(2)}, u32[]{:S(2)}) collective-permute-start(f32[2,2,2,32,128]{4,3,2,1,0:T(8,128)S(1)} %get-tuple-element.61), channel_id=1, source_target_pairs={{0,16},{16,0},{18,2},{2,18},{4,20},{20,4},{22,6},{6,22},{8,24},{24... | collective-permute-start | bytes 393224 | tf_op jit(solution)/shard_map/ppermute | solution.py:142
  60.2 5.0 %collective-permute-start.17 = (f32[2,2,2,16,2,128]{5,4,3,2,1,0:T(2,128)S(1)}, f32[2,2,2,16,2,128]{5,4,3,2,1,0:T(2,128)S(1)}, u32[]{:S(2)}, u32[]{:S(2)}) collective-permute-start(f32[2,2,2,16,2,128]{5,4,3,2,1,0:T(2,128)S(1)} %pad_maximum_fusion.39), channel_id=1, source_target_pairs={{0,1},{1,0},{2,3},{3,2},{4,5},{5,4},{6,7},{7,6},{8,9},{9,8},{10,11... | collective-permute-start | bytes 393224 | tf_op jit(solution)/shard_map/ppermute | solution.py:124
  61.8 6.3 %collective-permute-start.15 = (f32[2,2,2,32,128]{4,3,2,1,0:T(8,128)S(1)}, f32[2,2,2,32,128]{4,3,2,1,0:T(8,128)S(1)}, u32[]{:S(2)}, u32[]{:S(2)}) collective-permute-start(f32[2,2,2,32,128]{4,3,2,1,0:T(8,128)S(1)} %get-tuple-element.52), channel_id=1, source_target_pairs={{16,18},{18,16},{2,4},{4,2},{20,22},{22,20},{6,8},{8,6},{24,26},{2... | collective-permute-start | bytes 393224 | tf_op jit(solution)/shard_map/ppermute | solution.py:142
  62.7 5.3 %collective-permute-start.16 = (f32[2,2,2,32,128]{4,3,2,1,0:T(8,128)S(1)}, f32[2,2,2,32,128]{4,3,2,1,0:T(8,128)S(1)}, u32[]{:S(2)}, u32[]{:S(2)}) collective-permute-start(f32[2,2,2,32,128]{4,3,2,1,0:T(8,128)S(1)} %get-tuple-element.53), channel_id=1, source_target_pairs={{0,16},{16,0},{18,2},{2,18},{4,20},{20,4},{22,6},{6,22},{8,24},{24... | collective-permute-start | bytes 393224 | tf_op jit(solution)/shard_map/ppermute | solution.py:142
  72.2 5.0 %collective-permute-start.20 = (f32[2,2,2,16,2,128]{5,4,3,2,1,0:T(2,128)S(1)}, f32[2,2,2,16,2,128]{5,4,3,2,1,0:T(2,128)S(1)}, u32[]{:S(2)}, u32[]{:S(2)}) collective-permute-start(f32[2,2,2,16,2,128]{5,4,3,2,1,0:T(2,128)S(1)} %pad_maximum_fusion.40), channel_id=1, source_target_pairs={{0,1},{1,0},{2,3},{3,2},{4,5},{5,4},{6,7},{7,6},{8,9},{9,8},{10,11... | collective-permute-start | bytes 393224 | tf_op jit(solution)/shard_map/ppermute | solution.py:124
  72.8 6.3 %collective-permute-start.18 = (f32[2,2,2,32,128]{4,3,2,1,0:T(8,128)S(1)}, f32[2,2,2,32,128]{4,3,2,1,0:T(8,128)S(1)}, u32[]{:S(2)}, u32[]{:S(2)}) collective-permute-start(f32[2,2,2,32,128]{4,3,2,1,0:T(8,128)S(1)} %get-tuple-element.44), channel_id=1, source_target_pairs={{16,18},{18,16},{2,4},{4,2},{20,22},{22,20},{6,8},{8,6},{24,26},{2... | collective-permute-start | bytes 393224 | tf_op jit(solution)/shard_map/ppermute | solution.py:142
  73.7 5.3 %collective-permute-start.19 = (f32[2,2,2,32,128]{4,3,2,1,0:T(8,128)S(1)}, f32[2,2,2,32,128]{4,3,2,1,0:T(8,128)S(1)}, u32[]{:S(2)}, u32[]{:S(2)}) collective-permute-start(f32[2,2,2,32,128]{4,3,2,1,0:T(8,128)S(1)} %get-tuple-element.45), channel_id=1, source_target_pairs={{0,16},{16,0},{18,2},{2,18},{4,20},{20,4},{22,6},{6,22},{8,24},{24... | collective-permute-start | bytes 393224 | tf_op jit(solution)/shard_map/ppermute | solution.py:142
  83.4 5.0 %collective-permute-start.23 = (f32[2,2,2,16,2,128]{5,4,3,2,1,0:T(2,128)S(1)}, f32[2,2,2,16,2,128]{5,4,3,2,1,0:T(2,128)S(1)}, u32[]{:S(2)}, u32[]{:S(2)}) collective-permute-start(f32[2,2,2,16,2,128]{5,4,3,2,1,0:T(2,128)S(1)} %pad_maximum_fusion.41), channel_id=1, source_target_pairs={{0,1},{1,0},{2,3},{3,2},{4,5},{5,4},{6,7},{7,6},{8,9},{9,8},{10,11... | collective-permute-start | bytes 393224 | tf_op jit(solution)/shard_map/ppermute | solution.py:124
  85.0 6.3 %collective-permute-start.21 = (f32[2,2,2,32,128]{4,3,2,1,0:T(8,128)S(1)}, f32[2,2,2,32,128]{4,3,2,1,0:T(8,128)S(1)}, u32[]{:S(2)}, u32[]{:S(2)}) collective-permute-start(f32[2,2,2,32,128]{4,3,2,1,0:T(8,128)S(1)} %get-tuple-element.36), channel_id=1, source_target_pairs={{16,18},{18,16},{2,4},{4,2},{20,22},{22,20},{6,8},{8,6},{24,26},{2... | collective-permute-start | bytes 393224 | tf_op jit(solution)/shard_map/ppermute | solution.py:142
  86.0 5.3 %collective-permute-start.22 = (f32[2,2,2,32,128]{4,3,2,1,0:T(8,128)S(1)}, f32[2,2,2,32,128]{4,3,2,1,0:T(8,128)S(1)}, u32[]{:S(2)}, u32[]{:S(2)}) collective-permute-start(f32[2,2,2,32,128]{4,3,2,1,0:T(8,128)S(1)} %get-tuple-element.37), channel_id=1, source_target_pairs={{0,16},{16,0},{18,2},{2,18},{4,20},{20,4},{22,6},{6,22},{8,24},{24... | collective-permute-start | bytes 393224 | tf_op jit(solution)/shard_map/ppermute | solution.py:142
  95.6 5.0 %collective-permute-start.26 = (f32[2,2,2,16,2,128]{5,4,3,2,1,0:T(2,128)S(1)}, f32[2,2,2,16,2,128]{5,4,3,2,1,0:T(2,128)S(1)}, u32[]{:S(2)}, u32[]{:S(2)}) collective-permute-start(f32[2,2,2,16,2,128]{5,4,3,2,1,0:T(2,128)S(1)} %pad_maximum_fusion.42), channel_id=1, source_target_pairs={{0,1},{1,0},{2,3},{3,2},{4,5},{5,4},{6,7},{7,6},{8,9},{9,8},{10,11... | collective-permute-start | bytes 393224 | tf_op jit(solution)/shard_map/ppermute | solution.py:124
  96.2 6.3 %collective-permute-start.24 = (f32[2,2,2,32,128]{4,3,2,1,0:T(8,128)S(1)}, f32[2,2,2,32,128]{4,3,2,1,0:T(8,128)S(1)}, u32[]{:S(2)}, u32[]{:S(2)}) collective-permute-start(f32[2,2,2,32,128]{4,3,2,1,0:T(8,128)S(1)} %get-tuple-element.28), channel_id=1, source_target_pairs={{16,18},{18,16},{2,4},{4,2},{20,22},{22,20},{6,8},{8,6},{24,26},{2... | collective-permute-start | bytes 393224 | tf_op jit(solution)/shard_map/ppermute | solution.py:142
  97.1 6.4 %collective-permute-start.25 = (f32[2,2,2,32,128]{4,3,2,1,0:T(8,128)S(1)}, f32[2,2,2,32,128]{4,3,2,1,0:T(8,128)S(1)}, u32[]{:S(2)}, u32[]{:S(2)}) collective-permute-start(f32[2,2,2,32,128]{4,3,2,1,0:T(8,128)S(1)} %get-tuple-element.29), channel_id=1, source_target_pairs={{0,16},{16,0},{18,2},{2,18},{4,20},{20,4},{22,6},{6,22},{8,24},{24... | collective-permute-start | bytes 393224 | tf_op jit(solution)/shard_map/ppermute | solution.py:142
  97.1 16.1 %collective-permute-start.28 = (f32[1,2,16,32,128]{4,3,2,1,0:T(8,128)S(1)}, f32[1,2,16,32,128]{4,3,2,1,0:T(8,128)S(1)}, u32[]{:S(2)}, u32[]{:S(2)}) collective-permute-start(f32[1,2,16,32,128]{4,3,2,1,0:T(8,128)S(1)} %slice.1158), channel_id=1, source_target_pairs={{16,0},{17,1},{18,2},{19,3},{20,4},{21,5},{22,6},{23,7},{24,8},{25... | collective-permute-start | bytes 1572872 | tf_op jit(solution)/shard_map/ppermute | solution.py:249
  106.7 10.1 %collective-permute-start.27 = (f32[1,2,16,32,128]{4,3,2,1,0:T(8,128)S(1)}, f32[1,2,16,32,128]{4,3,2,1,0:T(8,128)S(1)}, u32[]{:S(2)}, u32[]{:S(2)}) collective-permute-start(f32[1,2,16,32,128]{4,3,2,1,0:T(8,128)S(1)} %convolution_bitcast_fusion.7), channel_id=1, source_target_pairs={{0,16},{1,17},{2,18},{3,19},{4,20},{5,21},{6,22},{7,23},{8,24},{9,... | collective-permute-start | bytes 1572872 | tf_op jit(solution)/shard_map/ppermute | solution.py:249
  108.4 8.4 %copy-start.2 = (f32[1,2,32,32,128]{4,3,2,1,0:T(8,128)}, f32[1,2,32,32,128]{4,3,2,1,0:T(8,128)S(1)}, u32[]{:S(2)}) copy-start(f32[1,2,32,32,128]{4,3,2,1,0:T(8,128)S(1)} %fusion.67) | copy-start | bytes 3145732
  (2 other events, 4.2 us)
